TPU v7x, 512 devices: a whole 4x8x8 slice. The times are simulated.
512 devices in a mesh: lat: 4 (over x_lo, core), lon: 128 (over y, z, x_hi).
Axes of the slice: x: 4 (x_hi: 2, x_lo: 2; x = x_hi * 2 + x_lo), y: 8, z: 8, core: 2. Of those that a mesh axis runs over, the one named last changes fastest.
Arguments:
- moisture: float32 [32, 128, 32768], P(None, 'lat', 'lon'), may hold values from 0.05 to 0.45
- conductance: float32 [128, 32768], P('lat', 'lon'), may hold values from 0.08 to 0.24
- inverse: float32 [128, 256, 1024], P('lat', 'lon'), may hold values from -1 to 1, as said below
- crop_mask: int32 [128, 32768], P('lat', 'lon'), may hold values 0 or 1
- adjoint_in: float32 [32, 128, 32768], P(None, 'lat', 'lon'), may hold values from -6 to 6
- foot_anchor: int32 [4, 128, 128, 2], P('lat', 'lon'), may hold values from -1 to 6384, as said below
- antenna_gain: float32 [4, 128, 128, 2, 512], P('lat', 'lon'), may hold values from -0.25 to 0.25
- obs_value: float32 [4, 128, 128, 2], P('lat', 'lon'), may hold values from -6 to 6
- obs_weight: float32 [4, 128, 128, 2], P('lat', 'lon'), may hold values from 0.5 to 5
Outputs:
- gradient: float32 [32, 128, 32768], P(None, 'lat', 'lon')
- residual: float32 [4, 128, 128, 2], P('lat', 'lon')
Inputs may be any that keep to these rules, and one draw needn't show every extreme that they name: `foot_anchor`: every live window lies inside its tile; some owner column receives all 2 slots live from every tile; some tiles fill all their slots. `inverse`: each matrix has a positive diagonal of 0.6 to 1.
All inputs are finite; a program needn't handle non-finite values. No bound on the sum of `crop_mask` on one device may be relied on, other than what follows from the above.
Results may differ from a plain program's by a relative error of at most 0.00005.
Values sent between devices are 32-bit elements; how exact they have to be, the bound alone decides.
No kernel may reach another device: no remote copies, remote signals or barrier semaphores. Data moves between devices by JAX's collectives and lax.ppermute only.
A program may use at most 64 MiB of HBM per device.

v0:
```python
import jax
import jax.numpy as jnp
from jax import lax
from jax.experimental import pallas as pl
from jax.experimental.pallas import tpu as pltpu
from jax.sharding import PartitionSpec as P

LG = 8
LTOP = 4
FH = 8
FW = 16
K = 512
LANES = 128


def neighbours(block, axis, dim):
    count = lax.axis_size(axis)
    forward = [(i, i + 1) for i in range(count - 1)]
    backward = [(target, source) for source, target in forward]
    size = block.shape[dim]
    low = lax.ppermute(lax.slice_in_dim(block, size - 1, size, axis=dim), axis, forward)
    high = lax.ppermute(lax.slice_in_dim(block, 0, 1, axis=dim), axis, backward)
    return low, high


def stencil(block):
    up, down = neighbours(block, "lat", 1)
    left, right = neighbours(block, "lon", 2)
    rows = block.shape[1]
    cols = block.shape[2]
    north = jnp.concatenate([up, lax.slice_in_dim(block, 0, rows - 1, axis=1)], 1)
    south = jnp.concatenate([lax.slice_in_dim(block, 1, rows, axis=1), down], 1)
    west = jnp.concatenate([left, lax.slice_in_dim(block, 0, cols - 1, axis=2)], 2)
    east = jnp.concatenate([lax.slice_in_dim(block, 1, cols, axis=2), right], 2)
    return north + south + west + east - 4.0 * block


def columns(matrices, field, transpose):
    levels, height, breadth = field.shape
    blocks = matrices.shape[1]
    grouped = field.reshape(levels, height, blocks, breadth // blocks)
    form = "rbji,jrbc->irbc" if transpose else "rbij,jrbc->irbc"
    out = jnp.einsum(form, matrices, grouped, precision=lax.Precision.HIGHEST)
    return out.reshape(out.shape[0], height, breadth)


def slot_place(anchor_ref, s, tile_rows, tile_cols):
    o = jnp.maximum(anchor_ref[s], 0)
    r = jnp.minimum(o // tile_cols, tile_rows - FH)
    c = jnp.minimum(o % tile_cols, tile_cols - FW)
    g0 = pl.multiple_of(jnp.minimum(r // FH, tile_rows // FH - 2) * FH, FH)
    return g0, r - g0, c


def placed_gain(gain_ref, s, off, c, tile_cols):
    g = gain_ref[s]
    g = pltpu.roll(g, off % FH, 1)
    g = pltpu.roll(g, c % LANES, 2)
    g = jnp.concatenate([g, g], axis=1)
    g = jnp.concatenate([g] * (tile_cols // LANES), axis=2)
    row = lax.broadcasted_iota(jnp.int32, g.shape, 1)
    lane = lax.broadcasted_iota(jnp.int32, g.shape, 2)
    inside = (row >= off) & (row < off + FH) & (lane >= c) & (lane < c + FW)
    return jnp.where(inside, g, 0.0)


def predict_kernel(anchor_ref, top_ref, gain_ref, out_ref):
    _, tile_rows, tile_cols = top_ref.shape
    slots = gain_ref.shape[0]

    def body(s, carry):
        g0, off, c = slot_place(anchor_ref, s, tile_rows, tile_cols)
        g = placed_gain(gain_ref, s, off, c, tile_cols)
        t = top_ref[:, pl.ds(g0, 2 * FH), :]
        part = jnp.sum(g * t, axis=0)
        part = part[:FH] + part[FH:]
        acc = part[:, 0:LANES]
        for q in range(1, tile_cols // LANES):
            acc = acc + part[:, q * LANES:(q + 1) * LANES]
        out_ref[s] = acc
        return carry

    lax.fori_loop(0, slots, body, 0, unroll=4)


def scatter_kernel(anchor_ref, res_ref, gain_ref, out_ref):
    _, tile_rows, tile_cols = out_ref.shape
    slots = gain_ref.shape[0]
    out_ref[...] = jnp.zeros(out_ref.shape, out_ref.dtype)

    def body(s, carry):
        g0, off, c = slot_place(anchor_ref, s, tile_rows, tile_cols)
        g = placed_gain(gain_ref, s, off, c, tile_cols)
        out_ref[:, pl.ds(g0, 2 * FH), :] += res_ref[s] * g
        return carry

    lax.fori_loop(0, slots, body, 0, unroll=4)


def predict(anchor, top, gain):
    slots = gain.shape[0]
    return pl.pallas_call(
        predict_kernel,
        out_shape=jax.ShapeDtypeStruct((slots, FH, LANES), jnp.float32),
        in_specs=[
            pl.BlockSpec(memory_space=pltpu.SMEM),
            pl.BlockSpec(memory_space=pltpu.VMEM),
            pl.BlockSpec(memory_space=pltpu.VMEM),
        ],
        out_specs=pl.BlockSpec(memory_space=pltpu.VMEM),
    )(anchor, top, gain)


def scatter(anchor, res, gain, top_shape):
    return pl.pallas_call(
        scatter_kernel,
        out_shape=jax.ShapeDtypeStruct(top_shape, jnp.float32),
        in_specs=[
            pl.BlockSpec(memory_space=pltpu.SMEM),
            pl.BlockSpec(memory_space=pltpu.SMEM),
            pl.BlockSpec(memory_space=pltpu.VMEM),
        ],
        out_specs=pl.BlockSpec(memory_space=pltpu.VMEM),
    )(anchor, res, gain)


def per_device(
    moisture,
    conductance,
    inverse,
    crop_mask,
    adjoint_in,
    foot_anchor,
    antenna_gain,
    obs_value,
    obs_weight,
):
    levels, tile_rows, tile_cols = moisture.shape
    mask_float = crop_mask.astype(jnp.float32)
    blocks = inverse.shape[1]
    matrices = inverse.reshape(tile_rows, blocks, levels, levels)

    owner_gain = antenna_gain[0, 0]
    owners, slots_per, _ = owner_gain.shape
    packed = jnp.concatenate(
        [owner_gain, obs_value[0, 0][..., None], obs_weight[0, 0][..., None]], -1
    )
    received = lax.all_to_all(packed, "lon", split_axis=0, concat_axis=0, tiled=True)
    slots = owners * slots_per
    gain = received[..., :K].reshape(slots, LTOP, FH, FW)
    gain = jnp.pad(gain, ((0, 0), (0, 0), (0, 0), (0, LANES - FW)))
    value = received[..., K].reshape(slots)
    weight = received[..., K + 1].reshape(slots)

    deep = moisture[levels - LG :]
    mixed = jnp.concatenate(
        [moisture[: levels - LG], deep + conductance * stencil(deep)], 0
    )
    solved_top = columns(matrices[:, :, :LTOP, :], mixed, False)
    topmost = solved_top * mask_float

    slot_anchor = foot_anchor[0, 0].reshape(slots)
    live = (slot_anchor >= 0).astype(jnp.float32)
    parts = predict(slot_anchor, topmost, gain)
    predicted = jnp.sum(parts, axis=(1, 2))
    residual = live * weight * (predicted - value)
    residual_out = lax.all_to_all(
        residual.reshape(owners, slots_per), "lon", split_axis=0, concat_axis=0, tiled=True
    )

    base = columns(matrices, adjoint_in, True)
    topbar = scatter(slot_anchor, residual, gain, topmost.shape) * mask_float
    mixedbar = base + columns(matrices[:, :, :LTOP, :], topbar, True)
    deepbar = mixedbar[levels - LG :]
    gradient = jnp.concatenate(
        [mixedbar[: levels - LG], deepbar + stencil(conductance * deepbar)], 0
    )
    return gradient, residual_out[None, None]


def solution(mesh):
    in_specs = (
        P(None, "lat", "lon"),
        P("lat", "lon"),
        P("lat", "lon", None),
        P("lat", "lon"),
        P(None, "lat", "lon"),
        P("lat", "lon", None, None),
        P("lat", "lon", None, None, None),
        P("lat", "lon", None, None),
        P("lat", "lon", None, None),
    )
    out_specs = (P(None, "lat", "lon"), P("lat", "lon", None, None))
    return jax.shard_map(
        per_device, mesh=mesh, in_specs=in_specs, out_specs=out_specs, check_vma=False
    )
```

profile of v0, /device:TPU:2, one launch (start us, length us, event | category | flops | bytes accessed | tf_op | source)
XLA Modules:
  0.0 148.8 jit_solution(16317696959983482175)
XLA Ops:
  0.6 0.0 copy-start
  0.6 1.8 %fusion.19 = (f32[8,32,1]{2,1,0:T(8,128)}, f32[8,32,1]{2,1,0:T(8,128)}) fusion(f32[32,32,256]{2,1,0:T(8,128)} %param.9), kind=kLoop, calls=%fused_computation.32 | loop fusion | bytes 4096 | tf_op jit(solution)/shard_map/slice | solution.py:22
  2.5 4.7 %collective-permute-start.2 = (f32[8,32,1]{2,1,0:T(8,128)}, f32[8,32,1]{2,1,0:T(8,128)}, u32[]{:S(2)}, u32[]{:S(2)}) collective-permute-start(f32[8,32,1]{2,1,0:T(8,128)} %get-tuple-element.9), channel_id=1, source_target_pairs={{0,1},{1,2},{2,3},{3,4},{4,5},{5,6},{6,7},{7,8},{8,9},{9,10},{10,1... | collective-permute-start | bytes 3080 | tf_op jit(solution)/shard_map/ppermute | solution.py:21
  7.1 1.3 collective-permute-start.3
  8.4 1.5 fusion.21
  9.9 1.9 %collective-permute-start = (f32[8,1,256]{2,1,0:T(1,128)}, f32[8,1,256]{2,1,0:T(1,128)S(1)}, u32[]{:S(2)}, u32[]{:S(2)}) collective-permute-start(f32[8,1,256]{2,1,0:T(1,128)} %get-tuple-element.13), channel_id=1, source_target_pairs={{0,128},{128,256},{256,384},{1,129},{129,257},{257,385},{2,130},{1... | collective-permute-start | bytes 24584 | tf_op jit(solution)/shard_map/ppermute | solution.py:21
  11.8 3.6 %collective-permute-start.1 = (f32[8,1,256]{2,1,0:T(1,128)}, f32[8,1,256]{2,1,0:T(1,128)S(1)}, u32[]{:S(2)}, u32[]{:S(2)}) collective-permute-start(f32[8,1,256]{2,1,0:T(1,128)} %get-tuple-element.12), channel_id=1, source_target_pairs={{128,0},{256,128},{384,256},{129,1},{257,129},{385,257},{130,2},{2... | collective-permute-start | bytes 24584 | tf_op jit(solution)/shard_map/ppermute | solution.py:22
  15.5 1.3 copy.34
  16.8 0.9 pad_maximum_fusion.2
  17.7 0.0 copy-start.2
  17.7 1.4 copy.35
  19.1 21.9 %all-to-all-start = ((f32[128,2,514]{2,1,0:T(2,128)}), f32[128,2,514]{2,1,0:T(2,128)}, u32[]{:S(2)}, u32[]{:S(2)}) async-start(f32[128,2,514]{2,1,0:T(2,128)} %copy.35), calls=%async_computation | async-start | bytes 1310720 | tf_op jit(solution)/shard_map/all_to_all | solution.py:148
  41.0 0.7 fusion.20
  41.8 1.4 reshape.80
  43.2 0.0 copy-start.8
  43.2 1.5 reshape.79
  44.7 4.6 %fusion.2 = f32[32,2,128,32]{2,3,1,0:T(8,128)} fusion(f32[32,2,32,32]{3,2,1,0:T(8,128)S(1)} %reshape.80, f32[32,32,2,128]{3,2,1,0:T(2,128)} %reshape.79), kind=kOutput, calls=%fused_computation.6 | convolution fusion | flops 100663296 | bytes 2359296 | tf_op jit(solution)/shard_map/rbji,jrbc->irbc/dot_general | solution.py:43
  49.3 0.9 fusion.18
  50.2 0.8 copy.33
  51.0 0.7 reshape_squeeze.13.anchor_ref
  51.8 1.4 fusion.8
  53.2 0.1 pad_maximum_fusion
  53.3 0.5 reshape.81
  53.8 1.6 %convolution_bitcast_fusion = f32[4,32,2,128]{3,0,2,1:T(4,128)S(1)} fusion(f32[32,32,2,128]{3,2,1,0:T(2,128)S(1)} %reshape.81, f32[32,2,32,32]{3,2,1,0:T(8,128)S(1)} %reshape.80), kind=kOutput, calls=%fused_computation.2 | convolution fusion | flops 12582912 | bytes 1310720 | tf_op jit(solution)/shard_map/rbij,jrbc->irbc/dot_general | solution.py:43
  55.4 0.1 copy.38
  55.5 0.1 reshape.82
  55.6 0.7 broadcast_multiply_fusion.2.top_ref
  56.3 7.1 %all-to-all-done = f32[128,2,514]{2,1,0:T(2,128)} async-done(((f32[128,2,514]{2,1,0:T(2,128)}), f32[128,2,514]{2,1,0:T(2,128)}, u32[]{:S(2)}, u32[]{:S(2)}) %all-to-all-start) | async-done | bytes 526368 | tf_op jit(solution)/shard_map/all_to_all | solution.py:148
  63.4 1.1 slice.115
  64.5 2.9 %reshape.83 = f32[256,4,8,16]{3,2,1,0:T(8,128)} reshape(f32[128,2,512]{2,1,0:T(2,128)S(1)} %slice.115) | data formatting | bytes 1048576 | tf_op jit(solution)/shard_map/reshape | solution.py:150
  67.3 4.6 %pad.4.gain_ref = f32[256,4,8,128]{3,2,1,0:T(8,128)} pad(f32[256,4,8,16]{3,2,1,0:T(8,128)} %reshape.83, f32[]{:T(128)} %constant.2.clone.1), padding=0_0x0_0x0_0x0_112 | pad | bytes 4718596 | tf_op jit(solution)/shard_map/jit(_pad)/pad | solution.py:151
  72.0 12.7 %shard_map.104 = f32[256,8,128]{2,1,0:T(8,128)} custom-call(s32[256]{0:T(256)} %reshape_squeeze.13.anchor_ref, f32[4,32,256]{2,1,0:T(8,128)} %broadcast_multiply_fusion.2.top_ref, f32[256,4,8,128]{3,2,1,0:T(8,128)} %pad.4.gain_ref), custom_call_target="tpu_custom_call" | custom-call | tf_op jit(solution)/shard_map/pallas_call | solution.py:102
  84.7 2.3 %reduce_sum.11 = f32[256]{0:T(256)S(1)} reduce(f32[256,8,128]{2,1,0:T(8,128)} %shard_map.104, f32[]{:T(128)} %constant.2.clone.1), dimensions={1,2}, to_apply=%region_0.1 | reduce | flops 261888 | bytes 1049604 | tf_op jit(solution)/shard_map/reduce_sum | solution.py:165
  87.0 1.2 fusion.22
  88.2 0.9 copy.47
  89.0 0.1 reshape_squeeze.14
  89.2 0.9 copy.48
  90.0 0.1 reshape_squeeze.15
  90.2 0.6 fusion.17.res_ref
  90.8 12.1 %shard_map.105 = f32[4,32,256]{2,1,0:T(8,128)} custom-call(s32[256]{0:T(256)} %reshape_squeeze.13.anchor_ref, f32[256]{0:T(256)} %fusion.17.res_ref, f32[256,4,8,128]{3,2,1,0:T(8,128)} %pad.4.gain_ref), custom_call_target="tpu_custom_call" | custom-call | tf_op jit(solution)/shard_map/pallas_call | solution.py:115
  102.9 0.9 broadcast_multiply_fusion.1
  103.8 0.1 reshape.84
  103.9 1.8 %fusion = f32[32,32,2,128]{3,0,2,1:T(8,128)S(1)} fusion(f32[32,2,128,32]{2,3,1,0:T(8,128)S(1)} %copy-done.1, f32[4,32,2,128]{3,2,1,0:T(2,128)S(1)} %reshape.84, f32[32,2,32,32]{3,2,1,0:T(8,128)S(1)} %reshape.80), kind=kOutput, calls=%fused_computation.1 | convolution fusion | flops 12845056 | bytes 2359296 | tf_op jit(solution)/shard_map/rbji,jrbc->irbc/dot_general | solution.py:43
  105.8 0.1 copy.42
  105.9 0.2 slice.104
  106.2 0.8 broadcast_multiply_fusion
  107.0 0.1 fusion.23
  107.1 0.8 fusion.24
  107.9 0.6 fusion.26
  108.5 0.1 reduce_sum.12
  108.6 4.0 %collective-permute-start.6 = (f32[8,32,1]{2,1,0:T(8,128)}, f32[8,32,1]{2,1,0:T(8,128)}, u32[]{:S(2)}, u32[]{:S(2)}) collective-permute-start(f32[8,32,1]{2,1,0:T(8,128)} %get-tuple-element.19), channel_id=1, source_target_pairs={{0,1},{1,2},{2,3},{3,4},{4,5},{5,6},{6,7},{7,8},{8,9},{9,10},{10,1... | collective-permute-start | bytes 3080 | tf_op jit(solution)/shard_map/ppermute | solution.py:21
  112.6 1.3 collective-permute-start.7
  113.9 1.9 %collective-permute-start.4 = (f32[8,1,256]{2,1,0:T(1,128)}, f32[8,1,256]{2,1,0:T(1,128)S(1)}, u32[]{:S(2)}, u32[]{:S(2)}) collective-permute-start(f32[8,1,256]{2,1,0:T(1,128)} %get-tuple-element.23), channel_id=1, source_target_pairs={{0,128},{128,256},{256,384},{1,129},{129,257},{257,385},{2,130},{1... | collective-permute-start | bytes 24584 | tf_op jit(solution)/shard_map/ppermute | solution.py:21
  115.8 3.6 %collective-permute-start.5 = (f32[8,1,256]{2,1,0:T(1,128)}, f32[8,1,256]{2,1,0:T(1,128)S(1)}, u32[]{:S(2)}, u32[]{:S(2)}) collective-permute-start(f32[8,1,256]{2,1,0:T(1,128)} %get-tuple-element.22), channel_id=1, source_target_pairs={{128,0},{256,128},{384,256},{129,1},{257,129},{385,257},{130,2},{2... | collective-permute-start | bytes 24584 | tf_op jit(solution)/shard_map/ppermute | solution.py:22
  119.5 1.5 fusion.16
  121.0 11.5 %all-to-all-start.1 = ((f32[128,1,2]{2,1,0:T(1,128)}), f32[128,1,2]{2,1,0:T(1,128)S(1)}, u32[]{:S(2)}, u32[]{:S(2)}) async-start(f32[128,1,2]{2,1,0:T(1,128)} %bitcast.8), calls=%async_computation.1 | async-start | bytes 131072 | tf_op jit(solution)/shard_map/all_to_all | solution.py:167
  132.5 0.8 fusion.25
  133.3 0.1 slice.117
  133.4 0.4 copy.41
  133.8 0.6 slice.102
  134.4 11.4 %all-to-all-done.1 = f32[128,1,2]{2,1,0:T(1,128)S(1)} async-done(((f32[128,1,2]{2,1,0:T(1,128)}), f32[128,1,2]{2,1,0:T(1,128)S(1)}, u32[]{:S(2)}, u32[]{:S(2)}) %all-to-all-start.1) | async-done | bytes 1056 | tf_op jit(solution)/shard_map/all_to_all | solution.py:167
  145.8 0.6 copy.45
  146.5 1.3 fusion.12
  147.8 1.0 pad_maximum_fusion.1
  (29 shorter events, 0.1 us)
Async XLA Ops:
  0.6 40.4 %copy-start = (f32[32,32,256]{2,1,0:T(8,128)S(1)}, f32[32,32,256]{2,1,0:T(8,128)}, u32[]{:S(2)}) copy-start(f32[32,32,256]{2,1,0:T(8,128)} %param.9) | copy-start | bytes 3145732
  2.5 49.3 %collective-permute-start.2 = (f32[8,32,1]{2,1,0:T(8,128)}, f32[8,32,1]{2,1,0:T(8,128)}, u32[]{:S(2)}, u32[]{:S(2)}) collective-permute-start(f32[8,32,1]{2,1,0:T(8,128)} %get-tuple-element.9), channel_id=1, source_target_pairs={{0,1},{1,2},{2,3},{3,4},{4,5},{5,6},{6,7},{7,8},{8,9},{9,10},{10,1... | collective-permute-start | bytes 3080 | tf_op jit(solution)/shard_map/ppermute | solution.py:21
  7.1 44.6 %collective-permute-start.3 = (f32[8,32,1]{2,1,0:T(8,128)}, f32[8,32,1]{2,1,0:T(8,128)}, u32[]{:S(2)}, u32[]{:S(2)}) collective-permute-start(f32[8,32,1]{2,1,0:T(8,128)} %get-tuple-element.8), channel_id=1, source_target_pairs={{1,0},{2,1},{3,2},{4,3},{5,4},{6,5},{7,6},{8,7},{9,8},{10,9},{11,1... | collective-permute-start | bytes 3080 | tf_op jit(solution)/shard_map/ppermute | solution.py:22
  9.9 41.8 %collective-permute-start = (f32[8,1,256]{2,1,0:T(1,128)}, f32[8,1,256]{2,1,0:T(1,128)S(1)}, u32[]{:S(2)}, u32[]{:S(2)}) collective-permute-start(f32[8,1,256]{2,1,0:T(1,128)} %get-tuple-element.13), channel_id=1, source_target_pairs={{0,128},{128,256},{256,384},{1,129},{129,257},{257,385},{2,130},{1... | collective-permute-start | bytes 24584 | tf_op jit(solution)/shard_map/ppermute | solution.py:21
  11.8 39.9 %collective-permute-start.1 = (f32[8,1,256]{2,1,0:T(1,128)}, f32[8,1,256]{2,1,0:T(1,128)S(1)}, u32[]{:S(2)}, u32[]{:S(2)}) collective-permute-start(f32[8,1,256]{2,1,0:T(1,128)} %get-tuple-element.12), channel_id=1, source_target_pairs={{128,0},{256,128},{384,256},{129,1},{257,129},{385,257},{130,2},{2... | collective-permute-start | bytes 24584 | tf_op jit(solution)/shard_map/ppermute | solution.py:22
  17.7 25.5 %copy-start.2 = (f32[32,32,256]{2,1,0:T(8,128)S(1)}, f32[32,32,256]{2,1,0:T(8,128)}, u32[]{:S(2)}) copy-start(f32[32,32,256]{2,1,0:T(8,128)} %param.13) | copy-start | bytes 3145732
  19.1 44.3 %all-to-all-start = ((f32[128,2,514]{2,1,0:T(2,128)}), f32[128,2,514]{2,1,0:T(2,128)}, u32[]{:S(2)}, u32[]{:S(2)}) async-start(f32[128,2,514]{2,1,0:T(2,128)} %copy.35), calls=%async_computation | async-start | bytes 1310720 | tf_op jit(solution)/shard_map/all_to_all | solution.py:148
  43.2 7.0 %copy-start.8 = (s32[32,256]{1,0:T(8,128)S(1)}, s32[32,256]{1,0:T(8,128)}, u32[]{:S(2)}) copy-start(s32[32,256]{1,0:T(8,128)} %param.12) | copy-start | bytes 98308
  43.2 8.6 %copy-start.5 = (f32[32,256]{1,0:T(8,128)S(1)}, f32[32,256]{1,0:T(8,128)}, u32[]{:S(2)}) copy-start(f32[32,256]{1,0:T(8,128)} %param.10) | copy-start | bytes 98308
  44.7 7.1 %copy-start.3 = (f32[8,31,256]{2,1,0:T(8,128)S(1)}, f32[8,31,256]{2,1,0:T(8,128)}, u32[]{:S(2)}) copy-start(f32[8,31,256]{2,1,0:T(8,128)} %get-tuple-element.11) | copy-start | bytes 761860
  44.7 8.4 %slice-start = ((f32[32,32,256]{2,1,0:T(8,128)}), f32[24,32,256]{2,1,0:T(8,128)S(1)}, s32[]{:S(2)}) async-start(f32[32,32,256]{2,1,0:T(8,128)} %param.9), calls=%async_computation.2 | async-start | bytes 1572864 | tf_op jit(solution)/shard_map/slice | solution.py:157
  50.2 6.0 %copy-start.6 = (f32[32,256]{1,0:T(8,128)}, f32[32,256]{1,0:T(8,128)S(1)}, u32[]{:S(2)}) copy-start(f32[32,256]{1,0:T(8,128)S(1)} %convert_element_type.6) | copy-start | bytes 98308
  51.0 5.2 %copy-start.4 = (s32[1,1,128,2]{3,2,1,0:T(8,128)}, s32[1,1,128,2]{3,2,1,0:T(8,128)S(1)}, u32[]{:S(2)}) copy-start(s32[1,1,128,2]{3,2,1,0:T(8,128)S(1)} %copy.33) | copy-start | bytes 3076
  72.0 18.2 %copy-start.9 = (s32[256]{0:T(256)S(1)}, s32[256]{0:T(256)}, u32[]{:S(2)}) copy-start(s32[256]{0:T(256)} %reshape_squeeze.13.anchor_ref) | copy-start | bytes 3076
  84.6 18.3 %copy-start.7 = (f32[32,256]{1,0:T(8,128)S(1)}, f32[32,256]{1,0:T(8,128)}, u32[]{:S(2)}) copy-start(f32[32,256]{1,0:T(8,128)} %copy-done.6) | copy-start | bytes 98308
  84.6 19.2 %copy-start.1 = (f32[32,2,128,32]{2,3,1,0:T(8,128)S(1)}, f32[32,2,128,32]{2,3,1,0:T(8,128)}, u32[]{:S(2)}) copy-start(f32[32,2,128,32]{2,3,1,0:T(8,128)} %fusion.2) | copy-start | bytes 3145732
  108.6 37.9 %collective-permute-start.6 = (f32[8,32,1]{2,1,0:T(8,128)}, f32[8,32,1]{2,1,0:T(8,128)}, u32[]{:S(2)}, u32[]{:S(2)}) collective-permute-start(f32[8,32,1]{2,1,0:T(8,128)} %get-tuple-element.19), channel_id=1, source_target_pairs={{0,1},{1,2},{2,3},{3,4},{4,5},{5,6},{6,7},{7,8},{8,9},{9,10},{10,1... | collective-permute-start | bytes 3080 | tf_op jit(solution)/shard_map/ppermute | solution.py:21
  112.6 33.8 %collective-permute-start.7 = (f32[8,32,1]{2,1,0:T(8,128)}, f32[8,32,1]{2,1,0:T(8,128)}, u32[]{:S(2)}, u32[]{:S(2)}) collective-permute-start(f32[8,32,1]{2,1,0:T(8,128)} %get-tuple-element.18), channel_id=1, source_target_pairs={{1,0},{2,1},{3,2},{4,3},{5,4},{6,5},{7,6},{8,7},{9,8},{10,9},{11,1... | collective-permute-start | bytes 3080 | tf_op jit(solution)/shard_map/ppermute | solution.py:22
  113.9 32.6 %collective-permute-start.4 = (f32[8,1,256]{2,1,0:T(1,128)}, f32[8,1,256]{2,1,0:T(1,128)S(1)}, u32[]{:S(2)}, u32[]{:S(2)}) collective-permute-start(f32[8,1,256]{2,1,0:T(1,128)} %get-tuple-element.23), channel_id=1, source_target_pairs={{0,128},{128,256},{256,384},{1,129},{129,257},{257,385},{2,130},{1... | collective-permute-start | bytes 24584 | tf_op jit(solution)/shard_map/ppermute | solution.py:21
  115.8 30.6 %collective-permute-start.5 = (f32[8,1,256]{2,1,0:T(1,128)}, f32[8,1,256]{2,1,0:T(1,128)S(1)}, u32[]{:S(2)}, u32[]{:S(2)}) collective-permute-start(f32[8,1,256]{2,1,0:T(1,128)} %get-tuple-element.22), channel_id=1, source_target_pairs={{128,0},{256,128},{384,256},{129,1},{257,129},{385,257},{130,2},{2... | collective-permute-start | bytes 24584 | tf_op jit(solution)/shard_map/ppermute | solution.py:22
  121.0 24.9 %all-to-all-start.1 = ((f32[128,1,2]{2,1,0:T(1,128)}), f32[128,1,2]{2,1,0:T(1,128)S(1)}, u32[]{:S(2)}, u32[]{:S(2)}) async-start(f32[128,1,2]{2,1,0:T(1,128)} %bitcast.8), calls=%async_computation.1 | async-start | bytes 131072 | tf_op jit(solution)/shard_map/all_to_all | solution.py:167
where the time goes:
time: 150 us; the launch traced here: 149 us
  starting transfers between devices  55.8 us (37%)
  local copies, waits for them, and re-layouts  29.2 us (19%)
  Pallas kernels  24.8 us (17%)
  waiting for transfers between devices  18.5 us (12%)
  other arithmetic  11.5 us (8%)
  matrix products  8.08 us (5%)
    all_to_all x1, starting transfers between devices, per_device(): lax.all_to_all(packed, 'lon', split_axis=0, concat_axis=0, tiled=True)  21.9 us
    pallas_call x1, Pallas kernels, predict(): pl.pallas_call(predict_kernel, out_shape=jax.ShapeDtypeStruct((slots, FH,...  12.7 us
    ppermute x4, starting transfers between devices, neighbours(): lax.ppermute(lax.slice_in_dim(block, size - 1, size, axis=dim), axis, for...  12.5 us
    pallas_call x1, Pallas kernels, scatter(): pl.pallas_call(scatter_kernel, out_shape=jax.ShapeDtypeStruct(top_shape,...  12.1 us
    all_to_all x1, starting transfers between devices, per_device(): lax.all_to_all(residual.reshape(owners, slots_per), 'lon', split_axis=0,...  11.5 us
    all_to_all x1, waiting for transfers between devices, per_device(): lax.all_to_all(residual.reshape(owners, slots_per), 'lon', split_axis=0,...  11.4 us
    ppermute x4, starting transfers between devices, neighbours(): high = lax.ppermute(lax.slice_in_dim(block, 0, 1, axis=dim), axis, backward)  9.84 us
    dot_general x3, matrix products, columns(): out = jnp.einsum(form, matrices, grouped, precision=lax.Precision.HIGHEST)  8.08 us
  transfers between devices with their start and end apart: 10, of which 2 were waited for; matrix products, arithmetic and copies ran while one was open for 16% of the time, Pallas kernels for 0%

commit v1 on v0

v1 whole, which is shorter than its diff:
```python
import jax
import jax.numpy as jnp
from jax import lax
from jax.experimental import pallas as pl
from jax.experimental.pallas import tpu as pltpu
from jax.sharding import PartitionSpec as P

LG = 8
LTOP = 4
FH = 8
FW = 16
K = 512
LANES = 128


def neighbours(block, axis, dim):
    count = lax.axis_size(axis)
    forward = [(i, i + 1) for i in range(count - 1)]
    backward = [(target, source) for source, target in forward]
    size = block.shape[dim]
    low = lax.ppermute(lax.slice_in_dim(block, size - 1, size, axis=dim), axis, forward)
    high = lax.ppermute(lax.slice_in_dim(block, 0, 1, axis=dim), axis, backward)
    return low, high


def stencil(block):
    up, down = neighbours(block, "lat", 1)
    left, right = neighbours(block, "lon", 2)
    rows = block.shape[1]
    cols = block.shape[2]
    north = jnp.concatenate([up, lax.slice_in_dim(block, 0, rows - 1, axis=1)], 1)
    south = jnp.concatenate([lax.slice_in_dim(block, 1, rows, axis=1), down], 1)
    west = jnp.concatenate([left, lax.slice_in_dim(block, 0, cols - 1, axis=2)], 2)
    east = jnp.concatenate([lax.slice_in_dim(block, 1, cols, axis=2), right], 2)
    return north + south + west + east - 4.0 * block


def columns(matrices, field, transpose):
    levels, height, breadth = field.shape
    blocks = matrices.shape[1]
    grouped = field.reshape(levels, height, blocks, breadth // blocks)
    form = "rbji,jrbc->irbc" if transpose else "rbij,jrbc->irbc"
    out = jnp.einsum(form, matrices, grouped, precision=lax.Precision.HIGHEST)
    return out.reshape(out.shape[0], height, breadth)


def footprint_kernel(anchor_ref, value_ref, weight_ref, top_ref, gain_ref, bar_ref, res_ref):
    layers, tile_rows, tile_cols = top_ref.shape
    slots = gain_ref.shape[0]
    groups = tile_cols // LANES
    bar_ref[...] = jnp.zeros(bar_ref.shape, bar_ref.dtype)
    row = lax.broadcasted_iota(jnp.int32, (2 * FH, tile_cols), 0)
    lane = lax.broadcasted_iota(jnp.int32, (2 * FH, tile_cols), 1)

    def body(s, carry):
        raw = anchor_ref[s]
        o = jnp.maximum(raw, 0)
        r = jnp.minimum(lax.div(o, tile_cols), tile_rows - FH)
        c = jnp.minimum(lax.rem(o, tile_cols), tile_cols - FW)
        flip = tile_rows - FH - r
        g0 = jnp.minimum(lax.div(flip, FH), tile_rows // FH - 2) * FH
        g0 = pl.multiple_of(g0, FH)
        off = flip - g0
        g = gain_ref[s]
        g = jnp.broadcast_to(g[:, None, :], (layers, FH, LANES))
        g = pltpu.roll(g, 0, 2, stride=FW, stride_axis=1)
        g = pltpu.roll(g, lax.rem(c + FW, LANES), 2)
        g = pltpu.roll(g, lax.rem(off, FH), 1)
        g = jnp.concatenate([g, g], axis=1)
        g = jnp.concatenate([g] * groups, axis=2)
        inside = (row >= off) & (row < off + FH) & (lane >= c) & (lane < c + FW)
        g = jnp.where(inside[None], g, 0.0)
        t = top_ref[:, pl.ds(g0, 2 * FH), :]
        part = jnp.sum(g * t, axis=0)
        part = part[:FH] + part[FH:]
        acc = part[:, 0:LANES]
        for q in range(1, groups):
            acc = acc + part[:, q * LANES:(q + 1) * LANES]
        predicted = jnp.sum(acc, axis=(0, 1), keepdims=True)
        live = jnp.where(raw >= 0, 1.0, 0.0).astype(jnp.float32)
        res = (live * weight_ref[s]) * (predicted - value_ref[s])
        res_ref[s] = jnp.broadcast_to(res, (FH, LANES))
        bar_ref[:, pl.ds(g0, 2 * FH), :] += res * g
        return carry

    lax.fori_loop(0, slots, body, 0, unroll=2)


def footprints(anchor, value, weight, top, gain):
    slots = gain.shape[0]
    smem = pl.BlockSpec(memory_space=pltpu.SMEM)
    vmem = pl.BlockSpec(memory_space=pltpu.VMEM)
    return pl.pallas_call(
        footprint_kernel,
        out_shape=(
            jax.ShapeDtypeStruct(top.shape, jnp.float32),
            jax.ShapeDtypeStruct((slots, FH, LANES), jnp.float32),
        ),
        in_specs=[smem, smem, smem, vmem, vmem],
        out_specs=(vmem, vmem),
    )(anchor, value, weight, top, gain)


def per_device(
    moisture,
    conductance,
    inverse,
    crop_mask,
    adjoint_in,
    foot_anchor,
    antenna_gain,
    obs_value,
    obs_weight,
):
    levels, tile_rows, tile_cols = moisture.shape
    mask_float = crop_mask.astype(jnp.float32)
    blocks = inverse.shape[1]
    matrices = inverse.reshape(tile_rows, blocks, levels, levels)

    owner_gain = antenna_gain[0, 0]
    owners, slots_per, _ = owner_gain.shape
    packed = jnp.concatenate(
        [owner_gain, obs_value[0, 0][..., None], obs_weight[0, 0][..., None]], -1
    )
    received = lax.all_to_all(packed, "lon", split_axis=0, concat_axis=0, tiled=True)
    slots = owners * slots_per
    gain = received[..., :K].reshape(slots, LTOP, LANES)
    value = received[..., K].reshape(slots)
    weight = received[..., K + 1].reshape(slots)

    deep = moisture[levels - LG :]
    mixed = jnp.concatenate(
        [moisture[: levels - LG], deep + conductance * stencil(deep)], 0
    )
    solved_top = columns(matrices[:, :, :LTOP, :], mixed, False)
    topmost = jnp.flip(solved_top * mask_float, 1)

    slot_anchor = foot_anchor[0, 0].reshape(slots)
    bar, rows = footprints(slot_anchor, value, weight, topmost, gain)
    residual = rows[:, 0, 0].reshape(owners, slots_per)
    residual_out = lax.all_to_all(residual, "lon", split_axis=0, concat_axis=0, tiled=True)

    base = columns(matrices, adjoint_in, True)
    topbar = jnp.flip(bar, 1) * mask_float
    mixedbar = base + columns(matrices[:, :, :LTOP, :], topbar, True)
    deepbar = mixedbar[levels - LG :]
    gradient = jnp.concatenate(
        [mixedbar[: levels - LG], deepbar + stencil(conductance * deepbar)], 0
    )
    return gradient, residual_out[None, None]


def solution(mesh):
    in_specs = (
        P(None, "lat", "lon"),
        P("lat", "lon"),
        P("lat", "lon", None),
        P("lat", "lon"),
        P(None, "lat", "lon"),
        P("lat", "lon", None, None),
        P("lat", "lon", None, None, None),
        P("lat", "lon", None, None),
        P("lat", "lon", None, None),
    )
    out_specs = (P(None, "lat", "lon"), P("lat", "lon", None, None))
    return jax.shard_map(
        per_device, mesh=mesh, in_specs=in_specs, out_specs=out_specs, check_vma=False
    )
```

time: 150 us -> 154 us (1.027)
  the two profiles are of different devices: /device:TPU:2 before, /device:TPU:32 now
where the time goes in v1:
time: 154 us; the launch traced here: 153 us
  starting transfers between devices  60.9 us (40%)
  Pallas kernels  39.2 us (25%)
  local copies, waits for them, and re-layouts  25.7 us (17%)
  waiting for transfers between devices  13.4 us (9%)
  matrix products  8.12 us (5%)
  other arithmetic  5.03 us (3%)
    pallas_call x1, Pallas kernels, footprints(): pl.pallas_call(footprint_kernel, out_shape=(jax.ShapeDtypeStruct(top.shap...  39.2 us
    ppermute x4, starting transfers between devices, neighbours(): high = lax.ppermute(lax.slice_in_dim(block, 0, 1, axis=dim), axis, backward)  22.8 us
    all_to_all x1, starting transfers between devices, per_device(): lax.all_to_all(packed, 'lon', split_axis=0, concat_axis=0, tiled=True)  15.4 us
    all_to_all x1, starting transfers between devices, per_device(): lax.all_to_all(residual, 'lon', split_axis=0, concat_axis=0, tiled=True)  12.8 us
    ppermute x4, starting transfers between devices, neighbours(): lax.ppermute(lax.slice_in_dim(block, size - 1, size, axis=dim), axis, for...  9.9 us
    ppermute x4, waiting for transfers between devices, neighbours(): lax.ppermute(lax.slice_in_dim(block, size - 1, size, axis=dim), axis, for...  9.85 us
    dot_general x3, matrix products, columns(): out = jnp.einsum(form, matrices, grouped, precision=lax.Precision.HIGHEST)  8.12 us
    slice x4, local copies, waits for them, and re-layouts, neighbours(): high = lax.ppermute(lax.slice_in_dim(block, 0, 1, axis=dim), axis, backward)  4.03 us
  transfers between devices with their start and end apart: 10, of which 3 were waited for; matrix products, arithmetic and copies ran while one was open for 14% of the time, Pallas kernels for 0%

profile of v1, /device:TPU:32, one launch (start us, length us, event | category | flops | bytes accessed | tf_op | source)
XLA Modules:
  0.0 153.4 jit_solution(9829881030035146152)
XLA Ops:
  0.6 1.5 %fusion.19 = (f32[8,1,256]{2,1,0:T(1,128)}, f32[8,1,256]{2,1,0:T(1,128)}) fusion(f32[32,32,256]{2,1,0:T(8,128)} %param.9), kind=kLoop, calls=%fused_computation.32 | loop fusion | bytes 32768 | tf_op jit(solution)/shard_map/slice | solution.py:22
  2.2 1.3 collective-permute-start.1
  3.5 3.0 %collective-permute-start = (f32[8,1,256]{2,1,0:T(1,128)}, f32[8,1,256]{2,1,0:T(1,128)S(1)}, u32[]{:S(2)}, u32[]{:S(2)}) collective-permute-start(f32[8,1,256]{2,1,0:T(1,128)} %get-tuple-element.19), channel_id=1, source_target_pairs={{0,128},{128,256},{256,384},{1,129},{129,257},{257,385},{2,130},{1... | collective-permute-start | bytes 24584 | tf_op jit(solution)/shard_map/ppermute | solution.py:21
  6.5 1.7 %fusion.17 = (f32[8,32,1]{2,1,0:T(8,128)}, f32[8,32,1]{2,1,0:T(8,128)}) fusion(f32[32,32,256]{2,1,0:T(8,128)} %param.9), kind=kLoop, calls=%fused_computation.30 | loop fusion | bytes 4096 | tf_op jit(solution)/shard_map/slice | solution.py:22
  8.2 13.3 %collective-permute-start.3 = (f32[8,32,1]{2,1,0:T(8,128)}, f32[8,32,1]{2,1,0:T(8,128)}, u32[]{:S(2)}, u32[]{:S(2)}) collective-permute-start(f32[8,32,1]{2,1,0:T(8,128)} %get-tuple-element.14), channel_id=1, source_target_pairs={{1,0},{2,1},{3,2},{4,3},{5,4},{6,5},{7,6},{8,7},{9,8},{10,9},{11,1... | collective-permute-start | bytes 3080 | tf_op jit(solution)/shard_map/ppermute | solution.py:22
  21.5 0.0 copy-start.5
  21.5 1.9 %collective-permute-start.2 = (f32[8,32,1]{2,1,0:T(8,128)}, f32[8,32,1]{2,1,0:T(8,128)}, u32[]{:S(2)}, u32[]{:S(2)}) collective-permute-start(f32[8,32,1]{2,1,0:T(8,128)} %get-tuple-element.15), channel_id=1, source_target_pairs={{0,1},{1,2},{2,3},{3,4},{4,5},{5,6},{6,7},{7,8},{8,9},{9,10},{10,1... | collective-permute-start | bytes 3080 | tf_op jit(solution)/shard_map/ppermute | solution.py:21
  23.5 0.2 copy.32
  23.6 0.0 copy-start.6
  23.6 0.7 copy-done.6
  24.3 0.2 copy.33
  24.5 0.0 copy-start
  24.5 1.2 pad_maximum_fusion.2
  25.7 15.4 %all-to-all-start = ((f32[128,2,514]{2,1,0:T(2,128)}), f32[128,2,514]{2,1,0:T(2,128)}, u32[]{:S(2)}, u32[]{:S(2)}) async-start(f32[128,2,514]{2,1,0:T(2,128)} %pad_maximum_fusion.2), calls=%async_computation | async-start | bytes 1310720 | tf_op jit(solution)/shard_map/all_to_all | solution.py:125
  41.1 0.0 copy-start.1
  41.1 0.7 fusion.18
  41.8 1.4 reshape.34
  43.3 1.5 reshape.33
  44.8 3.5 %fusion.2 = f32[32,2,128,32]{2,3,1,0:T(8,128)S(1)} fusion(f32[32,2,32,32]{3,2,1,0:T(8,128)S(1)} %reshape.34, f32[32,32,2,128]{3,2,1,0:T(2,128)} %reshape.33), kind=kOutput, calls=%fused_computation.6 | convolution fusion | flops 100663296 | bytes 2359296 | tf_op jit(solution)/shard_map/rbji,jrbc->irbc/dot_general | solution.py:43
  48.3 0.9 fusion.16
  49.1 0.8 copy-done.4
  49.9 0.8 copy.31
  50.7 0.7 reshape_squeeze.10.anchor_ref
  51.4 0.0 collective-permute-done.3
  51.4 0.0 collective-permute-done.2
  51.4 0.0 collective-permute-done
  51.4 0.0 copy-done.3
  51.4 1.5 fusion.8
  52.9 0.1 pad_maximum_fusion
  53.0 1.5 reshape.35
  54.5 2.8 %convolution_bitcast_fusion = f32[4,32,2,128]{3,0,2,1:T(4,128)S(1)} fusion(f32[32,32,2,128]{3,2,1,0:T(2,128)} %reshape.35, f32[32,2,32,32]{3,2,1,0:T(8,128)S(1)} %reshape.34), kind=kOutput, calls=%fused_computation.2 | convolution fusion | flops 12582912 | bytes 1310720 | tf_op jit(solution)/shard_map/rbij,jrbc->irbc/dot_general | solution.py:43
  57.3 0.1 copy.35
  57.4 0.1 reshape.36
  57.5 0.7 rev.7.top_ref
  58.2 3.3 %all-to-all-done = f32[128,2,514]{2,1,0:T(2,128)} async-done(((f32[128,2,514]{2,1,0:T(2,128)}), f32[128,2,514]{2,1,0:T(2,128)}, u32[]{:S(2)}, u32[]{:S(2)}) %all-to-all-start) | async-done | bytes 526368 | tf_op jit(solution)/shard_map/all_to_all | solution.py:125
  61.5 1.1 slice.120
  62.6 1.3 reshape.37.gain_ref
  63.9 1.5 slice_reduce_fusion
  65.4 0.7 reshape_squeeze.12.weight_ref
  66.1 0.7 reshape_squeeze.11.value_ref
  66.8 39.2 %shard_map.104 = (f32[4,32,256]{2,1,0:T(8,128)}, f32[256,8,128]{2,1,0:T(8,128)}) custom-call(s32[256]{0:T(256)} %reshape_squeeze.10.anchor_ref, f32[256]{0:T(256)} %reshape_squeeze.11.value_ref, f32[256]{0:T(256)} %reshape_squeeze.12.weight_ref, f32[4,32,256]{2,1,0:T(8,128)} %rev.7.top_ref, f32[256,4,128]{2,1,0:T(4,128)} %reshape.37.gain_ref), custom_call_target="tpu_custom_call" | custom-call | tf_op jit(solution)/shard_map/pallas_call | solution.py:93
  106.0 0.9 rev.8
  106.9 0.1 reshape.38
  107.0 1.8 %fusion = f32[32,32,2,128]{3,0,2,1:T(8,128)S(1)} fusion(f32[32,2,128,32]{2,3,1,0:T(8,128)S(1)} %fusion.2, f32[4,32,2,128]{3,2,1,0:T(2,128)S(1)} %reshape.38, f32[32,2,32,32]{3,2,1,0:T(8,128)S(1)} %reshape.34), kind=kOutput, calls=%fused_computation.1 | convolution fusion | flops 12845056 | bytes 2359296 | tf_op jit(solution)/shard_map/rbji,jrbc->irbc/dot_general | solution.py:43
  108.9 0.1 copy.38
  109.0 0.2 slice.107
  109.3 0.8 fusion.21
  110.1 2.3 %slice_reduce_fusion.2 = f32[256]{0:T(256)S(1)} fusion(f32[256,8,128]{2,1,0:T(8,128)} %get-tuple-element.5), kind=kLoop, calls=%fused_computation.23 | loop fusion | bytes 2048 | tf_op jit(solution)/shard_map/slice | solution.py:140
  112.4 0.8 all_to_all.10
  113.2 12.8 %all-to-all-start.1 = ((f32[128,1,2]{2,1,0:T(1,128)}), f32[128,1,2]{2,1,0:T(1,128)S(1)}, u32[]{:S(2)}, u32[]{:S(2)}) async-start(f32[128,1,2]{2,1,0:T(1,128)} %bitcast.5), calls=%async_computation.1 | async-start | bytes 131072 | tf_op jit(solution)/shard_map/all_to_all | solution.py:141
  126.0 1.3 collective-permute-start.5
  127.3 3.0 %collective-permute-start.4 = (f32[8,1,256]{2,1,0:T(1,128)S(1)}, f32[8,1,256]{2,1,0:T(1,128)S(1)}, u32[]{:S(2)}, u32[]{:S(2)}) collective-permute-start(f32[8,1,256]{2,1,0:T(1,128)S(1)} %get-tuple-element.27), channel_id=1, source_target_pairs={{0,128},{128,256},{256,384},{1,129},{129,257},{257,385},{2,130},{1... | collective-permute-start | bytes 24584 | tf_op jit(solution)/shard_map/ppermute | solution.py:21
  130.3 7.0 %collective-permute-start.7 = (f32[8,32,1]{2,1,0:T(8,128)}, f32[8,32,1]{2,1,0:T(8,128)}, u32[]{:S(2)}, u32[]{:S(2)}) collective-permute-start(f32[8,32,1]{2,1,0:T(8,128)} %get-tuple-element.22), channel_id=1, source_target_pairs={{1,0},{2,1},{3,2},{4,3},{5,4},{6,5},{7,6},{8,7},{9,8},{10,9},{11,1... | collective-permute-start | bytes 3080 | tf_op jit(solution)/shard_map/ppermute | solution.py:22
  137.3 1.9 %collective-permute-start.6 = (f32[8,32,1]{2,1,0:T(8,128)}, f32[8,32,1]{2,1,0:T(8,128)}, u32[]{:S(2)}, u32[]{:S(2)}) collective-permute-start(f32[8,32,1]{2,1,0:T(8,128)} %get-tuple-element.23), channel_id=1, source_target_pairs={{0,1},{1,2},{2,3},{3,4},{4,5},{5,6},{6,7},{7,8},{8,9},{9,10},{10,1... | collective-permute-start | bytes 3080 | tf_op jit(solution)/shard_map/ppermute | solution.py:21
  139.2 0.1 fusion.20
  139.4 0.1 slice.121
  139.4 0.4 copy.37
  139.9 0.6 slice.105
  140.5 0.6 copy.40
  141.1 0.2 collective-permute-done.7
  141.3 9.8 %collective-permute-done.6 = f32[8,32,1]{2,1,0:T(8,128)} collective-permute-done((f32[8,32,1]{2,1,0:T(8,128)}, f32[8,32,1]{2,1,0:T(8,128)}, u32[]{:S(2)}, u32[]{:S(2)}) %collective-permute-start.6) | collective-permute-done | bytes 1056 | tf_op jit(solution)/shard_map/ppermute | solution.py:21
  151.2 0.0 collective-permute-done.5
  151.2 1.2 fusion.12
  152.3 1.0 pad_maximum_fusion.1
  (19 shorter events, 0.2 us)
Async XLA Ops:
  0.6 23.8 %copy-start.2 = (f32[1,1,128,2,512]{4,3,2,1,0:T(2,128)S(1)}, f32[1,1,128,2,512]{4,3,2,1,0:T(2,128)}, u32[]{:S(2)}) copy-start(f32[1,1,128,2,512]{4,3,2,1,0:T(2,128)} %param.15) | copy-start | bytes 1572868
  2.2 49.2 %collective-permute-start.1 = (f32[8,1,256]{2,1,0:T(1,128)}, f32[8,1,256]{2,1,0:T(1,128)S(1)}, u32[]{:S(2)}, u32[]{:S(2)}) collective-permute-start(f32[8,1,256]{2,1,0:T(1,128)} %get-tuple-element.18), channel_id=1, source_target_pairs={{128,0},{256,128},{384,256},{129,1},{257,129},{385,257},{130,2},{2... | collective-permute-start | bytes 24584 | tf_op jit(solution)/shard_map/ppermute | solution.py:22
  3.5 47.9 %collective-permute-start = (f32[8,1,256]{2,1,0:T(1,128)}, f32[8,1,256]{2,1,0:T(1,128)S(1)}, u32[]{:S(2)}, u32[]{:S(2)}) collective-permute-start(f32[8,1,256]{2,1,0:T(1,128)} %get-tuple-element.19), channel_id=1, source_target_pairs={{0,128},{128,256},{256,384},{1,129},{129,257},{257,385},{2,130},{1... | collective-permute-start | bytes 24584 | tf_op jit(solution)/shard_map/ppermute | solution.py:21
  8.2 43.2 %collective-permute-start.3 = (f32[8,32,1]{2,1,0:T(8,128)}, f32[8,32,1]{2,1,0:T(8,128)}, u32[]{:S(2)}, u32[]{:S(2)}) collective-permute-start(f32[8,32,1]{2,1,0:T(8,128)} %get-tuple-element.14), channel_id=1, source_target_pairs={{1,0},{2,1},{3,2},{4,3},{5,4},{6,5},{7,6},{8,7},{9,8},{10,9},{11,1... | collective-permute-start | bytes 3080 | tf_op jit(solution)/shard_map/ppermute | solution.py:22
  21.5 1.9 %copy-start.5 = (f32[1,1,128,2]{2,3,1,0:T(2,128)S(1)}, f32[1,1,128,2]{2,3,1,0:T(2,128)}, u32[]{:S(2)}) copy-start(f32[1,1,128,2]{2,3,1,0:T(2,128)} %param.16) | copy-start | bytes 3076
  21.5 29.9 %collective-permute-start.2 = (f32[8,32,1]{2,1,0:T(8,128)}, f32[8,32,1]{2,1,0:T(8,128)}, u32[]{:S(2)}, u32[]{:S(2)}) collective-permute-start(f32[8,32,1]{2,1,0:T(8,128)} %get-tuple-element.15), channel_id=1, source_target_pairs={{0,1},{1,2},{2,3},{3,4},{4,5},{5,6},{6,7},{7,8},{8,9},{9,10},{10,1... | collective-permute-start | bytes 3080 | tf_op jit(solution)/shard_map/ppermute | solution.py:21
  23.6 0.7 copy-start.6
  24.5 16.6 %copy-start = (f32[32,32,256]{2,1,0:T(8,128)S(1)}, f32[32,32,256]{2,1,0:T(8,128)}, u32[]{:S(2)}) copy-start(f32[32,32,256]{2,1,0:T(8,128)} %param.9) | copy-start | bytes 3145732
  25.7 35.8 %all-to-all-start = ((f32[128,2,514]{2,1,0:T(2,128)}), f32[128,2,514]{2,1,0:T(2,128)}, u32[]{:S(2)}, u32[]{:S(2)}) async-start(f32[128,2,514]{2,1,0:T(2,128)} %pad_maximum_fusion.2), calls=%async_computation | async-start | bytes 1310720 | tf_op jit(solution)/shard_map/all_to_all | solution.py:125
  41.1 2.2 %copy-start.1 = (f32[32,32,256]{2,1,0:T(8,128)S(1)}, f32[32,32,256]{2,1,0:T(8,128)}, u32[]{:S(2)}) copy-start(f32[32,32,256]{2,1,0:T(8,128)} %param.13) | copy-start | bytes 3145732
  49.1 0.8 copy-start.4
  50.7 0.8 copy-start.3
  51.4 1.5 slice-start
  113.2 27.4 %all-to-all-start.1 = ((f32[128,1,2]{2,1,0:T(1,128)}), f32[128,1,2]{2,1,0:T(1,128)S(1)}, u32[]{:S(2)}, u32[]{:S(2)}) async-start(f32[128,1,2]{2,1,0:T(1,128)} %bitcast.5), calls=%async_computation.1 | async-start | bytes 131072 | tf_op jit(solution)/shard_map/all_to_all | solution.py:141
  126.0 25.2 %collective-permute-start.5 = (f32[8,1,256]{2,1,0:T(1,128)S(1)}, f32[8,1,256]{2,1,0:T(1,128)S(1)}, u32[]{:S(2)}, u32[]{:S(2)}) collective-permute-start(f32[8,1,256]{2,1,0:T(1,128)S(1)} %get-tuple-element.26), channel_id=1, source_target_pairs={{128,0},{256,128},{384,256},{129,1},{257,129},{385,257},{130,2},{2... | collective-permute-start | bytes 24584 | tf_op jit(solution)/shard_map/ppermute | solution.py:22
  127.3 23.9 %collective-permute-start.4 = (f32[8,1,256]{2,1,0:T(1,128)S(1)}, f32[8,1,256]{2,1,0:T(1,128)S(1)}, u32[]{:S(2)}, u32[]{:S(2)}) collective-permute-start(f32[8,1,256]{2,1,0:T(1,128)S(1)} %get-tuple-element.27), channel_id=1, source_target_pairs={{0,128},{128,256},{256,384},{1,129},{129,257},{257,385},{2,130},{1... | collective-permute-start | bytes 24584 | tf_op jit(solution)/shard_map/ppermute | solution.py:21
  130.3 11.0 %collective-permute-start.7 = (f32[8,32,1]{2,1,0:T(8,128)}, f32[8,32,1]{2,1,0:T(8,128)}, u32[]{:S(2)}, u32[]{:S(2)}) collective-permute-start(f32[8,32,1]{2,1,0:T(8,128)} %get-tuple-element.22), channel_id=1, source_target_pairs={{1,0},{2,1},{3,2},{4,3},{5,4},{6,5},{7,6},{8,7},{9,8},{10,9},{11,1... | collective-permute-start | bytes 3080 | tf_op jit(solution)/shard_map/ppermute | solution.py:22
  137.3 13.9 %collective-permute-start.6 = (f32[8,32,1]{2,1,0:T(8,128)}, f32[8,32,1]{2,1,0:T(8,128)}, u32[]{:S(2)}, u32[]{:S(2)}) collective-permute-start(f32[8,32,1]{2,1,0:T(8,128)} %get-tuple-element.23), channel_id=1, source_target_pairs={{0,1},{1,2},{2,3},{3,4},{4,5},{5,6},{6,7},{7,8},{8,9},{9,10},{10,1... | collective-permute-start | bytes 3080 | tf_op jit(solution)/shard_map/ppermute | solution.py:21

commit v2 on v1

--- a/solution.py
+++ b/solution.py
@@ -13,25 +13,22 @@
 LANES = 128
 
 
-def neighbours(block, axis, dim):
+def neighbours(edge_low, edge_high, axis):
     count = lax.axis_size(axis)
     forward = [(i, i + 1) for i in range(count - 1)]
     backward = [(target, source) for source, target in forward]
-    size = block.shape[dim]
-    low = lax.ppermute(lax.slice_in_dim(block, size - 1, size, axis=dim), axis, forward)
-    high = lax.ppermute(lax.slice_in_dim(block, 0, 1, axis=dim), axis, backward)
-    return low, high
+    return lax.ppermute(edge_high, axis, forward), lax.ppermute(edge_low, axis, backward)
 
 
 def stencil(block):
-    up, down = neighbours(block, "lat", 1)
-    left, right = neighbours(block, "lon", 2)
     rows = block.shape[1]
     cols = block.shape[2]
+    up, down = neighbours(block[:, 0:1, :], block[:, rows - 1 : rows, :], "lat")
+    left, right = neighbours(block[:, :, 0], block[:, :, cols - 1], "lon")
     north = jnp.concatenate([up, lax.slice_in_dim(block, 0, rows - 1, axis=1)], 1)
     south = jnp.concatenate([lax.slice_in_dim(block, 1, rows, axis=1), down], 1)
-    west = jnp.concatenate([left, lax.slice_in_dim(block, 0, cols - 1, axis=2)], 2)
-    east = jnp.concatenate([lax.slice_in_dim(block, 1, cols, axis=2), right], 2)
+    west = jnp.concatenate([left[:, :, None], lax.slice_in_dim(block, 0, cols - 1, axis=2)], 2)
+    east = jnp.concatenate([lax.slice_in_dim(block, 1, cols, axis=2), right[:, :, None]], 2)
     return north + south + west + east - 4.0 * block
 
 
@@ -48,13 +45,11 @@
     layers, tile_rows, tile_cols = top_ref.shape
     slots = gain_ref.shape[0]
     groups = tile_cols // LANES
-    bar_ref[...] = jnp.zeros(bar_ref.shape, bar_ref.dtype)
     row = lax.broadcasted_iota(jnp.int32, (2 * FH, tile_cols), 0)
     lane = lax.broadcasted_iota(jnp.int32, (2 * FH, tile_cols), 1)
 
-    def body(s, carry):
-        raw = anchor_ref[s]
-        o = jnp.maximum(raw, 0)
+    def placed(s):
+        o = jnp.maximum(anchor_ref[s], 0)
         r = jnp.minimum(lax.div(o, tile_cols), tile_rows - FH)
         c = jnp.minimum(lax.rem(o, tile_cols), tile_cols - FW)
         flip = tile_rows - FH - r
@@ -69,7 +64,10 @@
         g = jnp.concatenate([g, g], axis=1)
         g = jnp.concatenate([g] * groups, axis=2)
         inside = (row >= off) & (row < off + FH) & (lane >= c) & (lane < c + FW)
-        g = jnp.where(inside[None], g, 0.0)
+        return g0, jnp.where(inside[None], g, 0.0)
+
+    def predict(s, carry):
+        g0, g = placed(s)
         t = top_ref[:, pl.ds(g0, 2 * FH), :]
         part = jnp.sum(g * t, axis=0)
         part = part[:FH] + part[FH:]
@@ -77,13 +75,20 @@
         for q in range(1, groups):
             acc = acc + part[:, q * LANES:(q + 1) * LANES]
         predicted = jnp.sum(acc, axis=(0, 1), keepdims=True)
-        live = jnp.where(raw >= 0, 1.0, 0.0).astype(jnp.float32)
+        live = jnp.where(anchor_ref[s] >= 0, 1.0, 0.0).astype(jnp.float32)
         res = (live * weight_ref[s]) * (predicted - value_ref[s])
         res_ref[s] = jnp.broadcast_to(res, (FH, LANES))
+        return carry
+
+    def scatter(s, carry):
+        g0, g = placed(s)
+        res = res_ref[s][0:1, 0:1]
         bar_ref[:, pl.ds(g0, 2 * FH), :] += res * g
         return carry
 
-    lax.fori_loop(0, slots, body, 0, unroll=2)
+    lax.fori_loop(0, slots, predict, 0, unroll=4)
+    bar_ref[...] = jnp.zeros(bar_ref.shape, bar_ref.dtype)
+    lax.fori_loop(0, slots, scatter, 0, unroll=4)
 
 
 def footprints(anchor, value, weight, top, gain):

time: 154 us -> 141 us (0.916)
  waiting for transfers between devices: 13.4 us -> 3.71 us
  Pallas kernels: 39.2 us -> 32.1 us
  local copies, waits for them, and re-layouts: 25.7 us -> 29 us
    pallas_call x1, Pallas kernels: 39.2 us -> 32.1 us  [footprints(): pl.pallas_call(footprint_kernel, out_shape=(jax.ShapeDtypeStruct(top.shap...]
    ppermute x8, waiting for transfers between devices: 10 us -> 3.7 us  [the longest x4 3.69 us: neighbours(): lax.ppermute(edge_high, axis, forward)]
    all_to_all x1, starting transfers between devices: 12.8 us -> 16.4 us  [per_device(): lax.all_to_all(residual, 'lon', split_axis=0, concat_axis=0, tiled=True)]
    all_to_all x1, waiting for transfers between devices: 3.33 us -> 0.01 us  [per_device(): lax.all_to_all(packed, 'lon', split_axis=0, concat_axis=0, tiled=True)]
    all_to_all x1, starting transfers between devices: 15.4 us -> 12.3 us  [per_device(): lax.all_to_all(packed, 'lon', split_axis=0, concat_axis=0, tiled=True)]
    broadcast_in_dim x0 -> x4, local copies, waits for them, and re-layouts: none -> 2.51 us  [the longest x2 1.58 us: stencil(): left[:, :, None]]
    unnamed x16 -> x24, local copies, waits for them, and re-layouts: 2.91 us -> 4.86 us
  transfers between devices with their start and end apart: 10 -> 10, of which waited for: 3 -> 1; matrix products, arithmetic and copies ran while one was open for 14% -> 17% of each run, Pallas kernels for 0% -> 0%
where the time goes in v2:
time: 141 us; the launch traced here: 140 us
  starting transfers between devices  61.7 us (44%)
  Pallas kernels  32.1 us (23%)
  local copies, waits for them, and re-layouts  29 us (21%)
  matrix products  8.12 us (6%)
  other arithmetic  4.65 us (3%)
  waiting for transfers between devices  3.71 us (3%)
    pallas_call x1, Pallas kernels, footprints(): pl.pallas_call(footprint_kernel, out_shape=(jax.ShapeDtypeStruct(top.shap...  32.1 us
    ppermute x4, starting transfers between devices, neighbours(): lax.ppermute(edge_low, axis, backward)  20 us
    all_to_all x1, starting transfers between devices, per_device(): lax.all_to_all(residual, 'lon', split_axis=0, concat_axis=0, tiled=True)  16.4 us
    ppermute x4, starting transfers between devices, neighbours(): lax.ppermute(edge_high, axis, forward)  13 us
    all_to_all x1, starting transfers between devices, per_device(): lax.all_to_all(packed, 'lon', split_axis=0, concat_axis=0, tiled=True)  12.3 us
    dot_general x3, matrix products, columns(): out = jnp.einsum(form, matrices, grouped, precision=lax.Precision.HIGHEST)  8.12 us
    unnamed x24, local copies, waits for them, and re-layouts  4.86 us
    ppermute x4, waiting for transfers between devices, neighbours(): lax.ppermute(edge_high, axis, forward)  3.69 us
  transfers between devices with their start and end apart: 10, of which 1 were waited for; matrix products, arithmetic and copies ran while one was open for 17% of the time, Pallas kernels for 0%

profile of v2, /device:TPU:32, one launch (start us, length us, event | category | flops | bytes accessed | tf_op | source)
XLA Modules:
  0.0 140.2 jit_solution(18241320763897928597)
XLA Ops:
  0.6 1.5 %fusion.19 = (f32[8,1,256]{2,1,0:T(1,128)}, f32[8,1,256]{2,1,0:T(1,128)}) fusion(f32[32,32,256]{2,1,0:T(8,128)} %param.9), kind=kLoop, calls=%fused_computation.34 | loop fusion | bytes 32768 | tf_op jit(solution)/shard_map/slice | solution.py:26
  2.1 1.3 collective-permute-start.1
  3.4 3.2 %collective-permute-start = (f32[8,1,256]{2,1,0:T(1,128)}, f32[8,1,256]{2,1,0:T(1,128)S(1)}, u32[]{:S(2)}, u32[]{:S(2)}) collective-permute-start(f32[8,1,256]{2,1,0:T(1,128)} %get-tuple-element.23), channel_id=1, source_target_pairs={{0,128},{128,256},{256,384},{1,129},{129,257},{257,385},{2,130},{1... | collective-permute-start | bytes 24584 | tf_op jit(solution)/shard_map/ppermute | solution.py:20
  6.6 1.1 fusion.17
  7.7 0.7 copy.74
  8.4 4.9 %collective-permute-start.2 = (f32[8,32]{1,0:T(8,128)}, f32[8,32]{1,0:T(8,128)}, u32[]{:S(2)}, u32[]{:S(2)}) collective-permute-start(f32[8,32]{1,0:T(8,128)} %bitcast.3), channel_id=1, source_target_pairs={{0,1},{1,2},{2,3},{3,4},{4,5},{5,6},{6,7},{7,8},{8,9},{9,10},{10,1... | collective-permute-start | bytes 3080 | tf_op jit(solution)/shard_map/ppermute | solution.py:20
  13.3 0.1 copy.75
  13.4 10.4 %collective-permute-start.3 = (f32[8,32]{1,0:T(8,128)S(1)}, f32[8,32]{1,0:T(8,128)S(1)}, u32[]{:S(2)}, u32[]{:S(2)}) collective-permute-start(f32[8,32]{1,0:T(8,128)S(1)} %bitcast.21), channel_id=1, source_target_pairs={{1,0},{2,1},{3,2},{4,3},{5,4},{6,5},{7,6},{8,7},{9,8},{10,9},{11,1... | collective-permute-start | bytes 3080 | tf_op jit(solution)/shard_map/ppermute | solution.py:20
  23.8 0.2 copy.58
  24.0 0.7 copy-done.8
  24.7 0.2 copy.59
  24.9 1.2 pad_maximum_fusion.2
  26.1 12.3 %all-to-all-start = ((f32[128,2,514]{2,1,0:T(2,128)}), f32[128,2,514]{2,1,0:T(2,128)}, u32[]{:S(2)}, u32[]{:S(2)}) async-start(f32[128,2,514]{2,1,0:T(2,128)} %pad_maximum_fusion.2), calls=%async_computation | async-start | bytes 1310720 | tf_op jit(solution)/shard_map/all_to_all | solution.py:130
  38.5 0.7 fusion.18
  39.2 1.4 %reshape.34 = f32[32,2,32,32]{3,2,1,0:T(8,128)S(1)} reshape(f32[32,2,1024]{2,1,0:T(2,128)} %param.11) | data formatting | bytes 524288 | tf_op jit(solution)/shard_map/reshape | solution.py:123
  40.6 1.5 %reshape.33 = f32[32,32,2,128]{3,2,1,0:T(2,128)} reshape(f32[32,32,256]{2,1,0:T(8,128)S(1)} %copy-done.1) | data formatting | bytes 2097152 | tf_op jit(solution)/shard_map/reshape | solution.py:38
  42.1 3.5 %fusion.2 = f32[32,2,128,32]{2,3,1,0:T(8,128)S(1)} fusion(f32[32,2,32,32]{3,2,1,0:T(8,128)S(1)} %reshape.34, f32[32,32,2,128]{3,2,1,0:T(2,128)} %reshape.33), kind=kOutput, calls=%fused_computation.6 | convolution fusion | flops 100663296 | bytes 2359296 | tf_op jit(solution)/shard_map/rbji,jrbc->irbc/dot_general | solution.py:40
  45.6 0.9 fusion.16
  46.5 0.8 copy-done.5
  47.3 0.6 convert_element_type.3
  47.9 0.1 copy-done.9
  47.9 0.1 copy.57
  48.1 0.7 reshape_squeeze.10.anchor_ref
  48.8 0.6 copy-done.6
  49.4 0.8 copy.63
  50.1 1.5 %copy.61 = f32[8,32,1]{2,1,0:T(8,128)} copy(f32[8,32,1]{1,0,2:T(8,128)} %bitcast.4) | data formatting | bytes 2048 | tf_op jit(solution)/shard_map/broadcast_in_dim | solution.py:30
  51.6 1.4 %fusion.8 = f32[8,32,256]{2,1,0:T(8,128)S(1)} fusion(f32[8,31,256]{2,1,0:T(8,128)} %get-tuple-element.21, f32[8,1,256]{2,1,0:T(1,128)S(1)} %collective-permute-done, f32[8,1,256]{2,1,0:T(1,128)S(1)} %collective-permute-done.1, f32[8,31,256]{2,1,0:T(8,128)S(1)} %get-tuple-element.20, f32[8,32,255]{2,1,0:T(8,128)} %get-tuple-element.17, f32[8,32,1]{2,1,0:T(8,128)} %copy.61, ...), kind=kLoop, calls=%fused_computation.14 | loop fusion | flops 720896 | bytes 1605632 | tf_op jit(solution)/shard_map/add | solution.py:138
  53.0 0.1 pad_maximum_fusion
  53.1 1.5 %reshape.35 = f32[32,32,2,128]{3,2,1,0:T(2,128)} reshape(f32[32,32,256]{2,1,0:T(8,128)S(1)} %pad_maximum_fusion) | data formatting | bytes 2097152 | tf_op jit(solution)/shard_map/reshape | solution.py:38
  54.6 2.8 %convolution_bitcast_fusion = f32[4,32,2,128]{3,0,2,1:T(4,128)S(1)} fusion(f32[32,32,2,128]{3,2,1,0:T(2,128)} %reshape.35, f32[32,2,32,32]{3,2,1,0:T(8,128)S(1)} %reshape.34), kind=kOutput, calls=%fused_computation.2 | convolution fusion | flops 12582912 | bytes 1310720 | tf_op jit(solution)/shard_map/rbij,jrbc->irbc/dot_general | solution.py:40
  57.4 0.1 copy.65
  57.5 0.1 reshape.36
  57.6 0.6 copy-done.4
  58.3 0.7 rev.7.top_ref
  59.0 1.1 slice.120
  60.0 1.3 reshape.37.gain_ref
  61.4 1.5 %slice_reduce_fusion.2 = (f32[128,2]{1,0:T(8,128)S(1)}, f32[128,2]{1,0:T(8,128)S(1)}) fusion(f32[128,2,514]{2,1,0:T(2,128)} %all-to-all-done), kind=kLoop, calls=%fused_computation.22 | loop fusion | bytes 4096 | tf_op jit(solution)/shard_map/slice | solution.py:134
  62.8 0.7 reshape_squeeze.12.weight_ref
  63.6 0.7 reshape_squeeze.11.value_ref
  64.3 32.1 %shard_map.104 = (f32[4,32,256]{2,1,0:T(8,128)}, f32[256,8,128]{2,1,0:T(8,128)}) custom-call(s32[256]{0:T(256)} %reshape_squeeze.10.anchor_ref, f32[256]{0:T(256)} %reshape_squeeze.11.value_ref, f32[256]{0:T(256)} %reshape_squeeze.12.weight_ref, f32[4,32,256]{2,1,0:T(8,128)} %rev.7.top_ref, f32[256,4,128]{2,1,0:T(4,128)} %reshape.37.gain_ref), custom_call_target="tpu_custom_call" | custom-call | tf_op jit(solution)/shard_map/pallas_call | solution.py:98
  96.4 0.9 rev.8
  97.3 0.1 reshape.38
  97.4 1.8 %fusion = f32[32,32,2,128]{3,0,2,1:T(8,128)S(1)} fusion(f32[32,2,128,32]{2,3,1,0:T(8,128)S(1)} %fusion.2, f32[4,32,2,128]{3,2,1,0:T(2,128)S(1)} %reshape.38, f32[32,2,32,32]{3,2,1,0:T(8,128)S(1)} %reshape.34), kind=kOutput, calls=%fused_computation.1 | convolution fusion | flops 12845056 | bytes 2359296 | tf_op jit(solution)/shard_map/rbji,jrbc->irbc/dot_general | solution.py:40
  99.3 0.1 copy.68
  99.4 0.2 slice.107
  99.6 0.5 copy-done.3
  100.2 0.2 slice_reduce_fusion
  100.5 2.3 %slice_reduce_fusion.4 = f32[256]{0:T(256)S(1)} fusion(f32[256,8,128]{2,1,0:T(8,128)} %get-tuple-element.5), kind=kLoop, calls=%fused_computation.25 | loop fusion | bytes 2048 | tf_op jit(solution)/shard_map/slice | solution.py:145
  102.7 0.8 all_to_all.10
  103.5 16.4 %all-to-all-start.1 = ((f32[128,1,2]{2,1,0:T(1,128)}), f32[128,1,2]{2,1,0:T(1,128)S(1)}, u32[]{:S(2)}, u32[]{:S(2)}) async-start(f32[128,1,2]{2,1,0:T(1,128)} %bitcast.11), calls=%async_computation.1 | async-start | bytes 131072 | tf_op jit(solution)/shard_map/all_to_all | solution.py:146
  119.9 7.0 %collective-permute-start.7 = (f32[8,32]{1,0:T(8,128)S(1)}, f32[8,32]{1,0:T(8,128)S(1)}, u32[]{:S(2)}, u32[]{:S(2)}) collective-permute-start(f32[8,32]{1,0:T(8,128)S(1)} %get-tuple-element.14), channel_id=1, source_target_pairs={{1,0},{2,1},{3,2},{4,3},{5,4},{6,5},{7,6},{8,7},{9,8},{10,9},{11,1... | collective-permute-start | bytes 3080 | tf_op jit(solution)/shard_map/ppermute | solution.py:20
  126.8 1.9 %collective-permute-start.6 = (f32[8,32]{1,0:T(8,128)S(1)}, f32[8,32]{1,0:T(8,128)S(1)}, u32[]{:S(2)}, u32[]{:S(2)}) collective-permute-start(f32[8,32]{1,0:T(8,128)S(1)} %get-tuple-element.15), channel_id=1, source_target_pairs={{0,1},{1,2},{2,3},{3,4},{4,5},{5,6},{6,7},{7,8},{8,9},{9,10},{10,1... | collective-permute-start | bytes 3080 | tf_op jit(solution)/shard_map/ppermute | solution.py:20
  128.8 1.3 collective-permute-start.5
  130.1 3.0 %collective-permute-start.4 = (f32[8,1,256]{2,1,0:T(1,128)S(1)}, f32[8,1,256]{2,1,0:T(1,128)S(1)}, u32[]{:S(2)}, u32[]{:S(2)}) collective-permute-start(f32[8,1,256]{2,1,0:T(1,128)S(1)} %get-tuple-element.29), channel_id=1, source_target_pairs={{0,128},{128,256},{256,384},{1,129},{129,257},{257,385},{2,130},{1... | collective-permute-start | bytes 24584 | tf_op jit(solution)/shard_map/ppermute | solution.py:20
  133.1 0.1 fusion.20
  133.2 0.1 slice.121
  133.3 0.4 copy.67
  133.7 0.6 slice.105
  134.4 3.7 %collective-permute-done.6 = f32[8,32]{1,0:T(8,128)S(1)} collective-permute-done((f32[8,32]{1,0:T(8,128)S(1)}, f32[8,32]{1,0:T(8,128)S(1)}, u32[]{:S(2)}, u32[]{:S(2)}) %collective-permute-start.6) | collective-permute-done | bytes 1056 | tf_op jit(solution)/shard_map/ppermute | solution.py:20
  138.1 0.1 copy.69
  138.2 0.1 copy.70
  138.3 0.6 copy.72
  139.0 0.2 fusion.12
  139.2 1.0 pad_maximum_fusion.1
  (31 shorter events, 0.2 us)
Async XLA Ops:
  2.1 49.5 %collective-permute-start.1 = (f32[8,1,256]{2,1,0:T(1,128)}, f32[8,1,256]{2,1,0:T(1,128)S(1)}, u32[]{:S(2)}, u32[]{:S(2)}) collective-permute-start(f32[8,1,256]{2,1,0:T(1,128)} %get-tuple-element.22), channel_id=1, source_target_pairs={{128,0},{256,128},{384,256},{129,1},{257,129},{385,257},{130,2},{2... | collective-permute-start | bytes 24584 | tf_op jit(solution)/shard_map/ppermute | solution.py:20
  3.4 21.4 %copy-start.2 = (f32[1,1,128,2,512]{4,3,2,1,0:T(2,128)S(1)}, f32[1,1,128,2,512]{4,3,2,1,0:T(2,128)}, u32[]{:S(2)}) copy-start(f32[1,1,128,2,512]{4,3,2,1,0:T(2,128)} %param.15) | copy-start | bytes 1572868
  3.4 48.2 %collective-permute-start = (f32[8,1,256]{2,1,0:T(1,128)}, f32[8,1,256]{2,1,0:T(1,128)S(1)}, u32[]{:S(2)}, u32[]{:S(2)}) collective-permute-start(f32[8,1,256]{2,1,0:T(1,128)} %get-tuple-element.23), channel_id=1, source_target_pairs={{0,128},{128,256},{256,384},{1,129},{129,257},{257,385},{2,130},{1... | collective-permute-start | bytes 24584 | tf_op jit(solution)/shard_map/ppermute | solution.py:20
  8.4 41.8 %collective-permute-start.2 = (f32[8,32]{1,0:T(8,128)}, f32[8,32]{1,0:T(8,128)}, u32[]{:S(2)}, u32[]{:S(2)}) collective-permute-start(f32[8,32]{1,0:T(8,128)} %bitcast.3), channel_id=1, source_target_pairs={{0,1},{1,2},{2,3},{3,4},{4,5},{5,6},{6,7},{7,8},{8,9},{9,10},{10,1... | collective-permute-start | bytes 3080 | tf_op jit(solution)/shard_map/ppermute | solution.py:20
  13.4 10.4 %copy-start.7 = (f32[1,1,128,2]{2,3,1,0:T(2,128)S(1)}, f32[1,1,128,2]{2,3,1,0:T(2,128)}, u32[]{:S(2)}) copy-start(f32[1,1,128,2]{2,3,1,0:T(2,128)} %param.16) | copy-start | bytes 3076
  13.4 35.4 %collective-permute-start.3 = (f32[8,32]{1,0:T(8,128)S(1)}, f32[8,32]{1,0:T(8,128)S(1)}, u32[]{:S(2)}, u32[]{:S(2)}) collective-permute-start(f32[8,32]{1,0:T(8,128)S(1)} %bitcast.21), channel_id=1, source_target_pairs={{1,0},{2,1},{3,2},{4,3},{5,4},{6,5},{7,6},{8,7},{9,8},{10,9},{11,1... | collective-permute-start | bytes 3080 | tf_op jit(solution)/shard_map/ppermute | solution.py:20
  24.0 0.7 copy-start.8
  24.9 13.6 %copy-start = (f32[32,32,256]{2,1,0:T(8,128)S(1)}, f32[32,32,256]{2,1,0:T(8,128)}, u32[]{:S(2)}) copy-start(f32[32,32,256]{2,1,0:T(8,128)} %param.9) | copy-start | bytes 3145732
  26.1 32.9 %all-to-all-start = ((f32[128,2,514]{2,1,0:T(2,128)}), f32[128,2,514]{2,1,0:T(2,128)}, u32[]{:S(2)}, u32[]{:S(2)}) async-start(f32[128,2,514]{2,1,0:T(2,128)} %pad_maximum_fusion.2), calls=%async_computation | async-start | bytes 1310720 | tf_op jit(solution)/shard_map/all_to_all | solution.py:130
  38.5 2.2 %copy-start.1 = (f32[32,32,256]{2,1,0:T(8,128)S(1)}, f32[32,32,256]{2,1,0:T(8,128)}, u32[]{:S(2)}) copy-start(f32[32,32,256]{2,1,0:T(8,128)} %param.13) | copy-start | bytes 3145732
  46.5 0.8 copy-start.5
  47.3 0.7 copy-start.9
  48.8 0.6 copy-start.6
  51.6 1.4 %slice-start = ((f32[32,32,256]{2,1,0:T(8,128)}), f32[24,32,256]{2,1,0:T(8,128)S(1)}, s32[]{:S(2)}) async-start(f32[32,32,256]{2,1,0:T(8,128)} %param.9), calls=%async_computation.2 | async-start | bytes 1572864 | tf_op jit(solution)/shard_map/slice | solution.py:138
  57.5 0.8 copy-start.4
  99.4 0.8 copy-start.3
  103.5 34.8 %all-to-all-start.1 = ((f32[128,1,2]{2,1,0:T(1,128)}), f32[128,1,2]{2,1,0:T(1,128)S(1)}, u32[]{:S(2)}, u32[]{:S(2)}) async-start(f32[128,1,2]{2,1,0:T(1,128)} %bitcast.11), calls=%async_computation.1 | async-start | bytes 131072 | tf_op jit(solution)/shard_map/all_to_all | solution.py:146
  119.9 18.3 %collective-permute-start.7 = (f32[8,32]{1,0:T(8,128)S(1)}, f32[8,32]{1,0:T(8,128)S(1)}, u32[]{:S(2)}, u32[]{:S(2)}) collective-permute-start(f32[8,32]{1,0:T(8,128)S(1)} %get-tuple-element.14), channel_id=1, source_target_pairs={{1,0},{2,1},{3,2},{4,3},{5,4},{6,5},{7,6},{8,7},{9,8},{10,9},{11,1... | collective-permute-start | bytes 3080 | tf_op jit(solution)/shard_map/ppermute | solution.py:20
  126.8 11.2 %collective-permute-start.6 = (f32[8,32]{1,0:T(8,128)S(1)}, f32[8,32]{1,0:T(8,128)S(1)}, u32[]{:S(2)}, u32[]{:S(2)}) collective-permute-start(f32[8,32]{1,0:T(8,128)S(1)} %get-tuple-element.15), channel_id=1, source_target_pairs={{0,1},{1,2},{2,3},{3,4},{4,5},{5,6},{6,7},{7,8},{8,9},{9,10},{10,1... | collective-permute-start | bytes 3080 | tf_op jit(solution)/shard_map/ppermute | solution.py:20
  128.8 10.2 %collective-permute-start.5 = (f32[8,1,256]{2,1,0:T(1,128)S(1)}, f32[8,1,256]{2,1,0:T(1,128)S(1)}, u32[]{:S(2)}, u32[]{:S(2)}) collective-permute-start(f32[8,1,256]{2,1,0:T(1,128)S(1)} %get-tuple-element.28), channel_id=1, source_target_pairs={{128,0},{256,128},{384,256},{129,1},{257,129},{385,257},{130,2},{2... | collective-permute-start | bytes 24584 | tf_op jit(solution)/shard_map/ppermute | solution.py:20
  130.1 8.9 %collective-permute-start.4 = (f32[8,1,256]{2,1,0:T(1,128)S(1)}, f32[8,1,256]{2,1,0:T(1,128)S(1)}, u32[]{:S(2)}, u32[]{:S(2)}) collective-permute-start(f32[8,1,256]{2,1,0:T(1,128)S(1)} %get-tuple-element.29), channel_id=1, source_target_pairs={{0,128},{128,256},{256,384},{1,129},{129,257},{257,385},{2,130},{1... | collective-permute-start | bytes 24584 | tf_op jit(solution)/shard_map/ppermute | solution.py:20

commit v3 on v2

--- a/solution.py
+++ b/solution.py
@@ -42,38 +42,29 @@
 
 
 def footprint_kernel(anchor_ref, value_ref, weight_ref, top_ref, gain_ref, bar_ref, res_ref):
-    layers, tile_rows, tile_cols = top_ref.shape
+    tile_cols, wide = top_ref.shape
     slots = gain_ref.shape[0]
-    groups = tile_cols // LANES
-    row = lax.broadcasted_iota(jnp.int32, (2 * FH, tile_cols), 0)
-    lane = lax.broadcasted_iota(jnp.int32, (2 * FH, tile_cols), 1)
+    tile_rows = wide // LTOP
+    span = FW + FH
+    sub = lax.broadcasted_iota(jnp.int32, (FH, wide), 0)
 
     def placed(s):
         o = jnp.maximum(anchor_ref[s], 0)
         r = jnp.minimum(lax.div(o, tile_cols), tile_rows - FH)
         c = jnp.minimum(lax.rem(o, tile_cols), tile_cols - FW)
-        flip = tile_rows - FH - r
-        g0 = jnp.minimum(lax.div(flip, FH), tile_rows // FH - 2) * FH
-        g0 = pl.multiple_of(g0, FH)
-        off = flip - g0
-        g = gain_ref[s]
-        g = jnp.broadcast_to(g[:, None, :], (layers, FH, LANES))
-        g = pltpu.roll(g, 0, 2, stride=FW, stride_axis=1)
-        g = pltpu.roll(g, lax.rem(c + FW, LANES), 2)
-        g = pltpu.roll(g, lax.rem(off, FH), 1)
-        g = jnp.concatenate([g, g], axis=1)
-        g = jnp.concatenate([g] * groups, axis=2)
-        inside = (row >= off) & (row < off + FH) & (lane >= c) & (lane < c + FW)
-        return g0, jnp.where(inside[None], g, 0.0)
+        c8 = pl.multiple_of(jnp.minimum(lax.div(c, FH) * FH, tile_cols - span), FH)
+        off = c - c8
+        g = pltpu.roll(gain_ref[s], r, 1)
+        a = pltpu.roll(g[0:FH], lax.rem(off, FH), 0)
+        b = pltpu.roll(g[FH:FW], lax.rem(off, FH), 0)
+        low = sub >= off
+        parts = (jnp.where(low, a, 0.0), jnp.where(low, b, a), jnp.where(low, 0.0, b))
+        return c8, parts
 
     def predict(s, carry):
-        g0, g = placed(s)
-        t = top_ref[:, pl.ds(g0, 2 * FH), :]
-        part = jnp.sum(g * t, axis=0)
-        part = part[:FH] + part[FH:]
-        acc = part[:, 0:LANES]
-        for q in range(1, groups):
-            acc = acc + part[:, q * LANES:(q + 1) * LANES]
+        c8, parts = placed(s)
+        t = top_ref[pl.ds(c8, span), :]
+        acc = parts[0] * t[0:FH] + parts[1] * t[FH:FW] + parts[2] * t[FW:span]
         predicted = jnp.sum(acc, axis=(0, 1), keepdims=True)
         live = jnp.where(anchor_ref[s] >= 0, 1.0, 0.0).astype(jnp.float32)
         res = (live * weight_ref[s]) * (predicted - value_ref[s])
@@ -81,14 +72,14 @@
         return carry
 
     def scatter(s, carry):
-        g0, g = placed(s)
+        c8, parts = placed(s)
         res = res_ref[s][0:1, 0:1]
-        bar_ref[:, pl.ds(g0, 2 * FH), :] += res * g
+        bar_ref[pl.ds(c8, span), :] += res * jnp.concatenate(parts, axis=0)
         return carry
 
-    lax.fori_loop(0, slots, predict, 0, unroll=4)
+    lax.fori_loop(0, slots, predict, 0, unroll=8)
     bar_ref[...] = jnp.zeros(bar_ref.shape, bar_ref.dtype)
-    lax.fori_loop(0, slots, scatter, 0, unroll=4)
+    lax.fori_loop(0, slots, scatter, 0, unroll=8)
 
 
 def footprints(anchor, value, weight, top, gain):
@@ -129,7 +120,9 @@
     )
     received = lax.all_to_all(packed, "lon", split_axis=0, concat_axis=0, tiled=True)
     slots = owners * slots_per
-    gain = received[..., :K].reshape(slots, LTOP, LANES)
+    gain = received[..., :K].reshape(slots, LTOP, FH, FW).transpose(0, 3, 1, 2)
+    gain = jnp.pad(gain, ((0, 0), (0, 0), (0, 0), (0, tile_rows - FH)))
+    gain = gain.reshape(slots, FW, LTOP * tile_rows)
     value = received[..., K].reshape(slots)
     weight = received[..., K + 1].reshape(slots)
 
@@ -138,7 +131,7 @@
         [moisture[: levels - LG], deep + conductance * stencil(deep)], 0
     )
     solved_top = columns(matrices[:, :, :LTOP, :], mixed, False)
-    topmost = jnp.flip(solved_top * mask_float, 1)
+    topmost = (solved_top * mask_float).transpose(2, 0, 1).reshape(tile_cols, LTOP * tile_rows)
 
     slot_anchor = foot_anchor[0, 0].reshape(slots)
     bar, rows = footprints(slot_anchor, value, weight, topmost, gain)
@@ -146,7 +139,7 @@
     residual_out = lax.all_to_all(residual, "lon", split_axis=0, concat_axis=0, tiled=True)
 
     base = columns(matrices, adjoint_in, True)
-    topbar = jnp.flip(bar, 1) * mask_float
+    topbar = bar.reshape(tile_cols, LTOP, tile_rows).transpose(1, 2, 0) * mask_float
     mixedbar = base + columns(matrices[:, :, :LTOP, :], topbar, True)
     deepbar = mixedbar[levels - LG :]
     gradient = jnp.concatenate(

time: 141 us -> 154 us (1.092)
  the two profiles are of different devices: /device:TPU:32 before, /device:TPU:1 now
where the time goes in v3:
time: 154 us; the launch traced here: 153 us
  starting transfers between devices  59 us (38%)
  local copies, waits for them, and re-layouts  50.2 us (33%)
  waiting for transfers between devices  14.6 us (9%)
  Pallas kernels  13.3 us (9%)
  matrix products  8.01 us (5%)
  other arithmetic  6.58 us (4%)
    all_to_all x1, starting transfers between devices, per_device(): lax.all_to_all(packed, 'lon', split_axis=0, concat_axis=0, tiled=True)  21.5 us
    ppermute x4, starting transfers between devices, neighbours(): lax.ppermute(edge_high, axis, forward)  15.6 us
    all_to_all x1, starting transfers between devices, per_device(): lax.all_to_all(residual, 'lon', split_axis=0, concat_axis=0, tiled=True)  14.5 us
    pallas_call x1, Pallas kernels, footprints(): pl.pallas_call(footprint_kernel, out_shape=(jax.ShapeDtypeStruct(top.shap...  13.3 us
    reshape x1, local copies, waits for them, and re-layouts, per_device(): gain = gain.reshape(slots, FW, LTOP * tile_rows)  10.8 us
    pad x1, local copies, waits for them, and re-layouts, per_device(): gain = jnp.pad(gain, ((0, 0), (0, 0), (0, 0), (0, tile_rows - FH)))  10.1 us
    all_to_all x1, waiting for transfers between devices, per_device(): lax.all_to_all(residual, 'lon', split_axis=0, concat_axis=0, tiled=True)  10.1 us
    dot_general x3, matrix products, columns(): out = jnp.einsum(form, matrices, grouped, precision=lax.Precision.HIGHEST)  8.01 us
  transfers between devices with their start and end apart: 10, of which 2 were waited for; matrix products, arithmetic and copies ran while one was open for 19% of the time, Pallas kernels for 0%

profile of v3, /device:TPU:1, one launch (start us, length us, event | category | flops | bytes accessed | tf_op | source)
XLA Modules:
  0.0 152.7 jit_solution(1694957611397527650)
XLA Ops:
  0.6 0.0 copy-start
  0.7 1.2 fusion.17
  1.9 0.1 copy.88
  2.0 5.5 %collective-permute-start.2 = (f32[8,32]{1,0:T(8,128)S(1)}, f32[8,32]{1,0:T(8,128)S(1)}, u32[]{:S(2)}, u32[]{:S(2)}) collective-permute-start(f32[8,32]{1,0:T(8,128)S(1)} %bitcast.32), channel_id=1, source_target_pairs={{0,1},{1,2},{2,3},{3,4},{4,5},{5,6},{6,7},{7,8},{8,9},{9,10},{10,1... | collective-permute-start | bytes 3080 | tf_op jit(solution)/shard_map/ppermute | solution.py:20
  7.5 0.7 copy.89
  8.2 1.3 collective-permute-start.3
  9.5 1.5 fusion.19
  10.9 3.0 %collective-permute-start = (f32[8,1,256]{2,1,0:T(1,128)}, f32[8,1,256]{2,1,0:T(1,128)S(1)}, u32[]{:S(2)}, u32[]{:S(2)}) collective-permute-start(f32[8,1,256]{2,1,0:T(1,128)} %get-tuple-element.23), channel_id=1, source_target_pairs={{0,128},{128,256},{256,384},{1,129},{129,257},{257,385},{2,130},{1... | collective-permute-start | bytes 24584 | tf_op jit(solution)/shard_map/ppermute | solution.py:20
  14.0 2.8 %collective-permute-start.1 = (f32[8,1,256]{2,1,0:T(1,128)}, f32[8,1,256]{2,1,0:T(1,128)S(1)}, u32[]{:S(2)}, u32[]{:S(2)}) collective-permute-start(f32[8,1,256]{2,1,0:T(1,128)} %get-tuple-element.22), channel_id=1, source_target_pairs={{128,0},{256,128},{384,256},{129,1},{257,129},{385,257},{130,2},{2... | collective-permute-start | bytes 24584 | tf_op jit(solution)/shard_map/ppermute | solution.py:20
  16.8 0.8 copy.66
  17.7 0.8 copy.67
  18.5 2.3 %pad_maximum_fusion.2 = f32[128,2,514]{2,1,0:T(2,128)} fusion(f32[128,2,1]{2,1,0:T(2,128)S(1)} %copy.67, f32[128,2,1]{2,1,0:T(2,128)S(1)} %copy.66, f32[128,2,512]{2,1,0:T(2,128)} %bitcast.30), kind=kLoop, calls=%fused_computation.8 | loop fusion | flops 263168 | bytes 1052672 | tf_op jit(solution)/shard_map/concatenate | solution.py:118
  20.8 21.5 %all-to-all-start = ((f32[128,2,514]{2,1,0:T(2,128)}), f32[128,2,514]{2,1,0:T(2,128)}, u32[]{:S(2)}, u32[]{:S(2)}) async-start(f32[128,2,514]{2,1,0:T(2,128)} %pad_maximum_fusion.2), calls=%async_computation | async-start | bytes 1310720 | tf_op jit(solution)/shard_map/all_to_all | solution.py:121
  42.3 0.8 fusion.16
  43.0 1.4 reshape.43
  44.5 1.5 reshape.42
  46.0 4.6 %fusion.2 = f32[32,2,128,32]{2,3,1,0:T(8,128)} fusion(f32[32,2,32,32]{3,2,1,0:T(8,128)S(1)} %reshape.43, f32[32,32,2,128]{3,2,1,0:T(2,128)} %reshape.42), kind=kOutput, calls=%fused_computation.6 | convolution fusion | flops 100663296 | bytes 2359296 | tf_op jit(solution)/shard_map/rbji,jrbc->irbc/dot_general | solution.py:40
  50.6 0.8 fusion.18
  51.4 0.6 convert_element_type.5
  52.0 0.1 copy.65
  52.1 0.7 reshape_squeeze.10.anchor_ref
  52.8 0.6 copy-done.7
  53.4 0.8 copy.69
  54.2 1.5 copy.71
  55.7 1.3 fusion.8
  57.0 0.1 pad_maximum_fusion
  57.1 0.5 reshape.44
  57.7 1.6 %convolution_bitcast_fusion = f32[4,32,2,128]{3,0,2,1:T(4,128)S(1)} fusion(f32[32,32,2,128]{3,2,1,0:T(2,128)S(1)} %reshape.44, f32[32,2,32,32]{3,2,1,0:T(8,128)S(1)} %reshape.43), kind=kOutput, calls=%fused_computation.2 | convolution fusion | flops 12582912 | bytes 1310720 | tf_op jit(solution)/shard_map/rbij,jrbc->irbc/dot_general | solution.py:40
  59.2 0.1 copy.73
  59.3 0.1 reshape.45
  59.5 0.8 copy.75.top_ref
  60.2 4.5 %all-to-all-done = f32[128,2,514]{2,1,0:T(2,128)} async-done(((f32[128,2,514]{2,1,0:T(2,128)}), f32[128,2,514]{2,1,0:T(2,128)}, u32[]{:S(2)}, u32[]{:S(2)}) %all-to-all-start) | async-done | bytes 526368 | tf_op jit(solution)/shard_map/all_to_all | solution.py:121
  64.7 1.5 slice_reduce_fusion.2
  66.2 0.7 reshape_squeeze.11.value_ref
  66.9 0.7 reshape_squeeze.12.weight_ref
  67.7 1.1 slice.120
  68.8 2.8 %reshape.47 = f32[256,4,8,16]{3,2,1,0:T(8,128)} reshape(f32[128,2,512]{2,1,0:T(2,128)S(1)} %slice.120) | data formatting | bytes 1048576 | tf_op jit(solution)/shard_map/reshape | solution.py:123
  71.5 10.1 %pad.4 = f32[256,16,4,32]{1,3,2,0:T(8,128)} pad(f32[256,16,4,8]{1,3,2,0:T(8,128)} %bitcast.27, f32[]{:T(128)} %constant.4.clone.1), padding=0_0x0_0x0_0x0_24 | pad | bytes 2621444 | tf_op jit(solution)/shard_map/jit(_pad)/pad | solution.py:124
  81.7 10.8 %copy.76.gain_ref = f32[256,16,128]{2,1,0:T(8,128)} copy(f32[256,16,128]{1,2,0:T(8,128)} %bitcast.26) | data formatting | bytes 4194304 | tf_op jit(solution)/shard_map/reshape | solution.py:125
  92.4 13.3 %shard_map.104 = (f32[256,128]{1,0:T(8,128)}, f32[256,8,128]{2,1,0:T(8,128)}) custom-call(s32[256]{0:T(256)} %reshape_squeeze.10.anchor_ref, f32[256]{0:T(256)} %reshape_squeeze.11.value_ref, f32[256]{0:T(256)} %reshape_squeeze.12.weight_ref, f32[256,128]{1,0:T(8,128)} %copy.75.top_ref, f32[256,16,128]{2,1,0:T(8,128)} %copy.76.gain_ref), custom_call_target="tpu_custom_call" | custom-call | tf_op jit(solution)/shard_map/pallas_call | solution.py:89
  105.7 1.0 copy.77
  106.8 0.1 reshape.50
  106.9 1.8 %fusion = f32[32,32,2,128]{3,0,2,1:T(8,128)S(1)} fusion(f32[32,2,128,32]{2,3,1,0:T(8,128)S(1)} %copy-done.1, f32[4,32,2,128]{3,2,1,0:T(2,128)S(1)} %reshape.50, f32[32,2,32,32]{3,2,1,0:T(8,128)S(1)} %reshape.43), kind=kOutput, calls=%fused_computation.1 | convolution fusion | flops 12845056 | bytes 2359296 | tf_op jit(solution)/shard_map/rbji,jrbc->irbc/dot_general | solution.py:40
  108.8 0.1 copy.80
  108.9 0.2 slice.107
  109.2 0.1 fusion.20
  109.3 0.2 slice_reduce_fusion
  109.5 2.6 %collective-permute-start.6 = (f32[8,32]{1,0:T(8,128)S(1)}, f32[8,32]{1,0:T(8,128)S(1)}, u32[]{:S(2)}, u32[]{:S(2)}) collective-permute-start(f32[8,32]{1,0:T(8,128)S(1)} %get-tuple-element.15), channel_id=1, source_target_pairs={{0,1},{1,2},{2,3},{3,4},{4,5},{5,6},{6,7},{7,8},{8,9},{9,10},{10,1... | collective-permute-start | bytes 3080 | tf_op jit(solution)/shard_map/ppermute | solution.py:20
  112.2 1.3 collective-permute-start.7
  113.5 4.5 %collective-permute-start.4 = (f32[8,1,256]{2,1,0:T(1,128)S(1)}, f32[8,1,256]{2,1,0:T(1,128)S(1)}, u32[]{:S(2)}, u32[]{:S(2)}) collective-permute-start(f32[8,1,256]{2,1,0:T(1,128)S(1)} %get-tuple-element.29), channel_id=1, source_target_pairs={{0,128},{128,256},{256,384},{1,129},{129,257},{257,385},{2,130},{1... | collective-permute-start | bytes 24584 | tf_op jit(solution)/shard_map/ppermute | solution.py:20
  118.0 1.9 %collective-permute-start.5 = (f32[8,1,256]{2,1,0:T(1,128)S(1)}, f32[8,1,256]{2,1,0:T(1,128)S(1)}, u32[]{:S(2)}, u32[]{:S(2)}) collective-permute-start(f32[8,1,256]{2,1,0:T(1,128)S(1)} %get-tuple-element.28), channel_id=1, source_target_pairs={{128,0},{256,128},{384,256},{129,1},{257,129},{385,257},{130,2},{2... | collective-permute-start | bytes 24584 | tf_op jit(solution)/shard_map/ppermute | solution.py:20
  119.9 2.3 %slice_reduce_fusion.4 = f32[256]{0:T(256)S(1)} fusion(f32[256,8,128]{2,1,0:T(8,128)} %get-tuple-element.5), kind=kLoop, calls=%fused_computation.25 | loop fusion | bytes 2048 | tf_op jit(solution)/shard_map/slice | solution.py:138
  122.1 0.8 all_to_all.10
  122.9 14.5 %all-to-all-start.1 = ((f32[128,1,2]{2,1,0:T(1,128)}), f32[128,1,2]{2,1,0:T(1,128)S(1)}, u32[]{:S(2)}, u32[]{:S(2)}) async-start(f32[128,1,2]{2,1,0:T(1,128)} %bitcast.17), calls=%async_computation.1 | async-start | bytes 131072 | tf_op jit(solution)/shard_map/all_to_all | solution.py:139
  137.5 0.8 fusion.21
  138.3 0.1 slice.121
  138.4 0.4 copy.79
  138.8 0.6 slice.105
  139.4 0.1 copy.81
  139.6 0.1 copy.82
  139.7 10.1 %all-to-all-done.1 = f32[128,1,2]{2,1,0:T(1,128)S(1)} async-done(((f32[128,1,2]{2,1,0:T(1,128)}), f32[128,1,2]{2,1,0:T(1,128)S(1)}, u32[]{:S(2)}, u32[]{:S(2)}) %all-to-all-start.1) | async-done | bytes 1056 | tf_op jit(solution)/shard_map/all_to_all | solution.py:139
  149.8 0.6 copy.84
  150.4 1.2 fusion.12
  151.7 1.0 pad_maximum_fusion.1
  (31 shorter events, 0.2 us)
Async XLA Ops:
  0.6 41.6 %copy-start = (f32[32,32,256]{2,1,0:T(8,128)S(1)}, f32[32,32,256]{2,1,0:T(8,128)}, u32[]{:S(2)}) copy-start(f32[32,32,256]{2,1,0:T(8,128)} %param.9) | copy-start | bytes 3145732
  0.6 43.8 %copy-start.2 = (f32[32,32,256]{2,1,0:T(8,128)S(1)}, f32[32,32,256]{2,1,0:T(8,128)}, u32[]{:S(2)}) copy-start(f32[32,32,256]{2,1,0:T(8,128)} %param.13) | copy-start | bytes 3145732
  2.0 50.8 %collective-permute-start.2 = (f32[8,32]{1,0:T(8,128)S(1)}, f32[8,32]{1,0:T(8,128)S(1)}, u32[]{:S(2)}, u32[]{:S(2)}) collective-permute-start(f32[8,32]{1,0:T(8,128)S(1)} %bitcast.32), channel_id=1, source_target_pairs={{0,1},{1,2},{2,3},{3,4},{4,5},{5,6},{6,7},{7,8},{8,9},{9,10},{10,1... | collective-permute-start | bytes 3080 | tf_op jit(solution)/shard_map/ppermute | solution.py:20
  8.2 46.1 %collective-permute-start.3 = (f32[8,32]{1,0:T(8,128)}, f32[8,32]{1,0:T(8,128)}, u32[]{:S(2)}, u32[]{:S(2)}) collective-permute-start(f32[8,32]{1,0:T(8,128)} %bitcast.5), channel_id=1, source_target_pairs={{1,0},{2,1},{3,2},{4,3},{5,4},{6,5},{7,6},{8,7},{9,8},{10,9},{11,1... | collective-permute-start | bytes 3080 | tf_op jit(solution)/shard_map/ppermute | solution.py:20
  10.9 44.8 %collective-permute-start = (f32[8,1,256]{2,1,0:T(1,128)}, f32[8,1,256]{2,1,0:T(1,128)S(1)}, u32[]{:S(2)}, u32[]{:S(2)}) collective-permute-start(f32[8,1,256]{2,1,0:T(1,128)} %get-tuple-element.23), channel_id=1, source_target_pairs={{0,128},{128,256},{256,384},{1,129},{129,257},{257,385},{2,130},{1... | collective-permute-start | bytes 24584 | tf_op jit(solution)/shard_map/ppermute | solution.py:20
  14.0 41.7 %collective-permute-start.1 = (f32[8,1,256]{2,1,0:T(1,128)}, f32[8,1,256]{2,1,0:T(1,128)S(1)}, u32[]{:S(2)}, u32[]{:S(2)}) collective-permute-start(f32[8,1,256]{2,1,0:T(1,128)} %get-tuple-element.22), channel_id=1, source_target_pairs={{128,0},{256,128},{384,256},{129,1},{257,129},{385,257},{130,2},{2... | collective-permute-start | bytes 24584 | tf_op jit(solution)/shard_map/ppermute | solution.py:20
  20.8 43.9 %all-to-all-start = ((f32[128,2,514]{2,1,0:T(2,128)}), f32[128,2,514]{2,1,0:T(2,128)}, u32[]{:S(2)}, u32[]{:S(2)}) async-start(f32[128,2,514]{2,1,0:T(2,128)} %pad_maximum_fusion.2), calls=%async_computation | async-start | bytes 1310720 | tf_op jit(solution)/shard_map/all_to_all | solution.py:121
  44.5 6.9 %copy-start.6 = (s32[32,256]{1,0:T(8,128)S(1)}, s32[32,256]{1,0:T(8,128)}, u32[]{:S(2)}) copy-start(s32[32,256]{1,0:T(8,128)} %param.12) | copy-start | bytes 98308
  44.5 7.5 %copy-start.8 = (s32[1,1,128,2]{2,3,1,0:T(2,128)S(1)}, s32[1,1,128,2]{2,3,1,0:T(2,128)}, u32[]{:S(2)}) copy-start(s32[1,1,128,2]{2,3,1,0:T(2,128)} %param.14) | copy-start | bytes 3076
  46.0 9.7 %copy-start.3 = (f32[8,32,255]{2,1,0:T(8,128)S(1)}, f32[8,32,255]{2,1,0:T(8,128)}, u32[]{:S(2)}) copy-start(f32[8,32,255]{2,1,0:T(8,128)} %get-tuple-element.17) | copy-start | bytes 783364
  46.0 11.0 %slice-start = ((f32[32,32,256]{2,1,0:T(8,128)}), f32[24,32,256]{2,1,0:T(8,128)S(1)}, s32[]{:S(2)}) async-start(f32[32,32,256]{2,1,0:T(8,128)} %param.9), calls=%async_computation.2 | async-start | bytes 1572864 | tf_op jit(solution)/shard_map/slice | solution.py:131
  52.8 0.6 copy-start.7
  57.0 2.5 %copy-start.5 = (f32[32,256]{1,0:T(8,128)S(1)}, f32[32,256]{1,0:T(8,128)}, u32[]{:S(2)}) copy-start(f32[32,256]{1,0:T(8,128)} %convert_element_type.5) | copy-start | bytes 98308
  81.7 25.2 %copy-start.1 = (f32[32,2,128,32]{2,3,1,0:T(8,128)S(1)}, f32[32,2,128,32]{2,3,1,0:T(8,128)}, u32[]{:S(2)}) copy-start(f32[32,2,128,32]{2,3,1,0:T(8,128)} %fusion.2) | copy-start | bytes 3145732
  92.4 16.7 %copy-start.4 = (f32[32,256]{1,0:T(8,128)S(1)}, f32[32,256]{1,0:T(8,128)}, u32[]{:S(2)}) copy-start(f32[32,256]{1,0:T(8,128)} %param.10) | copy-start | bytes 98308
  109.5 29.9 %collective-permute-start.6 = (f32[8,32]{1,0:T(8,128)S(1)}, f32[8,32]{1,0:T(8,128)S(1)}, u32[]{:S(2)}, u32[]{:S(2)}) collective-permute-start(f32[8,32]{1,0:T(8,128)S(1)} %get-tuple-element.15), channel_id=1, source_target_pairs={{0,1},{1,2},{2,3},{3,4},{4,5},{5,6},{6,7},{7,8},{8,9},{9,10},{10,1... | collective-permute-start | bytes 3080 | tf_op jit(solution)/shard_map/ppermute | solution.py:20
  112.2 27.4 %collective-permute-start.7 = (f32[8,32]{1,0:T(8,128)S(1)}, f32[8,32]{1,0:T(8,128)S(1)}, u32[]{:S(2)}, u32[]{:S(2)}) collective-permute-start(f32[8,32]{1,0:T(8,128)S(1)} %get-tuple-element.14), channel_id=1, source_target_pairs={{1,0},{2,1},{3,2},{4,3},{5,4},{6,5},{7,6},{8,7},{9,8},{10,9},{11,1... | collective-permute-start | bytes 3080 | tf_op jit(solution)/shard_map/ppermute | solution.py:20
  113.5 36.9 %collective-permute-start.4 = (f32[8,1,256]{2,1,0:T(1,128)S(1)}, f32[8,1,256]{2,1,0:T(1,128)S(1)}, u32[]{:S(2)}, u32[]{:S(2)}) collective-permute-start(f32[8,1,256]{2,1,0:T(1,128)S(1)} %get-tuple-element.29), channel_id=1, source_target_pairs={{0,128},{128,256},{256,384},{1,129},{129,257},{257,385},{2,130},{1... | collective-permute-start | bytes 24584 | tf_op jit(solution)/shard_map/ppermute | solution.py:20
  118.0 32.5 %collective-permute-start.5 = (f32[8,1,256]{2,1,0:T(1,128)S(1)}, f32[8,1,256]{2,1,0:T(1,128)S(1)}, u32[]{:S(2)}, u32[]{:S(2)}) collective-permute-start(f32[8,1,256]{2,1,0:T(1,128)S(1)} %get-tuple-element.28), channel_id=1, source_target_pairs={{128,0},{256,128},{384,256},{129,1},{257,129},{385,257},{130,2},{2... | collective-permute-start | bytes 24584 | tf_op jit(solution)/shard_map/ppermute | solution.py:20
  122.9 26.9 %all-to-all-start.1 = ((f32[128,1,2]{2,1,0:T(1,128)}), f32[128,1,2]{2,1,0:T(1,128)S(1)}, u32[]{:S(2)}, u32[]{:S(2)}) async-start(f32[128,1,2]{2,1,0:T(1,128)} %bitcast.17), calls=%async_computation.1 | async-start | bytes 131072 | tf_op jit(solution)/shard_map/all_to_all | solution.py:139

commit v4 on v3

--- a/solution.py
+++ b/solution.py
@@ -43,10 +43,11 @@
 
 def footprint_kernel(anchor_ref, value_ref, weight_ref, top_ref, gain_ref, bar_ref, res_ref):
     tile_cols, wide = top_ref.shape
-    slots = gain_ref.shape[0]
+    slots, _, narrow = gain_ref.shape
     tile_rows = wide // LTOP
     span = FW + FH
     sub = lax.broadcasted_iota(jnp.int32, (FH, wide), 0)
+    pad = jnp.zeros((FW, wide - narrow), jnp.float32)
 
     def placed(s):
         o = jnp.maximum(anchor_ref[s], 0)
@@ -54,7 +55,8 @@
         c = jnp.minimum(lax.rem(o, tile_cols), tile_cols - FW)
         c8 = pl.multiple_of(jnp.minimum(lax.div(c, FH) * FH, tile_cols - span), FH)
         off = c - c8
-        g = pltpu.roll(gain_ref[s], r, 1)
+        g = jnp.concatenate([gain_ref[s], pad], axis=1)
+        g = pltpu.roll(g, r * LTOP, 1)
         a = pltpu.roll(g[0:FH], lax.rem(off, FH), 0)
         b = pltpu.roll(g[FH:FW], lax.rem(off, FH), 0)
         low = sub >= off
@@ -120,9 +122,14 @@
     )
     received = lax.all_to_all(packed, "lon", split_axis=0, concat_axis=0, tiled=True)
     slots = owners * slots_per
-    gain = received[..., :K].reshape(slots, LTOP, FH, FW).transpose(0, 3, 1, 2)
-    gain = jnp.pad(gain, ((0, 0), (0, 0), (0, 0), (0, tile_rows - FH)))
-    gain = gain.reshape(slots, FW, LTOP * tile_rows)
+    source = lax.broadcasted_iota(jnp.int32, (K, K), 0)
+    target = lax.broadcasted_iota(jnp.int32, (K, K), 1)
+    layer_of = source // (FH * FW)
+    row_of = (source // FW) % FH
+    col_of = source % FW
+    reorder = (target == (col_of * FH + row_of) * LTOP + layer_of).astype(jnp.float32)
+    gain = jnp.dot(received[..., :K].reshape(slots, K), reorder, precision=lax.Precision.HIGHEST)
+    gain = gain.reshape(slots, FW, FH * LTOP)
     value = received[..., K].reshape(slots)
     weight = received[..., K + 1].reshape(slots)
 
@@ -131,7 +138,7 @@
         [moisture[: levels - LG], deep + conductance * stencil(deep)], 0
     )
     solved_top = columns(matrices[:, :, :LTOP, :], mixed, False)
-    topmost = (solved_top * mask_float).transpose(2, 0, 1).reshape(tile_cols, LTOP * tile_rows)
+    topmost = (solved_top * mask_float).transpose(2, 1, 0).reshape(tile_cols, tile_rows * LTOP)
 
     slot_anchor = foot_anchor[0, 0].reshape(slots)
     bar, rows = footprints(slot_anchor, value, weight, topmost, gain)
@@ -139,7 +146,7 @@
     residual_out = lax.all_to_all(residual, "lon", split_axis=0, concat_axis=0, tiled=True)
 
     base = columns(matrices, adjoint_in, True)
-    topbar = bar.reshape(tile_cols, LTOP, tile_rows).transpose(1, 2, 0) * mask_float
+    topbar = bar.reshape(tile_cols, tile_rows, LTOP).transpose(2, 1, 0) * mask_float
     mixedbar = base + columns(matrices[:, :, :LTOP, :], topbar, True)
     deepbar = mixedbar[levels - LG :]
     gradient = jnp.concatenate(

time: 154 us -> 134 us (0.87)
  local copies, waits for them, and re-layouts: 50.2 us -> 28.8 us
  other arithmetic: 6.58 us -> 9.07 us
  waiting for transfers between devices: 14.6 us -> 12.9 us
    reshape x3 -> x4, local copies, waits for them, and re-layouts: 14.3 us -> 1.2 us  [the longest x2 0.8 us: per_device(): (solved_top * mask_float).transpose(2, 1, 0)]
    pad x1 -> x0, local copies, waits for them, and re-layouts: 10.1 us -> none  [per_device(): gain = jnp.pad(gain, ((0, 0), (0, 0), (0, 0), (0, tile_rows - FH)))]
    dot_general x0 -> x1, local copies, waits for them, and re-layouts: none -> 2.48 us  [per_device(): jnp.dot(received[..., :K].reshape(slots, K), reorder, precision=lax.Preci...]
    all_to_all x1, waiting for transfers between devices: 4.5 us -> 2.79 us  [per_device(): lax.all_to_all(packed, 'lon', split_axis=0, concat_axis=0, tiled=True)]
    all_to_all x1, starting transfers between devices: 14.5 us -> 16.2 us  [per_device(): lax.all_to_all(residual, 'lon', split_axis=0, concat_axis=0, tiled=True)]
  transfers between devices with their start and end apart: 10 -> 10, of which waited for: 2 -> 2; matrix products, arithmetic and copies ran while one was open for 19% -> 23% of each run, Pallas kernels for 0% -> 0%
where the time goes in v4:
time: 134 us; the launch traced here: 133 us
  starting transfers between devices  60.3 us (45%)
  local copies, waits for them, and re-layouts  28.8 us (21%)
  Pallas kernels  13.5 us (10%)
  waiting for transfers between devices  12.9 us (10%)
  other arithmetic  9.07 us (7%)
  matrix products  7.39 us (6%)
    all_to_all x1, starting transfers between devices, per_device(): lax.all_to_all(packed, 'lon', split_axis=0, concat_axis=0, tiled=True)  21.5 us
    all_to_all x1, starting transfers between devices, per_device(): lax.all_to_all(residual, 'lon', split_axis=0, concat_axis=0, tiled=True)  16.2 us
    ppermute x4, starting transfers between devices, neighbours(): lax.ppermute(edge_high, axis, forward)  15.3 us
    pallas_call x1, Pallas kernels, footprints(): pl.pallas_call(footprint_kernel, out_shape=(jax.ShapeDtypeStruct(top.shap...  13.5 us
    all_to_all x1, waiting for transfers between devices, per_device(): lax.all_to_all(residual, 'lon', split_axis=0, concat_axis=0, tiled=True)  10.1 us
    ppermute x4, starting transfers between devices, neighbours(): lax.ppermute(edge_low, axis, backward)  7.32 us
    dot_general x3, matrix products, columns(): out = jnp.einsum(form, matrices, grouped, precision=lax.Precision.HIGHEST)  6.71 us
    all_to_all x1, waiting for transfers between devices, per_device(): lax.all_to_all(packed, 'lon', split_axis=0, concat_axis=0, tiled=True)  2.79 us
  transfers between devices with their start and end apart: 10, of which 2 were waited for; matrix products, arithmetic and copies ran while one was open for 23% of the time, Pallas kernels for 0%

profile of v4, /device:TPU:1, one launch (start us, length us, event | category | flops | bytes accessed | tf_op | source)
XLA Modules:
  0.0 133.2 jit_solution(11610037357583914530)
XLA Ops:
  0.6 1.1 fusion.50
  1.8 0.1 copy.89
  1.9 5.5 %collective-permute-start.2 = (f32[8,32]{1,0:T(8,128)S(1)}, f32[8,32]{1,0:T(8,128)S(1)}, u32[]{:S(2)}, u32[]{:S(2)}) collective-permute-start(f32[8,32]{1,0:T(8,128)S(1)} %bitcast.29), channel_id=1, source_target_pairs={{0,1},{1,2},{2,3},{3,4},{4,5},{5,6},{6,7},{7,8},{8,9},{9,10},{10,1... | collective-permute-start | bytes 3080 | tf_op jit(solution)/shard_map/ppermute | solution.py:20
  7.4 0.7 copy.90
  8.1 1.3 collective-permute-start.3
  9.4 1.5 %fusion.52 = (f32[8,1,256]{2,1,0:T(1,128)}, f32[8,1,256]{2,1,0:T(1,128)}) fusion(f32[32,32,256]{2,1,0:T(8,128)} %param.9), kind=kLoop, calls=%fused_computation.79 | loop fusion | bytes 32768 | tf_op jit(solution)/shard_map/slice | solution.py:26
  10.9 3.0 %collective-permute-start = (f32[8,1,256]{2,1,0:T(1,128)}, f32[8,1,256]{2,1,0:T(1,128)S(1)}, u32[]{:S(2)}, u32[]{:S(2)}) collective-permute-start(f32[8,1,256]{2,1,0:T(1,128)} %get-tuple-element.23), channel_id=1, source_target_pairs={{0,128},{128,256},{256,384},{1,129},{129,257},{257,385},{2,130},{1... | collective-permute-start | bytes 24584 | tf_op jit(solution)/shard_map/ppermute | solution.py:20
  13.9 2.8 %collective-permute-start.1 = (f32[8,1,256]{2,1,0:T(1,128)}, f32[8,1,256]{2,1,0:T(1,128)S(1)}, u32[]{:S(2)}, u32[]{:S(2)}) collective-permute-start(f32[8,1,256]{2,1,0:T(1,128)} %get-tuple-element.22), channel_id=1, source_target_pairs={{128,0},{256,128},{384,256},{129,1},{257,129},{385,257},{130,2},{2... | collective-permute-start | bytes 24584 | tf_op jit(solution)/shard_map/ppermute | solution.py:20
  16.8 0.8 copy.68
  17.6 0.8 copy.69
  18.4 2.3 %pad_maximum_fusion.2 = f32[128,2,514]{2,1,0:T(2,128)} fusion(f32[128,2,1]{2,1,0:T(2,128)S(1)} %copy.69, f32[128,2,1]{2,1,0:T(2,128)S(1)} %copy.68, f32[128,2,512]{2,1,0:T(2,128)} %bitcast.27), kind=kLoop, calls=%fused_computation.19 | loop fusion | flops 263168 | bytes 1052672 | tf_op jit(solution)/shard_map/concatenate | solution.py:120
  20.7 21.5 %all-to-all-start = ((f32[128,2,514]{2,1,0:T(2,128)}), f32[128,2,514]{2,1,0:T(2,128)}, u32[]{:S(2)}, u32[]{:S(2)}) async-start(f32[128,2,514]{2,1,0:T(2,128)} %pad_maximum_fusion.2), calls=%async_computation | async-start | bytes 1310720 | tf_op jit(solution)/shard_map/all_to_all | solution.py:123
  42.2 0.8 fusion.49
  43.0 0.9 fusion.51
  43.9 0.6 iota_shift-right-logical_fusion
  44.4 0.6 iota_and_fusion.1
  45.0 0.6 broadcast_add_fusion
  45.6 0.6 multiply_add_fusion
  46.2 0.5 reshape.108
  46.7 1.7 %reshape.107 = f32[32,32,2,128]{3,2,1,0:T(2,128)S(1)} reshape(f32[32,32,256]{2,1,0:T(8,128)} %param.13) | data formatting | bytes 2097152 | tf_op jit(solution)/shard_map/reshape | solution.py:38
  48.5 3.3 %fusion.7 = f32[32,2,128,32]{2,3,1,0:T(8,128)} fusion(f32[32,2,32,32]{3,2,1,0:T(8,128)S(1)} %reshape.108, f32[32,32,2,128]{3,2,1,0:T(2,128)S(1)} %reshape.107), kind=kOutput, calls=%fused_computation.16 | convolution fusion | flops 100663296 | bytes 2359296 | tf_op jit(solution)/shard_map/rbji,jrbc->irbc/dot_general | solution.py:40
  51.7 0.6 fusion.42
  52.3 0.5 fusion.44
  52.9 0.6 convert_element_type.4
  53.5 0.1 copy.67
  53.6 0.7 reshape_squeeze.10.anchor_ref
  54.3 0.6 copy-done.10
  54.9 0.8 copy.71
  55.7 1.4 %copy.73 = f32[8,32,1]{2,1,0:T(8,128)} copy(f32[8,32,1]{1,0,2:T(8,128)} %bitcast.6) | data formatting | bytes 2048 | tf_op jit(solution)/shard_map/broadcast_in_dim | solution.py:31
  57.1 1.3 fusion.29
  58.5 0.5 reshape.109
  59.1 1.6 %convolution_bitcast_fusion = f32[4,32,2,128]{3,0,2,1:T(4,128)S(1)} fusion(f32[32,32,2,128]{3,2,1,0:T(2,128)S(1)} %reshape.109, f32[32,2,32,32]{3,2,1,0:T(8,128)S(1)} %reshape.108), kind=kOutput, calls=%fused_computation.7 | convolution fusion | flops 12582912 | bytes 1310720 | tf_op jit(solution)/shard_map/rbij,jrbc->irbc/dot_general | solution.py:40
  61.1 0.8 copy.77.top_ref
  61.9 2.8 %all-to-all-done = f32[128,2,514]{2,1,0:T(2,128)} async-done(((f32[128,2,514]{2,1,0:T(2,128)}), f32[128,2,514]{2,1,0:T(2,128)}, u32[]{:S(2)}, u32[]{:S(2)}) %all-to-all-start) | async-done | bytes 526368 | tf_op jit(solution)/shard_map/all_to_all | solution.py:123
  64.7 1.1 slice.120
  65.8 0.4 reshape.115
  66.2 0.7 fusion.9
  66.9 2.5 %copy.78.gain_ref = f32[256,16,32]{2,1,0:T(8,128)} copy(f32[256,16,32]{0,2,1:T(8,128)S(1)} %fusion.9) | data formatting | bytes 1048576 | tf_op jit(solution)/shard_map/dot_general | solution.py:131
  69.4 1.6 %slice_reduce_fusion.2 = (f32[128,2]{1,0:T(8,128)S(1)}, f32[128,2]{1,0:T(8,128)S(1)}) fusion(f32[128,2,514]{2,1,0:T(2,128)} %all-to-all-done), kind=kLoop, calls=%fused_computation.47 | loop fusion | bytes 4096 | tf_op jit(solution)/shard_map/slice | solution.py:134
  71.0 0.7 reshape_squeeze.11.value_ref
  71.7 0.7 reshape_squeeze.12.weight_ref
  72.3 13.5 %shard_map.104 = (f32[256,128]{1,0:T(8,128)}, f32[256,8,128]{2,1,0:T(8,128)}) custom-call(s32[256]{0:T(256)} %reshape_squeeze.10.anchor_ref, f32[256]{0:T(256)} %reshape_squeeze.11.value_ref, f32[256]{0:T(256)} %reshape_squeeze.12.weight_ref, f32[256,128]{1,0:T(8,128)} %copy.77.top_ref, f32[256,16,32]{2,1,0:T(8,128)} %copy.78.gain_ref), custom_call_target="tpu_custom_call" | custom-call | tf_op jit(solution)/shard_map/pallas_call | solution.py:91
  85.8 1.0 copy.79
  87.0 1.8 %fusion = f32[32,32,2,128]{3,0,2,1:T(8,128)S(1)} fusion(f32[32,2,128,32]{2,3,1,0:T(8,128)S(1)} %copy-done.1, f32[4,32,2,128]{3,2,1,0:T(2,128)S(1)} %reshape.114, f32[32,2,32,32]{3,2,1,0:T(8,128)S(1)} %reshape.108), kind=kOutput, calls=%fused_computation.6 | convolution fusion | flops 12845056 | bytes 2359296 | tf_op jit(solution)/shard_map/rbji,jrbc->irbc/dot_general | solution.py:40
  88.9 0.1 copy.83
  89.1 0.2 slice.107
  89.3 0.1 fusion.53
  89.4 0.2 slice_reduce_fusion
  89.7 3.0 %collective-permute-start.6 = (f32[8,32]{1,0:T(8,128)S(1)}, f32[8,32]{1,0:T(8,128)S(1)}, u32[]{:S(2)}, u32[]{:S(2)}) collective-permute-start(f32[8,32]{1,0:T(8,128)S(1)} %get-tuple-element.15), channel_id=1, source_target_pairs={{0,1},{1,2},{2,3},{3,4},{4,5},{5,6},{6,7},{7,8},{8,9},{9,10},{10,1... | collective-permute-start | bytes 3080 | tf_op jit(solution)/shard_map/ppermute | solution.py:20
  92.7 1.3 collective-permute-start.7
  94.0 3.7 %collective-permute-start.4 = (f32[8,1,256]{2,1,0:T(1,128)S(1)}, f32[8,1,256]{2,1,0:T(1,128)S(1)}, u32[]{:S(2)}, u32[]{:S(2)}) collective-permute-start(f32[8,1,256]{2,1,0:T(1,128)S(1)} %get-tuple-element.29), channel_id=1, source_target_pairs={{0,128},{128,256},{256,384},{1,129},{129,257},{257,385},{2,130},{1... | collective-permute-start | bytes 24584 | tf_op jit(solution)/shard_map/ppermute | solution.py:20
  97.7 1.9 %collective-permute-start.5 = (f32[8,1,256]{2,1,0:T(1,128)S(1)}, f32[8,1,256]{2,1,0:T(1,128)S(1)}, u32[]{:S(2)}, u32[]{:S(2)}) collective-permute-start(f32[8,1,256]{2,1,0:T(1,128)S(1)} %get-tuple-element.28), channel_id=1, source_target_pairs={{128,0},{256,128},{384,256},{129,1},{257,129},{385,257},{130,2},{2... | collective-permute-start | bytes 24584 | tf_op jit(solution)/shard_map/ppermute | solution.py:20
  99.7 2.3 %slice_reduce_fusion.4 = f32[256]{0:T(256)S(1)} fusion(f32[256,8,128]{2,1,0:T(8,128)} %get-tuple-element.5), kind=kLoop, calls=%fused_computation.51 | loop fusion | bytes 2048 | tf_op jit(solution)/shard_map/slice | solution.py:145
  101.9 0.8 all_to_all.10
  102.7 16.2 %all-to-all-start.1 = ((f32[128,1,2]{2,1,0:T(1,128)}), f32[128,1,2]{2,1,0:T(1,128)S(1)}, u32[]{:S(2)}, u32[]{:S(2)}) async-start(f32[128,1,2]{2,1,0:T(1,128)} %bitcast.13), calls=%async_computation.1 | async-start | bytes 131072 | tf_op jit(solution)/shard_map/all_to_all | solution.py:146
  118.9 0.8 fusion.54
  119.9 0.4 copy.82
  120.3 0.6 slice.105
  120.9 0.1 copy.84
  121.1 0.1 copy.85
  121.2 10.1 %all-to-all-done.1 = f32[128,1,2]{2,1,0:T(1,128)S(1)} async-done(((f32[128,1,2]{2,1,0:T(1,128)}), f32[128,1,2]{2,1,0:T(1,128)S(1)}, u32[]{:S(2)}, u32[]{:S(2)}) %all-to-all-start.1) | async-done | bytes 1056 | tf_op jit(solution)/shard_map/all_to_all | solution.py:146
  131.3 0.6 copy.87
  131.9 0.2 fusion.33
  132.2 1.0 pad_maximum_fusion.1
  (64 shorter events, 0.8 us)
Async XLA Ops:
  0.6 41.6 %copy-start = (f32[32,32,256]{2,1,0:T(8,128)S(1)}, f32[32,32,256]{2,1,0:T(8,128)}, u32[]{:S(2)}) copy-start(f32[32,32,256]{2,1,0:T(8,128)} %param.9) | copy-start | bytes 3145732
  1.9 52.4 %collective-permute-start.2 = (f32[8,32]{1,0:T(8,128)S(1)}, f32[8,32]{1,0:T(8,128)S(1)}, u32[]{:S(2)}, u32[]{:S(2)}) collective-permute-start(f32[8,32]{1,0:T(8,128)S(1)} %bitcast.29), channel_id=1, source_target_pairs={{0,1},{1,2},{2,3},{3,4},{4,5},{5,6},{6,7},{7,8},{8,9},{9,10},{10,1... | collective-permute-start | bytes 3080 | tf_op jit(solution)/shard_map/ppermute | solution.py:20
  8.1 47.6 %collective-permute-start.3 = (f32[8,32]{1,0:T(8,128)}, f32[8,32]{1,0:T(8,128)}, u32[]{:S(2)}, u32[]{:S(2)}) collective-permute-start(f32[8,32]{1,0:T(8,128)} %bitcast.5), channel_id=1, source_target_pairs={{1,0},{2,1},{3,2},{4,3},{5,4},{6,5},{7,6},{8,7},{9,8},{10,9},{11,1... | collective-permute-start | bytes 3080 | tf_op jit(solution)/shard_map/ppermute | solution.py:20
  10.9 46.3 %collective-permute-start = (f32[8,1,256]{2,1,0:T(1,128)}, f32[8,1,256]{2,1,0:T(1,128)S(1)}, u32[]{:S(2)}, u32[]{:S(2)}) collective-permute-start(f32[8,1,256]{2,1,0:T(1,128)} %get-tuple-element.23), channel_id=1, source_target_pairs={{0,128},{128,256},{256,384},{1,129},{129,257},{257,385},{2,130},{1... | collective-permute-start | bytes 24584 | tf_op jit(solution)/shard_map/ppermute | solution.py:20
  13.9 43.2 %collective-permute-start.1 = (f32[8,1,256]{2,1,0:T(1,128)}, f32[8,1,256]{2,1,0:T(1,128)S(1)}, u32[]{:S(2)}, u32[]{:S(2)}) collective-permute-start(f32[8,1,256]{2,1,0:T(1,128)} %get-tuple-element.22), channel_id=1, source_target_pairs={{128,0},{256,128},{384,256},{129,1},{257,129},{385,257},{130,2},{2... | collective-permute-start | bytes 24584 | tf_op jit(solution)/shard_map/ppermute | solution.py:20
  18.4 27.8 %copy-start.7 = (f32[32,2,1024]{2,1,0:T(2,128)S(1)}, f32[32,2,1024]{2,1,0:T(2,128)}, u32[]{:S(2)}) copy-start(f32[32,2,1024]{2,1,0:T(2,128)} %param.11) | copy-start | bytes 786436
  20.7 43.9 %all-to-all-start = ((f32[128,2,514]{2,1,0:T(2,128)}), f32[128,2,514]{2,1,0:T(2,128)}, u32[]{:S(2)}, u32[]{:S(2)}) async-start(f32[128,2,514]{2,1,0:T(2,128)} %pad_maximum_fusion.2), calls=%async_computation | async-start | bytes 1310720 | tf_op jit(solution)/shard_map/all_to_all | solution.py:123
  48.4 4.4 %copy-start.8 = (s32[32,256]{1,0:T(8,128)S(1)}, s32[32,256]{1,0:T(8,128)}, u32[]{:S(2)}) copy-start(s32[32,256]{1,0:T(8,128)} %param.12) | copy-start | bytes 98308
  48.4 5.0 %copy-start.17 = (s32[1,1,128,2]{2,3,1,0:T(2,128)S(1)}, s32[1,1,128,2]{2,3,1,0:T(2,128)}, u32[]{:S(2)}) copy-start(s32[1,1,128,2]{2,3,1,0:T(2,128)} %param.14) | copy-start | bytes 3076
  51.7 5.4 %copy-start.2 = (f32[8,32,255]{2,1,0:T(8,128)S(1)}, f32[8,32,255]{2,1,0:T(8,128)}, u32[]{:S(2)}) copy-start(f32[8,32,255]{2,1,0:T(8,128)} %get-tuple-element.17) | copy-start | bytes 783364
  51.7 6.7 %slice-start = ((f32[32,32,256]{2,1,0:T(8,128)}), f32[24,32,256]{2,1,0:T(8,128)S(1)}, s32[]{:S(2)}) async-start(f32[32,32,256]{2,1,0:T(8,128)} %param.9), calls=%async_computation.2 | async-start | bytes 1572864 | tf_op jit(solution)/shard_map/slice | solution.py:138
  54.3 0.6 copy-start.10
  58.5 2.4 %copy-start.6 = (f32[32,256]{1,0:T(8,128)S(1)}, f32[32,256]{1,0:T(8,128)}, u32[]{:S(2)}) copy-start(f32[32,256]{1,0:T(8,128)} %convert_element_type.4) | copy-start | bytes 98308
  60.7 5.5 %copy-start.9 = (s32[16,32]{1,0:T(8,128)S(1)}, s32[16,32]{1,0:T(8,128)}, u32[]{:S(2)}) copy-start(s32[16,32]{1,0:T(8,128)} %multiply_add_fusion) | copy-start | bytes 6148
  60.7 5.5 %copy-start.11 = (s32[512]{0:T(512)S(1)}, s32[512]{0:T(512)}, u32[]{:S(2)}) copy-start(s32[512]{0:T(512)} %get-tuple-element.30) | copy-start | bytes 6148
  60.7 5.5 %copy-start.12 = (s32[512]{0:T(512)S(1)}, s32[512]{0:T(512)}, u32[]{:S(2)}) copy-start(s32[512]{0:T(512)} %get-tuple-element.31) | copy-start | bytes 6148
  60.7 5.5 %copy-start.13 = (s32[512]{0:T(512)S(1)}, s32[512]{0:T(512)}, u32[]{:S(2)}) copy-start(s32[512]{0:T(512)} %get-tuple-element.32) | copy-start | bytes 6148
  60.7 5.5 %copy-start.14 = (s32[512]{0:T(512)S(1)}, s32[512]{0:T(512)}, u32[]{:S(2)}) copy-start(s32[512]{0:T(512)} %get-tuple-element.33) | copy-start | bytes 6148
  60.7 5.5 %copy-start.15 = (s32[512]{0:T(512)S(1)}, s32[512]{0:T(512)}, u32[]{:S(2)}) copy-start(s32[512]{0:T(512)} %get-tuple-element.36) | copy-start | bytes 6148
  60.7 5.5 %copy-start.16 = (s32[512]{0:T(512)S(1)}, s32[512]{0:T(512)}, u32[]{:S(2)}) copy-start(s32[512]{0:T(512)} %get-tuple-element.37) | copy-start | bytes 6148
  60.7 5.5 %copy-start.18 = (pred[512]{0:T(512)(128)(4,1)S(1)}, pred[512]{0:T(512)(128)(4,1)}, u32[]{:S(2)}) copy-start(pred[512]{0:T(512)(128)(4,1)} %get-tuple-element.34) | copy-start | bytes 1540
  60.8 5.5 %copy-start.19 = (pred[512]{0:T(512)(128)(4,1)S(1)}, pred[512]{0:T(512)(128)(4,1)}, u32[]{:S(2)}) copy-start(pred[512]{0:T(512)(128)(4,1)} %get-tuple-element.35) | copy-start | bytes 1540
  60.8 5.5 %copy-start.20 = (pred[512]{0:T(512)(128)(4,1)S(1)}, pred[512]{0:T(512)(128)(4,1)}, u32[]{:S(2)}) copy-start(pred[512]{0:T(512)(128)(4,1)} %fusion.44) | copy-start | bytes 1540
  69.4 17.6 %copy-start.1 = (f32[32,2,128,32]{2,3,1,0:T(8,128)S(1)}, f32[32,2,128,32]{2,3,1,0:T(8,128)}, u32[]{:S(2)}) copy-start(f32[32,2,128,32]{2,3,1,0:T(8,128)} %fusion.7) | copy-start | bytes 3145732
  87.0 2.3 %copy-start.5 = (f32[32,256]{1,0:T(8,128)S(1)}, f32[32,256]{1,0:T(8,128)}, u32[]{:S(2)}) copy-start(f32[32,256]{1,0:T(8,128)} %param.10) | copy-start | bytes 98308
  89.7 31.3 %collective-permute-start.6 = (f32[8,32]{1,0:T(8,128)S(1)}, f32[8,32]{1,0:T(8,128)S(1)}, u32[]{:S(2)}, u32[]{:S(2)}) collective-permute-start(f32[8,32]{1,0:T(8,128)S(1)} %get-tuple-element.15), channel_id=1, source_target_pairs={{0,1},{1,2},{2,3},{3,4},{4,5},{5,6},{6,7},{7,8},{8,9},{9,10},{10,1... | collective-permute-start | bytes 3080 | tf_op jit(solution)/shard_map/ppermute | solution.py:20
  92.7 28.4 %collective-permute-start.7 = (f32[8,32]{1,0:T(8,128)S(1)}, f32[8,32]{1,0:T(8,128)S(1)}, u32[]{:S(2)}, u32[]{:S(2)}) collective-permute-start(f32[8,32]{1,0:T(8,128)S(1)} %get-tuple-element.14), channel_id=1, source_target_pairs={{1,0},{2,1},{3,2},{4,3},{5,4},{6,5},{7,6},{8,7},{9,8},{10,9},{11,1... | collective-permute-start | bytes 3080 | tf_op jit(solution)/shard_map/ppermute | solution.py:20
  94.0 37.9 %collective-permute-start.4 = (f32[8,1,256]{2,1,0:T(1,128)S(1)}, f32[8,1,256]{2,1,0:T(1,128)S(1)}, u32[]{:S(2)}, u32[]{:S(2)}) collective-permute-start(f32[8,1,256]{2,1,0:T(1,128)S(1)} %get-tuple-element.29), channel_id=1, source_target_pairs={{0,128},{128,256},{256,384},{1,129},{129,257},{257,385},{2,130},{1... | collective-permute-start | bytes 24584 | tf_op jit(solution)/shard_map/ppermute | solution.py:20
  97.7 34.2 %collective-permute-start.5 = (f32[8,1,256]{2,1,0:T(1,128)S(1)}, f32[8,1,256]{2,1,0:T(1,128)S(1)}, u32[]{:S(2)}, u32[]{:S(2)}) collective-permute-start(f32[8,1,256]{2,1,0:T(1,128)S(1)} %get-tuple-element.28), channel_id=1, source_target_pairs={{128,0},{256,128},{384,256},{129,1},{257,129},{385,257},{130,2},{2... | collective-permute-start | bytes 24584 | tf_op jit(solution)/shard_map/ppermute | solution.py:20
  102.7 28.6 %all-to-all-start.1 = ((f32[128,1,2]{2,1,0:T(1,128)}), f32[128,1,2]{2,1,0:T(1,128)S(1)}, u32[]{:S(2)}, u32[]{:S(2)}) async-start(f32[128,1,2]{2,1,0:T(1,128)} %bitcast.13), calls=%async_computation.1 | async-start | bytes 131072 | tf_op jit(solution)/shard_map/all_to_all | solution.py:146
  119.9 12.1 %copy-start.3 = (f32[8,31,256]{2,1,0:T(8,128)S(1)}, f32[8,31,256]{2,1,0:T(8,128)}, u32[]{:S(2)}) copy-start(f32[8,31,256]{2,1,0:T(8,128)} %get-tuple-element.26) | copy-start | bytes 761860
  119.9 12.1 %copy-start.4 = (f32[8,31,256]{2,1,0:T(8,128)S(1)}, f32[8,31,256]{2,1,0:T(8,128)}, u32[]{:S(2)}) copy-start(f32[8,31,256]{2,1,0:T(8,128)} %get-tuple-element.27) | copy-start | bytes 761860

commit v5 on v4

v5 whole, which is shorter than its diff:
```python
import jax
import numpy as np
import jax.numpy as jnp
from jax import lax
from jax.experimental import pallas as pl
from jax.experimental.pallas import tpu as pltpu
from jax.sharding import PartitionSpec as P

LG = 8
LTOP = 4
FH = 8
FW = 16
K = 512
LANES = 128


def neighbours(edge_low, edge_high, axis):
    count = lax.axis_size(axis)
    forward = [(i, i + 1) for i in range(count - 1)]
    backward = [(target, source) for source, target in forward]
    return lax.ppermute(edge_high, axis, forward), lax.ppermute(edge_low, axis, backward)


def stencil(block):
    rows = block.shape[1]
    cols = block.shape[2]
    up, down = neighbours(block[:, 0:1, :], block[:, rows - 1 : rows, :], "lat")
    left, right = neighbours(block[:, :, 0], block[:, :, cols - 1], "lon")
    north = jnp.concatenate([up, lax.slice_in_dim(block, 0, rows - 1, axis=1)], 1)
    south = jnp.concatenate([lax.slice_in_dim(block, 1, rows, axis=1), down], 1)
    west = jnp.concatenate([left[:, :, None], lax.slice_in_dim(block, 0, cols - 1, axis=2)], 2)
    east = jnp.concatenate([lax.slice_in_dim(block, 1, cols, axis=2), right[:, :, None]], 2)
    return north + south + west + east - 4.0 * block


def columns(matrices, field, transpose):
    levels, height, breadth = field.shape
    blocks = matrices.shape[1]
    grouped = field.reshape(levels, height, blocks, breadth // blocks)
    form = "rbji,jrbc->irbc" if transpose else "rbij,jrbc->irbc"
    out = jnp.einsum(form, matrices, grouped, precision=lax.Precision.HIGHEST)
    return out.reshape(out.shape[0], height, breadth)


def window_gain(anchor_ref, gain_ref, s, tile_cols, tile_rows, sub, pad):
    span = FW + FH
    o = jnp.maximum(anchor_ref[s // 2, s % 2], 0)
    r = jnp.minimum(lax.div(o, tile_cols), tile_rows - FH)
    c = jnp.minimum(lax.rem(o, tile_cols), tile_cols - FW)
    c8 = pl.multiple_of(jnp.minimum(lax.div(c, FH) * FH, tile_cols - span), FH)
    off = c - c8
    g = jnp.concatenate([gain_ref[s], pad], axis=1)
    g = pltpu.roll(g, r * LTOP, 1)
    a = pltpu.roll(g[0:FH], lax.rem(off, FH), 0)
    b = pltpu.roll(g[FH:FW], lax.rem(off, FH), 0)
    low = sub >= off
    return c8, (jnp.where(low, a, 0.0), jnp.where(low, b, a), jnp.where(low, 0.0, b))


def predict_kernel(anchor_ref, obs_ref, top_ref, gain_ref, res_ref):
    tile_cols, wide = top_ref.shape
    _, _, narrow = gain_ref.shape
    tile_rows = wide // LTOP
    span = FW + FH
    sub = lax.broadcasted_iota(jnp.int32, (FH, wide), 0)
    pad = jnp.zeros((FW, wide - narrow), jnp.float32)

    def block(q, carry):
        out = jnp.zeros((FH, LANES), jnp.float32)
        for t in range(FH):
            s = q * FH + t
            c8, parts = window_gain(anchor_ref, gain_ref, s, tile_cols, tile_rows, sub, pad)
            win = top_ref[pl.ds(c8, span), :]
            acc = parts[0] * win[0:FH] + parts[1] * win[FH:FW] + parts[2] * win[FW:span]
            predicted = jnp.sum(acc, axis=(0, 1), keepdims=True)
            k = q * (FH // 2) + t // 2
            live = jnp.where(anchor_ref[k, t % 2] >= 0, 1.0, 0.0).astype(jnp.float32)
            res = (live * obs_ref[k, t % 2, 1]) * (predicted - obs_ref[k, t % 2, 0])
            out = jnp.where(sub[:, :LANES] == t, res, out)
        res_ref[q] = out
        return carry

    lax.fori_loop(0, res_ref.shape[0], block, 0)


def scatter_kernel(anchor_ref, res_ref, gain_ref, bar_ref):
    tile_cols, wide = bar_ref.shape
    _, _, narrow = gain_ref.shape
    tile_rows = wide // LTOP
    span = FW + FH
    sub = lax.broadcasted_iota(jnp.int32, (FH, wide), 0)
    pad = jnp.zeros((FW, wide - narrow), jnp.float32)
    bar_ref[...] = jnp.zeros(bar_ref.shape, bar_ref.dtype)

    def block(q, carry):
        res_block = res_ref[q]
        for t in range(FH):
            s = q * FH + t
            c8, parts = window_gain(anchor_ref, gain_ref, s, tile_cols, tile_rows, sub, pad)
            res = res_block[t:t + 1, 0:1]
            bar_ref[pl.ds(c8, span), :] += res * jnp.concatenate(parts, axis=0)
        return carry

    lax.fori_loop(0, res_ref.shape[0], block, 0)


def predict(anchor, obs, top, gain):
    slots = gain.shape[0]
    smem = pl.BlockSpec(memory_space=pltpu.SMEM)
    vmem = pl.BlockSpec(memory_space=pltpu.VMEM)
    return pl.pallas_call(
        predict_kernel,
        out_shape=jax.ShapeDtypeStruct((slots // FH, FH, LANES), jnp.float32),
        in_specs=[smem, smem, vmem, vmem],
        out_specs=vmem,
    )(anchor, obs, top, gain)


def scatter(anchor, res, gain, top_shape):
    smem = pl.BlockSpec(memory_space=pltpu.SMEM)
    vmem = pl.BlockSpec(memory_space=pltpu.VMEM)
    return pl.pallas_call(
        scatter_kernel,
        out_shape=jax.ShapeDtypeStruct(top_shape, jnp.float32),
        in_specs=[smem, vmem, vmem],
        out_specs=vmem,
    )(anchor, res, gain)


def reorder_matrix():
    source = np.arange(K)
    layer_of = source // (FH * FW)
    row_of = (source // FW) % FH
    col_of = source % FW
    matrix = np.zeros((K, K), np.float32)
    matrix[source, (col_of * FH + row_of) * LTOP + layer_of] = 1.0
    return matrix


def per_device(
    moisture,
    conductance,
    inverse,
    crop_mask,
    adjoint_in,
    foot_anchor,
    antenna_gain,
    obs_value,
    obs_weight,
):
    levels, tile_rows, tile_cols = moisture.shape
    mask_float = crop_mask.astype(jnp.float32)
    blocks = inverse.shape[1]
    matrices = inverse.reshape(tile_rows, blocks, levels, levels)

    owner_gain = antenna_gain[0, 0]
    owners, slots_per, _ = owner_gain.shape
    packed = jnp.concatenate(
        [owner_gain, obs_value[0, 0][..., None], obs_weight[0, 0][..., None]], -1
    )
    received = lax.all_to_all(packed, "lon", split_axis=0, concat_axis=0, tiled=True)
    slots = owners * slots_per
    gain = jnp.dot(
        received[..., :K].reshape(slots, K), jnp.asarray(reorder_matrix()), precision=lax.Precision.HIGHEST
    )
    gain = gain.reshape(slots, FW, FH * LTOP)
    obs = received[..., K : K + 2]

    deep = moisture[levels - LG :]
    mixed = jnp.concatenate(
        [moisture[: levels - LG], deep + conductance * stencil(deep)], 0
    )
    solved_top = columns(matrices[:, :, :LTOP, :], mixed, False)
    topmost = (solved_top * mask_float).transpose(2, 1, 0).reshape(tile_cols, tile_rows * LTOP)

    slot_anchor = foot_anchor[0, 0]
    res_rows = predict(slot_anchor, obs, topmost, gain)
    residual_out = lax.all_to_all(
        res_rows[:, :, 0].reshape(owners, slots_per), "lon", split_axis=0, concat_axis=0, tiled=True
    )

    base = columns(matrices, adjoint_in, True)
    bar = scatter(slot_anchor, res_rows, gain, topmost.shape)
    topbar = bar.reshape(tile_cols, tile_rows, LTOP).transpose(2, 1, 0) * mask_float
    mixedbar = base + columns(matrices[:, :, :LTOP, :], topbar, True)
    deepbar = mixedbar[levels - LG :]
    gradient = jnp.concatenate(
        [mixedbar[: levels - LG], deepbar + stencil(conductance * deepbar)], 0
    )
    return gradient, residual_out[None, None]


def solution(mesh):
    in_specs = (
        P(None, "lat", "lon"),
        P("lat", "lon"),
        P("lat", "lon", None),
        P("lat", "lon"),
        P(None, "lat", "lon"),
        P("lat", "lon", None, None),
        P("lat", "lon", None, None, None),
        P("lat", "lon", None, None),
        P("lat", "lon", None, None),
    )
    out_specs = (P(None, "lat", "lon"), P("lat", "lon", None, None))
    return jax.shard_map(
        per_device, mesh=mesh, in_specs=in_specs, out_specs=out_specs, check_vma=False
    )
```

time: 134 us -> 136 us (1.015)
  Pallas kernels: 13.5 us -> 21 us
  waiting for transfers between devices: 12.9 us -> 16.6 us
  other arithmetic: 9.07 us -> 5.58 us
  local copies, waits for them, and re-layouts: 28.8 us -> 25.7 us
  starting transfers between devices: 60.3 us -> 57.2 us
    pallas_call x1 -> x2, Pallas kernels: 13.5 us -> 21 us  [the longest x1 13.7 us: predict(): pl.pallas_call(predict_kernel, out_shape=jax.ShapeDtypeStruct((slots // F...]
    all_to_all x1, starting transfers between devices: 16.2 us -> 12.5 us  [per_device(): lax.all_to_all(res_rows[:, :, 0].reshape(owners, slots_per), 'lon', split...]
    all_to_all x1, waiting for transfers between devices: 2.79 us -> 6.48 us  [per_device(): lax.all_to_all(packed, 'lon', split_axis=0, concat_axis=0, tiled=True)]
    slice x2, local copies, waits for them, and re-layouts: 3.81 us -> 1.66 us  [the longest x1 1.55 us: per_device(): obs = received[..., K:K + 2]]
    another operation x3 -> x0, local copies, waits for them, and re-layouts: 2.07 us -> none  [the longest x1 0.71 us: per_device(): slot_anchor = foot_anchor[0, 0].reshape(slots)]
    unnamed x46 -> x32, local copies, waits for them, and re-layouts: 2.25 us -> 2.82 us
  transfers between devices with their start and end apart: 10 -> 10, of which waited for: 2 -> 2; matrix products, arithmetic and copies ran while one was open for 23% -> 18% of each run, Pallas kernels for 0% -> 0%
where the time goes in v5:
time: 136 us; the launch traced here: 135 us
  starting transfers between devices  57.2 us (42%)
  local copies, waits for them, and re-layouts  25.7 us (19%)
  Pallas kernels  21 us (15%)
  waiting for transfers between devices  16.6 us (12%)
  matrix products  7.73 us (6%)
  other arithmetic  5.58 us (4%)
    all_to_all x1, starting transfers between devices, per_device(): lax.all_to_all(packed, 'lon', split_axis=0, concat_axis=0, tiled=True)  21.5 us
    ppermute x4, starting transfers between devices, neighbours(): lax.ppermute(edge_high, axis, forward)  15.6 us
    pallas_call x1, Pallas kernels, predict(): pl.pallas_call(predict_kernel, out_shape=jax.ShapeDtypeStruct((slots // F...  13.7 us
    all_to_all x1, starting transfers between devices, per_device(): lax.all_to_all(res_rows[:, :, 0].reshape(owners, slots_per), 'lon', split...  12.5 us
    all_to_all x1, waiting for transfers between devices, per_device(): lax.all_to_all(res_rows[:, :, 0].reshape(owners, slots_per), 'lon', split...  10.1 us
    ppermute x4, starting transfers between devices, neighbours(): lax.ppermute(edge_low, axis, backward)  7.54 us
    pallas_call x1, Pallas kernels, scatter(): pl.pallas_call(scatter_kernel, out_shape=jax.ShapeDtypeStruct(top_shape,...  7.32 us
    dot_general x3, matrix products, columns(): out = jnp.einsum(form, matrices, grouped, precision=lax.Precision.HIGHEST)  6.71 us
  transfers between devices with their start and end apart: 10, of which 2 were waited for; matrix products, arithmetic and copies ran while one was open for 18% of the time, Pallas kernels for 0%

profile of v5, /device:TPU:1, one launch (start us, length us, event | category | flops | bytes accessed | tf_op | source)
XLA Modules:
  0.0 134.8 jit_solution(8927234654902334409)
XLA Ops:
  0.6 0.0 copy-start
  0.6 1.1 fusion.17
  1.8 0.1 copy.95
  1.9 5.5 %collective-permute-start.2 = (f32[8,32]{1,0:T(8,128)S(1)}, f32[8,32]{1,0:T(8,128)S(1)}, u32[]{:S(2)}, u32[]{:S(2)}) collective-permute-start(f32[8,32]{1,0:T(8,128)S(1)} %bitcast.31), channel_id=1, source_target_pairs={{0,1},{1,2},{2,3},{3,4},{4,5},{5,6},{6,7},{7,8},{8,9},{9,10},{10,1... | collective-permute-start | bytes 3080 | tf_op jit(solution)/shard_map/ppermute | solution.py:21
  7.4 0.7 copy.96
  8.1 1.3 collective-permute-start.3
  9.4 1.5 %fusion.19 = (f32[8,1,256]{2,1,0:T(1,128)}, f32[8,1,256]{2,1,0:T(1,128)}) fusion(f32[32,32,256]{2,1,0:T(8,128)} %param.10), kind=kLoop, calls=%fused_computation.32 | loop fusion | bytes 32768 | tf_op jit(solution)/shard_map/slice | solution.py:27
  10.9 3.0 %collective-permute-start = (f32[8,1,256]{2,1,0:T(1,128)}, f32[8,1,256]{2,1,0:T(1,128)S(1)}, u32[]{:S(2)}, u32[]{:S(2)}) collective-permute-start(f32[8,1,256]{2,1,0:T(1,128)} %get-tuple-element.17), channel_id=1, source_target_pairs={{0,128},{128,256},{256,384},{1,129},{129,257},{257,385},{2,130},{1... | collective-permute-start | bytes 24584 | tf_op jit(solution)/shard_map/ppermute | solution.py:21
  13.9 2.8 %collective-permute-start.1 = (f32[8,1,256]{2,1,0:T(1,128)}, f32[8,1,256]{2,1,0:T(1,128)S(1)}, u32[]{:S(2)}, u32[]{:S(2)}) collective-permute-start(f32[8,1,256]{2,1,0:T(1,128)} %get-tuple-element.16), channel_id=1, source_target_pairs={{128,0},{256,128},{384,256},{129,1},{257,129},{385,257},{130,2},{2... | collective-permute-start | bytes 24584 | tf_op jit(solution)/shard_map/ppermute | solution.py:21
  16.8 0.8 copy.73
  17.6 0.8 copy.74
  18.4 2.3 %pad_maximum_fusion.2 = f32[128,2,514]{2,1,0:T(2,128)} fusion(f32[128,2,1]{2,1,0:T(2,128)S(1)} %copy.74, f32[128,2,1]{2,1,0:T(2,128)S(1)} %copy.73, f32[128,2,512]{2,1,0:T(2,128)} %bitcast.29), kind=kLoop, calls=%fused_computation.8 | loop fusion | flops 263168 | bytes 1052672 | tf_op jit(solution)/shard_map/concatenate | solution.py:158
  20.7 21.5 %all-to-all-start = ((f32[128,2,514]{2,1,0:T(2,128)}), f32[128,2,514]{2,1,0:T(2,128)}, u32[]{:S(2)}, u32[]{:S(2)}) async-start(f32[128,2,514]{2,1,0:T(2,128)} %pad_maximum_fusion.2), calls=%async_computation | async-start | bytes 1310720 | tf_op jit(solution)/shard_map/all_to_all | solution.py:161
  42.2 0.8 fusion.16
  43.0 0.5 reshape.42
  43.4 1.7 %reshape.41 = f32[32,32,2,128]{3,2,1,0:T(2,128)S(1)} reshape(f32[32,32,256]{2,1,0:T(8,128)} %param.14) | data formatting | bytes 2097152 | tf_op jit(solution)/shard_map/reshape | solution.py:39
  45.2 3.3 %fusion.2 = f32[32,2,128,32]{2,3,1,0:T(8,128)} fusion(f32[32,2,32,32]{3,2,1,0:T(8,128)S(1)} %reshape.42, f32[32,32,2,128]{3,2,1,0:T(2,128)S(1)} %reshape.41), kind=kOutput, calls=%fused_computation.6 | convolution fusion | flops 100663296 | bytes 2359296 | tf_op jit(solution)/shard_map/rbji,jrbc->irbc/dot_general | solution.py:41
  48.5 0.8 fusion.18
  49.3 0.6 convert_element_type.3
  49.9 0.7 copy.72
  50.7 0.6 copy-done.12
  51.2 0.8 copy.76
  52.0 1.4 %copy.78 = f32[8,32,1]{2,1,0:T(8,128)} copy(f32[8,32,1]{1,0,2:T(8,128)} %bitcast.7) | data formatting | bytes 2048 | tf_op jit(solution)/shard_map/broadcast_in_dim | solution.py:32
  53.5 1.3 fusion.8
  54.8 0.1 pad_maximum_fusion
  54.9 0.5 reshape.43
  55.5 1.6 %convolution_bitcast_fusion = f32[4,32,2,128]{3,0,2,1:T(4,128)S(1)} fusion(f32[32,32,2,128]{3,2,1,0:T(2,128)S(1)} %reshape.43, f32[32,2,32,32]{3,2,1,0:T(8,128)S(1)} %reshape.42), kind=kOutput, calls=%fused_computation.2 | convolution fusion | flops 12582912 | bytes 1310720 | tf_op jit(solution)/shard_map/rbij,jrbc->irbc/dot_general | solution.py:41
  57.0 0.0 copy-start.3
  57.1 0.1 copy.80
  57.1 0.1 reshape.44
  57.3 0.1 copy.81
  57.4 0.7 copy.82.top_ref
  58.2 6.5 %all-to-all-done = f32[128,2,514]{2,1,0:T(2,128)} async-done(((f32[128,2,514]{2,1,0:T(2,128)}), f32[128,2,514]{2,1,0:T(2,128)}, u32[]{:S(2)}, u32[]{:S(2)}) %all-to-all-start) | async-done | bytes 526368 | tf_op jit(solution)/shard_map/all_to_all | solution.py:161
  64.7 1.1 slice.115
  65.7 0.4 reshape.49
  66.1 1.0 fusion.23
  67.1 2.5 %copy.83.gain_ref = f32[256,16,32]{2,1,0:T(8,128)} copy(f32[256,16,32]{0,2,1:T(8,128)S(1)} %fusion.23) | data formatting | bytes 1048576 | tf_op jit(solution)/shard_map/dot_general | solution.py:163
  69.6 1.6 %slice.113.obs_ref = f32[128,2,2]{2,1,0:T(2,128)} slice(f32[128,2,514]{2,1,0:T(2,128)} %all-to-all-done), slice={[0:128], [0:2], [512:514]} | slice | bytes 4096 | tf_op jit(solution)/shard_map/slice | solution.py:167
  71.2 13.7 %shard_map.113.res_ref = f32[32,8,128]{2,1,0:T(8,128)} custom-call(s32[128,2]{1,0:T(8,128)} %bitcast.27, f32[128,2,2]{2,1,0:T(2,128)} %slice.113.obs_ref, f32[256,128]{1,0:T(8,128)} %copy.82.top_ref, f32[256,16,32]{2,1,0:T(8,128)} %copy.83.gain_ref), custom_call_target="tpu_custom_call" | custom-call | tf_op jit(solution)/shard_map/pallas_call | solution.py:111
  84.8 7.3 %shard_map.114 = f32[256,128]{1,0:T(8,128)} custom-call(s32[128,2]{1,0:T(8,128)} %bitcast.28, f32[32,8,128]{2,1,0:T(8,128)} %shard_map.113.res_ref, f32[256,16,32]{2,1,0:T(8,128)} %copy.83.gain_ref), custom_call_target="tpu_custom_call" | custom-call | tf_op jit(solution)/shard_map/pallas_call | solution.py:122
  92.1 1.0 copy.85
  93.2 0.1 reshape.48
  93.3 1.8 %fusion = f32[32,32,2,128]{3,0,2,1:T(8,128)S(1)} fusion(f32[32,2,128,32]{2,3,1,0:T(8,128)S(1)} %copy-done.1, f32[4,32,2,128]{3,2,1,0:T(2,128)S(1)} %reshape.48, f32[32,2,32,32]{3,2,1,0:T(8,128)S(1)} %reshape.42), kind=kOutput, calls=%fused_computation.1 | convolution fusion | flops 12845056 | bytes 2359296 | tf_op jit(solution)/shard_map/rbji,jrbc->irbc/dot_general | solution.py:41
  95.2 0.1 copy.89
  95.4 0.2 slice.103
  95.6 0.8 fusion.20
  96.4 0.2 slice_reduce_fusion.1
  96.6 0.1 slice_reduce_fusion
  96.7 2.9 %collective-permute-start.6 = (f32[8,32]{1,0:T(8,128)S(1)}, f32[8,32]{1,0:T(8,128)S(1)}, u32[]{:S(2)}, u32[]{:S(2)}) collective-permute-start(f32[8,32]{1,0:T(8,128)S(1)} %get-tuple-element.9), channel_id=1, source_target_pairs={{0,1},{1,2},{2,3},{3,4},{4,5},{5,6},{6,7},{7,8},{8,9},{9,10},{10,1... | collective-permute-start | bytes 3080 | tf_op jit(solution)/shard_map/ppermute | solution.py:21
  99.7 1.5 %collective-permute-start.7 = (f32[8,32]{1,0:T(8,128)S(1)}, f32[8,32]{1,0:T(8,128)S(1)}, u32[]{:S(2)}, u32[]{:S(2)}) collective-permute-start(f32[8,32]{1,0:T(8,128)S(1)} %get-tuple-element.8), channel_id=1, source_target_pairs={{1,0},{2,1},{3,2},{4,3},{5,4},{6,5},{7,6},{8,7},{9,8},{10,9},{11,1... | collective-permute-start | bytes 3080 | tf_op jit(solution)/shard_map/ppermute | solution.py:21
  101.2 4.2 %collective-permute-start.4 = (f32[8,1,256]{2,1,0:T(1,128)S(1)}, f32[8,1,256]{2,1,0:T(1,128)S(1)}, u32[]{:S(2)}, u32[]{:S(2)}) collective-permute-start(f32[8,1,256]{2,1,0:T(1,128)S(1)} %get-tuple-element.23), channel_id=1, source_target_pairs={{0,128},{128,256},{256,384},{1,129},{129,257},{257,385},{2,130},{1... | collective-permute-start | bytes 24584 | tf_op jit(solution)/shard_map/ppermute | solution.py:21
  105.4 1.9 %collective-permute-start.5 = (f32[8,1,256]{2,1,0:T(1,128)S(1)}, f32[8,1,256]{2,1,0:T(1,128)S(1)}, u32[]{:S(2)}, u32[]{:S(2)}) collective-permute-start(f32[8,1,256]{2,1,0:T(1,128)S(1)} %get-tuple-element.22), channel_id=1, source_target_pairs={{128,0},{256,128},{384,256},{129,1},{257,129},{385,257},{130,2},{2... | collective-permute-start | bytes 24584 | tf_op jit(solution)/shard_map/ppermute | solution.py:21
  107.3 0.7 all_to_all.10
  108.0 12.5 %all-to-all-start.1 = ((f32[128,1,2]{2,1,0:T(1,128)}), f32[128,1,2]{2,1,0:T(1,128)S(1)}, u32[]{:S(2)}, u32[]{:S(2)}) async-start(f32[128,1,2]{2,1,0:T(1,128)} %bitcast.14), calls=%async_computation.1 | async-start | bytes 131072 | tf_op jit(solution)/shard_map/all_to_all | solution.py:178
  120.6 0.8 fusion.21
  121.4 0.1 slice.116
  121.5 0.4 copy.88
  121.9 0.6 slice.101
  122.6 0.1 copy.90
  122.7 0.1 copy.91
  122.8 10.1 %all-to-all-done.1 = f32[128,1,2]{2,1,0:T(1,128)S(1)} async-done(((f32[128,1,2]{2,1,0:T(1,128)}), f32[128,1,2]{2,1,0:T(1,128)S(1)}, u32[]{:S(2)}, u32[]{:S(2)}) %all-to-all-start.1) | async-done | bytes 1056 | tf_op jit(solution)/shard_map/all_to_all | solution.py:178
  132.9 0.6 copy.93
  133.6 0.2 fusion.12
  133.8 1.0 pad_maximum_fusion.1
  (42 shorter events, 0.3 us)
Async XLA Ops:
  0.6 41.5 %copy-start = (f32[32,32,256]{2,1,0:T(8,128)S(1)}, f32[32,32,256]{2,1,0:T(8,128)}, u32[]{:S(2)}) copy-start(f32[32,32,256]{2,1,0:T(8,128)} %param.10) | copy-start | bytes 3145732
  1.9 48.7 %collective-permute-start.2 = (f32[8,32]{1,0:T(8,128)S(1)}, f32[8,32]{1,0:T(8,128)S(1)}, u32[]{:S(2)}, u32[]{:S(2)}) collective-permute-start(f32[8,32]{1,0:T(8,128)S(1)} %bitcast.31), channel_id=1, source_target_pairs={{0,1},{1,2},{2,3},{3,4},{4,5},{5,6},{6,7},{7,8},{8,9},{9,10},{10,1... | collective-permute-start | bytes 3080 | tf_op jit(solution)/shard_map/ppermute | solution.py:21
  7.4 35.6 %copy-start.10 = (f32[32,2,1024]{2,1,0:T(2,128)S(1)}, f32[32,2,1024]{2,1,0:T(2,128)}, u32[]{:S(2)}) copy-start(f32[32,2,1024]{2,1,0:T(2,128)} %param.12) | copy-start | bytes 786436
  8.1 43.9 %collective-permute-start.3 = (f32[8,32]{1,0:T(8,128)}, f32[8,32]{1,0:T(8,128)}, u32[]{:S(2)}, u32[]{:S(2)}) collective-permute-start(f32[8,32]{1,0:T(8,128)} %bitcast.6), channel_id=1, source_target_pairs={{1,0},{2,1},{3,2},{4,3},{5,4},{6,5},{7,6},{8,7},{9,8},{10,9},{11,1... | collective-permute-start | bytes 3080 | tf_op jit(solution)/shard_map/ppermute | solution.py:21
  10.9 42.6 %collective-permute-start = (f32[8,1,256]{2,1,0:T(1,128)}, f32[8,1,256]{2,1,0:T(1,128)S(1)}, u32[]{:S(2)}, u32[]{:S(2)}) collective-permute-start(f32[8,1,256]{2,1,0:T(1,128)} %get-tuple-element.17), channel_id=1, source_target_pairs={{0,128},{128,256},{256,384},{1,129},{129,257},{257,385},{2,130},{1... | collective-permute-start | bytes 24584 | tf_op jit(solution)/shard_map/ppermute | solution.py:21
  13.9 39.6 %collective-permute-start.1 = (f32[8,1,256]{2,1,0:T(1,128)}, f32[8,1,256]{2,1,0:T(1,128)S(1)}, u32[]{:S(2)}, u32[]{:S(2)}) collective-permute-start(f32[8,1,256]{2,1,0:T(1,128)} %get-tuple-element.16), channel_id=1, source_target_pairs={{128,0},{256,128},{384,256},{129,1},{257,129},{385,257},{130,2},{2... | collective-permute-start | bytes 24584 | tf_op jit(solution)/shard_map/ppermute | solution.py:21
  20.7 43.9 %all-to-all-start = ((f32[128,2,514]{2,1,0:T(2,128)}), f32[128,2,514]{2,1,0:T(2,128)}, u32[]{:S(2)}, u32[]{:S(2)}) async-start(f32[128,2,514]{2,1,0:T(2,128)} %pad_maximum_fusion.2), calls=%async_computation | async-start | bytes 1310720 | tf_op jit(solution)/shard_map/all_to_all | solution.py:161
  48.5 0.8 copy-start.11
  48.5 1.5 %copy-start.13 = (s32[1,1,128,2]{2,3,1,0:T(2,128)S(1)}, s32[1,1,128,2]{2,3,1,0:T(2,128)}, u32[]{:S(2)}) copy-start(s32[1,1,128,2]{2,3,1,0:T(2,128)} %param.15) | copy-start | bytes 3076
  48.5 5.0 %copy-start.7 = (f32[8,32,255]{2,1,0:T(8,128)S(1)}, f32[8,32,255]{2,1,0:T(8,128)}, u32[]{:S(2)}) copy-start(f32[8,32,255]{2,1,0:T(8,128)} %get-tuple-element.11) | copy-start | bytes 783364
  49.3 5.5 %slice-start = ((f32[32,32,256]{2,1,0:T(8,128)}), f32[24,32,256]{2,1,0:T(8,128)S(1)}, s32[]{:S(2)}) async-start(f32[32,32,256]{2,1,0:T(8,128)} %param.10), calls=%async_computation.2 | async-start | bytes 1572864 | tf_op jit(solution)/shard_map/slice | solution.py:171
  50.7 0.6 copy-start.12
  54.9 2.4 %copy-start.9 = (f32[32,256]{1,0:T(8,128)S(1)}, f32[32,256]{1,0:T(8,128)}, u32[]{:S(2)}) copy-start(f32[32,256]{1,0:T(8,128)} %convert_element_type.3) | copy-start | bytes 98308
  57.0 9.1 %copy-start.3 = (f32[16,32,512]{2,1,0:T(8,128)S(1)}, f32[16,32,512]{2,1,0:T(8,128)}, u32[]{:S(2)}) copy-start(f32[16,32,512]{2,1,0:T(8,128)} %constant.11) | copy-start | bytes 3145732
  84.8 8.5 %copy-start.1 = (f32[32,2,128,32]{2,3,1,0:T(8,128)S(1)}, f32[32,2,128,32]{2,3,1,0:T(8,128)}, u32[]{:S(2)}) copy-start(f32[32,2,128,32]{2,3,1,0:T(8,128)} %fusion.2) | copy-start | bytes 3145732
  93.3 2.3 %copy-start.8 = (f32[32,256]{1,0:T(8,128)S(1)}, f32[32,256]{1,0:T(8,128)}, u32[]{:S(2)}) copy-start(f32[32,256]{1,0:T(8,128)} %param.11) | copy-start | bytes 98308
  95.2 1.5 %copy-start.2 = (f32[32,8,128]{2,1,0:T(8,128)S(1)}, f32[32,8,128]{2,1,0:T(8,128)}, u32[]{:S(2)}) copy-start(f32[32,8,128]{2,1,0:T(8,128)} %shard_map.113.res_ref) | copy-start | bytes 393220
  96.7 25.8 %collective-permute-start.6 = (f32[8,32]{1,0:T(8,128)S(1)}, f32[8,32]{1,0:T(8,128)S(1)}, u32[]{:S(2)}, u32[]{:S(2)}) collective-permute-start(f32[8,32]{1,0:T(8,128)S(1)} %get-tuple-element.9), channel_id=1, source_target_pairs={{0,1},{1,2},{2,3},{3,4},{4,5},{5,6},{6,7},{7,8},{8,9},{9,10},{10,1... | collective-permute-start | bytes 3080 | tf_op jit(solution)/shard_map/ppermute | solution.py:21
  99.7 23.0 %collective-permute-start.7 = (f32[8,32]{1,0:T(8,128)S(1)}, f32[8,32]{1,0:T(8,128)S(1)}, u32[]{:S(2)}, u32[]{:S(2)}) collective-permute-start(f32[8,32]{1,0:T(8,128)S(1)} %get-tuple-element.8), channel_id=1, source_target_pairs={{1,0},{2,1},{3,2},{4,3},{5,4},{6,5},{7,6},{8,7},{9,8},{10,9},{11,1... | collective-permute-start | bytes 3080 | tf_op jit(solution)/shard_map/ppermute | solution.py:21
  101.2 32.3 %collective-permute-start.4 = (f32[8,1,256]{2,1,0:T(1,128)S(1)}, f32[8,1,256]{2,1,0:T(1,128)S(1)}, u32[]{:S(2)}, u32[]{:S(2)}) collective-permute-start(f32[8,1,256]{2,1,0:T(1,128)S(1)} %get-tuple-element.23), channel_id=1, source_target_pairs={{0,128},{128,256},{256,384},{1,129},{129,257},{257,385},{2,130},{1... | collective-permute-start | bytes 24584 | tf_op jit(solution)/shard_map/ppermute | solution.py:21
  105.4 28.2 %collective-permute-start.5 = (f32[8,1,256]{2,1,0:T(1,128)S(1)}, f32[8,1,256]{2,1,0:T(1,128)S(1)}, u32[]{:S(2)}, u32[]{:S(2)}) collective-permute-start(f32[8,1,256]{2,1,0:T(1,128)S(1)} %get-tuple-element.22), channel_id=1, source_target_pairs={{128,0},{256,128},{384,256},{129,1},{257,129},{385,257},{130,2},{2... | collective-permute-start | bytes 24584 | tf_op jit(solution)/shard_map/ppermute | solution.py:21
  108.0 24.9 %all-to-all-start.1 = ((f32[128,1,2]{2,1,0:T(1,128)}), f32[128,1,2]{2,1,0:T(1,128)S(1)}, u32[]{:S(2)}, u32[]{:S(2)}) async-start(f32[128,1,2]{2,1,0:T(1,128)} %bitcast.14), calls=%async_computation.1 | async-start | bytes 131072 | tf_op jit(solution)/shard_map/all_to_all | solution.py:178
  121.5 12.1 %copy-start.4 = (f32[8,32,255]{2,1,0:T(8,128)S(1)}, f32[8,32,255]{2,1,0:T(8,128)}, u32[]{:S(2)}) copy-start(f32[8,32,255]{2,1,0:T(8,128)} %get-tuple-element.19) | copy-start | bytes 783364
  121.5 12.1 %copy-start.5 = (f32[8,31,256]{2,1,0:T(8,128)S(1)}, f32[8,31,256]{2,1,0:T(8,128)}, u32[]{:S(2)}) copy-start(f32[8,31,256]{2,1,0:T(8,128)} %get-tuple-element.20) | copy-start | bytes 761860
  121.5 12.1 %copy-start.6 = (f32[8,31,256]{2,1,0:T(8,128)S(1)}, f32[8,31,256]{2,1,0:T(8,128)}, u32[]{:S(2)}) copy-start(f32[8,31,256]{2,1,0:T(8,128)} %get-tuple-element.21) | copy-start | bytes 761860

commit v6 on v5

--- a/solution.py
+++ b/solution.py
@@ -175,9 +175,10 @@
 
     slot_anchor = foot_anchor[0, 0]
     res_rows = predict(slot_anchor, obs, topmost, gain)
-    residual_out = lax.all_to_all(
-        res_rows[:, :, 0].reshape(owners, slots_per), "lon", split_axis=0, concat_axis=0, tiled=True
-    )
+    residual = res_rows[:, :, 0].reshape(owners, 1, slots_per)
+    column = lax.broadcasted_iota(jnp.int32, (1, owners, 1), 1) == lax.axis_index("lon")
+    spread = jnp.where(column, residual, 0.0)
+    residual_out = lax.psum_scatter(spread, "lon", scatter_dimension=0, tiled=True)[0]
 
     base = columns(matrices, adjoint_in, True)
     bar = scatter(slot_anchor, res_rows, gain, topmost.shape)

time: 136 us -> 1350 us (9.93)
  the two profiles are of different devices: /device:TPU:1 before, /device:TPU:8 now
where the time goes in v6:
time: 1350 us
  waiting for transfers between devices  1230 us (91%)
  starting transfers between devices  45.6 us (3%)
  local copies, waits for them, and re-layouts  27.6 us (2%)
  Pallas kernels  21 us (2%)
  between operations  14.5 us (1%)
    unnamed x2, waiting for transfers between devices  1220 us
  transfers between devices with their start and end apart: 10, of which 3 were waited for; matrix products, arithmetic and copies ran while one was open for 2% of the time, Pallas kernels for 0%

profile of v6, /device:TPU:8, one launch (start us, length us, event | category | flops | bytes accessed | tf_op | source)
XLA Modules:
  0.0 1354.0 jit_solution(9326712514029027317)
XLA Ops:
  7.2 1.1 fusion.17
  8.3 0.1 copy.90
  8.4 4.9 collective-permute-start.2
  13.4 0.7 copy.91
  14.1 10.3 collective-permute-start.3
  24.4 1.5 fusion.19
  25.9 1.4 collective-permute-start
  27.3 1.3 collective-permute-start.1
  28.6 0.8 copy.70
  29.4 0.8 copy.71
  30.3 2.3 pad_maximum_fusion.2
  32.6 12.2 all-to-all-start
  44.8 0.2 all-reduce.3.cloned.1.call-start
  45.0 0.8 fusion.16
  45.8 0.5 reshape.44
  46.3 1.7 reshape.43
  48.0 3.3 fusion.2
  51.3 0.8 fusion.18
  52.1 0.5 iota_compare_fusion
  52.6 0.6 convert_element_type.3
  53.3 0.8 copy.69
  54.0 1.3 dynamic-slice
  55.3 0.6 copy-done.12
  55.9 0.8 copy.73
  56.7 1.4 copy.75
  58.1 1.3 fusion.8
  59.4 0.1 pad_maximum_fusion
  59.5 0.5 reshape.45
  60.1 1.6 convolution_bitcast_fusion
  61.8 0.1 reshape.46
  61.9 0.1 copy.78
  62.1 0.7 copy.79.top_ref
  62.8 4.8 all-to-all-done
  67.6 1.1 slice.115
  68.7 0.4 reshape.51
  69.1 1.0 fusion.23
  70.1 2.5 copy.80.gain_ref
  72.6 1.6 slice.113.obs_ref
  74.1 13.7 %shard_map.113.res_ref = f32[32,8,128]{2,1,0:T(8,128)} custom-call(s32[128,2]{1,0:T(8,128)} %bitcast.28, f32[128,2,2]{2,1,0:T(2,128)} %slice.113.obs_ref, f32[256,128]{1,0:T(8,128)} %copy.79.top_ref, f32[256,16,32]{2,1,0:T(8,128)} %copy.80.gain_ref), custom_call_target="tpu_custom_call" | custom-call | tf_op jit(solution)/shard_map/pallas_call | solution.py:111
  87.8 7.3 shard_map.114
  95.1 1.0 copy.82
  96.3 1.8 fusion
  98.2 0.1 copy.86
  98.4 0.2 slice.103
  98.6 0.8 fusion.20
  99.4 0.8 fusion.21
  100.2 0.2 slice_reduce_fusion.1
  100.5 0.1 slice_reduce_fusion
  100.6 3.3 collective-permute-start.6
  103.9 7.0 collective-permute-start.7
  111.0 3.6 collective-permute-start.4
  114.5 1.3 collective-permute-start.5
  115.8 0.1 broadcast_in_dim.43
  115.9 0.9 broadcast_select_fusion
  116.8 0.1 slice.116
  116.9 0.4 copy.85
  117.3 0.6 slice.101
  118.0 0.1 copy.87
  118.1 0.1 copy.88
  118.2 1.3 collective-permute-done.5
  119.5 0.2 fusion.12
  119.8 1.0 pad_maximum_fusion.1
  120.8 1224.5 %all-reduce.3.cloned.1.call-done = f32[128,128,2]{1,2,0:T(2,128)} async-done(((f32[128,128,2]{1,2,0:T(2,128)}), f32[128,128,2]{1,2,0:T(2,128)}) %all-reduce.3.cloned.1.call-update) | async-done | bytes 131088
  1345.3 1.8 dynamic-slice_bitcast_fusion
  (48 shorter events, 0.5 us)
Async XLA Ops:
  7.2 37.8 %copy-start = (f32[32,32,256]{2,1,0:T(8,128)S(1)}, f32[32,32,256]{2,1,0:T(8,128)}, u32[]{:S(2)}) copy-start(f32[32,32,256]{2,1,0:T(8,128)} %param.10) | copy-start | bytes 3145732
  8.4 46.9 %collective-permute-start.2 = (f32[8,32]{1,0:T(8,128)S(1)}, f32[8,32]{1,0:T(8,128)S(1)}, u32[]{:S(2)}, u32[]{:S(2)}) collective-permute-start(f32[8,32]{1,0:T(8,128)S(1)} %bitcast.31), channel_id=1, source_target_pairs={{0,1},{1,2},{2,3},{3,4},{4,5},{5,6},{6,7},{7,8},{8,9},{9,10},{10,1... | collective-permute-start | bytes 3080 | tf_op jit(solution)/shard_map/ppermute | solution.py:21
  13.4 32.4 %copy-start.10 = (f32[32,2,1024]{2,1,0:T(2,128)S(1)}, f32[32,2,1024]{2,1,0:T(2,128)}, u32[]{:S(2)}) copy-start(f32[32,2,1024]{2,1,0:T(2,128)} %param.12) | copy-start | bytes 786436
  14.1 42.6 %collective-permute-start.3 = (f32[8,32]{1,0:T(8,128)}, f32[8,32]{1,0:T(8,128)}, u32[]{:S(2)}, u32[]{:S(2)}) collective-permute-start(f32[8,32]{1,0:T(8,128)} %bitcast.6), channel_id=1, source_target_pairs={{1,0},{2,1},{3,2},{4,3},{5,4},{6,5},{7,6},{8,7},{9,8},{10,9},{11,1... | collective-permute-start | bytes 3080 | tf_op jit(solution)/shard_map/ppermute | solution.py:21
  25.9 32.3 %collective-permute-start = (f32[8,1,256]{2,1,0:T(1,128)}, f32[8,1,256]{2,1,0:T(1,128)S(1)}, u32[]{:S(2)}, u32[]{:S(2)}) collective-permute-start(f32[8,1,256]{2,1,0:T(1,128)} %get-tuple-element.11), channel_id=1, source_target_pairs={{0,128},{128,256},{256,384},{1,129},{129,257},{257,385},{2,130},{1... | collective-permute-start | bytes 24584 | tf_op jit(solution)/shard_map/ppermute | solution.py:21
  27.3 30.8 %collective-permute-start.1 = (f32[8,1,256]{2,1,0:T(1,128)}, f32[8,1,256]{2,1,0:T(1,128)S(1)}, u32[]{:S(2)}, u32[]{:S(2)}) collective-permute-start(f32[8,1,256]{2,1,0:T(1,128)} %get-tuple-element.10), channel_id=1, source_target_pairs={{128,0},{256,128},{384,256},{129,1},{257,129},{385,257},{130,2},{2... | collective-permute-start | bytes 24584 | tf_op jit(solution)/shard_map/ppermute | solution.py:21
  32.6 35.1 %all-to-all-start = ((f32[128,2,514]{2,1,0:T(2,128)}), f32[128,2,514]{2,1,0:T(2,128)}, u32[]{:S(2)}, u32[]{:S(2)}) async-start(f32[128,2,514]{2,1,0:T(2,128)} %pad_maximum_fusion.2), calls=%async_computation | async-start | bytes 1310720 | tf_op jit(solution)/shard_map/all_to_all | solution.py:161
  44.8 1300.5 %all-reduce.3.cloned.1.call-start = ((), (), s32[]{:S(2)}) async-start(), calls=%async_computation.1 | async-start | bytes 262144
  51.3 1.4 copy-start.11
  51.3 2.0 copy-start.13
  51.3 6.9 copy-start.7
  52.1 7.3 slice-start
  55.3 0.6 copy-start.12
  59.5 2.4 copy-start.9
  61.7 7.4 copy-start.3
  87.8 8.5 copy-start.1
  96.3 2.3 copy-start.8
  98.2 2.2 copy-start.2
  98.2 17.7 %copy-start.14 = (pred[128]{0:T(512)(128)(4,1)S(1)}, pred[128]{0:T(512)(128)(4,1)}, u32[]{:S(2)}) copy-start(pred[128]{0:T(512)(128)(4,1)} %iota_compare_fusion) | copy-start | bytes 388
  100.6 17.4 %collective-permute-start.6 = (f32[8,32]{1,0:T(8,128)S(1)}, f32[8,32]{1,0:T(8,128)S(1)}, u32[]{:S(2)}, u32[]{:S(2)}) collective-permute-start(f32[8,32]{1,0:T(8,128)S(1)} %get-tuple-element.3), channel_id=1, source_target_pairs={{0,1},{1,2},{2,3},{3,4},{4,5},{5,6},{6,7},{7,8},{8,9},{9,10},{10,1... | collective-permute-start | bytes 3080 | tf_op jit(solution)/shard_map/ppermute | solution.py:21
  103.9 14.2 %collective-permute-start.7 = (f32[8,32]{1,0:T(8,128)S(1)}, f32[8,32]{1,0:T(8,128)S(1)}, u32[]{:S(2)}, u32[]{:S(2)}) collective-permute-start(f32[8,32]{1,0:T(8,128)S(1)} %get-tuple-element.2), channel_id=1, source_target_pairs={{1,0},{2,1},{3,2},{4,3},{5,4},{6,5},{7,6},{8,7},{9,8},{10,9},{11,1... | collective-permute-start | bytes 3080 | tf_op jit(solution)/shard_map/ppermute | solution.py:21
  111.0 7.3 collective-permute-start.4
  114.5 5.0 collective-permute-start.5
  116.8 2.7 copy-start.4
  116.8 2.7 copy-start.5
  116.9 2.7 copy-start.6
Sparse Core Ops, SparseCore 0:
  118.1 1227.1 all-reduce.2

commit v7 on v5

--- a/solution.py
+++ b/solution.py
@@ -59,49 +59,42 @@
 
 def predict_kernel(anchor_ref, obs_ref, top_ref, gain_ref, res_ref):
     tile_cols, wide = top_ref.shape
-    _, _, narrow = gain_ref.shape
+    slots, _, narrow = gain_ref.shape
     tile_rows = wide // LTOP
     span = FW + FH
     sub = lax.broadcasted_iota(jnp.int32, (FH, wide), 0)
     pad = jnp.zeros((FW, wide - narrow), jnp.float32)
 
-    def block(q, carry):
-        out = jnp.zeros((FH, LANES), jnp.float32)
-        for t in range(FH):
-            s = q * FH + t
-            c8, parts = window_gain(anchor_ref, gain_ref, s, tile_cols, tile_rows, sub, pad)
-            win = top_ref[pl.ds(c8, span), :]
-            acc = parts[0] * win[0:FH] + parts[1] * win[FH:FW] + parts[2] * win[FW:span]
-            predicted = jnp.sum(acc, axis=(0, 1), keepdims=True)
-            k = q * (FH // 2) + t // 2
-            live = jnp.where(anchor_ref[k, t % 2] >= 0, 1.0, 0.0).astype(jnp.float32)
-            res = (live * obs_ref[k, t % 2, 1]) * (predicted - obs_ref[k, t % 2, 0])
-            out = jnp.where(sub[:, :LANES] == t, res, out)
-        res_ref[q] = out
+    def predict(s, carry):
+        c8, parts = window_gain(anchor_ref, gain_ref, s, tile_cols, tile_rows, sub, pad)
+        win = top_ref[pl.ds(c8, span), :]
+        acc = parts[0] * win[0:FH] + parts[1] * win[FH:FW] + parts[2] * win[FW:span]
+        predicted = jnp.sum(acc, axis=(0, 1), keepdims=True)
+        k = s // 2
+        live = jnp.where(anchor_ref[k, s % 2] >= 0, 1.0, 0.0).astype(jnp.float32)
+        res = (live * obs_ref[k, s % 2, 1]) * (predicted - obs_ref[k, s % 2, 0])
+        res_ref[s] = jnp.broadcast_to(res, (1, LANES))
         return carry
 
-    lax.fori_loop(0, res_ref.shape[0], block, 0)
+    lax.fori_loop(0, slots, predict, 0, unroll=8)
 
 
 def scatter_kernel(anchor_ref, res_ref, gain_ref, bar_ref):
     tile_cols, wide = bar_ref.shape
-    _, _, narrow = gain_ref.shape
+    slots, _, narrow = gain_ref.shape
     tile_rows = wide // LTOP
     span = FW + FH
     sub = lax.broadcasted_iota(jnp.int32, (FH, wide), 0)
     pad = jnp.zeros((FW, wide - narrow), jnp.float32)
     bar_ref[...] = jnp.zeros(bar_ref.shape, bar_ref.dtype)
 
-    def block(q, carry):
-        res_block = res_ref[q]
-        for t in range(FH):
-            s = q * FH + t
-            c8, parts = window_gain(anchor_ref, gain_ref, s, tile_cols, tile_rows, sub, pad)
-            res = res_block[t:t + 1, 0:1]
-            bar_ref[pl.ds(c8, span), :] += res * jnp.concatenate(parts, axis=0)
+    def scatter(s, carry):
+        c8, parts = window_gain(anchor_ref, gain_ref, s, tile_cols, tile_rows, sub, pad)
+        res = res_ref[s][0:1, 0:1]
+        bar_ref[pl.ds(c8, span), :] += res * jnp.concatenate(parts, axis=0)
         return carry
 
-    lax.fori_loop(0, res_ref.shape[0], block, 0)
+    lax.fori_loop(0, slots, scatter, 0, unroll=8)
 
 
 def predict(anchor, obs, top, gain):
@@ -110,7 +103,7 @@
     vmem = pl.BlockSpec(memory_space=pltpu.VMEM)
     return pl.pallas_call(
         predict_kernel,
-        out_shape=jax.ShapeDtypeStruct((slots // FH, FH, LANES), jnp.float32),
+        out_shape=jax.ShapeDtypeStruct((slots, 1, LANES), jnp.float32),
         in_specs=[smem, smem, vmem, vmem],
         out_specs=vmem,
     )(anchor, obs, top, gain)
@@ -176,11 +169,12 @@
     slot_anchor = foot_anchor[0, 0]
     res_rows = predict(slot_anchor, obs, topmost, gain)
     residual_out = lax.all_to_all(
-        res_rows[:, :, 0].reshape(owners, slots_per), "lon", split_axis=0, concat_axis=0, tiled=True
-    )
+        res_rows[:, 0, 0].reshape(owners, slots_per), "lon", split_axis=0, concat_axis=0, tiled=True
+    )
+    bar = scatter(slot_anchor, res_rows, gain, topmost.shape)
+    bar, residual_out = lax.optimization_barrier((bar, residual_out))
 
     base = columns(matrices, adjoint_in, True)
-    bar = scatter(slot_anchor, res_rows, gain, topmost.shape)
     topbar = bar.reshape(tile_cols, tile_rows, LTOP).transpose(2, 1, 0) * mask_float
     mixedbar = base + columns(matrices[:, :, :LTOP, :], topbar, True)
     deepbar = mixedbar[levels - LG :]

time: 136 us -> 131 us (0.963)
  the two profiles are of different devices: /device:TPU:1 before, /device:TPU:9 now
where the time goes in v7:
time: 131 us; the launch traced here: 130 us
  starting transfers between devices  55.7 us (43%)
  local copies, waits for them, and re-layouts  26.7 us (20%)
  Pallas kernels  20.8 us (16%)
  waiting for transfers between devices  13.7 us (10%)
  matrix products  6.75 us (5%)
  other arithmetic  5.6 us (4%)
    ppermute x4, starting transfers between devices, neighbours(): lax.ppermute(edge_low, axis, backward)  21.6 us
    ppermute x4, starting transfers between devices, neighbours(): lax.ppermute(edge_high, axis, forward)  15.8 us
    pallas_call x1, Pallas kernels, predict(): pl.pallas_call(predict_kernel, out_shape=jax.ShapeDtypeStruct((slots, 1,...  13.6 us
    all_to_all x1, starting transfers between devices, per_device(): lax.all_to_all(packed, 'lon', split_axis=0, concat_axis=0, tiled=True)  12.4 us
    all_to_all x1, waiting for transfers between devices, per_device(): lax.all_to_all(packed, 'lon', split_axis=0, concat_axis=0, tiled=True)  9.96 us
    pallas_call x1, Pallas kernels, scatter(): pl.pallas_call(scatter_kernel, out_shape=jax.ShapeDtypeStruct(top_shape,...  7.18 us
    all_to_all x1, starting transfers between devices, per_device(): lax.all_to_all(res_rows[:, 0, 0].reshape(owners, slots_per), 'lon', split...  5.94 us
    dot_general x3, matrix products, columns(): out = jnp.einsum(form, matrices, grouped, precision=lax.Precision.HIGHEST)  5.74 us
  transfers between devices with their start and end apart: 10, of which 3 were waited for; matrix products, arithmetic and copies ran while one was open for 18% of the time, Pallas kernels for 6%

profile of v7, /device:TPU:9, one launch (start us, length us, event | category | flops | bytes accessed | tf_op | source)
XLA Modules:
  0.0 130.2 jit_solution(13050548387326184469)
XLA Ops:
  0.6 0.0 copy-start
  0.6 1.1 fusion.17
  1.8 0.1 copy.95
  1.9 4.7 %collective-permute-start.2 = (f32[8,32]{1,0:T(8,128)S(1)}, f32[8,32]{1,0:T(8,128)S(1)}, u32[]{:S(2)}, u32[]{:S(2)}) collective-permute-start(f32[8,32]{1,0:T(8,128)S(1)} %bitcast.32), channel_id=1, source_target_pairs={{0,1},{1,2},{2,3},{3,4},{4,5},{5,6},{6,7},{7,8},{8,9},{9,10},{10,1... | collective-permute-start | bytes 3080 | tf_op jit(solution)/shard_map/ppermute | solution.py:21
  6.6 0.7 copy.96
  7.3 10.3 %collective-permute-start.3 = (f32[8,32]{1,0:T(8,128)}, f32[8,32]{1,0:T(8,128)}, u32[]{:S(2)}, u32[]{:S(2)}) collective-permute-start(f32[8,32]{1,0:T(8,128)} %bitcast.6), channel_id=1, source_target_pairs={{1,0},{2,1},{3,2},{4,3},{5,4},{6,5},{7,6},{8,7},{9,8},{10,9},{11,1... | collective-permute-start | bytes 3080 | tf_op jit(solution)/shard_map/ppermute | solution.py:21
  17.6 1.5 %fusion.19 = (f32[8,1,256]{2,1,0:T(1,128)}, f32[8,1,256]{2,1,0:T(1,128)}) fusion(f32[32,32,256]{2,1,0:T(8,128)} %param.10), kind=kLoop, calls=%fused_computation.32 | loop fusion | bytes 32768 | tf_op jit(solution)/shard_map/slice | solution.py:27
  19.1 3.0 %collective-permute-start = (f32[8,1,256]{2,1,0:T(1,128)}, f32[8,1,256]{2,1,0:T(1,128)S(1)}, u32[]{:S(2)}, u32[]{:S(2)}) collective-permute-start(f32[8,1,256]{2,1,0:T(1,128)} %get-tuple-element.21), channel_id=1, source_target_pairs={{0,128},{128,256},{256,384},{1,129},{129,257},{257,385},{2,130},{1... | collective-permute-start | bytes 24584 | tf_op jit(solution)/shard_map/ppermute | solution.py:21
  22.1 1.9 %collective-permute-start.1 = (f32[8,1,256]{2,1,0:T(1,128)}, f32[8,1,256]{2,1,0:T(1,128)S(1)}, u32[]{:S(2)}, u32[]{:S(2)}) collective-permute-start(f32[8,1,256]{2,1,0:T(1,128)} %get-tuple-element.20), channel_id=1, source_target_pairs={{128,0},{256,128},{384,256},{129,1},{257,129},{385,257},{130,2},{2... | collective-permute-start | bytes 24584 | tf_op jit(solution)/shard_map/ppermute | solution.py:21
  24.0 0.8 copy.73
  24.9 0.8 copy.74
  25.7 2.3 %pad_maximum_fusion.2 = f32[128,2,514]{2,1,0:T(2,128)} fusion(f32[128,2,1]{2,1,0:T(2,128)S(1)} %copy.74, f32[128,2,1]{2,1,0:T(2,128)S(1)} %copy.73, f32[128,2,512]{2,1,0:T(2,128)} %bitcast.30), kind=kLoop, calls=%fused_computation.8 | loop fusion | flops 263168 | bytes 1052672 | tf_op jit(solution)/shard_map/concatenate | solution.py:151
  28.0 12.4 %all-to-all-start = ((f32[128,2,514]{2,1,0:T(2,128)}), f32[128,2,514]{2,1,0:T(2,128)}, u32[]{:S(2)}, u32[]{:S(2)}) async-start(f32[128,2,514]{2,1,0:T(2,128)} %pad_maximum_fusion.2), calls=%async_computation | async-start | bytes 1310720 | tf_op jit(solution)/shard_map/all_to_all | solution.py:154
  40.4 0.1 fusion.16
  40.6 0.8 fusion.18
  41.4 0.5 reshape.41
  41.9 0.6 convert_element_type.3
  42.6 0.7 copy.72
  43.3 2.8 %reshape.40 = f32[32,32,2,128]{3,2,1,0:T(2,128)} reshape(f32[32,32,256]{2,1,0:T(8,128)} %param.14) | data formatting | bytes 2097152 | tf_op jit(solution)/shard_map/reshape | solution.py:39
  46.1 0.6 copy-done.7
  46.6 0.8 copy.76
  47.4 1.5 %copy.78 = f32[8,32,1]{2,1,0:T(8,128)} copy(f32[8,32,1]{1,0,2:T(8,128)} %bitcast.7) | data formatting | bytes 2048 | tf_op jit(solution)/shard_map/broadcast_in_dim | solution.py:32
  48.9 1.3 fusion.8
  50.2 0.1 pad_maximum_fusion
  50.3 0.5 reshape.42
  50.8 1.6 %convolution_bitcast_fusion = f32[4,32,2,128]{3,0,2,1:T(4,128)S(1)} fusion(f32[32,32,2,128]{3,2,1,0:T(2,128)S(1)} %reshape.42, f32[32,2,32,32]{3,2,1,0:T(8,128)S(1)} %reshape.41), kind=kOutput, calls=%fused_computation.2 | convolution fusion | flops 12582912 | bytes 1310720 | tf_op jit(solution)/shard_map/rbij,jrbc->irbc/dot_general | solution.py:41
  52.4 0.0 copy-start.2
  52.4 0.1 copy.80
  52.5 0.1 reshape.43
  52.7 0.1 copy.81
  52.8 0.8 copy.82.top_ref
  53.6 10.0 %all-to-all-done = f32[128,2,514]{2,1,0:T(2,128)} async-done(((f32[128,2,514]{2,1,0:T(2,128)}), f32[128,2,514]{2,1,0:T(2,128)}, u32[]{:S(2)}, u32[]{:S(2)}) %all-to-all-start) | async-done | bytes 526368 | tf_op jit(solution)/shard_map/all_to_all | solution.py:154
  63.5 1.1 slice.115
  64.6 0.4 reshape.48
  65.0 1.0 fusion.23
  66.0 2.5 %copy.83.gain_ref = f32[256,16,32]{2,1,0:T(8,128)} copy(f32[256,16,32]{0,2,1:T(8,128)S(1)} %fusion.23) | data formatting | bytes 1048576 | tf_op jit(solution)/shard_map/dot_general | solution.py:156
  68.5 1.6 %slice.113.obs_ref = f32[128,2,2]{2,1,0:T(2,128)} slice(f32[128,2,514]{2,1,0:T(2,128)} %all-to-all-done), slice={[0:128], [0:2], [512:514]} | slice | bytes 4096 | tf_op jit(solution)/shard_map/slice | solution.py:160
  70.1 13.6 %shard_map.113.res_ref = f32[256,1,128]{2,1,0:T(1,128)} custom-call(s32[128,2]{1,0:T(8,128)} %bitcast.28, f32[128,2,2]{2,1,0:T(2,128)} %slice.113.obs_ref, f32[256,128]{1,0:T(8,128)} %copy.82.top_ref, f32[256,16,32]{2,1,0:T(8,128)} %copy.83.gain_ref), custom_call_target="tpu_custom_call" | custom-call | tf_op jit(solution)/shard_map/pallas_call | solution.py:104
  83.7 1.9 %slice_reduce_fusion.2 = f32[256]{0:T(256)S(1)} fusion(f32[256,1,128]{2,1,0:T(1,128)} %shard_map.113.res_ref), kind=kLoop, calls=%fused_computation.22 | loop fusion | bytes 2048 | tf_op jit(solution)/shard_map/slice | solution.py:172
  85.7 0.8 all_to_all.12
  86.4 5.9 %all-to-all-start.1 = ((f32[128,1,2]{2,1,0:T(1,128)}), f32[128,1,2]{2,1,0:T(1,128)S(1)}, u32[]{:S(2)}, u32[]{:S(2)}) async-start(f32[128,1,2]{2,1,0:T(1,128)} %bitcast.10), calls=%async_computation.1 | async-start | bytes 131072 | tf_op jit(solution)/shard_map/all_to_all | solution.py:171
  92.4 2.3 %fusion.2 = f32[32,2,128,32]{2,3,1,0:T(8,128)S(1)} fusion(f32[32,2,32,32]{3,2,1,0:T(8,128)S(1)} %reshape.41, f32[32,32,2,128]{3,2,1,0:T(2,128)S(1)} %copy-done.1), kind=kOutput, calls=%fused_computation.6 | convolution fusion | flops 100663296 | bytes 2359296 | tf_op jit(solution)/shard_map/rbji,jrbc->irbc/dot_general | solution.py:41
  94.7 7.2 %shard_map.114 = f32[256,128]{1,0:T(8,128)} custom-call(s32[128,2]{1,0:T(8,128)} %bitcast.29, f32[256,1,128]{2,1,0:T(1,128)} %shard_map.113.res_ref, f32[256,16,32]{2,1,0:T(8,128)} %copy.83.gain_ref), custom_call_target="tpu_custom_call" | custom-call | tf_op jit(solution)/shard_map/pallas_call | solution.py:115
  101.9 2.7 %all-to-all-done.1 = f32[128,1,2]{2,1,0:T(1,128)S(1)} async-done(((f32[128,1,2]{2,1,0:T(1,128)}), f32[128,1,2]{2,1,0:T(1,128)S(1)}, u32[]{:S(2)}, u32[]{:S(2)}) %all-to-all-start.1) | async-done | bytes 1056 | tf_op jit(solution)/shard_map/all_to_all | solution.py:171
  104.6 1.0 copy.86
  105.7 0.1 reshape.47
  105.8 1.8 %fusion = f32[32,32,2,128]{3,0,2,1:T(8,128)S(1)} fusion(f32[32,2,128,32]{2,3,1,0:T(8,128)S(1)} %fusion.2, f32[4,32,2,128]{3,2,1,0:T(2,128)S(1)} %reshape.47, f32[32,2,32,32]{3,2,1,0:T(8,128)S(1)} %reshape.41), kind=kOutput, calls=%fused_computation.1 | convolution fusion | flops 12845056 | bytes 2359296 | tf_op jit(solution)/shard_map/rbji,jrbc->irbc/dot_general | solution.py:41
  107.7 0.1 copy.90
  107.8 0.2 slice.104
  108.1 0.1 fusion.20
  108.2 0.2 slice_reduce_fusion
  108.4 2.3 %collective-permute-start.6 = (f32[8,32]{1,0:T(8,128)S(1)}, f32[8,32]{1,0:T(8,128)S(1)}, u32[]{:S(2)}, u32[]{:S(2)}) collective-permute-start(f32[8,32]{1,0:T(8,128)S(1)} %get-tuple-element.13), channel_id=1, source_target_pairs={{0,1},{1,2},{2,3},{3,4},{4,5},{5,6},{6,7},{7,8},{8,9},{9,10},{10,1... | collective-permute-start | bytes 3080 | tf_op jit(solution)/shard_map/ppermute | solution.py:21
  110.8 7.5 %collective-permute-start.7 = (f32[8,32]{1,0:T(8,128)S(1)}, f32[8,32]{1,0:T(8,128)S(1)}, u32[]{:S(2)}, u32[]{:S(2)}) collective-permute-start(f32[8,32]{1,0:T(8,128)S(1)} %get-tuple-element.12), channel_id=1, source_target_pairs={{1,0},{2,1},{3,2},{4,3},{5,4},{6,5},{7,6},{8,7},{9,8},{10,9},{11,1... | collective-permute-start | bytes 3080 | tf_op jit(solution)/shard_map/ppermute | solution.py:21
  118.3 5.7 %collective-permute-start.4 = (f32[8,1,256]{2,1,0:T(1,128)S(1)}, f32[8,1,256]{2,1,0:T(1,128)S(1)}, u32[]{:S(2)}, u32[]{:S(2)}) collective-permute-start(f32[8,1,256]{2,1,0:T(1,128)S(1)} %get-tuple-element.27), channel_id=1, source_target_pairs={{0,128},{128,256},{256,384},{1,129},{129,257},{257,385},{2,130},{1... | collective-permute-start | bytes 24584 | tf_op jit(solution)/shard_map/ppermute | solution.py:21
  124.0 1.9 %collective-permute-start.5 = (f32[8,1,256]{2,1,0:T(1,128)S(1)}, f32[8,1,256]{2,1,0:T(1,128)S(1)}, u32[]{:S(2)}, u32[]{:S(2)}) collective-permute-start(f32[8,1,256]{2,1,0:T(1,128)S(1)} %get-tuple-element.26), channel_id=1, source_target_pairs={{128,0},{256,128},{384,256},{129,1},{257,129},{385,257},{130,2},{2... | collective-permute-start | bytes 24584 | tf_op jit(solution)/shard_map/ppermute | solution.py:21
  126.0 0.1 slice.117
  126.1 0.4 copy.89
  126.5 0.6 slice.102
  127.1 0.6 copy.93
  127.8 0.1 copy.91
  127.9 0.1 copy.92
  128.0 1.0 collective-permute-done.5
  129.0 0.2 fusion.12
  129.2 1.0 pad_maximum_fusion.1
  (32 shorter events, 0.3 us)
Async XLA Ops:
  0.6 39.8 %copy-start = (f32[32,32,256]{2,1,0:T(8,128)S(1)}, f32[32,32,256]{2,1,0:T(8,128)}, u32[]{:S(2)}) copy-start(f32[32,32,256]{2,1,0:T(8,128)} %param.10) | copy-start | bytes 3145732
  1.9 44.2 %collective-permute-start.2 = (f32[8,32]{1,0:T(8,128)S(1)}, f32[8,32]{1,0:T(8,128)S(1)}, u32[]{:S(2)}, u32[]{:S(2)}) collective-permute-start(f32[8,32]{1,0:T(8,128)S(1)} %bitcast.32), channel_id=1, source_target_pairs={{0,1},{1,2},{2,3},{3,4},{4,5},{5,6},{6,7},{7,8},{8,9},{9,10},{10,1... | collective-permute-start | bytes 3080 | tf_op jit(solution)/shard_map/ppermute | solution.py:21
  7.3 40.2 %collective-permute-start.3 = (f32[8,32]{1,0:T(8,128)}, f32[8,32]{1,0:T(8,128)}, u32[]{:S(2)}, u32[]{:S(2)}) collective-permute-start(f32[8,32]{1,0:T(8,128)} %bitcast.6), channel_id=1, source_target_pairs={{1,0},{2,1},{3,2},{4,3},{5,4},{6,5},{7,6},{8,7},{9,8},{10,9},{11,1... | collective-permute-start | bytes 3080 | tf_op jit(solution)/shard_map/ppermute | solution.py:21
  19.1 29.8 %collective-permute-start = (f32[8,1,256]{2,1,0:T(1,128)}, f32[8,1,256]{2,1,0:T(1,128)S(1)}, u32[]{:S(2)}, u32[]{:S(2)}) collective-permute-start(f32[8,1,256]{2,1,0:T(1,128)} %get-tuple-element.21), channel_id=1, source_target_pairs={{0,128},{128,256},{256,384},{1,129},{129,257},{257,385},{2,130},{1... | collective-permute-start | bytes 24584 | tf_op jit(solution)/shard_map/ppermute | solution.py:21
  22.1 26.8 %collective-permute-start.1 = (f32[8,1,256]{2,1,0:T(1,128)}, f32[8,1,256]{2,1,0:T(1,128)S(1)}, u32[]{:S(2)}, u32[]{:S(2)}) collective-permute-start(f32[8,1,256]{2,1,0:T(1,128)} %get-tuple-element.20), channel_id=1, source_target_pairs={{128,0},{256,128},{384,256},{129,1},{257,129},{385,257},{130,2},{2... | collective-permute-start | bytes 24584 | tf_op jit(solution)/shard_map/ppermute | solution.py:21
  28.0 35.5 %all-to-all-start = ((f32[128,2,514]{2,1,0:T(2,128)}), f32[128,2,514]{2,1,0:T(2,128)}, u32[]{:S(2)}, u32[]{:S(2)}) async-start(f32[128,2,514]{2,1,0:T(2,128)} %pad_maximum_fusion.2), calls=%async_computation | async-start | bytes 1310720 | tf_op jit(solution)/shard_map/all_to_all | solution.py:154
  40.4 1.0 copy-start.5
  40.6 1.3 %copy-start.6 = (s32[32,256]{1,0:T(8,128)S(1)}, s32[32,256]{1,0:T(8,128)}, u32[]{:S(2)}) copy-start(s32[32,256]{1,0:T(8,128)} %param.13) | copy-start | bytes 98308
  40.6 2.0 %copy-start.8 = (s32[1,1,128,2]{2,3,1,0:T(2,128)S(1)}, s32[1,1,128,2]{2,3,1,0:T(2,128)}, u32[]{:S(2)}) copy-start(s32[1,1,128,2]{2,3,1,0:T(2,128)} %param.15) | copy-start | bytes 3076
  43.3 6.9 %slice-start = ((f32[32,32,256]{2,1,0:T(8,128)}), f32[24,32,256]{2,1,0:T(8,128)S(1)}, s32[]{:S(2)}) async-start(f32[32,32,256]{2,1,0:T(8,128)} %param.10), calls=%async_computation.2 | async-start | bytes 1572864 | tf_op jit(solution)/shard_map/slice | solution.py:164
  46.1 0.6 copy-start.7
  50.3 2.4 %copy-start.4 = (f32[32,256]{1,0:T(8,128)S(1)}, f32[32,256]{1,0:T(8,128)}, u32[]{:S(2)}) copy-start(f32[32,256]{1,0:T(8,128)} %convert_element_type.3) | copy-start | bytes 98308
  52.4 12.6 %copy-start.2 = (f32[16,32,512]{2,1,0:T(8,128)S(1)}, f32[16,32,512]{2,1,0:T(8,128)}, u32[]{:S(2)}) copy-start(f32[16,32,512]{2,1,0:T(8,128)} %constant.11) | copy-start | bytes 3145732
  68.5 23.9 %copy-start.1 = (f32[32,32,2,128]{3,2,1,0:T(2,128)S(1)}, f32[32,32,2,128]{3,2,1,0:T(2,128)}, u32[]{:S(2)}) copy-start(f32[32,32,2,128]{3,2,1,0:T(2,128)} %reshape.40) | copy-start | bytes 3145732
  86.4 18.2 %all-to-all-start.1 = ((f32[128,1,2]{2,1,0:T(1,128)}), f32[128,1,2]{2,1,0:T(1,128)S(1)}, u32[]{:S(2)}, u32[]{:S(2)}) async-start(f32[128,1,2]{2,1,0:T(1,128)} %bitcast.10), calls=%async_computation.1 | async-start | bytes 131072 | tf_op jit(solution)/shard_map/all_to_all | solution.py:171
  105.8 2.3 %copy-start.3 = (f32[32,256]{1,0:T(8,128)S(1)}, f32[32,256]{1,0:T(8,128)}, u32[]{:S(2)}) copy-start(f32[32,256]{1,0:T(8,128)} %param.11) | copy-start | bytes 98308
  108.4 19.3 %collective-permute-start.6 = (f32[8,32]{1,0:T(8,128)S(1)}, f32[8,32]{1,0:T(8,128)S(1)}, u32[]{:S(2)}, u32[]{:S(2)}) collective-permute-start(f32[8,32]{1,0:T(8,128)S(1)} %get-tuple-element.13), channel_id=1, source_target_pairs={{0,1},{1,2},{2,3},{3,4},{4,5},{5,6},{6,7},{7,8},{8,9},{9,10},{10,1... | collective-permute-start | bytes 3080 | tf_op jit(solution)/shard_map/ppermute | solution.py:21
  110.8 17.1 %collective-permute-start.7 = (f32[8,32]{1,0:T(8,128)S(1)}, f32[8,32]{1,0:T(8,128)S(1)}, u32[]{:S(2)}, u32[]{:S(2)}) collective-permute-start(f32[8,32]{1,0:T(8,128)S(1)} %get-tuple-element.12), channel_id=1, source_target_pairs={{1,0},{2,1},{3,2},{4,3},{5,4},{6,5},{7,6},{8,7},{9,8},{10,9},{11,1... | collective-permute-start | bytes 3080 | tf_op jit(solution)/shard_map/ppermute | solution.py:21
  118.3 9.8 %collective-permute-start.4 = (f32[8,1,256]{2,1,0:T(1,128)S(1)}, f32[8,1,256]{2,1,0:T(1,128)S(1)}, u32[]{:S(2)}, u32[]{:S(2)}) collective-permute-start(f32[8,1,256]{2,1,0:T(1,128)S(1)} %get-tuple-element.27), channel_id=1, source_target_pairs={{0,128},{128,256},{256,384},{1,129},{129,257},{257,385},{2,130},{1... | collective-permute-start | bytes 24584 | tf_op jit(solution)/shard_map/ppermute | solution.py:21
  124.0 5.0 %collective-permute-start.5 = (f32[8,1,256]{2,1,0:T(1,128)S(1)}, f32[8,1,256]{2,1,0:T(1,128)S(1)}, u32[]{:S(2)}, u32[]{:S(2)}) collective-permute-start(f32[8,1,256]{2,1,0:T(1,128)S(1)} %get-tuple-element.26), channel_id=1, source_target_pairs={{128,0},{256,128},{384,256},{129,1},{257,129},{385,257},{130,2},{2... | collective-permute-start | bytes 24584 | tf_op jit(solution)/shard_map/ppermute | solution.py:21

commit v8 on v7

--- a/solution.py
+++ b/solution.py
@@ -57,7 +57,7 @@
     return c8, (jnp.where(low, a, 0.0), jnp.where(low, b, a), jnp.where(low, 0.0, b))
 
 
-def predict_kernel(anchor_ref, obs_ref, top_ref, gain_ref, res_ref):
+def predict_kernel(anchor_ref, top_ref, gain_ref, part_ref):
     tile_cols, wide = top_ref.shape
     slots, _, narrow = gain_ref.shape
     tile_rows = wide // LTOP
@@ -68,12 +68,7 @@
     def predict(s, carry):
         c8, parts = window_gain(anchor_ref, gain_ref, s, tile_cols, tile_rows, sub, pad)
         win = top_ref[pl.ds(c8, span), :]
-        acc = parts[0] * win[0:FH] + parts[1] * win[FH:FW] + parts[2] * win[FW:span]
-        predicted = jnp.sum(acc, axis=(0, 1), keepdims=True)
-        k = s // 2
-        live = jnp.where(anchor_ref[k, s % 2] >= 0, 1.0, 0.0).astype(jnp.float32)
-        res = (live * obs_ref[k, s % 2, 1]) * (predicted - obs_ref[k, s % 2, 0])
-        res_ref[s] = jnp.broadcast_to(res, (1, LANES))
+        part_ref[s] = parts[0] * win[0:FH] + parts[1] * win[FH:FW] + parts[2] * win[FW:span]
         return carry
 
     lax.fori_loop(0, slots, predict, 0, unroll=8)
@@ -90,23 +85,22 @@
 
     def scatter(s, carry):
         c8, parts = window_gain(anchor_ref, gain_ref, s, tile_cols, tile_rows, sub, pad)
-        res = res_ref[s][0:1, 0:1]
-        bar_ref[pl.ds(c8, span), :] += res * jnp.concatenate(parts, axis=0)
+        bar_ref[pl.ds(c8, span), :] += res_ref[s] * jnp.concatenate(parts, axis=0)
         return carry
 
     lax.fori_loop(0, slots, scatter, 0, unroll=8)
 
 
-def predict(anchor, obs, top, gain):
+def predict(anchor, top, gain):
     slots = gain.shape[0]
     smem = pl.BlockSpec(memory_space=pltpu.SMEM)
     vmem = pl.BlockSpec(memory_space=pltpu.VMEM)
     return pl.pallas_call(
         predict_kernel,
-        out_shape=jax.ShapeDtypeStruct((slots, 1, LANES), jnp.float32),
-        in_specs=[smem, smem, vmem, vmem],
+        out_shape=jax.ShapeDtypeStruct((slots, FH, top.shape[1]), jnp.float32),
+        in_specs=[smem, vmem, vmem],
         out_specs=vmem,
-    )(anchor, obs, top, gain)
+    )(anchor, top, gain)
 
 
 def scatter(anchor, res, gain, top_shape):
@@ -115,7 +109,7 @@
     return pl.pallas_call(
         scatter_kernel,
         out_shape=jax.ShapeDtypeStruct(top_shape, jnp.float32),
-        in_specs=[smem, vmem, vmem],
+        in_specs=[smem, smem, vmem],
         out_specs=vmem,
     )(anchor, res, gain)
 
@@ -157,7 +151,8 @@
         received[..., :K].reshape(slots, K), jnp.asarray(reorder_matrix()), precision=lax.Precision.HIGHEST
     )
     gain = gain.reshape(slots, FW, FH * LTOP)
-    obs = received[..., K : K + 2]
+    value = received[..., K]
+    weight = received[..., K + 1]
 
     deep = moisture[levels - LG :]
     mixed = jnp.concatenate(
@@ -167,11 +162,12 @@
     topmost = (solved_top * mask_float).transpose(2, 1, 0).reshape(tile_cols, tile_rows * LTOP)
 
     slot_anchor = foot_anchor[0, 0]
-    res_rows = predict(slot_anchor, obs, topmost, gain)
-    residual_out = lax.all_to_all(
-        res_rows[:, 0, 0].reshape(owners, slots_per), "lon", split_axis=0, concat_axis=0, tiled=True
-    )
-    bar = scatter(slot_anchor, res_rows, gain, topmost.shape)
+    parts = predict(slot_anchor, topmost, gain)
+    predicted = jnp.sum(parts, axis=(1, 2)).reshape(owners, slots_per)
+    live = (slot_anchor >= 0).astype(jnp.float32)
+    residual = live * weight * (predicted - value)
+    residual_out = lax.all_to_all(residual, "lon", split_axis=0, concat_axis=0, tiled=True)
+    bar = scatter(slot_anchor, residual.reshape(slots), gain, topmost.shape)
     bar, residual_out = lax.optimization_barrier((bar, residual_out))
 
     base = columns(matrices, adjoint_in, True)

time: 131 us -> 128 us (0.977)
  the two profiles are of different devices: /device:TPU:9 before, /device:TPU:1 now
where the time goes in v8:
time: 128 us; the launch traced here: 127 us
  starting transfers between devices  57.8 us (45%)
  local copies, waits for them, and re-layouts  27.1 us (21%)
  Pallas kernels  14.3 us (11%)
  waiting for transfers between devices  11.4 us (9%)
  other arithmetic  7.74 us (6%)
  matrix products  7.73 us (6%)
    all_to_all x1, starting transfers between devices, per_device(): lax.all_to_all(packed, 'lon', split_axis=0, concat_axis=0, tiled=True)  21.5 us
    ppermute x4, starting transfers between devices, neighbours(): lax.ppermute(edge_high, axis, forward)  20 us
    all_to_all x1, starting transfers between devices, per_device(): lax.all_to_all(residual, 'lon', split_axis=0, concat_axis=0, tiled=True)  8.91 us
    ppermute x4, starting transfers between devices, neighbours(): lax.ppermute(edge_low, axis, backward)  7.45 us
    pallas_call x1, Pallas kernels, predict(): pl.pallas_call(predict_kernel, out_shape=jax.ShapeDtypeStruct((slots, FH,...  7.34 us
    pallas_call x1, Pallas kernels, scatter(): pl.pallas_call(scatter_kernel, out_shape=jax.ShapeDtypeStruct(top_shape,...  6.94 us
    dot_general x3, matrix products, columns(): out = jnp.einsum(form, matrices, grouped, precision=lax.Precision.HIGHEST)  6.71 us
    all_to_all x1, waiting for transfers between devices, per_device(): lax.all_to_all(packed, 'lon', split_axis=0, concat_axis=0, tiled=True)  6.44 us
  transfers between devices with their start and end apart: 10, of which 3 were waited for; matrix products, arithmetic and copies ran while one was open for 19% of the time, Pallas kernels for 5%

profile of v8, /device:TPU:1, one launch (start us, length us, event | category | flops | bytes accessed | tf_op | source)
XLA Modules:
  0.0 127.2 jit_solution(5144360702347997856)
XLA Ops:
  0.6 1.1 fusion.18
  1.7 0.1 copy.104
  1.8 5.5 %collective-permute-start.2 = (f32[8,32]{1,0:T(8,128)S(1)}, f32[8,32]{1,0:T(8,128)S(1)}, u32[]{:S(2)}, u32[]{:S(2)}) collective-permute-start(f32[8,32]{1,0:T(8,128)S(1)} %bitcast.48), channel_id=1, source_target_pairs={{0,1},{1,2},{2,3},{3,4},{4,5},{5,6},{6,7},{7,8},{8,9},{9,10},{10,1... | collective-permute-start | bytes 3080 | tf_op jit(solution)/shard_map/ppermute | solution.py:21
  7.3 0.7 copy.105
  8.0 1.3 %collective-permute-start.3 = (f32[8,32]{1,0:T(8,128)}, f32[8,32]{1,0:T(8,128)}, u32[]{:S(2)}, u32[]{:S(2)}) collective-permute-start(f32[8,32]{1,0:T(8,128)} %bitcast.6), channel_id=1, source_target_pairs={{1,0},{2,1},{3,2},{4,3},{5,4},{6,5},{7,6},{8,7},{9,8},{10,9},{11,1... | collective-permute-start | bytes 3080 | tf_op jit(solution)/shard_map/ppermute | solution.py:21
  9.3 1.5 %fusion.20 = (f32[8,1,256]{2,1,0:T(1,128)}, f32[8,1,256]{2,1,0:T(1,128)}) fusion(f32[32,32,256]{2,1,0:T(8,128)} %param.10), kind=kLoop, calls=%fused_computation.36 | loop fusion | bytes 32768 | tf_op jit(solution)/shard_map/slice | solution.py:27
  10.8 3.0 %collective-permute-start = (f32[8,1,256]{2,1,0:T(1,128)}, f32[8,1,256]{2,1,0:T(1,128)S(1)}, u32[]{:S(2)}, u32[]{:S(2)}) collective-permute-start(f32[8,1,256]{2,1,0:T(1,128)} %get-tuple-element.23), channel_id=1, source_target_pairs={{0,128},{128,256},{256,384},{1,129},{129,257},{257,385},{2,130},{1... | collective-permute-start | bytes 24584 | tf_op jit(solution)/shard_map/ppermute | solution.py:21
  13.8 3.0 %collective-permute-start.1 = (f32[8,1,256]{2,1,0:T(1,128)}, f32[8,1,256]{2,1,0:T(1,128)S(1)}, u32[]{:S(2)}, u32[]{:S(2)}) collective-permute-start(f32[8,1,256]{2,1,0:T(1,128)} %get-tuple-element.22), channel_id=1, source_target_pairs={{128,0},{256,128},{384,256},{129,1},{257,129},{385,257},{130,2},{2... | collective-permute-start | bytes 24584 | tf_op jit(solution)/shard_map/ppermute | solution.py:21
  16.8 1.3 %copy.79 = f32[1,1,128,2,512]{2,3,4,1,0:T(2,128)S(1)} copy(f32[1,1,128,2,512]{4,3,2,1,0:T(2,128)} %param.16) | data formatting | bytes 1048576 | tf_op args[6]
  18.1 1.0 pad_maximum_fusion.2
  19.1 1.4 %copy.80 = f32[128,2,514]{2,1,0:T(2,128)} copy(f32[128,2,514]{0,1,2:T(2,128)S(1)} %pad_maximum_fusion.2) | data formatting | bytes 1052672 | tf_op jit(solution)/shard_map/concatenate | solution.py:145
  20.4 21.5 %all-to-all-start = ((f32[128,2,514]{2,1,0:T(2,128)}), f32[128,2,514]{2,1,0:T(2,128)}, u32[]{:S(2)}, u32[]{:S(2)}) async-start(f32[128,2,514]{2,1,0:T(2,128)} %copy.80), calls=%async_computation | async-start | bytes 1310720 | tf_op jit(solution)/shard_map/all_to_all | solution.py:148
  41.9 0.8 fusion.17
  42.7 0.5 reshape.91
  43.2 1.7 %reshape.90 = f32[32,32,2,128]{3,2,1,0:T(2,128)S(1)} reshape(f32[32,32,256]{2,1,0:T(8,128)} %param.14) | data formatting | bytes 2097152 | tf_op jit(solution)/shard_map/reshape | solution.py:39
  44.9 3.3 %fusion.2 = f32[32,2,128,32]{2,3,1,0:T(8,128)} fusion(f32[32,2,32,32]{3,2,1,0:T(8,128)S(1)} %reshape.91, f32[32,32,2,128]{3,2,1,0:T(2,128)S(1)} %reshape.90), kind=kOutput, calls=%fused_computation.6 | convolution fusion | flops 100663296 | bytes 2359296 | tf_op jit(solution)/shard_map/rbji,jrbc->irbc/dot_general | solution.py:41
  48.2 0.8 fusion.19
  49.1 0.6 convert_element_type.4
  49.7 0.7 copy.77
  50.4 0.6 copy-done.11
  51.0 0.8 copy.83
  51.8 1.5 %copy.85 = f32[8,32,1]{2,1,0:T(8,128)} copy(f32[8,32,1]{1,0,2:T(8,128)} %bitcast.7) | data formatting | bytes 2048 | tf_op jit(solution)/shard_map/broadcast_in_dim | solution.py:32
  53.3 1.3 fusion.8
  54.7 0.5 reshape.92
  55.2 1.6 %convolution_bitcast_fusion = f32[4,32,2,128]{3,0,2,1:T(4,128)S(1)} fusion(f32[32,32,2,128]{3,2,1,0:T(2,128)S(1)} %reshape.92, f32[32,2,32,32]{3,2,1,0:T(8,128)S(1)} %reshape.91), kind=kOutput, calls=%fused_computation.2 | convolution fusion | flops 12582912 | bytes 1310720 | tf_op jit(solution)/shard_map/rbij,jrbc->irbc/dot_general | solution.py:41
  57.2 0.7 copy.89.top_ref
  57.9 6.4 %all-to-all-done = f32[128,2,514]{2,1,0:T(2,128)} async-done(((f32[128,2,514]{2,1,0:T(2,128)}), f32[128,2,514]{2,1,0:T(2,128)}, u32[]{:S(2)}, u32[]{:S(2)}) %all-to-all-start) | async-done | bytes 526368 | tf_op jit(solution)/shard_map/all_to_all | solution.py:148
  64.4 1.1 slice.115
  65.5 0.4 reshape.99
  65.8 1.0 fusion.25
  66.9 2.5 %copy.90.gain_ref = f32[256,16,32]{2,1,0:T(8,128)} copy(f32[256,16,32]{0,2,1:T(8,128)S(1)} %fusion.25) | data formatting | bytes 1048576 | tf_op jit(solution)/shard_map/dot_general | solution.py:150
  69.4 7.3 %shard_map.113 = f32[256,8,128]{2,1,0:T(8,128)} custom-call(s32[128,2]{1,0:T(8,128)} %bitcast.45, f32[256,128]{1,0:T(8,128)} %copy.89.top_ref, f32[256,16,32]{2,1,0:T(8,128)} %copy.90.gain_ref), custom_call_target="tpu_custom_call" | custom-call | tf_op jit(solution)/shard_map/pallas_call | solution.py:98
  76.7 2.3 %reduce_sum.9 = f32[256]{0:T(256)S(1)} reduce(f32[256,8,128]{2,1,0:T(8,128)} %shard_map.113, f32[]{:T(128)} %constant.3.clone.1), dimensions={1,2}, to_apply=%region_0.0 | reduce | flops 261888 | bytes 1049604 | tf_op jit(solution)/shard_map/reduce_sum | solution.py:166
  78.9 0.1 reshape.96
  79.1 1.2 fusion.21
  80.3 0.9 copy.103
  81.1 0.9 copy.106
  82.0 0.1 squeeze.30
  82.1 0.1 squeeze.33
  82.3 0.6 fusion.16
  82.9 0.1 ge.22
  83.1 8.9 %all-to-all-start.1 = ((f32[128,1,2]{2,1,0:T(1,128)}), f32[128,1,2]{2,1,0:T(1,128)S(1)}, u32[]{:S(2)}, u32[]{:S(2)}) async-start(f32[128,1,2]{2,1,0:T(1,128)} %bitcast.13), calls=%async_computation.1 | async-start | bytes 131072 | tf_op jit(solution)/shard_map/all_to_all | solution.py:169
  92.0 0.6 subtract_multiply_fusion.res_ref
  92.6 6.9 %shard_map.114 = f32[256,128]{1,0:T(8,128)} custom-call(s32[128,2]{1,0:T(8,128)} %bitcast.46, f32[256]{0:T(256)} %subtract_multiply_fusion.res_ref, f32[256,16,32]{2,1,0:T(8,128)} %copy.90.gain_ref), custom_call_target="tpu_custom_call" | custom-call | tf_op jit(solution)/shard_map/pallas_call | solution.py:109
  99.5 4.8 %all-to-all-done.1 = f32[128,1,2]{2,1,0:T(1,128)S(1)} async-done(((f32[128,1,2]{2,1,0:T(1,128)}), f32[128,1,2]{2,1,0:T(1,128)S(1)}, u32[]{:S(2)}, u32[]{:S(2)}) %all-to-all-start.1) | async-done | bytes 1056 | tf_op jit(solution)/shard_map/all_to_all | solution.py:169
  104.3 1.0 copy.94
  105.5 1.8 %fusion = f32[32,32,2,128]{3,0,2,1:T(8,128)S(1)} fusion(f32[32,2,128,32]{2,3,1,0:T(8,128)S(1)} %copy-done.1, f32[4,32,2,128]{3,2,1,0:T(2,128)S(1)} %reshape.98, f32[32,2,32,32]{3,2,1,0:T(8,128)S(1)} %reshape.91), kind=kOutput, calls=%fused_computation.1 | convolution fusion | flops 12845056 | bytes 2359296 | tf_op jit(solution)/shard_map/rbji,jrbc->irbc/dot_general | solution.py:41
  107.4 0.1 copy.98
  107.6 0.2 slice.104
  107.8 0.1 fusion.22
  108.0 0.2 slice_reduce_fusion
  108.2 1.3 %collective-permute-start.7 = (f32[8,32]{1,0:T(8,128)S(1)}, f32[8,32]{1,0:T(8,128)S(1)}, u32[]{:S(2)}, u32[]{:S(2)}) collective-permute-start(f32[8,32]{1,0:T(8,128)S(1)} %get-tuple-element.12), channel_id=1, source_target_pairs={{1,0},{2,1},{3,2},{4,3},{5,4},{6,5},{7,6},{8,7},{9,8},{10,9},{11,1... | collective-permute-start | bytes 3080 | tf_op jit(solution)/shard_map/ppermute | solution.py:21
  109.5 5.5 %collective-permute-start.6 = (f32[8,32]{1,0:T(8,128)S(1)}, f32[8,32]{1,0:T(8,128)S(1)}, u32[]{:S(2)}, u32[]{:S(2)}) collective-permute-start(f32[8,32]{1,0:T(8,128)S(1)} %get-tuple-element.13), channel_id=1, source_target_pairs={{0,1},{1,2},{2,3},{3,4},{4,5},{5,6},{6,7},{7,8},{8,9},{9,10},{10,1... | collective-permute-start | bytes 3080 | tf_op jit(solution)/shard_map/ppermute | solution.py:21
  115.0 6.0 %collective-permute-start.4 = (f32[8,1,256]{2,1,0:T(1,128)S(1)}, f32[8,1,256]{2,1,0:T(1,128)S(1)}, u32[]{:S(2)}, u32[]{:S(2)}) collective-permute-start(f32[8,1,256]{2,1,0:T(1,128)S(1)} %get-tuple-element.31), channel_id=1, source_target_pairs={{0,128},{128,256},{256,384},{1,129},{129,257},{257,385},{2,130},{1... | collective-permute-start | bytes 24584 | tf_op jit(solution)/shard_map/ppermute | solution.py:21
  121.0 1.9 %collective-permute-start.5 = (f32[8,1,256]{2,1,0:T(1,128)S(1)}, f32[8,1,256]{2,1,0:T(1,128)S(1)}, u32[]{:S(2)}, u32[]{:S(2)}) collective-permute-start(f32[8,1,256]{2,1,0:T(1,128)S(1)} %get-tuple-element.30), channel_id=1, source_target_pairs={{128,0},{256,128},{384,256},{129,1},{257,129},{385,257},{130,2},{2... | collective-permute-start | bytes 24584 | tf_op jit(solution)/shard_map/ppermute | solution.py:21
  122.9 0.8 fusion.23
  123.8 0.4 copy.97
  124.2 0.6 slice.102
  124.9 0.6 copy.101
  125.5 0.1 copy.100
  125.6 0.1 copy.99
  125.8 0.2 collective-permute-done.5
  125.9 0.2 fusion.12
  126.1 1.0 pad_maximum_fusion.1
  (47 shorter events, 0.8 us)
Async XLA Ops:
  1.8 48.6 %collective-permute-start.2 = (f32[8,32]{1,0:T(8,128)S(1)}, f32[8,32]{1,0:T(8,128)S(1)}, u32[]{:S(2)}, u32[]{:S(2)}) collective-permute-start(f32[8,32]{1,0:T(8,128)S(1)} %bitcast.48), channel_id=1, source_target_pairs={{0,1},{1,2},{2,3},{3,4},{4,5},{5,6},{6,7},{7,8},{8,9},{9,10},{10,1... | collective-permute-start | bytes 3080 | tf_op jit(solution)/shard_map/ppermute | solution.py:21
  8.0 43.8 %collective-permute-start.3 = (f32[8,32]{1,0:T(8,128)}, f32[8,32]{1,0:T(8,128)}, u32[]{:S(2)}, u32[]{:S(2)}) collective-permute-start(f32[8,32]{1,0:T(8,128)} %bitcast.6), channel_id=1, source_target_pairs={{1,0},{2,1},{3,2},{4,3},{5,4},{6,5},{7,6},{8,7},{9,8},{10,9},{11,1... | collective-permute-start | bytes 3080 | tf_op jit(solution)/shard_map/ppermute | solution.py:21
  10.8 42.5 %collective-permute-start = (f32[8,1,256]{2,1,0:T(1,128)}, f32[8,1,256]{2,1,0:T(1,128)S(1)}, u32[]{:S(2)}, u32[]{:S(2)}) collective-permute-start(f32[8,1,256]{2,1,0:T(1,128)} %get-tuple-element.23), channel_id=1, source_target_pairs={{0,128},{128,256},{256,384},{1,129},{129,257},{257,385},{2,130},{1... | collective-permute-start | bytes 24584 | tf_op jit(solution)/shard_map/ppermute | solution.py:21
  13.8 28.1 %copy-start = (f32[32,32,256]{2,1,0:T(8,128)S(1)}, f32[32,32,256]{2,1,0:T(8,128)}, u32[]{:S(2)}) copy-start(f32[32,32,256]{2,1,0:T(8,128)} %param.10) | copy-start | bytes 3145732
  13.8 39.4 %collective-permute-start.1 = (f32[8,1,256]{2,1,0:T(1,128)}, f32[8,1,256]{2,1,0:T(1,128)S(1)}, u32[]{:S(2)}, u32[]{:S(2)}) collective-permute-start(f32[8,1,256]{2,1,0:T(1,128)} %get-tuple-element.22), channel_id=1, source_target_pairs={{128,0},{256,128},{384,256},{129,1},{257,129},{385,257},{130,2},{2... | collective-permute-start | bytes 24584 | tf_op jit(solution)/shard_map/ppermute | solution.py:21
  18.1 24.6 %copy-start.9 = (f32[32,2,1024]{2,1,0:T(2,128)S(1)}, f32[32,2,1024]{2,1,0:T(2,128)}, u32[]{:S(2)}) copy-start(f32[32,2,1024]{2,1,0:T(2,128)} %param.12) | copy-start | bytes 786436
  20.4 43.9 %all-to-all-start = ((f32[128,2,514]{2,1,0:T(2,128)}), f32[128,2,514]{2,1,0:T(2,128)}, u32[]{:S(2)}, u32[]{:S(2)}) async-start(f32[128,2,514]{2,1,0:T(2,128)} %copy.80), calls=%async_computation | async-start | bytes 1310720 | tf_op jit(solution)/shard_map/all_to_all | solution.py:148
  44.9 4.1 %copy-start.10 = (s32[32,256]{1,0:T(8,128)S(1)}, s32[32,256]{1,0:T(8,128)}, u32[]{:S(2)}) copy-start(s32[32,256]{1,0:T(8,128)} %param.13) | copy-start | bytes 98308
  48.2 1.5 %copy-start.12 = (s32[1,1,128,2]{2,3,1,0:T(2,128)S(1)}, s32[1,1,128,2]{2,3,1,0:T(2,128)}, u32[]{:S(2)}) copy-start(s32[1,1,128,2]{2,3,1,0:T(2,128)} %param.15) | copy-start | bytes 3076
  48.2 5.1 %copy-start.6 = (f32[8,32,255]{2,1,0:T(8,128)S(1)}, f32[8,32,255]{2,1,0:T(8,128)}, u32[]{:S(2)}) copy-start(f32[8,32,255]{2,1,0:T(8,128)} %get-tuple-element.17) | copy-start | bytes 783364
  49.0 5.5 %slice-start = ((f32[32,32,256]{2,1,0:T(8,128)}), f32[24,32,256]{2,1,0:T(8,128)S(1)}, s32[]{:S(2)}) async-start(f32[32,32,256]{2,1,0:T(8,128)} %param.10), calls=%async_computation.2 | async-start | bytes 1572864 | tf_op jit(solution)/shard_map/slice | solution.py:159
  50.4 0.6 copy-start.11
  54.7 2.4 %copy-start.8 = (f32[32,256]{1,0:T(8,128)S(1)}, f32[32,256]{1,0:T(8,128)}, u32[]{:S(2)}) copy-start(f32[32,256]{1,0:T(8,128)} %convert_element_type.4) | copy-start | bytes 98308
  56.8 9.0 %copy-start.3 = (f32[16,32,512]{2,1,0:T(8,128)S(1)}, f32[16,32,512]{2,1,0:T(8,128)}, u32[]{:S(2)}) copy-start(f32[16,32,512]{2,1,0:T(8,128)} %constant.16) | copy-start | bytes 3145732
  69.4 12.9 %copy-start.2 = (s32[1,1,128,2]{3,2,1,0:T(8,128)S(1)}, s32[1,1,128,2]{3,2,1,0:T(8,128)}, u32[]{:S(2)}) copy-start(s32[1,1,128,2]{3,2,1,0:T(8,128)} %copy.77) | copy-start | bytes 3076
  81.1 24.4 %copy-start.1 = (f32[32,2,128,32]{2,3,1,0:T(8,128)S(1)}, f32[32,2,128,32]{2,3,1,0:T(8,128)}, u32[]{:S(2)}) copy-start(f32[32,2,128,32]{2,3,1,0:T(8,128)} %fusion.2) | copy-start | bytes 3145732
  83.1 21.3 %all-to-all-start.1 = ((f32[128,1,2]{2,1,0:T(1,128)}), f32[128,1,2]{2,1,0:T(1,128)S(1)}, u32[]{:S(2)}, u32[]{:S(2)}) async-start(f32[128,1,2]{2,1,0:T(1,128)} %bitcast.13), calls=%async_computation.1 | async-start | bytes 131072 | tf_op jit(solution)/shard_map/all_to_all | solution.py:169
  105.5 2.3 %copy-start.7 = (f32[32,256]{1,0:T(8,128)S(1)}, f32[32,256]{1,0:T(8,128)}, u32[]{:S(2)}) copy-start(f32[32,256]{1,0:T(8,128)} %param.11) | copy-start | bytes 98308
  108.2 17.3 %collective-permute-start.7 = (f32[8,32]{1,0:T(8,128)S(1)}, f32[8,32]{1,0:T(8,128)S(1)}, u32[]{:S(2)}, u32[]{:S(2)}) collective-permute-start(f32[8,32]{1,0:T(8,128)S(1)} %get-tuple-element.12), channel_id=1, source_target_pairs={{1,0},{2,1},{3,2},{4,3},{5,4},{6,5},{7,6},{8,7},{9,8},{10,9},{11,1... | collective-permute-start | bytes 3080 | tf_op jit(solution)/shard_map/ppermute | solution.py:21
  109.5 16.1 %collective-permute-start.6 = (f32[8,32]{1,0:T(8,128)S(1)}, f32[8,32]{1,0:T(8,128)S(1)}, u32[]{:S(2)}, u32[]{:S(2)}) collective-permute-start(f32[8,32]{1,0:T(8,128)S(1)} %get-tuple-element.13), channel_id=1, source_target_pairs={{0,1},{1,2},{2,3},{3,4},{4,5},{5,6},{6,7},{7,8},{8,9},{9,10},{10,1... | collective-permute-start | bytes 3080 | tf_op jit(solution)/shard_map/ppermute | solution.py:21
  115.0 10.8 %collective-permute-start.4 = (f32[8,1,256]{2,1,0:T(1,128)S(1)}, f32[8,1,256]{2,1,0:T(1,128)S(1)}, u32[]{:S(2)}, u32[]{:S(2)}) collective-permute-start(f32[8,1,256]{2,1,0:T(1,128)S(1)} %get-tuple-element.31), channel_id=1, source_target_pairs={{0,128},{128,256},{256,384},{1,129},{129,257},{257,385},{2,130},{1... | collective-permute-start | bytes 24584 | tf_op jit(solution)/shard_map/ppermute | solution.py:21
  121.0 5.0 %collective-permute-start.5 = (f32[8,1,256]{2,1,0:T(1,128)S(1)}, f32[8,1,256]{2,1,0:T(1,128)S(1)}, u32[]{:S(2)}, u32[]{:S(2)}) collective-permute-start(f32[8,1,256]{2,1,0:T(1,128)S(1)} %get-tuple-element.30), channel_id=1, source_target_pairs={{128,0},{256,128},{384,256},{129,1},{257,129},{385,257},{130,2},{2... | collective-permute-start | bytes 24584 | tf_op jit(solution)/shard_map/ppermute | solution.py:21
  123.8 2.1 %copy-start.4 = (f32[8,31,256]{2,1,0:T(8,128)S(1)}, f32[8,31,256]{2,1,0:T(8,128)}, u32[]{:S(2)}) copy-start(f32[8,31,256]{2,1,0:T(8,128)} %get-tuple-element.28) | copy-start | bytes 761860
  123.8 2.1 %copy-start.5 = (f32[8,31,256]{2,1,0:T(8,128)S(1)}, f32[8,31,256]{2,1,0:T(8,128)}, u32[]{:S(2)}) copy-start(f32[8,31,256]{2,1,0:T(8,128)} %get-tuple-element.29) | copy-start | bytes 761860

commit v9 on v8

--- a/solution.py
+++ b/solution.py
@@ -142,9 +142,8 @@
 
     owner_gain = antenna_gain[0, 0]
     owners, slots_per, _ = owner_gain.shape
-    packed = jnp.concatenate(
-        [owner_gain, obs_value[0, 0][..., None], obs_weight[0, 0][..., None]], -1
-    )
+    packed = jnp.pad(owner_gain, ((0, 0), (0, 0), (0, 2)))
+    packed = packed.at[:, :, K].set(obs_value[0, 0]).at[:, :, K + 1].set(obs_weight[0, 0])
     received = lax.all_to_all(packed, "lon", split_axis=0, concat_axis=0, tiled=True)
     slots = owners * slots_per
     gain = jnp.dot(

time: 128 us -> 145 us (1.13)
  the two profiles are of different devices: /device:TPU:1 before, /device:TPU:9 now
where the time goes in v9:
time: 145 us; the launch traced here: 144 us
  starting transfers between devices  58.6 us (40%)
  local copies, waits for them, and re-layouts  43.7 us (30%)
  Pallas kernels  14.3 us (10%)
  waiting for transfers between devices  11.9 us (8%)
  matrix products  7.73 us (5%)
  other arithmetic  6.77 us (5%)
    ppermute x4, starting transfers between devices, neighbours(): lax.ppermute(edge_low, axis, backward)  21.6 us
    ppermute x4, starting transfers between devices, neighbours(): lax.ppermute(edge_high, axis, forward)  16.1 us
    scatter x2, local copies, waits for them, and re-layouts, per_device(): packed.at[:, :, K].set(obs_value[0, 0]).at[:, :, K + 1]  15.3 us
    all_to_all x1, starting transfers between devices, per_device(): lax.all_to_all(packed, 'lon', split_axis=0, concat_axis=0, tiled=True)  12.4 us
    all_to_all x1, starting transfers between devices, per_device(): lax.all_to_all(residual, 'lon', split_axis=0, concat_axis=0, tiled=True)  8.52 us
    pallas_call x1, Pallas kernels, predict(): pl.pallas_call(predict_kernel, out_shape=jax.ShapeDtypeStruct((slots, FH,...  7.34 us
    all_to_all x1, waiting for transfers between devices, per_device(): lax.all_to_all(packed, 'lon', split_axis=0, concat_axis=0, tiled=True)  7.07 us
    pallas_call x1, Pallas kernels, scatter(): pl.pallas_call(scatter_kernel, out_shape=jax.ShapeDtypeStruct(top_shape,...  6.97 us
  transfers between devices with their start and end apart: 10, of which 3 were waited for; matrix products, arithmetic and copies ran while one was open for 28% of the time, Pallas kernels for 5%

profile of v9, /device:TPU:9, one launch (start us, length us, event | category | flops | bytes accessed | tf_op | source)
XLA Modules:
  0.0 144.1 jit_solution(4306042333211224307)
XLA Ops:
  0.6 1.1 fusion.18
  1.9 4.7 %collective-permute-start.2 = (f32[8,32]{1,0:T(8,128)S(1)}, f32[8,32]{1,0:T(8,128)S(1)}, u32[]{:S(2)}, u32[]{:S(2)}) collective-permute-start(f32[8,32]{1,0:T(8,128)S(1)} %bitcast.48), channel_id=1, source_target_pairs={{0,1},{1,2},{2,3},{3,4},{4,5},{5,6},{6,7},{7,8},{8,9},{9,10},{10,1... | collective-permute-start | bytes 3080 | tf_op jit(solution)/shard_map/ppermute | solution.py:21
  6.6 0.7 copy.132
  7.3 10.3 %collective-permute-start.3 = (f32[8,32]{1,0:T(8,128)}, f32[8,32]{1,0:T(8,128)}, u32[]{:S(2)}, u32[]{:S(2)}) collective-permute-start(f32[8,32]{1,0:T(8,128)} %bitcast.6), channel_id=1, source_target_pairs={{1,0},{2,1},{3,2},{4,3},{5,4},{6,5},{7,6},{8,7},{9,8},{10,9},{11,1... | collective-permute-start | bytes 3080 | tf_op jit(solution)/shard_map/ppermute | solution.py:21
  17.6 1.5 %fusion.20 = (f32[8,1,256]{2,1,0:T(1,128)}, f32[8,1,256]{2,1,0:T(1,128)}) fusion(f32[32,32,256]{2,1,0:T(8,128)} %param.14), kind=kLoop, calls=%fused_computation.35 | loop fusion | bytes 32768 | tf_op jit(solution)/shard_map/slice | solution.py:27
  19.0 3.0 %collective-permute-start = (f32[8,1,256]{2,1,0:T(1,128)}, f32[8,1,256]{2,1,0:T(1,128)S(1)}, u32[]{:S(2)}, u32[]{:S(2)}) collective-permute-start(f32[8,1,256]{2,1,0:T(1,128)} %get-tuple-element.49), channel_id=1, source_target_pairs={{0,128},{128,256},{256,384},{1,129},{129,257},{257,385},{2,130},{1... | collective-permute-start | bytes 24584 | tf_op jit(solution)/shard_map/ppermute | solution.py:21
  22.1 1.9 %collective-permute-start.1 = (f32[8,1,256]{2,1,0:T(1,128)}, f32[8,1,256]{2,1,0:T(1,128)S(1)}, u32[]{:S(2)}, u32[]{:S(2)}) collective-permute-start(f32[8,1,256]{2,1,0:T(1,128)} %get-tuple-element.48), channel_id=1, source_target_pairs={{128,0},{256,128},{384,256},{129,1},{257,129},{385,257},{130,2},{2... | collective-permute-start | bytes 24584 | tf_op jit(solution)/shard_map/ppermute | solution.py:21
  24.0 0.8 copy.106
  24.9 0.9 copy.107
  25.7 2.1 %pad.8 = f32[128,2,514]{2,1,0:T(2,128)} pad(f32[128,2,512]{2,1,0:T(2,128)} %bitcast.46, f32[]{:T(128)} %constant.63.clone.1), padding=0_0x0_0x0_2 | pad | bytes 1050628 | tf_op jit(solution)/shard_map/jit(_pad)/pad | solution.py:145
  27.8 3.4 %scatter.6 = f32[128,2,514]{2,1,0:T(2,128)} dynamic-update-slice(f32[128,2,514]{2,1,0:T(2,128)} %pad.8, f32[128,2,1]{2,1,0:T(2,128)S(1)} %copy.106, s32[]{:T(128)} %constant.62.clone.1, s32[]{:T(128)} %constant.62.clone.1, s32[]{:T(128)} %constant.64.clone.1) | dynamic-update-slice | bytes 2052 | tf_op jit(solution)/shard_map/scatter | solution.py:146
  31.2 12.0 %scatter.9 = f32[128,2,514]{2,1,0:T(2,128)} dynamic-update-slice(f32[128,2,514]{2,1,0:T(2,128)} %scatter.6, f32[128,2,1]{2,1,0:T(2,128)S(1)} %copy.107, s32[]{:T(128)} %constant.62.clone.1, s32[]{:T(128)} %constant.62.clone.1, s32[]{:T(128)} %constant.65.clone.1) | dynamic-update-slice | bytes 2052 | tf_op jit(solution)/shard_map/scatter | solution.py:146
  43.2 12.4 %all-to-all-start = ((f32[128,2,514]{2,1,0:T(2,128)}), f32[128,2,514]{2,1,0:T(2,128)}, u32[]{:S(2)}, u32[]{:S(2)}) async-start(f32[128,2,514]{2,1,0:T(2,128)} %scatter.9), calls=%async_computation | async-start | bytes 1310720 | tf_op jit(solution)/shard_map/all_to_all | solution.py:147
  55.6 0.8 fusion.17
  56.4 0.5 reshape.152
  56.9 1.7 %reshape.151 = f32[32,32,2,128]{3,2,1,0:T(2,128)S(1)} reshape(f32[32,32,256]{2,1,0:T(8,128)} %param.18) | data formatting | bytes 2097152 | tf_op jit(solution)/shard_map/reshape | solution.py:39
  58.6 3.3 %fusion.2 = f32[32,2,128,32]{2,3,1,0:T(8,128)} fusion(f32[32,2,32,32]{3,2,1,0:T(8,128)S(1)} %reshape.152, f32[32,32,2,128]{3,2,1,0:T(2,128)S(1)} %reshape.151), kind=kOutput, calls=%fused_computation.6 | convolution fusion | flops 100663296 | bytes 2359296 | tf_op jit(solution)/shard_map/rbji,jrbc->irbc/dot_general | solution.py:41
  61.9 0.8 fusion.19
  62.8 0.6 convert_element_type.6
  63.4 0.7 copy.104
  64.1 0.6 copy-done.11
  64.7 0.8 copy.110
  65.5 1.5 %copy.112 = f32[8,32,1]{2,1,0:T(8,128)} copy(f32[8,32,1]{1,0,2:T(8,128)} %bitcast.7) | data formatting | bytes 2048 | tf_op jit(solution)/shard_map/broadcast_in_dim | solution.py:32
  67.0 1.3 fusion.8
  68.4 0.5 reshape.155
  68.9 1.6 %convolution_bitcast_fusion = f32[4,32,2,128]{3,0,2,1:T(4,128)S(1)} fusion(f32[32,32,2,128]{3,2,1,0:T(2,128)S(1)} %reshape.155, f32[32,2,32,32]{3,2,1,0:T(8,128)S(1)} %reshape.152), kind=kOutput, calls=%fused_computation.2 | convolution fusion | flops 12582912 | bytes 1310720 | tf_op jit(solution)/shard_map/rbij,jrbc->irbc/dot_general | solution.py:41
  70.9 0.7 copy.116.top_ref
  71.6 7.1 %all-to-all-done = f32[128,2,514]{2,1,0:T(2,128)} async-done(((f32[128,2,514]{2,1,0:T(2,128)}), f32[128,2,514]{2,1,0:T(2,128)}, u32[]{:S(2)}, u32[]{:S(2)}) %all-to-all-start) | async-done | bytes 526368 | tf_op jit(solution)/shard_map/all_to_all | solution.py:147
  78.7 1.1 slice.155
  79.8 0.4 reshape.162
  80.2 1.0 fusion.25
  81.2 2.5 %copy.117.gain_ref = f32[256,16,32]{2,1,0:T(8,128)} copy(f32[256,16,32]{0,2,1:T(8,128)S(1)} %fusion.25) | data formatting | bytes 1048576 | tf_op jit(solution)/shard_map/dot_general | solution.py:149
  83.7 7.3 %shard_map.113 = f32[256,8,128]{2,1,0:T(8,128)} custom-call(s32[128,2]{1,0:T(8,128)} %bitcast.44, f32[256,128]{1,0:T(8,128)} %copy.116.top_ref, f32[256,16,32]{2,1,0:T(8,128)} %copy.117.gain_ref), custom_call_target="tpu_custom_call" | custom-call | tf_op jit(solution)/shard_map/pallas_call | solution.py:98
  91.0 2.3 %reduce_sum.9 = f32[256]{0:T(256)S(1)} reduce(f32[256,8,128]{2,1,0:T(8,128)} %shard_map.113, f32[]{:T(128)} %constant.63.clone.1), dimensions={1,2}, to_apply=%region_0.1 | reduce | flops 261888 | bytes 1049604 | tf_op jit(solution)/shard_map/reduce_sum | solution.py:165
  93.3 0.1 reshape.159
  93.4 1.2 fusion.21
  94.6 0.9 copy.130
  95.5 0.9 copy.133
  96.3 0.1 squeeze.32
  96.5 0.1 squeeze.35
  96.6 0.6 fusion.16
  97.3 0.1 ge.22
  97.4 8.5 %all-to-all-start.1 = ((f32[128,1,2]{2,1,0:T(1,128)}), f32[128,1,2]{2,1,0:T(1,128)S(1)}, u32[]{:S(2)}, u32[]{:S(2)}) async-start(f32[128,1,2]{2,1,0:T(1,128)} %bitcast.13), calls=%async_computation.1 | async-start | bytes 131072 | tf_op jit(solution)/shard_map/all_to_all | solution.py:168
  105.9 0.6 subtract_multiply_fusion.res_ref
  106.5 7.0 %shard_map.114 = f32[256,128]{1,0:T(8,128)} custom-call(s32[128,2]{1,0:T(8,128)} %bitcast.45, f32[256]{0:T(256)} %subtract_multiply_fusion.res_ref, f32[256,16,32]{2,1,0:T(8,128)} %copy.117.gain_ref), custom_call_target="tpu_custom_call" | custom-call | tf_op jit(solution)/shard_map/pallas_call | solution.py:109
  113.5 4.6 %all-to-all-done.1 = f32[128,1,2]{2,1,0:T(1,128)S(1)} async-done(((f32[128,1,2]{2,1,0:T(1,128)}), f32[128,1,2]{2,1,0:T(1,128)S(1)}, u32[]{:S(2)}, u32[]{:S(2)}) %all-to-all-start.1) | async-done | bytes 1056 | tf_op jit(solution)/shard_map/all_to_all | solution.py:168
  118.1 1.0 copy.121
  119.3 1.8 %fusion = f32[32,32,2,128]{3,0,2,1:T(8,128)S(1)} fusion(f32[32,2,128,32]{2,3,1,0:T(8,128)S(1)} %copy-done.1, f32[4,32,2,128]{3,2,1,0:T(2,128)S(1)} %reshape.161, f32[32,2,32,32]{3,2,1,0:T(8,128)S(1)} %reshape.152), kind=kOutput, calls=%fused_computation.1 | convolution fusion | flops 12845056 | bytes 2359296 | tf_op jit(solution)/shard_map/rbji,jrbc->irbc/dot_general | solution.py:41
  121.2 0.1 copy.125
  121.4 0.2 slice.144
  121.8 0.2 slice_reduce_fusion
  122.0 2.3 %collective-permute-start.6 = (f32[8,32]{1,0:T(8,128)S(1)}, f32[8,32]{1,0:T(8,128)S(1)}, u32[]{:S(2)}, u32[]{:S(2)}) collective-permute-start(f32[8,32]{1,0:T(8,128)S(1)} %get-tuple-element.39), channel_id=1, source_target_pairs={{0,1},{1,2},{2,3},{3,4},{4,5},{5,6},{6,7},{7,8},{8,9},{9,10},{10,1... | collective-permute-start | bytes 3080 | tf_op jit(solution)/shard_map/ppermute | solution.py:21
  124.3 7.5 %collective-permute-start.7 = (f32[8,32]{1,0:T(8,128)S(1)}, f32[8,32]{1,0:T(8,128)S(1)}, u32[]{:S(2)}, u32[]{:S(2)}) collective-permute-start(f32[8,32]{1,0:T(8,128)S(1)} %get-tuple-element.38), channel_id=1, source_target_pairs={{1,0},{2,1},{3,2},{4,3},{5,4},{6,5},{7,6},{8,7},{9,8},{10,9},{11,1... | collective-permute-start | bytes 3080 | tf_op jit(solution)/shard_map/ppermute | solution.py:21
  131.8 6.1 %collective-permute-start.4 = (f32[8,1,256]{2,1,0:T(1,128)S(1)}, f32[8,1,256]{2,1,0:T(1,128)S(1)}, u32[]{:S(2)}, u32[]{:S(2)}) collective-permute-start(f32[8,1,256]{2,1,0:T(1,128)S(1)} %get-tuple-element.57), channel_id=1, source_target_pairs={{0,128},{128,256},{256,384},{1,129},{129,257},{257,385},{2,130},{1... | collective-permute-start | bytes 24584 | tf_op jit(solution)/shard_map/ppermute | solution.py:21
  137.9 1.9 %collective-permute-start.5 = (f32[8,1,256]{2,1,0:T(1,128)S(1)}, f32[8,1,256]{2,1,0:T(1,128)S(1)}, u32[]{:S(2)}, u32[]{:S(2)}) collective-permute-start(f32[8,1,256]{2,1,0:T(1,128)S(1)} %get-tuple-element.56), channel_id=1, source_target_pairs={{128,0},{256,128},{384,256},{129,1},{257,129},{385,257},{130,2},{2... | collective-permute-start | bytes 24584 | tf_op jit(solution)/shard_map/ppermute | solution.py:21
  139.8 0.8 fusion.23
  140.7 0.4 copy.124
  141.2 0.6 slice.142
  141.8 0.6 copy.128
  142.4 0.1 copy.126
  142.6 0.1 copy.127
  142.7 0.2 collective-permute-done.5
  142.9 0.2 fusion.12
  143.1 1.0 pad_maximum_fusion.1
  (49 shorter events, 1.0 us)
Async XLA Ops:
  0.6 55.0 %copy-start = (f32[32,32,256]{2,1,0:T(8,128)S(1)}, f32[32,32,256]{2,1,0:T(8,128)}, u32[]{:S(2)}) copy-start(f32[32,32,256]{2,1,0:T(8,128)} %param.14) | copy-start | bytes 3145732
  1.9 62.2 %collective-permute-start.2 = (f32[8,32]{1,0:T(8,128)S(1)}, f32[8,32]{1,0:T(8,128)S(1)}, u32[]{:S(2)}, u32[]{:S(2)}) collective-permute-start(f32[8,32]{1,0:T(8,128)S(1)} %bitcast.48), channel_id=1, source_target_pairs={{0,1},{1,2},{2,3},{3,4},{4,5},{5,6},{6,7},{7,8},{8,9},{9,10},{10,1... | collective-permute-start | bytes 3080 | tf_op jit(solution)/shard_map/ppermute | solution.py:21
  7.3 58.2 %collective-permute-start.3 = (f32[8,32]{1,0:T(8,128)}, f32[8,32]{1,0:T(8,128)}, u32[]{:S(2)}, u32[]{:S(2)}) collective-permute-start(f32[8,32]{1,0:T(8,128)} %bitcast.6), channel_id=1, source_target_pairs={{1,0},{2,1},{3,2},{4,3},{5,4},{6,5},{7,6},{8,7},{9,8},{10,9},{11,1... | collective-permute-start | bytes 3080 | tf_op jit(solution)/shard_map/ppermute | solution.py:21
  19.0 47.9 %collective-permute-start = (f32[8,1,256]{2,1,0:T(1,128)}, f32[8,1,256]{2,1,0:T(1,128)S(1)}, u32[]{:S(2)}, u32[]{:S(2)}) collective-permute-start(f32[8,1,256]{2,1,0:T(1,128)} %get-tuple-element.49), channel_id=1, source_target_pairs={{0,128},{128,256},{256,384},{1,129},{129,257},{257,385},{2,130},{1... | collective-permute-start | bytes 24584 | tf_op jit(solution)/shard_map/ppermute | solution.py:21
  22.1 44.9 %collective-permute-start.1 = (f32[8,1,256]{2,1,0:T(1,128)}, f32[8,1,256]{2,1,0:T(1,128)S(1)}, u32[]{:S(2)}, u32[]{:S(2)}) collective-permute-start(f32[8,1,256]{2,1,0:T(1,128)} %get-tuple-element.48), channel_id=1, source_target_pairs={{128,0},{256,128},{384,256},{129,1},{257,129},{385,257},{130,2},{2... | collective-permute-start | bytes 24584 | tf_op jit(solution)/shard_map/ppermute | solution.py:21
  24.9 31.5 %copy-start.9 = (f32[32,2,1024]{2,1,0:T(2,128)S(1)}, f32[32,2,1024]{2,1,0:T(2,128)}, u32[]{:S(2)}) copy-start(f32[32,2,1024]{2,1,0:T(2,128)} %param.16) | copy-start | bytes 786436
  43.2 35.5 %all-to-all-start = ((f32[128,2,514]{2,1,0:T(2,128)}), f32[128,2,514]{2,1,0:T(2,128)}, u32[]{:S(2)}, u32[]{:S(2)}) async-start(f32[128,2,514]{2,1,0:T(2,128)} %scatter.9), calls=%async_computation | async-start | bytes 1310720 | tf_op jit(solution)/shard_map/all_to_all | solution.py:147
  58.6 4.1 %copy-start.10 = (s32[32,256]{1,0:T(8,128)S(1)}, s32[32,256]{1,0:T(8,128)}, u32[]{:S(2)}) copy-start(s32[32,256]{1,0:T(8,128)} %param.17) | copy-start | bytes 98308
  61.9 1.5 %copy-start.12 = (s32[1,1,128,2]{2,3,1,0:T(2,128)S(1)}, s32[1,1,128,2]{2,3,1,0:T(2,128)}, u32[]{:S(2)}) copy-start(s32[1,1,128,2]{2,3,1,0:T(2,128)} %param.19) | copy-start | bytes 3076
  61.9 5.1 %copy-start.6 = (f32[8,32,255]{2,1,0:T(8,128)S(1)}, f32[8,32,255]{2,1,0:T(8,128)}, u32[]{:S(2)}) copy-start(f32[8,32,255]{2,1,0:T(8,128)} %get-tuple-element.43) | copy-start | bytes 783364
  62.8 5.5 %slice-start = ((f32[32,32,256]{2,1,0:T(8,128)}), f32[24,32,256]{2,1,0:T(8,128)S(1)}, s32[]{:S(2)}) async-start(f32[32,32,256]{2,1,0:T(8,128)} %param.14), calls=%async_computation.2 | async-start | bytes 1572864 | tf_op jit(solution)/shard_map/slice | solution.py:158
  64.1 0.6 copy-start.11
  68.4 2.4 %copy-start.8 = (f32[32,256]{1,0:T(8,128)S(1)}, f32[32,256]{1,0:T(8,128)}, u32[]{:S(2)}) copy-start(f32[32,256]{1,0:T(8,128)} %convert_element_type.6) | copy-start | bytes 98308
  70.5 9.7 %copy-start.3 = (f32[16,32,512]{2,1,0:T(8,128)S(1)}, f32[16,32,512]{2,1,0:T(8,128)}, u32[]{:S(2)}) copy-start(f32[16,32,512]{2,1,0:T(8,128)} %constant.76) | copy-start | bytes 3145732
  83.7 12.9 %copy-start.2 = (s32[1,1,128,2]{3,2,1,0:T(8,128)S(1)}, s32[1,1,128,2]{3,2,1,0:T(8,128)}, u32[]{:S(2)}) copy-start(s32[1,1,128,2]{3,2,1,0:T(8,128)} %copy.104) | copy-start | bytes 3076
  95.5 23.8 %copy-start.1 = (f32[32,2,128,32]{2,3,1,0:T(8,128)S(1)}, f32[32,2,128,32]{2,3,1,0:T(8,128)}, u32[]{:S(2)}) copy-start(f32[32,2,128,32]{2,3,1,0:T(8,128)} %fusion.2) | copy-start | bytes 3145732
  97.4 20.7 %all-to-all-start.1 = ((f32[128,1,2]{2,1,0:T(1,128)}), f32[128,1,2]{2,1,0:T(1,128)S(1)}, u32[]{:S(2)}, u32[]{:S(2)}) async-start(f32[128,1,2]{2,1,0:T(1,128)} %bitcast.13), calls=%async_computation.1 | async-start | bytes 131072 | tf_op jit(solution)/shard_map/all_to_all | solution.py:168
  119.3 2.3 %copy-start.7 = (f32[32,256]{1,0:T(8,128)S(1)}, f32[32,256]{1,0:T(8,128)}, u32[]{:S(2)}) copy-start(f32[32,256]{1,0:T(8,128)} %param.15) | copy-start | bytes 98308
  122.0 20.5 %collective-permute-start.6 = (f32[8,32]{1,0:T(8,128)S(1)}, f32[8,32]{1,0:T(8,128)S(1)}, u32[]{:S(2)}, u32[]{:S(2)}) collective-permute-start(f32[8,32]{1,0:T(8,128)S(1)} %get-tuple-element.39), channel_id=1, source_target_pairs={{0,1},{1,2},{2,3},{3,4},{4,5},{5,6},{6,7},{7,8},{8,9},{9,10},{10,1... | collective-permute-start | bytes 3080 | tf_op jit(solution)/shard_map/ppermute | solution.py:21
  124.3 18.2 %collective-permute-start.7 = (f32[8,32]{1,0:T(8,128)S(1)}, f32[8,32]{1,0:T(8,128)S(1)}, u32[]{:S(2)}, u32[]{:S(2)}) collective-permute-start(f32[8,32]{1,0:T(8,128)S(1)} %get-tuple-element.38), channel_id=1, source_target_pairs={{1,0},{2,1},{3,2},{4,3},{5,4},{6,5},{7,6},{8,7},{9,8},{10,9},{11,1... | collective-permute-start | bytes 3080 | tf_op jit(solution)/shard_map/ppermute | solution.py:21
  131.8 10.9 %collective-permute-start.4 = (f32[8,1,256]{2,1,0:T(1,128)S(1)}, f32[8,1,256]{2,1,0:T(1,128)S(1)}, u32[]{:S(2)}, u32[]{:S(2)}) collective-permute-start(f32[8,1,256]{2,1,0:T(1,128)S(1)} %get-tuple-element.57), channel_id=1, source_target_pairs={{0,128},{128,256},{256,384},{1,129},{129,257},{257,385},{2,130},{1... | collective-permute-start | bytes 24584 | tf_op jit(solution)/shard_map/ppermute | solution.py:21
  137.9 5.0 %collective-permute-start.5 = (f32[8,1,256]{2,1,0:T(1,128)S(1)}, f32[8,1,256]{2,1,0:T(1,128)S(1)}, u32[]{:S(2)}, u32[]{:S(2)}) collective-permute-start(f32[8,1,256]{2,1,0:T(1,128)S(1)} %get-tuple-element.56), channel_id=1, source_target_pairs={{128,0},{256,128},{384,256},{129,1},{257,129},{385,257},{130,2},{2... | collective-permute-start | bytes 24584 | tf_op jit(solution)/shard_map/ppermute | solution.py:21
  140.7 2.1 %copy-start.4 = (f32[8,31,256]{2,1,0:T(8,128)S(1)}, f32[8,31,256]{2,1,0:T(8,128)}, u32[]{:S(2)}) copy-start(f32[8,31,256]{2,1,0:T(8,128)} %get-tuple-element.54) | copy-start | bytes 761860
  140.7 2.1 %copy-start.5 = (f32[8,31,256]{2,1,0:T(8,128)S(1)}, f32[8,31,256]{2,1,0:T(8,128)}, u32[]{:S(2)}) copy-start(f32[8,31,256]{2,1,0:T(8,128)} %get-tuple-element.55) | copy-start | bytes 761860

commit v10 on v8

--- a/solution.py
+++ b/solution.py
@@ -143,16 +143,16 @@
     owner_gain = antenna_gain[0, 0]
     owners, slots_per, _ = owner_gain.shape
     packed = jnp.concatenate(
-        [owner_gain, obs_value[0, 0][..., None], obs_weight[0, 0][..., None]], -1
+        [owner_gain.reshape(owners, slots_per * K), obs_value[0, 0], obs_weight[0, 0]], -1
     )
     received = lax.all_to_all(packed, "lon", split_axis=0, concat_axis=0, tiled=True)
     slots = owners * slots_per
     gain = jnp.dot(
-        received[..., :K].reshape(slots, K), jnp.asarray(reorder_matrix()), precision=lax.Precision.HIGHEST
+        received[:, : slots_per * K].reshape(slots, K), jnp.asarray(reorder_matrix()), precision=lax.Precision.HIGHEST
     )
     gain = gain.reshape(slots, FW, FH * LTOP)
-    value = received[..., K]
-    weight = received[..., K + 1]
+    value = received[:, slots_per * K : slots_per * (K + 1)]
+    weight = received[:, slots_per * (K + 1) :]
 
     deep = moisture[levels - LG :]
     mixed = jnp.concatenate(

time: 128 us -> 127 us (level)
  the two profiles are of different devices: /device:TPU:1 before, /device:TPU:9 now
where the time goes in v10:
time: 127 us; the launch traced here: 126 us
  starting transfers between devices  59.1 us (47%)
  local copies, waits for them, and re-layouts  28 us (22%)
  Pallas kernels  14.3 us (11%)
  matrix products  9.17 us (7%)
  waiting for transfers between devices  8.65 us (7%)
  other arithmetic  5.95 us (5%)
    ppermute x4, starting transfers between devices, neighbours(): lax.ppermute(edge_low, axis, backward)  20.7 us
    ppermute x4, starting transfers between devices, neighbours(): lax.ppermute(edge_high, axis, forward)  17.1 us
    all_to_all x1, starting transfers between devices, per_device(): lax.all_to_all(packed, 'lon', split_axis=0, concat_axis=0, tiled=True)  12 us
    all_to_all x1, starting transfers between devices, per_device(): lax.all_to_all(residual, 'lon', split_axis=0, concat_axis=0, tiled=True)  9.2 us
    pallas_call x1, Pallas kernels, predict(): pl.pallas_call(predict_kernel, out_shape=jax.ShapeDtypeStruct((slots, FH,...  7.33 us
    pallas_call x1, Pallas kernels, scatter(): pl.pallas_call(scatter_kernel, out_shape=jax.ShapeDtypeStruct(top_shape,...  7 us
    dot_general x3, matrix products, columns(): out = jnp.einsum(form, matrices, grouped, precision=lax.Precision.HIGHEST)  6.92 us
    all_to_all x1, waiting for transfers between devices, per_device(): lax.all_to_all(packed, 'lon', split_axis=0, concat_axis=0, tiled=True)  6.38 us
  transfers between devices with their start and end apart: 10, of which 3 were waited for; matrix products, arithmetic and copies ran while one was open for 22% of the time, Pallas kernels for 6%

profile of v10, /device:TPU:9, one launch (start us, length us, event | category | flops | bytes accessed | tf_op | source)
XLA Modules:
  0.0 126.3 jit_solution(9250442017120530058)
XLA Ops:
  0.6 1.1 fusion.18
  1.7 0.7 copy.125
  2.4 4.6 %collective-permute-start.2 = (f32[8,32]{1,0:T(8,128)}, f32[8,32]{1,0:T(8,128)}, u32[]{:S(2)}, u32[]{:S(2)}) collective-permute-start(f32[8,32]{1,0:T(8,128)} %bitcast.7), channel_id=1, source_target_pairs={{0,1},{1,2},{2,3},{3,4},{4,5},{5,6},{6,7},{7,8},{8,9},{9,10},{10,1... | collective-permute-start | bytes 3080 | tf_op jit(solution)/shard_map/ppermute | solution.py:21
  7.1 0.7 copy.126
  7.8 10.3 %collective-permute-start.3 = (f32[8,32]{1,0:T(8,128)}, f32[8,32]{1,0:T(8,128)}, u32[]{:S(2)}, u32[]{:S(2)}) collective-permute-start(f32[8,32]{1,0:T(8,128)} %bitcast.9), channel_id=1, source_target_pairs={{1,0},{2,1},{3,2},{4,3},{5,4},{6,5},{7,6},{8,7},{9,8},{10,9},{11,1... | collective-permute-start | bytes 3080 | tf_op jit(solution)/shard_map/ppermute | solution.py:21
  18.0 1.5 %fusion.20 = (f32[8,1,256]{2,1,0:T(1,128)}, f32[8,1,256]{2,1,0:T(1,128)}) fusion(f32[32,32,256]{2,1,0:T(8,128)} %param.10), kind=kLoop, calls=%fused_computation.34 | loop fusion | bytes 32768 | tf_op jit(solution)/shard_map/slice | solution.py:27
  19.5 3.0 %collective-permute-start = (f32[8,1,256]{2,1,0:T(1,128)}, f32[8,1,256]{2,1,0:T(1,128)S(1)}, u32[]{:S(2)}, u32[]{:S(2)}) collective-permute-start(f32[8,1,256]{2,1,0:T(1,128)} %get-tuple-element.25), channel_id=1, source_target_pairs={{0,128},{128,256},{256,384},{1,129},{129,257},{257,385},{2,130},{1... | collective-permute-start | bytes 24584 | tf_op jit(solution)/shard_map/ppermute | solution.py:21
  22.6 0.0 copy-start
  22.6 2.1 %collective-permute-start.1 = (f32[8,1,256]{2,1,0:T(1,128)}, f32[8,1,256]{2,1,0:T(1,128)S(1)}, u32[]{:S(2)}, u32[]{:S(2)}) collective-permute-start(f32[8,1,256]{2,1,0:T(1,128)} %get-tuple-element.24), channel_id=1, source_target_pairs={{128,0},{256,128},{384,256},{129,1},{257,129},{385,257},{130,2},{2... | collective-permute-start | bytes 24584 | tf_op jit(solution)/shard_map/ppermute | solution.py:21
  24.7 1.2 copy.97
  25.9 0.8 concatenate.33
  26.7 1.5 %copy.98 = f32[128,1,1028]{2,1,0:T(1,128)} copy(f32[128,1,1028]{0,2,1:T(8,128)S(1)} %bitcast.37) | data formatting | bytes 1052672 | tf_op jit(solution)/shard_map/all_to_all | solution.py:148
  28.2 12.0 %all-to-all-start = ((f32[128,1,1028]{2,1,0:T(1,128)}), f32[128,1,1028]{2,1,0:T(1,128)S(1)}, u32[]{:S(2)}, u32[]{:S(2)}) async-start(f32[128,1,1028]{2,1,0:T(1,128)} %copy.98), calls=%async_computation | async-start | bytes 1179648 | tf_op jit(solution)/shard_map/all_to_all | solution.py:148
  40.3 0.0 copy-start.7
  40.3 0.9 fusion.17
  41.2 0.8 fusion.19
  42.0 0.5 reshape.48
  42.5 0.7 copy.96
  43.2 2.8 %reshape.47 = f32[32,32,2,128]{3,2,1,0:T(2,128)} reshape(f32[32,32,256]{2,1,0:T(8,128)} %param.14) | data formatting | bytes 2097152 | tf_op jit(solution)/shard_map/reshape | solution.py:39
  46.0 1.5 %copy.102 = f32[8,32,1]{2,1,0:T(8,128)} copy(f32[8,32,1]{1,0,2:T(8,128)} %bitcast.8) | data formatting | bytes 2048 | tf_op jit(solution)/shard_map/broadcast_in_dim | solution.py:31
  47.5 1.4 %copy.104 = f32[8,32,1]{2,1,0:T(8,128)} copy(f32[8,32,1]{1,0,2:T(8,128)} %bitcast.10) | data formatting | bytes 2048 | tf_op jit(solution)/shard_map/broadcast_in_dim | solution.py:32
  48.9 1.5 %fusion.8 = f32[8,32,256]{2,1,0:T(8,128)S(1)} fusion(f32[8,31,256]{2,1,0:T(8,128)} %get-tuple-element.23, f32[8,1,256]{2,1,0:T(1,128)S(1)} %collective-permute-done, f32[8,1,256]{2,1,0:T(1,128)S(1)} %collective-permute-done.1, f32[8,31,256]{2,1,0:T(8,128)} %get-tuple-element.22, f32[8,32,255]{2,1,0:T(8,128)} %get-tuple-element.19, f32[8,32,1]{2,1,0:T(8,128)} %copy.102, ...), kind=kLoop, calls=%fused_computation.14 | loop fusion | flops 720896 | bytes 1605632 | tf_op jit(solution)/shard_map/add | solution.py:159
  50.4 0.1 pad_maximum_fusion
  50.5 1.5 %reshape.49 = f32[32,32,2,128]{3,2,1,0:T(2,128)} reshape(f32[32,32,256]{2,1,0:T(8,128)S(1)} %pad_maximum_fusion) | data formatting | bytes 2097152 | tf_op jit(solution)/shard_map/reshape | solution.py:39
  52.1 2.8 %convolution_bitcast_fusion = f32[4,32,2,128]{3,0,2,1:T(4,128)S(1)} fusion(f32[32,32,2,128]{3,2,1,0:T(2,128)} %reshape.49, f32[32,2,32,32]{3,2,1,0:T(8,128)S(1)} %reshape.48), kind=kOutput, calls=%fused_computation.2 | convolution fusion | flops 12582912 | bytes 1310720 | tf_op jit(solution)/shard_map/rbij,jrbc->irbc/dot_general | solution.py:41
  54.8 0.1 copy.106
  54.9 0.1 reshape.50
  55.1 0.1 copy.107
  55.2 0.7 copy.109.top_ref
  55.9 6.4 %all-to-all-done = f32[128,1,1028]{2,1,0:T(1,128)S(1)} async-done(((f32[128,1,1028]{2,1,0:T(1,128)}), f32[128,1,1028]{2,1,0:T(1,128)S(1)}, u32[]{:S(2)}, u32[]{:S(2)}) %all-to-all-start) | async-done | bytes 526368 | tf_op jit(solution)/shard_map/all_to_all | solution.py:148
  62.3 0.9 copy.99
  63.3 0.2 copy.108
  63.5 0.1 reshape.57
  63.6 2.2 %fusion.24 = f32[256,16,32]{0,2,1:T(8,128)S(1)} fusion(f32[256,512,1]{1,0,2:T(8,128)S(1)} %reshape.57, f32[16,32,512]{2,1,0:T(8,128)} %constant.16), kind=kOutput, calls=%fused_computation.38 | convolution fusion | flops 805306368 | bytes 2097152 | tf_op jit(solution)/shard_map/dot_general | solution.py:150
  65.8 2.5 %copy.110.gain_ref = f32[256,16,32]{2,1,0:T(8,128)} copy(f32[256,16,32]{0,2,1:T(8,128)S(1)} %fusion.24) | data formatting | bytes 1048576 | tf_op jit(solution)/shard_map/dot_general | solution.py:150
  68.3 7.3 %shard_map.113 = f32[256,8,128]{2,1,0:T(8,128)} custom-call(s32[128,2]{1,0:T(8,128)} %bitcast.40, f32[256,128]{1,0:T(8,128)} %copy.109.top_ref, f32[256,16,32]{2,1,0:T(8,128)} %copy.110.gain_ref), custom_call_target="tpu_custom_call" | custom-call | tf_op jit(solution)/shard_map/pallas_call | solution.py:98
  75.6 2.3 %reduce_sum.9 = f32[256]{0:T(256)S(1)} reduce(f32[256,8,128]{2,1,0:T(8,128)} %shard_map.113, f32[]{:T(128)} %constant.3.clone.1), dimensions={1,2}, to_apply=%region_0.0 | reduce | flops 261888 | bytes 1049604 | tf_op jit(solution)/shard_map/reduce_sum | solution.py:166
  77.9 0.1 reshape.53
  78.1 0.7 fusion.16
  78.8 9.2 %all-to-all-start.1 = ((f32[128,1,2]{2,1,0:T(1,128)}), f32[128,1,2]{2,1,0:T(1,128)S(1)}, u32[]{:S(2)}, u32[]{:S(2)}) async-start(f32[128,1,2]{2,1,0:T(1,128)} %bitcast.15), calls=%async_computation.1 | async-start | bytes 131072 | tf_op jit(solution)/shard_map/all_to_all | solution.py:169
  88.1 2.3 %fusion.2 = f32[32,2,128,32]{2,3,1,0:T(8,128)S(1)} fusion(f32[32,2,32,32]{3,2,1,0:T(8,128)S(1)} %reshape.48, f32[32,32,2,128]{3,2,1,0:T(2,128)S(1)} %copy-done.1), kind=kOutput, calls=%fused_computation.6 | convolution fusion | flops 100663296 | bytes 2359296 | tf_op jit(solution)/shard_map/rbji,jrbc->irbc/dot_general | solution.py:41
  90.4 1.5 %reshape.54.res_ref = f32[256]{0:T(256)} reshape(f32[128,2]{1,0:T(8,128)} %fusion.16) | data formatting | bytes 2048 | tf_op jit(solution)/shard_map/reshape | solution.py:170
  91.9 7.0 %shard_map.114 = f32[256,128]{1,0:T(8,128)} custom-call(s32[128,2]{1,0:T(8,128)} %bitcast.41, f32[256]{0:T(256)} %reshape.54.res_ref, f32[256,16,32]{2,1,0:T(8,128)} %copy.110.gain_ref), custom_call_target="tpu_custom_call" | custom-call | tf_op jit(solution)/shard_map/pallas_call | solution.py:109
  98.9 1.3 %all-to-all-done.1 = f32[128,1,2]{2,1,0:T(1,128)S(1)} async-done(((f32[128,1,2]{2,1,0:T(1,128)}), f32[128,1,2]{2,1,0:T(1,128)S(1)}, u32[]{:S(2)}, u32[]{:S(2)}) %all-to-all-start.1) | async-done | bytes 1056 | tf_op jit(solution)/shard_map/all_to_all | solution.py:169
  100.2 1.0 copy.114
  101.3 0.1 reshape.56
  101.4 1.8 %fusion = f32[32,32,2,128]{3,0,2,1:T(8,128)S(1)} fusion(f32[32,2,128,32]{2,3,1,0:T(8,128)S(1)} %fusion.2, f32[4,32,2,128]{3,2,1,0:T(2,128)S(1)} %reshape.56, f32[32,2,32,32]{3,2,1,0:T(8,128)S(1)} %reshape.48), kind=kOutput, calls=%fused_computation.1 | convolution fusion | flops 12845056 | bytes 2359296 | tf_op jit(solution)/shard_map/rbji,jrbc->irbc/dot_general | solution.py:41
  103.3 0.1 copy.118
  103.5 0.2 slice.104
  103.7 0.1 fusion.21
  103.9 0.2 slice_reduce_fusion
  104.1 3.3 %collective-permute-start.6 = (f32[8,32]{1,0:T(8,128)S(1)}, f32[8,32]{1,0:T(8,128)S(1)}, u32[]{:S(2)}, u32[]{:S(2)}) collective-permute-start(f32[8,32]{1,0:T(8,128)S(1)} %get-tuple-element.17), channel_id=1, source_target_pairs={{0,1},{1,2},{2,3},{3,4},{4,5},{5,6},{6,7},{7,8},{8,9},{9,10},{10,1... | collective-permute-start | bytes 3080 | tf_op jit(solution)/shard_map/ppermute | solution.py:21
  107.4 6.5 %collective-permute-start.7 = (f32[8,32]{1,0:T(8,128)S(1)}, f32[8,32]{1,0:T(8,128)S(1)}, u32[]{:S(2)}, u32[]{:S(2)}) collective-permute-start(f32[8,32]{1,0:T(8,128)S(1)} %get-tuple-element.16), channel_id=1, source_target_pairs={{1,0},{2,1},{3,2},{4,3},{5,4},{6,5},{7,6},{8,7},{9,8},{10,9},{11,1... | collective-permute-start | bytes 3080 | tf_op jit(solution)/shard_map/ppermute | solution.py:21
  113.9 6.1 %collective-permute-start.4 = (f32[8,1,256]{2,1,0:T(1,128)S(1)}, f32[8,1,256]{2,1,0:T(1,128)S(1)}, u32[]{:S(2)}, u32[]{:S(2)}) collective-permute-start(f32[8,1,256]{2,1,0:T(1,128)S(1)} %get-tuple-element.31), channel_id=1, source_target_pairs={{0,128},{128,256},{256,384},{1,129},{129,257},{257,385},{2,130},{1... | collective-permute-start | bytes 24584 | tf_op jit(solution)/shard_map/ppermute | solution.py:21
  120.0 1.9 %collective-permute-start.5 = (f32[8,1,256]{2,1,0:T(1,128)S(1)}, f32[8,1,256]{2,1,0:T(1,128)S(1)}, u32[]{:S(2)}, u32[]{:S(2)}) collective-permute-start(f32[8,1,256]{2,1,0:T(1,128)S(1)} %get-tuple-element.30), channel_id=1, source_target_pairs={{128,0},{256,128},{384,256},{129,1},{257,129},{385,257},{130,2},{2... | collective-permute-start | bytes 24584 | tf_op jit(solution)/shard_map/ppermute | solution.py:21
  122.0 0.1 slice.117
  122.1 0.4 copy.117
  122.5 0.6 slice.102
  123.2 0.6 copy.121
  123.8 0.1 copy.119
  123.9 0.1 copy.120
  124.1 1.0 collective-permute-done.5
  125.0 0.2 fusion.12
  125.2 1.0 pad_maximum_fusion.1
  (38 shorter events, 0.4 us)
Async XLA Ops:
  2.4 43.6 %collective-permute-start.2 = (f32[8,32]{1,0:T(8,128)}, f32[8,32]{1,0:T(8,128)}, u32[]{:S(2)}, u32[]{:S(2)}) collective-permute-start(f32[8,32]{1,0:T(8,128)} %bitcast.7), channel_id=1, source_target_pairs={{0,1},{1,2},{2,3},{3,4},{4,5},{5,6},{6,7},{7,8},{8,9},{9,10},{10,1... | collective-permute-start | bytes 3080 | tf_op jit(solution)/shard_map/ppermute | solution.py:21
  7.8 39.7 %collective-permute-start.3 = (f32[8,32]{1,0:T(8,128)}, f32[8,32]{1,0:T(8,128)}, u32[]{:S(2)}, u32[]{:S(2)}) collective-permute-start(f32[8,32]{1,0:T(8,128)} %bitcast.9), channel_id=1, source_target_pairs={{1,0},{2,1},{3,2},{4,3},{5,4},{6,5},{7,6},{8,7},{9,8},{10,9},{11,1... | collective-permute-start | bytes 3080 | tf_op jit(solution)/shard_map/ppermute | solution.py:21
  19.5 29.4 %collective-permute-start = (f32[8,1,256]{2,1,0:T(1,128)}, f32[8,1,256]{2,1,0:T(1,128)S(1)}, u32[]{:S(2)}, u32[]{:S(2)}) collective-permute-start(f32[8,1,256]{2,1,0:T(1,128)} %get-tuple-element.25), channel_id=1, source_target_pairs={{0,128},{128,256},{256,384},{1,129},{129,257},{257,385},{2,130},{1... | collective-permute-start | bytes 24584 | tf_op jit(solution)/shard_map/ppermute | solution.py:21
  22.6 17.7 %copy-start = (f32[32,32,256]{2,1,0:T(8,128)S(1)}, f32[32,32,256]{2,1,0:T(8,128)}, u32[]{:S(2)}) copy-start(f32[32,32,256]{2,1,0:T(8,128)} %param.10) | copy-start | bytes 3145732
  22.6 26.3 %collective-permute-start.1 = (f32[8,1,256]{2,1,0:T(1,128)}, f32[8,1,256]{2,1,0:T(1,128)S(1)}, u32[]{:S(2)}, u32[]{:S(2)}) collective-permute-start(f32[8,1,256]{2,1,0:T(1,128)} %get-tuple-element.24), channel_id=1, source_target_pairs={{128,0},{256,128},{384,256},{129,1},{257,129},{385,257},{130,2},{2... | collective-permute-start | bytes 24584 | tf_op jit(solution)/shard_map/ppermute | solution.py:21
  28.2 34.1 %all-to-all-start = ((f32[128,1,1028]{2,1,0:T(1,128)}), f32[128,1,1028]{2,1,0:T(1,128)S(1)}, u32[]{:S(2)}, u32[]{:S(2)}) async-start(f32[128,1,1028]{2,1,0:T(1,128)} %copy.98), calls=%async_computation | async-start | bytes 1179648 | tf_op jit(solution)/shard_map/all_to_all | solution.py:148
  40.3 1.7 %copy-start.7 = (f32[32,2,1024]{2,1,0:T(2,128)S(1)}, f32[32,2,1024]{2,1,0:T(2,128)}, u32[]{:S(2)}) copy-start(f32[32,2,1024]{2,1,0:T(2,128)} %param.12) | copy-start | bytes 786436
  41.1 1.3 %copy-start.8 = (s32[32,256]{1,0:T(8,128)S(1)}, s32[32,256]{1,0:T(8,128)}, u32[]{:S(2)}) copy-start(s32[32,256]{1,0:T(8,128)} %param.13) | copy-start | bytes 98308
  41.1 1.3 %copy-start.9 = (s32[1,1,128,2]{2,3,1,0:T(2,128)S(1)}, s32[1,1,128,2]{2,3,1,0:T(2,128)}, u32[]{:S(2)}) copy-start(s32[1,1,128,2]{2,3,1,0:T(2,128)} %param.15) | copy-start | bytes 3076
  42.0 7.0 %copy-start.3 = (f32[32,256]{1,0:T(8,128)S(1)}, f32[32,256]{1,0:T(8,128)}, u32[]{:S(2)}) copy-start(f32[32,256]{1,0:T(8,128)} %param.11) | copy-start | bytes 98308
  42.5 12.5 %copy-start.5 = (f32[32,256]{1,0:T(8,128)}, f32[32,256]{1,0:T(8,128)S(1)}, u32[]{:S(2)}) copy-start(f32[32,256]{1,0:T(8,128)S(1)} %convert_element_type.4) | copy-start | bytes 98308
  43.2 7.2 %slice-start = ((f32[32,32,256]{2,1,0:T(8,128)}), f32[24,32,256]{2,1,0:T(8,128)S(1)}, s32[]{:S(2)}) async-start(f32[32,32,256]{2,1,0:T(8,128)} %param.10), calls=%async_computation.2 | async-start | bytes 1572864 | tf_op jit(solution)/shard_map/slice | solution.py:159
  68.3 9.9 %copy-start.2 = (s32[1,1,128,2]{3,2,1,0:T(8,128)S(1)}, s32[1,1,128,2]{3,2,1,0:T(8,128)}, u32[]{:S(2)}) copy-start(s32[1,1,128,2]{3,2,1,0:T(8,128)} %copy.96) | copy-start | bytes 3076
  75.6 12.5 %copy-start.1 = (f32[32,32,2,128]{3,2,1,0:T(2,128)S(1)}, f32[32,32,2,128]{3,2,1,0:T(2,128)}, u32[]{:S(2)}) copy-start(f32[32,32,2,128]{3,2,1,0:T(2,128)} %reshape.47) | copy-start | bytes 3145732
  78.8 21.4 %all-to-all-start.1 = ((f32[128,1,2]{2,1,0:T(1,128)}), f32[128,1,2]{2,1,0:T(1,128)S(1)}, u32[]{:S(2)}, u32[]{:S(2)}) async-start(f32[128,1,2]{2,1,0:T(1,128)} %bitcast.15), calls=%async_computation.1 | async-start | bytes 131072 | tf_op jit(solution)/shard_map/all_to_all | solution.py:169
  90.4 10.9 %copy-start.6 = (f32[32,256]{1,0:T(8,128)S(1)}, f32[32,256]{1,0:T(8,128)}, u32[]{:S(2)}) copy-start(f32[32,256]{1,0:T(8,128)} %copy-done.5) | copy-start | bytes 98308
  101.4 2.3 %copy-start.4 = (f32[32,256]{1,0:T(8,128)S(1)}, f32[32,256]{1,0:T(8,128)}, u32[]{:S(2)}) copy-start(f32[32,256]{1,0:T(8,128)} %param.11) | copy-start | bytes 98308
  104.1 19.7 %collective-permute-start.6 = (f32[8,32]{1,0:T(8,128)S(1)}, f32[8,32]{1,0:T(8,128)S(1)}, u32[]{:S(2)}, u32[]{:S(2)}) collective-permute-start(f32[8,32]{1,0:T(8,128)S(1)} %get-tuple-element.17), channel_id=1, source_target_pairs={{0,1},{1,2},{2,3},{3,4},{4,5},{5,6},{6,7},{7,8},{8,9},{9,10},{10,1... | collective-permute-start | bytes 3080 | tf_op jit(solution)/shard_map/ppermute | solution.py:21
  107.4 16.5 %collective-permute-start.7 = (f32[8,32]{1,0:T(8,128)S(1)}, f32[8,32]{1,0:T(8,128)S(1)}, u32[]{:S(2)}, u32[]{:S(2)}) collective-permute-start(f32[8,32]{1,0:T(8,128)S(1)} %get-tuple-element.16), channel_id=1, source_target_pairs={{1,0},{2,1},{3,2},{4,3},{5,4},{6,5},{7,6},{8,7},{9,8},{10,9},{11,1... | collective-permute-start | bytes 3080 | tf_op jit(solution)/shard_map/ppermute | solution.py:21
  113.9 10.2 %collective-permute-start.4 = (f32[8,1,256]{2,1,0:T(1,128)S(1)}, f32[8,1,256]{2,1,0:T(1,128)S(1)}, u32[]{:S(2)}, u32[]{:S(2)}) collective-permute-start(f32[8,1,256]{2,1,0:T(1,128)S(1)} %get-tuple-element.31), channel_id=1, source_target_pairs={{0,128},{128,256},{256,384},{1,129},{129,257},{257,385},{2,130},{1... | collective-permute-start | bytes 24584 | tf_op jit(solution)/shard_map/ppermute | solution.py:21
  120.0 5.0 %collective-permute-start.5 = (f32[8,1,256]{2,1,0:T(1,128)S(1)}, f32[8,1,256]{2,1,0:T(1,128)S(1)}, u32[]{:S(2)}, u32[]{:S(2)}) collective-permute-start(f32[8,1,256]{2,1,0:T(1,128)S(1)} %get-tuple-element.30), channel_id=1, source_target_pairs={{128,0},{256,128},{384,256},{129,1},{257,129},{385,257},{130,2},{2... | collective-permute-start | bytes 24584 | tf_op jit(solution)/shard_map/ppermute | solution.py:21

commit v11 on v10

--- a/solution.py
+++ b/solution.py
@@ -71,7 +71,7 @@
         part_ref[s] = parts[0] * win[0:FH] + parts[1] * win[FH:FW] + parts[2] * win[FW:span]
         return carry
 
-    lax.fori_loop(0, slots, predict, 0, unroll=8)
+    lax.fori_loop(0, slots, predict, 0, unroll=16)
 
 
 def scatter_kernel(anchor_ref, res_ref, gain_ref, bar_ref):
@@ -88,7 +88,7 @@
         bar_ref[pl.ds(c8, span), :] += res_ref[s] * jnp.concatenate(parts, axis=0)
         return carry
 
-    lax.fori_loop(0, slots, scatter, 0, unroll=8)
+    lax.fori_loop(0, slots, scatter, 0, unroll=16)
 
 
 def predict(anchor, top, gain):

time: 127 us -> 126 us (level)
  Pallas kernels: 14.3 us -> 12.7 us
  transfers between devices with their start and end apart: 10 -> 10, of which waited for: 3 -> 3; matrix products, arithmetic and copies ran while one was open for 22% -> 22% of each run, Pallas kernels for 6% -> 5%
where the time goes in v11:
time: 126 us; the launch traced here: 125 us
  starting transfers between devices  59.1 us (47%)
  local copies, waits for them, and re-layouts  28 us (22%)
  Pallas kernels  12.7 us (10%)
  waiting for transfers between devices  9.38 us (7%)
  matrix products  9.17 us (7%)
  other arithmetic  5.95 us (5%)
    ppermute x4, starting transfers between devices, neighbours(): lax.ppermute(edge_low, axis, backward)  21.5 us
    ppermute x4, starting transfers between devices, neighbours(): lax.ppermute(edge_high, axis, forward)  16.4 us
    all_to_all x1, starting transfers between devices, per_device(): lax.all_to_all(packed, 'lon', split_axis=0, concat_axis=0, tiled=True)  12 us
    all_to_all x1, starting transfers between devices, per_device(): lax.all_to_all(residual, 'lon', split_axis=0, concat_axis=0, tiled=True)  9.2 us
    dot_general x3, matrix products, columns(): out = jnp.einsum(form, matrices, grouped, precision=lax.Precision.HIGHEST)  6.92 us
    pallas_call x1, Pallas kernels, predict(): pl.pallas_call(predict_kernel, out_shape=jax.ShapeDtypeStruct((slots, FH,...  6.41 us
    all_to_all x1, waiting for transfers between devices, per_device(): lax.all_to_all(packed, 'lon', split_axis=0, concat_axis=0, tiled=True)  6.38 us
    pallas_call x1, Pallas kernels, scatter(): pl.pallas_call(scatter_kernel, out_shape=jax.ShapeDtypeStruct(top_shape,...  6.27 us
  transfers between devices with their start and end apart: 10, of which 3 were waited for; matrix products, arithmetic and copies ran while one was open for 22% of the time, Pallas kernels for 5%

profile of v11, /device:TPU:9, one launch (start us, length us, event | category | flops | bytes accessed | tf_op | source)
XLA Modules:
  0.0 125.4 jit_solution(9082654316180787815)
XLA Ops:
  0.6 1.1 fusion.18
  1.7 0.7 copy.125
  2.4 4.6 %collective-permute-start.2 = (f32[8,32]{1,0:T(8,128)}, f32[8,32]{1,0:T(8,128)}, u32[]{:S(2)}, u32[]{:S(2)}) collective-permute-start(f32[8,32]{1,0:T(8,128)} %bitcast.7), channel_id=1, source_target_pairs={{0,1},{1,2},{2,3},{3,4},{4,5},{5,6},{6,7},{7,8},{8,9},{9,10},{10,1... | collective-permute-start | bytes 3080 | tf_op jit(solution)/shard_map/ppermute | solution.py:21
  7.1 0.7 copy.126
  7.8 10.3 %collective-permute-start.3 = (f32[8,32]{1,0:T(8,128)}, f32[8,32]{1,0:T(8,128)}, u32[]{:S(2)}, u32[]{:S(2)}) collective-permute-start(f32[8,32]{1,0:T(8,128)} %bitcast.9), channel_id=1, source_target_pairs={{1,0},{2,1},{3,2},{4,3},{5,4},{6,5},{7,6},{8,7},{9,8},{10,9},{11,1... | collective-permute-start | bytes 3080 | tf_op jit(solution)/shard_map/ppermute | solution.py:21
  18.0 1.5 %fusion.20 = (f32[8,1,256]{2,1,0:T(1,128)}, f32[8,1,256]{2,1,0:T(1,128)}) fusion(f32[32,32,256]{2,1,0:T(8,128)} %param.10), kind=kLoop, calls=%fused_computation.34 | loop fusion | bytes 32768 | tf_op jit(solution)/shard_map/slice | solution.py:27
  19.5 3.0 %collective-permute-start = (f32[8,1,256]{2,1,0:T(1,128)}, f32[8,1,256]{2,1,0:T(1,128)S(1)}, u32[]{:S(2)}, u32[]{:S(2)}) collective-permute-start(f32[8,1,256]{2,1,0:T(1,128)} %get-tuple-element.25), channel_id=1, source_target_pairs={{0,128},{128,256},{256,384},{1,129},{129,257},{257,385},{2,130},{1... | collective-permute-start | bytes 24584 | tf_op jit(solution)/shard_map/ppermute | solution.py:21
  22.6 0.0 copy-start
  22.6 2.1 %collective-permute-start.1 = (f32[8,1,256]{2,1,0:T(1,128)}, f32[8,1,256]{2,1,0:T(1,128)S(1)}, u32[]{:S(2)}, u32[]{:S(2)}) collective-permute-start(f32[8,1,256]{2,1,0:T(1,128)} %get-tuple-element.24), channel_id=1, source_target_pairs={{128,0},{256,128},{384,256},{129,1},{257,129},{385,257},{130,2},{2... | collective-permute-start | bytes 24584 | tf_op jit(solution)/shard_map/ppermute | solution.py:21
  24.7 1.2 copy.97
  25.9 0.8 concatenate.33
  26.7 1.5 %copy.98 = f32[128,1,1028]{2,1,0:T(1,128)} copy(f32[128,1,1028]{0,2,1:T(8,128)S(1)} %bitcast.37) | data formatting | bytes 1052672 | tf_op jit(solution)/shard_map/all_to_all | solution.py:148
  28.2 12.0 %all-to-all-start = ((f32[128,1,1028]{2,1,0:T(1,128)}), f32[128,1,1028]{2,1,0:T(1,128)S(1)}, u32[]{:S(2)}, u32[]{:S(2)}) async-start(f32[128,1,1028]{2,1,0:T(1,128)} %copy.98), calls=%async_computation | async-start | bytes 1179648 | tf_op jit(solution)/shard_map/all_to_all | solution.py:148
  40.3 0.0 copy-start.7
  40.3 0.9 fusion.17
  41.2 0.8 fusion.19
  42.0 0.5 reshape.48
  42.5 0.7 copy.96
  43.2 2.8 %reshape.47 = f32[32,32,2,128]{3,2,1,0:T(2,128)} reshape(f32[32,32,256]{2,1,0:T(8,128)} %param.14) | data formatting | bytes 2097152 | tf_op jit(solution)/shard_map/reshape | solution.py:39
  46.0 1.5 %copy.102 = f32[8,32,1]{2,1,0:T(8,128)} copy(f32[8,32,1]{1,0,2:T(8,128)} %bitcast.8) | data formatting | bytes 2048 | tf_op jit(solution)/shard_map/broadcast_in_dim | solution.py:31
  47.5 1.4 %copy.104 = f32[8,32,1]{2,1,0:T(8,128)} copy(f32[8,32,1]{1,0,2:T(8,128)} %bitcast.10) | data formatting | bytes 2048 | tf_op jit(solution)/shard_map/broadcast_in_dim | solution.py:32
  48.9 1.5 %fusion.8 = f32[8,32,256]{2,1,0:T(8,128)S(1)} fusion(f32[8,31,256]{2,1,0:T(8,128)} %get-tuple-element.23, f32[8,1,256]{2,1,0:T(1,128)S(1)} %collective-permute-done, f32[8,1,256]{2,1,0:T(1,128)S(1)} %collective-permute-done.1, f32[8,31,256]{2,1,0:T(8,128)} %get-tuple-element.22, f32[8,32,255]{2,1,0:T(8,128)} %get-tuple-element.19, f32[8,32,1]{2,1,0:T(8,128)} %copy.102, ...), kind=kLoop, calls=%fused_computation.14 | loop fusion | flops 720896 | bytes 1605632 | tf_op jit(solution)/shard_map/add | solution.py:159
  50.4 0.1 pad_maximum_fusion
  50.5 1.5 %reshape.49 = f32[32,32,2,128]{3,2,1,0:T(2,128)} reshape(f32[32,32,256]{2,1,0:T(8,128)S(1)} %pad_maximum_fusion) | data formatting | bytes 2097152 | tf_op jit(solution)/shard_map/reshape | solution.py:39
  52.1 2.8 %convolution_bitcast_fusion = f32[4,32,2,128]{3,0,2,1:T(4,128)S(1)} fusion(f32[32,32,2,128]{3,2,1,0:T(2,128)} %reshape.49, f32[32,2,32,32]{3,2,1,0:T(8,128)S(1)} %reshape.48), kind=kOutput, calls=%fused_computation.2 | convolution fusion | flops 12582912 | bytes 1310720 | tf_op jit(solution)/shard_map/rbij,jrbc->irbc/dot_general | solution.py:41
  54.8 0.1 copy.106
  54.9 0.1 reshape.50
  55.1 0.1 copy.107
  55.2 0.7 copy.109.top_ref
  55.9 6.4 %all-to-all-done = f32[128,1,1028]{2,1,0:T(1,128)S(1)} async-done(((f32[128,1,1028]{2,1,0:T(1,128)}), f32[128,1,1028]{2,1,0:T(1,128)S(1)}, u32[]{:S(2)}, u32[]{:S(2)}) %all-to-all-start) | async-done | bytes 526368 | tf_op jit(solution)/shard_map/all_to_all | solution.py:148
  62.3 0.9 copy.99
  63.3 0.2 copy.108
  63.5 0.1 reshape.57
  63.6 2.2 %fusion.24 = f32[256,16,32]{0,2,1:T(8,128)S(1)} fusion(f32[256,512,1]{1,0,2:T(8,128)S(1)} %reshape.57, f32[16,32,512]{2,1,0:T(8,128)} %constant.16), kind=kOutput, calls=%fused_computation.38 | convolution fusion | flops 805306368 | bytes 2097152 | tf_op jit(solution)/shard_map/dot_general | solution.py:150
  65.8 2.5 %copy.110.gain_ref = f32[256,16,32]{2,1,0:T(8,128)} copy(f32[256,16,32]{0,2,1:T(8,128)S(1)} %fusion.24) | data formatting | bytes 1048576 | tf_op jit(solution)/shard_map/dot_general | solution.py:150
  68.3 6.4 %shard_map.113 = f32[256,8,128]{2,1,0:T(8,128)} custom-call(s32[128,2]{1,0:T(8,128)} %bitcast.40, f32[256,128]{1,0:T(8,128)} %copy.109.top_ref, f32[256,16,32]{2,1,0:T(8,128)} %copy.110.gain_ref), custom_call_target="tpu_custom_call" | custom-call | tf_op jit(solution)/shard_map/pallas_call | solution.py:98
  74.7 2.3 %reduce_sum.9 = f32[256]{0:T(256)S(1)} reduce(f32[256,8,128]{2,1,0:T(8,128)} %shard_map.113, f32[]{:T(128)} %constant.3.clone.1), dimensions={1,2}, to_apply=%region_0.0 | reduce | flops 261888 | bytes 1049604 | tf_op jit(solution)/shard_map/reduce_sum | solution.py:166
  77.0 0.1 reshape.53
  77.2 0.7 fusion.16
  77.9 9.2 %all-to-all-start.1 = ((f32[128,1,2]{2,1,0:T(1,128)}), f32[128,1,2]{2,1,0:T(1,128)S(1)}, u32[]{:S(2)}, u32[]{:S(2)}) async-start(f32[128,1,2]{2,1,0:T(1,128)} %bitcast.15), calls=%async_computation.1 | async-start | bytes 131072 | tf_op jit(solution)/shard_map/all_to_all | solution.py:169
  87.1 2.3 %fusion.2 = f32[32,2,128,32]{2,3,1,0:T(8,128)S(1)} fusion(f32[32,2,32,32]{3,2,1,0:T(8,128)S(1)} %reshape.48, f32[32,32,2,128]{3,2,1,0:T(2,128)S(1)} %copy-done.1), kind=kOutput, calls=%fused_computation.6 | convolution fusion | flops 100663296 | bytes 2359296 | tf_op jit(solution)/shard_map/rbji,jrbc->irbc/dot_general | solution.py:41
  89.5 1.5 %reshape.54.res_ref = f32[256]{0:T(256)} reshape(f32[128,2]{1,0:T(8,128)} %fusion.16) | data formatting | bytes 2048 | tf_op jit(solution)/shard_map/reshape | solution.py:170
  91.0 6.3 %shard_map.114 = f32[256,128]{1,0:T(8,128)} custom-call(s32[128,2]{1,0:T(8,128)} %bitcast.41, f32[256]{0:T(256)} %reshape.54.res_ref, f32[256,16,32]{2,1,0:T(8,128)} %copy.110.gain_ref), custom_call_target="tpu_custom_call" | custom-call | tf_op jit(solution)/shard_map/pallas_call | solution.py:109
  97.3 2.0 %all-to-all-done.1 = f32[128,1,2]{2,1,0:T(1,128)S(1)} async-done(((f32[128,1,2]{2,1,0:T(1,128)}), f32[128,1,2]{2,1,0:T(1,128)S(1)}, u32[]{:S(2)}, u32[]{:S(2)}) %all-to-all-start.1) | async-done | bytes 1056 | tf_op jit(solution)/shard_map/all_to_all | solution.py:169
  99.3 1.0 copy.114
  100.4 0.1 reshape.56
  100.5 1.8 %fusion = f32[32,32,2,128]{3,0,2,1:T(8,128)S(1)} fusion(f32[32,2,128,32]{2,3,1,0:T(8,128)S(1)} %fusion.2, f32[4,32,2,128]{3,2,1,0:T(2,128)S(1)} %reshape.56, f32[32,2,32,32]{3,2,1,0:T(8,128)S(1)} %reshape.48), kind=kOutput, calls=%fused_computation.1 | convolution fusion | flops 12845056 | bytes 2359296 | tf_op jit(solution)/shard_map/rbji,jrbc->irbc/dot_general | solution.py:41
  102.4 0.1 copy.118
  102.5 0.2 slice.104
  102.8 0.1 fusion.21
  102.9 0.2 slice_reduce_fusion
  103.2 2.6 %collective-permute-start.6 = (f32[8,32]{1,0:T(8,128)S(1)}, f32[8,32]{1,0:T(8,128)S(1)}, u32[]{:S(2)}, u32[]{:S(2)}) collective-permute-start(f32[8,32]{1,0:T(8,128)S(1)} %get-tuple-element.17), channel_id=1, source_target_pairs={{0,1},{1,2},{2,3},{3,4},{4,5},{5,6},{6,7},{7,8},{8,9},{9,10},{10,1... | collective-permute-start | bytes 3080 | tf_op jit(solution)/shard_map/ppermute | solution.py:21
  105.7 7.2 %collective-permute-start.7 = (f32[8,32]{1,0:T(8,128)S(1)}, f32[8,32]{1,0:T(8,128)S(1)}, u32[]{:S(2)}, u32[]{:S(2)}) collective-permute-start(f32[8,32]{1,0:T(8,128)S(1)} %get-tuple-element.16), channel_id=1, source_target_pairs={{1,0},{2,1},{3,2},{4,3},{5,4},{6,5},{7,6},{8,7},{9,8},{10,9},{11,1... | collective-permute-start | bytes 3080 | tf_op jit(solution)/shard_map/ppermute | solution.py:21
  113.0 6.1 %collective-permute-start.4 = (f32[8,1,256]{2,1,0:T(1,128)S(1)}, f32[8,1,256]{2,1,0:T(1,128)S(1)}, u32[]{:S(2)}, u32[]{:S(2)}) collective-permute-start(f32[8,1,256]{2,1,0:T(1,128)S(1)} %get-tuple-element.31), channel_id=1, source_target_pairs={{0,128},{128,256},{256,384},{1,129},{129,257},{257,385},{2,130},{1... | collective-permute-start | bytes 24584 | tf_op jit(solution)/shard_map/ppermute | solution.py:21
  119.1 1.9 %collective-permute-start.5 = (f32[8,1,256]{2,1,0:T(1,128)S(1)}, f32[8,1,256]{2,1,0:T(1,128)S(1)}, u32[]{:S(2)}, u32[]{:S(2)}) collective-permute-start(f32[8,1,256]{2,1,0:T(1,128)S(1)} %get-tuple-element.30), channel_id=1, source_target_pairs={{128,0},{256,128},{384,256},{129,1},{257,129},{385,257},{130,2},{2... | collective-permute-start | bytes 24584 | tf_op jit(solution)/shard_map/ppermute | solution.py:21
  121.1 0.1 slice.117
  121.2 0.4 copy.117
  121.6 0.6 slice.102
  122.2 0.6 copy.121
  122.9 0.1 copy.119
  123.0 0.1 copy.120
  123.1 1.0 collective-permute-done.5
  124.1 0.2 fusion.12
  124.3 1.0 pad_maximum_fusion.1
  (38 shorter events, 0.4 us)
Async XLA Ops:
  2.4 43.6 %collective-permute-start.2 = (f32[8,32]{1,0:T(8,128)}, f32[8,32]{1,0:T(8,128)}, u32[]{:S(2)}, u32[]{:S(2)}) collective-permute-start(f32[8,32]{1,0:T(8,128)} %bitcast.7), channel_id=1, source_target_pairs={{0,1},{1,2},{2,3},{3,4},{4,5},{5,6},{6,7},{7,8},{8,9},{9,10},{10,1... | collective-permute-start | bytes 3080 | tf_op jit(solution)/shard_map/ppermute | solution.py:21
  7.8 39.7 %collective-permute-start.3 = (f32[8,32]{1,0:T(8,128)}, f32[8,32]{1,0:T(8,128)}, u32[]{:S(2)}, u32[]{:S(2)}) collective-permute-start(f32[8,32]{1,0:T(8,128)} %bitcast.9), channel_id=1, source_target_pairs={{1,0},{2,1},{3,2},{4,3},{5,4},{6,5},{7,6},{8,7},{9,8},{10,9},{11,1... | collective-permute-start | bytes 3080 | tf_op jit(solution)/shard_map/ppermute | solution.py:21
  19.5 29.4 %collective-permute-start = (f32[8,1,256]{2,1,0:T(1,128)}, f32[8,1,256]{2,1,0:T(1,128)S(1)}, u32[]{:S(2)}, u32[]{:S(2)}) collective-permute-start(f32[8,1,256]{2,1,0:T(1,128)} %get-tuple-element.25), channel_id=1, source_target_pairs={{0,128},{128,256},{256,384},{1,129},{129,257},{257,385},{2,130},{1... | collective-permute-start | bytes 24584 | tf_op jit(solution)/shard_map/ppermute | solution.py:21
  22.6 17.7 %copy-start = (f32[32,32,256]{2,1,0:T(8,128)S(1)}, f32[32,32,256]{2,1,0:T(8,128)}, u32[]{:S(2)}) copy-start(f32[32,32,256]{2,1,0:T(8,128)} %param.10) | copy-start | bytes 3145732
  22.6 26.3 %collective-permute-start.1 = (f32[8,1,256]{2,1,0:T(1,128)}, f32[8,1,256]{2,1,0:T(1,128)S(1)}, u32[]{:S(2)}, u32[]{:S(2)}) collective-permute-start(f32[8,1,256]{2,1,0:T(1,128)} %get-tuple-element.24), channel_id=1, source_target_pairs={{128,0},{256,128},{384,256},{129,1},{257,129},{385,257},{130,2},{2... | collective-permute-start | bytes 24584 | tf_op jit(solution)/shard_map/ppermute | solution.py:21
  28.2 34.1 %all-to-all-start = ((f32[128,1,1028]{2,1,0:T(1,128)}), f32[128,1,1028]{2,1,0:T(1,128)S(1)}, u32[]{:S(2)}, u32[]{:S(2)}) async-start(f32[128,1,1028]{2,1,0:T(1,128)} %copy.98), calls=%async_computation | async-start | bytes 1179648 | tf_op jit(solution)/shard_map/all_to_all | solution.py:148
  40.3 1.7 %copy-start.7 = (f32[32,2,1024]{2,1,0:T(2,128)S(1)}, f32[32,2,1024]{2,1,0:T(2,128)}, u32[]{:S(2)}) copy-start(f32[32,2,1024]{2,1,0:T(2,128)} %param.12) | copy-start | bytes 786436
  41.1 1.3 %copy-start.8 = (s32[32,256]{1,0:T(8,128)S(1)}, s32[32,256]{1,0:T(8,128)}, u32[]{:S(2)}) copy-start(s32[32,256]{1,0:T(8,128)} %param.13) | copy-start | bytes 98308
  41.1 1.3 %copy-start.9 = (s32[1,1,128,2]{2,3,1,0:T(2,128)S(1)}, s32[1,1,128,2]{2,3,1,0:T(2,128)}, u32[]{:S(2)}) copy-start(s32[1,1,128,2]{2,3,1,0:T(2,128)} %param.15) | copy-start | bytes 3076
  42.0 7.0 %copy-start.3 = (f32[32,256]{1,0:T(8,128)S(1)}, f32[32,256]{1,0:T(8,128)}, u32[]{:S(2)}) copy-start(f32[32,256]{1,0:T(8,128)} %param.11) | copy-start | bytes 98308
  42.5 12.5 %copy-start.5 = (f32[32,256]{1,0:T(8,128)}, f32[32,256]{1,0:T(8,128)S(1)}, u32[]{:S(2)}) copy-start(f32[32,256]{1,0:T(8,128)S(1)} %convert_element_type.4) | copy-start | bytes 98308
  43.2 7.2 %slice-start = ((f32[32,32,256]{2,1,0:T(8,128)}), f32[24,32,256]{2,1,0:T(8,128)S(1)}, s32[]{:S(2)}) async-start(f32[32,32,256]{2,1,0:T(8,128)} %param.10), calls=%async_computation.2 | async-start | bytes 1572864 | tf_op jit(solution)/shard_map/slice | solution.py:159
  68.3 8.9 %copy-start.2 = (s32[1,1,128,2]{3,2,1,0:T(8,128)S(1)}, s32[1,1,128,2]{3,2,1,0:T(8,128)}, u32[]{:S(2)}) copy-start(s32[1,1,128,2]{3,2,1,0:T(8,128)} %copy.96) | copy-start | bytes 3076
  74.7 12.5 %copy-start.1 = (f32[32,32,2,128]{3,2,1,0:T(2,128)S(1)}, f32[32,32,2,128]{3,2,1,0:T(2,128)}, u32[]{:S(2)}) copy-start(f32[32,32,2,128]{3,2,1,0:T(2,128)} %reshape.47) | copy-start | bytes 3145732
  77.9 21.4 %all-to-all-start.1 = ((f32[128,1,2]{2,1,0:T(1,128)}), f32[128,1,2]{2,1,0:T(1,128)S(1)}, u32[]{:S(2)}, u32[]{:S(2)}) async-start(f32[128,1,2]{2,1,0:T(1,128)} %bitcast.15), calls=%async_computation.1 | async-start | bytes 131072 | tf_op jit(solution)/shard_map/all_to_all | solution.py:169
  89.5 10.9 %copy-start.6 = (f32[32,256]{1,0:T(8,128)S(1)}, f32[32,256]{1,0:T(8,128)}, u32[]{:S(2)}) copy-start(f32[32,256]{1,0:T(8,128)} %copy-done.5) | copy-start | bytes 98308
  100.5 2.3 %copy-start.4 = (f32[32,256]{1,0:T(8,128)S(1)}, f32[32,256]{1,0:T(8,128)}, u32[]{:S(2)}) copy-start(f32[32,256]{1,0:T(8,128)} %param.11) | copy-start | bytes 98308
  103.2 19.7 %collective-permute-start.6 = (f32[8,32]{1,0:T(8,128)S(1)}, f32[8,32]{1,0:T(8,128)S(1)}, u32[]{:S(2)}, u32[]{:S(2)}) collective-permute-start(f32[8,32]{1,0:T(8,128)S(1)} %get-tuple-element.17), channel_id=1, source_target_pairs={{0,1},{1,2},{2,3},{3,4},{4,5},{5,6},{6,7},{7,8},{8,9},{9,10},{10,1... | collective-permute-start | bytes 3080 | tf_op jit(solution)/shard_map/ppermute | solution.py:21
  105.7 17.3 %collective-permute-start.7 = (f32[8,32]{1,0:T(8,128)S(1)}, f32[8,32]{1,0:T(8,128)S(1)}, u32[]{:S(2)}, u32[]{:S(2)}) collective-permute-start(f32[8,32]{1,0:T(8,128)S(1)} %get-tuple-element.16), channel_id=1, source_target_pairs={{1,0},{2,1},{3,2},{4,3},{5,4},{6,5},{7,6},{8,7},{9,8},{10,9},{11,1... | collective-permute-start | bytes 3080 | tf_op jit(solution)/shard_map/ppermute | solution.py:21
  113.0 10.2 %collective-permute-start.4 = (f32[8,1,256]{2,1,0:T(1,128)S(1)}, f32[8,1,256]{2,1,0:T(1,128)S(1)}, u32[]{:S(2)}, u32[]{:S(2)}) collective-permute-start(f32[8,1,256]{2,1,0:T(1,128)S(1)} %get-tuple-element.31), channel_id=1, source_target_pairs={{0,128},{128,256},{256,384},{1,129},{129,257},{257,385},{2,130},{1... | collective-permute-start | bytes 24584 | tf_op jit(solution)/shard_map/ppermute | solution.py:21
  119.1 5.0 %collective-permute-start.5 = (f32[8,1,256]{2,1,0:T(1,128)S(1)}, f32[8,1,256]{2,1,0:T(1,128)S(1)}, u32[]{:S(2)}, u32[]{:S(2)}) collective-permute-start(f32[8,1,256]{2,1,0:T(1,128)S(1)} %get-tuple-element.30), channel_id=1, source_target_pairs={{128,0},{256,128},{384,256},{129,1},{257,129},{385,257},{130,2},{2... | collective-permute-start | bytes 24584 | tf_op jit(solution)/shard_map/ppermute | solution.py:21

commit v12 on v11

--- a/solution.py
+++ b/solution.py
@@ -71,7 +71,7 @@
         part_ref[s] = parts[0] * win[0:FH] + parts[1] * win[FH:FW] + parts[2] * win[FW:span]
         return carry
 
-    lax.fori_loop(0, slots, predict, 0, unroll=16)
+    lax.fori_loop(0, slots, predict, 0, unroll=32)
 
 
 def scatter_kernel(anchor_ref, res_ref, gain_ref, bar_ref):

time: 126 us -> 126 us (level)
  no operation moved by 1% of the time
where the time goes in v12:
time: 126 us; the launch traced here: 125 us
  starting transfers between devices  59.1 us (47%)
  local copies, waits for them, and re-layouts  28 us (22%)
  Pallas kernels  12.6 us (10%)
  waiting for transfers between devices  9.39 us (7%)
  matrix products  9.17 us (7%)
  other arithmetic  5.95 us (5%)
    ppermute x4, starting transfers between devices, neighbours(): lax.ppermute(edge_low, axis, backward)  21.5 us
    ppermute x4, starting transfers between devices, neighbours(): lax.ppermute(edge_high, axis, forward)  16.4 us
    all_to_all x1, starting transfers between devices, per_device(): lax.all_to_all(packed, 'lon', split_axis=0, concat_axis=0, tiled=True)  12 us
    all_to_all x1, starting transfers between devices, per_device(): lax.all_to_all(residual, 'lon', split_axis=0, concat_axis=0, tiled=True)  9.2 us
    dot_general x3, matrix products, columns(): out = jnp.einsum(form, matrices, grouped, precision=lax.Precision.HIGHEST)  6.92 us
    pallas_call x1, Pallas kernels, predict(): pl.pallas_call(predict_kernel, out_shape=jax.ShapeDtypeStruct((slots, FH,...  6.38 us
    all_to_all x1, waiting for transfers between devices, per_device(): lax.all_to_all(packed, 'lon', split_axis=0, concat_axis=0, tiled=True)  6.38 us
    pallas_call x1, Pallas kernels, scatter(): pl.pallas_call(scatter_kernel, out_shape=jax.ShapeDtypeStruct(top_shape,...  6.26 us
  transfers between devices with their start and end apart: 10, of which 3 were waited for; matrix products, arithmetic and copies ran while one was open for 22% of the time, Pallas kernels for 5%

profile of v12, /device:TPU:9, one launch (start us, length us, event | category | flops | bytes accessed | tf_op | source)
XLA Modules:
  0.0 125.3 jit_solution(17614718152772486117)
XLA Ops:
  0.6 1.1 fusion.18
  1.7 0.7 copy.125
  2.4 4.6 %collective-permute-start.2 = (f32[8,32]{1,0:T(8,128)}, f32[8,32]{1,0:T(8,128)}, u32[]{:S(2)}, u32[]{:S(2)}) collective-permute-start(f32[8,32]{1,0:T(8,128)} %bitcast.7), channel_id=1, source_target_pairs={{0,1},{1,2},{2,3},{3,4},{4,5},{5,6},{6,7},{7,8},{8,9},{9,10},{10,1... | collective-permute-start | bytes 3080 | tf_op jit(solution)/shard_map/ppermute | solution.py:21
  7.1 0.7 copy.126
  7.8 10.3 %collective-permute-start.3 = (f32[8,32]{1,0:T(8,128)}, f32[8,32]{1,0:T(8,128)}, u32[]{:S(2)}, u32[]{:S(2)}) collective-permute-start(f32[8,32]{1,0:T(8,128)} %bitcast.9), channel_id=1, source_target_pairs={{1,0},{2,1},{3,2},{4,3},{5,4},{6,5},{7,6},{8,7},{9,8},{10,9},{11,1... | collective-permute-start | bytes 3080 | tf_op jit(solution)/shard_map/ppermute | solution.py:21
  18.0 1.5 %fusion.20 = (f32[8,1,256]{2,1,0:T(1,128)}, f32[8,1,256]{2,1,0:T(1,128)}) fusion(f32[32,32,256]{2,1,0:T(8,128)} %param.10), kind=kLoop, calls=%fused_computation.34 | loop fusion | bytes 32768 | tf_op jit(solution)/shard_map/slice | solution.py:27
  19.5 3.0 %collective-permute-start = (f32[8,1,256]{2,1,0:T(1,128)}, f32[8,1,256]{2,1,0:T(1,128)S(1)}, u32[]{:S(2)}, u32[]{:S(2)}) collective-permute-start(f32[8,1,256]{2,1,0:T(1,128)} %get-tuple-element.25), channel_id=1, source_target_pairs={{0,128},{128,256},{256,384},{1,129},{129,257},{257,385},{2,130},{1... | collective-permute-start | bytes 24584 | tf_op jit(solution)/shard_map/ppermute | solution.py:21
  22.6 0.0 copy-start
  22.6 2.1 %collective-permute-start.1 = (f32[8,1,256]{2,1,0:T(1,128)}, f32[8,1,256]{2,1,0:T(1,128)S(1)}, u32[]{:S(2)}, u32[]{:S(2)}) collective-permute-start(f32[8,1,256]{2,1,0:T(1,128)} %get-tuple-element.24), channel_id=1, source_target_pairs={{128,0},{256,128},{384,256},{129,1},{257,129},{385,257},{130,2},{2... | collective-permute-start | bytes 24584 | tf_op jit(solution)/shard_map/ppermute | solution.py:21
  24.7 1.2 copy.97
  25.9 0.8 concatenate.33
  26.7 1.5 %copy.98 = f32[128,1,1028]{2,1,0:T(1,128)} copy(f32[128,1,1028]{0,2,1:T(8,128)S(1)} %bitcast.37) | data formatting | bytes 1052672 | tf_op jit(solution)/shard_map/all_to_all | solution.py:148
  28.2 12.0 %all-to-all-start = ((f32[128,1,1028]{2,1,0:T(1,128)}), f32[128,1,1028]{2,1,0:T(1,128)S(1)}, u32[]{:S(2)}, u32[]{:S(2)}) async-start(f32[128,1,1028]{2,1,0:T(1,128)} %copy.98), calls=%async_computation | async-start | bytes 1179648 | tf_op jit(solution)/shard_map/all_to_all | solution.py:148
  40.3 0.9 fusion.17
  41.2 0.8 fusion.19
  42.0 0.5 reshape.48
  42.5 0.7 copy.96
  43.2 2.8 %reshape.47 = f32[32,32,2,128]{3,2,1,0:T(2,128)} reshape(f32[32,32,256]{2,1,0:T(8,128)} %param.14) | data formatting | bytes 2097152 | tf_op jit(solution)/shard_map/reshape | solution.py:39
  46.0 1.5 %copy.102 = f32[8,32,1]{2,1,0:T(8,128)} copy(f32[8,32,1]{1,0,2:T(8,128)} %bitcast.8) | data formatting | bytes 2048 | tf_op jit(solution)/shard_map/broadcast_in_dim | solution.py:31
  47.5 1.4 %copy.104 = f32[8,32,1]{2,1,0:T(8,128)} copy(f32[8,32,1]{1,0,2:T(8,128)} %bitcast.10) | data formatting | bytes 2048 | tf_op jit(solution)/shard_map/broadcast_in_dim | solution.py:32
  48.9 1.5 %fusion.8 = f32[8,32,256]{2,1,0:T(8,128)S(1)} fusion(f32[8,31,256]{2,1,0:T(8,128)} %get-tuple-element.23, f32[8,1,256]{2,1,0:T(1,128)S(1)} %collective-permute-done, f32[8,1,256]{2,1,0:T(1,128)S(1)} %collective-permute-done.1, f32[8,31,256]{2,1,0:T(8,128)} %get-tuple-element.22, f32[8,32,255]{2,1,0:T(8,128)} %get-tuple-element.19, f32[8,32,1]{2,1,0:T(8,128)} %copy.102, ...), kind=kLoop, calls=%fused_computation.14 | loop fusion | flops 720896 | bytes 1605632 | tf_op jit(solution)/shard_map/add | solution.py:159
  50.4 0.1 pad_maximum_fusion
  50.5 1.5 %reshape.49 = f32[32,32,2,128]{3,2,1,0:T(2,128)} reshape(f32[32,32,256]{2,1,0:T(8,128)S(1)} %pad_maximum_fusion) | data formatting | bytes 2097152 | tf_op jit(solution)/shard_map/reshape | solution.py:39
  52.1 2.8 %convolution_bitcast_fusion = f32[4,32,2,128]{3,0,2,1:T(4,128)S(1)} fusion(f32[32,32,2,128]{3,2,1,0:T(2,128)} %reshape.49, f32[32,2,32,32]{3,2,1,0:T(8,128)S(1)} %reshape.48), kind=kOutput, calls=%fused_computation.2 | convolution fusion | flops 12582912 | bytes 1310720 | tf_op jit(solution)/shard_map/rbij,jrbc->irbc/dot_general | solution.py:41
  54.8 0.1 copy.106
  54.9 0.1 reshape.50
  55.1 0.1 copy.107
  55.2 0.7 copy.109.top_ref
  55.9 6.4 %all-to-all-done = f32[128,1,1028]{2,1,0:T(1,128)S(1)} async-done(((f32[128,1,1028]{2,1,0:T(1,128)}), f32[128,1,1028]{2,1,0:T(1,128)S(1)}, u32[]{:S(2)}, u32[]{:S(2)}) %all-to-all-start) | async-done | bytes 526368 | tf_op jit(solution)/shard_map/all_to_all | solution.py:148
  62.3 0.9 copy.99
  63.3 0.2 copy.108
  63.5 0.1 reshape.57
  63.6 2.2 %fusion.24 = f32[256,16,32]{0,2,1:T(8,128)S(1)} fusion(f32[256,512,1]{1,0,2:T(8,128)S(1)} %reshape.57, f32[16,32,512]{2,1,0:T(8,128)} %constant.16), kind=kOutput, calls=%fused_computation.38 | convolution fusion | flops 805306368 | bytes 2097152 | tf_op jit(solution)/shard_map/dot_general | solution.py:150
  65.8 2.5 %copy.110.gain_ref = f32[256,16,32]{2,1,0:T(8,128)} copy(f32[256,16,32]{0,2,1:T(8,128)S(1)} %fusion.24) | data formatting | bytes 1048576 | tf_op jit(solution)/shard_map/dot_general | solution.py:150
  68.3 6.4 %shard_map.113 = f32[256,8,128]{2,1,0:T(8,128)} custom-call(s32[128,2]{1,0:T(8,128)} %bitcast.40, f32[256,128]{1,0:T(8,128)} %copy.109.top_ref, f32[256,16,32]{2,1,0:T(8,128)} %copy.110.gain_ref), custom_call_target="tpu_custom_call" | custom-call | tf_op jit(solution)/shard_map/pallas_call | solution.py:98
  74.7 2.3 %reduce_sum.9 = f32[256]{0:T(256)S(1)} reduce(f32[256,8,128]{2,1,0:T(8,128)} %shard_map.113, f32[]{:T(128)} %constant.3.clone.1), dimensions={1,2}, to_apply=%region_0.0 | reduce | flops 261888 | bytes 1049604 | tf_op jit(solution)/shard_map/reduce_sum | solution.py:166
  77.0 0.1 reshape.53
  77.2 0.7 fusion.16
  77.9 9.2 %all-to-all-start.1 = ((f32[128,1,2]{2,1,0:T(1,128)}), f32[128,1,2]{2,1,0:T(1,128)S(1)}, u32[]{:S(2)}, u32[]{:S(2)}) async-start(f32[128,1,2]{2,1,0:T(1,128)} %bitcast.15), calls=%async_computation.1 | async-start | bytes 131072 | tf_op jit(solution)/shard_map/all_to_all | solution.py:169
  87.1 2.3 %fusion.2 = f32[32,2,128,32]{2,3,1,0:T(8,128)S(1)} fusion(f32[32,2,32,32]{3,2,1,0:T(8,128)S(1)} %reshape.48, f32[32,32,2,128]{3,2,1,0:T(2,128)S(1)} %copy-done.1), kind=kOutput, calls=%fused_computation.6 | convolution fusion | flops 100663296 | bytes 2359296 | tf_op jit(solution)/shard_map/rbji,jrbc->irbc/dot_general | solution.py:41
  89.4 1.5 %reshape.54.res_ref = f32[256]{0:T(256)} reshape(f32[128,2]{1,0:T(8,128)} %fusion.16) | data formatting | bytes 2048 | tf_op jit(solution)/shard_map/reshape | solution.py:170
  91.0 6.3 %shard_map.114 = f32[256,128]{1,0:T(8,128)} custom-call(s32[128,2]{1,0:T(8,128)} %bitcast.41, f32[256]{0:T(256)} %reshape.54.res_ref, f32[256,16,32]{2,1,0:T(8,128)} %copy.110.gain_ref), custom_call_target="tpu_custom_call" | custom-call | tf_op jit(solution)/shard_map/pallas_call | solution.py:109
  97.2 2.0 %all-to-all-done.1 = f32[128,1,2]{2,1,0:T(1,128)S(1)} async-done(((f32[128,1,2]{2,1,0:T(1,128)}), f32[128,1,2]{2,1,0:T(1,128)S(1)}, u32[]{:S(2)}, u32[]{:S(2)}) %all-to-all-start.1) | async-done | bytes 1056 | tf_op jit(solution)/shard_map/all_to_all | solution.py:169
  99.3 1.0 copy.114
  100.4 0.1 reshape.56
  100.5 0.0 copy-start.4
  100.5 1.8 %fusion = f32[32,32,2,128]{3,0,2,1:T(8,128)S(1)} fusion(f32[32,2,128,32]{2,3,1,0:T(8,128)S(1)} %fusion.2, f32[4,32,2,128]{3,2,1,0:T(2,128)S(1)} %reshape.56, f32[32,2,32,32]{3,2,1,0:T(8,128)S(1)} %reshape.48), kind=kOutput, calls=%fused_computation.1 | convolution fusion | flops 12845056 | bytes 2359296 | tf_op jit(solution)/shard_map/rbji,jrbc->irbc/dot_general | solution.py:41
  102.4 0.1 copy.118
  102.5 0.2 slice.104
  102.8 0.1 fusion.21
  102.9 0.2 slice_reduce_fusion
  103.1 2.6 %collective-permute-start.6 = (f32[8,32]{1,0:T(8,128)S(1)}, f32[8,32]{1,0:T(8,128)S(1)}, u32[]{:S(2)}, u32[]{:S(2)}) collective-permute-start(f32[8,32]{1,0:T(8,128)S(1)} %get-tuple-element.17), channel_id=1, source_target_pairs={{0,1},{1,2},{2,3},{3,4},{4,5},{5,6},{6,7},{7,8},{8,9},{9,10},{10,1... | collective-permute-start | bytes 3080 | tf_op jit(solution)/shard_map/ppermute | solution.py:21
  105.7 7.2 %collective-permute-start.7 = (f32[8,32]{1,0:T(8,128)S(1)}, f32[8,32]{1,0:T(8,128)S(1)}, u32[]{:S(2)}, u32[]{:S(2)}) collective-permute-start(f32[8,32]{1,0:T(8,128)S(1)} %get-tuple-element.16), channel_id=1, source_target_pairs={{1,0},{2,1},{3,2},{4,3},{5,4},{6,5},{7,6},{8,7},{9,8},{10,9},{11,1... | collective-permute-start | bytes 3080 | tf_op jit(solution)/shard_map/ppermute | solution.py:21
  113.0 6.1 %collective-permute-start.4 = (f32[8,1,256]{2,1,0:T(1,128)S(1)}, f32[8,1,256]{2,1,0:T(1,128)S(1)}, u32[]{:S(2)}, u32[]{:S(2)}) collective-permute-start(f32[8,1,256]{2,1,0:T(1,128)S(1)} %get-tuple-element.31), channel_id=1, source_target_pairs={{0,128},{128,256},{256,384},{1,129},{129,257},{257,385},{2,130},{1... | collective-permute-start | bytes 24584 | tf_op jit(solution)/shard_map/ppermute | solution.py:21
  119.1 1.9 %collective-permute-start.5 = (f32[8,1,256]{2,1,0:T(1,128)S(1)}, f32[8,1,256]{2,1,0:T(1,128)S(1)}, u32[]{:S(2)}, u32[]{:S(2)}) collective-permute-start(f32[8,1,256]{2,1,0:T(1,128)S(1)} %get-tuple-element.30), channel_id=1, source_target_pairs={{128,0},{256,128},{384,256},{129,1},{257,129},{385,257},{130,2},{2... | collective-permute-start | bytes 24584 | tf_op jit(solution)/shard_map/ppermute | solution.py:21
  121.1 0.1 slice.117
  121.2 0.4 copy.117
  121.6 0.6 slice.102
  122.2 0.6 copy.121
  122.9 0.1 copy.119
  123.0 0.1 copy.120
  123.1 1.0 collective-permute-done.5
  124.1 0.2 fusion.12
  124.3 1.0 pad_maximum_fusion.1
  (38 shorter events, 0.4 us)
Async XLA Ops:
  2.4 43.6 %collective-permute-start.2 = (f32[8,32]{1,0:T(8,128)}, f32[8,32]{1,0:T(8,128)}, u32[]{:S(2)}, u32[]{:S(2)}) collective-permute-start(f32[8,32]{1,0:T(8,128)} %bitcast.7), channel_id=1, source_target_pairs={{0,1},{1,2},{2,3},{3,4},{4,5},{5,6},{6,7},{7,8},{8,9},{9,10},{10,1... | collective-permute-start | bytes 3080 | tf_op jit(solution)/shard_map/ppermute | solution.py:21
  7.8 39.7 %collective-permute-start.3 = (f32[8,32]{1,0:T(8,128)}, f32[8,32]{1,0:T(8,128)}, u32[]{:S(2)}, u32[]{:S(2)}) collective-permute-start(f32[8,32]{1,0:T(8,128)} %bitcast.9), channel_id=1, source_target_pairs={{1,0},{2,1},{3,2},{4,3},{5,4},{6,5},{7,6},{8,7},{9,8},{10,9},{11,1... | collective-permute-start | bytes 3080 | tf_op jit(solution)/shard_map/ppermute | solution.py:21
  19.5 29.4 %collective-permute-start = (f32[8,1,256]{2,1,0:T(1,128)}, f32[8,1,256]{2,1,0:T(1,128)S(1)}, u32[]{:S(2)}, u32[]{:S(2)}) collective-permute-start(f32[8,1,256]{2,1,0:T(1,128)} %get-tuple-element.25), channel_id=1, source_target_pairs={{0,128},{128,256},{256,384},{1,129},{129,257},{257,385},{2,130},{1... | collective-permute-start | bytes 24584 | tf_op jit(solution)/shard_map/ppermute | solution.py:21
  22.6 17.7 %copy-start = (f32[32,32,256]{2,1,0:T(8,128)S(1)}, f32[32,32,256]{2,1,0:T(8,128)}, u32[]{:S(2)}) copy-start(f32[32,32,256]{2,1,0:T(8,128)} %param.10) | copy-start | bytes 3145732
  22.6 26.3 %collective-permute-start.1 = (f32[8,1,256]{2,1,0:T(1,128)}, f32[8,1,256]{2,1,0:T(1,128)S(1)}, u32[]{:S(2)}, u32[]{:S(2)}) collective-permute-start(f32[8,1,256]{2,1,0:T(1,128)} %get-tuple-element.24), channel_id=1, source_target_pairs={{128,0},{256,128},{384,256},{129,1},{257,129},{385,257},{130,2},{2... | collective-permute-start | bytes 24584 | tf_op jit(solution)/shard_map/ppermute | solution.py:21
  28.2 34.1 %all-to-all-start = ((f32[128,1,1028]{2,1,0:T(1,128)}), f32[128,1,1028]{2,1,0:T(1,128)S(1)}, u32[]{:S(2)}, u32[]{:S(2)}) async-start(f32[128,1,1028]{2,1,0:T(1,128)} %copy.98), calls=%async_computation | async-start | bytes 1179648 | tf_op jit(solution)/shard_map/all_to_all | solution.py:148
  40.3 1.7 %copy-start.7 = (f32[32,2,1024]{2,1,0:T(2,128)S(1)}, f32[32,2,1024]{2,1,0:T(2,128)}, u32[]{:S(2)}) copy-start(f32[32,2,1024]{2,1,0:T(2,128)} %param.12) | copy-start | bytes 786436
  41.1 1.3 %copy-start.8 = (s32[32,256]{1,0:T(8,128)S(1)}, s32[32,256]{1,0:T(8,128)}, u32[]{:S(2)}) copy-start(s32[32,256]{1,0:T(8,128)} %param.13) | copy-start | bytes 98308
  41.1 1.3 %copy-start.9 = (s32[1,1,128,2]{2,3,1,0:T(2,128)S(1)}, s32[1,1,128,2]{2,3,1,0:T(2,128)}, u32[]{:S(2)}) copy-start(s32[1,1,128,2]{2,3,1,0:T(2,128)} %param.15) | copy-start | bytes 3076
  42.0 7.0 %copy-start.3 = (f32[32,256]{1,0:T(8,128)S(1)}, f32[32,256]{1,0:T(8,128)}, u32[]{:S(2)}) copy-start(f32[32,256]{1,0:T(8,128)} %param.11) | copy-start | bytes 98308
  42.5 12.5 %copy-start.5 = (f32[32,256]{1,0:T(8,128)}, f32[32,256]{1,0:T(8,128)S(1)}, u32[]{:S(2)}) copy-start(f32[32,256]{1,0:T(8,128)S(1)} %convert_element_type.4) | copy-start | bytes 98308
  43.2 7.2 %slice-start = ((f32[32,32,256]{2,1,0:T(8,128)}), f32[24,32,256]{2,1,0:T(8,128)S(1)}, s32[]{:S(2)}) async-start(f32[32,32,256]{2,1,0:T(8,128)} %param.10), calls=%async_computation.2 | async-start | bytes 1572864 | tf_op jit(solution)/shard_map/slice | solution.py:159
  68.3 8.9 %copy-start.2 = (s32[1,1,128,2]{3,2,1,0:T(8,128)S(1)}, s32[1,1,128,2]{3,2,1,0:T(8,128)}, u32[]{:S(2)}) copy-start(s32[1,1,128,2]{3,2,1,0:T(8,128)} %copy.96) | copy-start | bytes 3076
  74.7 12.5 %copy-start.1 = (f32[32,32,2,128]{3,2,1,0:T(2,128)S(1)}, f32[32,32,2,128]{3,2,1,0:T(2,128)}, u32[]{:S(2)}) copy-start(f32[32,32,2,128]{3,2,1,0:T(2,128)} %reshape.47) | copy-start | bytes 3145732
  77.9 21.4 %all-to-all-start.1 = ((f32[128,1,2]{2,1,0:T(1,128)}), f32[128,1,2]{2,1,0:T(1,128)S(1)}, u32[]{:S(2)}, u32[]{:S(2)}) async-start(f32[128,1,2]{2,1,0:T(1,128)} %bitcast.15), calls=%async_computation.1 | async-start | bytes 131072 | tf_op jit(solution)/shard_map/all_to_all | solution.py:169
  89.4 10.9 %copy-start.6 = (f32[32,256]{1,0:T(8,128)S(1)}, f32[32,256]{1,0:T(8,128)}, u32[]{:S(2)}) copy-start(f32[32,256]{1,0:T(8,128)} %copy-done.5) | copy-start | bytes 98308
  100.5 2.3 %copy-start.4 = (f32[32,256]{1,0:T(8,128)S(1)}, f32[32,256]{1,0:T(8,128)}, u32[]{:S(2)}) copy-start(f32[32,256]{1,0:T(8,128)} %param.11) | copy-start | bytes 98308
  103.1 19.7 %collective-permute-start.6 = (f32[8,32]{1,0:T(8,128)S(1)}, f32[8,32]{1,0:T(8,128)S(1)}, u32[]{:S(2)}, u32[]{:S(2)}) collective-permute-start(f32[8,32]{1,0:T(8,128)S(1)} %get-tuple-element.17), channel_id=1, source_target_pairs={{0,1},{1,2},{2,3},{3,4},{4,5},{5,6},{6,7},{7,8},{8,9},{9,10},{10,1... | collective-permute-start | bytes 3080 | tf_op jit(solution)/shard_map/ppermute | solution.py:21
  105.7 17.3 %collective-permute-start.7 = (f32[8,32]{1,0:T(8,128)S(1)}, f32[8,32]{1,0:T(8,128)S(1)}, u32[]{:S(2)}, u32[]{:S(2)}) collective-permute-start(f32[8,32]{1,0:T(8,128)S(1)} %get-tuple-element.16), channel_id=1, source_target_pairs={{1,0},{2,1},{3,2},{4,3},{5,4},{6,5},{7,6},{8,7},{9,8},{10,9},{11,1... | collective-permute-start | bytes 3080 | tf_op jit(solution)/shard_map/ppermute | solution.py:21
  113.0 10.2 %collective-permute-start.4 = (f32[8,1,256]{2,1,0:T(1,128)S(1)}, f32[8,1,256]{2,1,0:T(1,128)S(1)}, u32[]{:S(2)}, u32[]{:S(2)}) collective-permute-start(f32[8,1,256]{2,1,0:T(1,128)S(1)} %get-tuple-element.31), channel_id=1, source_target_pairs={{0,128},{128,256},{256,384},{1,129},{129,257},{257,385},{2,130},{1... | collective-permute-start | bytes 24584 | tf_op jit(solution)/shard_map/ppermute | solution.py:21
  119.1 5.0 %collective-permute-start.5 = (f32[8,1,256]{2,1,0:T(1,128)S(1)}, f32[8,1,256]{2,1,0:T(1,128)S(1)}, u32[]{:S(2)}, u32[]{:S(2)}) collective-permute-start(f32[8,1,256]{2,1,0:T(1,128)S(1)} %get-tuple-element.30), channel_id=1, source_target_pairs={{128,0},{256,128},{384,256},{129,1},{257,129},{385,257},{130,2},{2... | collective-permute-start | bytes 24584 | tf_op jit(solution)/shard_map/ppermute | solution.py:21

commit v13 on v11

--- a/solution.py
+++ b/solution.py
@@ -68,7 +68,8 @@
     def predict(s, carry):
         c8, parts = window_gain(anchor_ref, gain_ref, s, tile_cols, tile_rows, sub, pad)
         win = top_ref[pl.ds(c8, span), :]
-        part_ref[s] = parts[0] * win[0:FH] + parts[1] * win[FH:FW] + parts[2] * win[FW:span]
+        acc = parts[0] * win[0:FH] + parts[1] * win[FH:FW] + parts[2] * win[FW:span]
+        part_ref[s] = jnp.sum(acc, axis=0, keepdims=True)
         return carry
 
     lax.fori_loop(0, slots, predict, 0, unroll=16)
@@ -97,7 +98,7 @@
     vmem = pl.BlockSpec(memory_space=pltpu.VMEM)
     return pl.pallas_call(
         predict_kernel,
-        out_shape=jax.ShapeDtypeStruct((slots, FH, top.shape[1]), jnp.float32),
+        out_shape=jax.ShapeDtypeStruct((slots, 1, top.shape[1]), jnp.float32),
         in_specs=[smem, vmem, vmem],
         out_specs=vmem,
     )(anchor, top, gain)

time: 126 us -> 126 us (level)
  no operation moved by 1% of the time
where the time goes in v13:
time: 126 us; the launch traced here: 125 us
  starting transfers between devices  59.1 us (47%)
  local copies, waits for them, and re-layouts  28 us (22%)
  Pallas kernels  12.4 us (10%)
  waiting for transfers between devices  9.38 us (7%)
  matrix products  9.17 us (7%)
  other arithmetic  5.54 us (4%)
    ppermute x4, starting transfers between devices, neighbours(): lax.ppermute(edge_low, axis, backward)  21.5 us
    ppermute x4, starting transfers between devices, neighbours(): lax.ppermute(edge_high, axis, forward)  16.4 us
    all_to_all x1, starting transfers between devices, per_device(): lax.all_to_all(packed, 'lon', split_axis=0, concat_axis=0, tiled=True)  12 us
    all_to_all x1, starting transfers between devices, per_device(): lax.all_to_all(residual, 'lon', split_axis=0, concat_axis=0, tiled=True)  9.21 us
    dot_general x3, matrix products, columns(): out = jnp.einsum(form, matrices, grouped, precision=lax.Precision.HIGHEST)  6.92 us
    all_to_all x1, waiting for transfers between devices, per_device(): lax.all_to_all(packed, 'lon', split_axis=0, concat_axis=0, tiled=True)  6.37 us
    pallas_call x1, Pallas kernels, scatter(): pl.pallas_call(scatter_kernel, out_shape=jax.ShapeDtypeStruct(top_shape,...  6.27 us
    pallas_call x1, Pallas kernels, predict(): pl.pallas_call(predict_kernel, out_shape=jax.ShapeDtypeStruct((slots, 1,...  6.14 us
  transfers between devices with their start and end apart: 10, of which 3 were waited for; matrix products, arithmetic and copies ran while one was open for 22% of the time, Pallas kernels for 5%

profile of v13, /device:TPU:9, one launch (start us, length us, event | category | flops | bytes accessed | tf_op | source)
XLA Modules:
  0.0 124.7 jit_solution(13569488138810082087)
XLA Ops:
  0.6 1.1 fusion.18
  1.7 0.7 copy.125
  2.4 4.6 %collective-permute-start.2 = (f32[8,32]{1,0:T(8,128)}, f32[8,32]{1,0:T(8,128)}, u32[]{:S(2)}, u32[]{:S(2)}) collective-permute-start(f32[8,32]{1,0:T(8,128)} %bitcast.7), channel_id=1, source_target_pairs={{0,1},{1,2},{2,3},{3,4},{4,5},{5,6},{6,7},{7,8},{8,9},{9,10},{10,1... | collective-permute-start | bytes 3080 | tf_op jit(solution)/shard_map/ppermute | solution.py:21
  7.1 0.7 copy.126
  7.8 10.3 %collective-permute-start.3 = (f32[8,32]{1,0:T(8,128)}, f32[8,32]{1,0:T(8,128)}, u32[]{:S(2)}, u32[]{:S(2)}) collective-permute-start(f32[8,32]{1,0:T(8,128)} %bitcast.9), channel_id=1, source_target_pairs={{1,0},{2,1},{3,2},{4,3},{5,4},{6,5},{7,6},{8,7},{9,8},{10,9},{11,1... | collective-permute-start | bytes 3080 | tf_op jit(solution)/shard_map/ppermute | solution.py:21
  18.0 1.5 %fusion.20 = (f32[8,1,256]{2,1,0:T(1,128)}, f32[8,1,256]{2,1,0:T(1,128)}) fusion(f32[32,32,256]{2,1,0:T(8,128)} %param.10), kind=kLoop, calls=%fused_computation.34 | loop fusion | bytes 32768 | tf_op jit(solution)/shard_map/slice | solution.py:27
  19.5 3.0 %collective-permute-start = (f32[8,1,256]{2,1,0:T(1,128)}, f32[8,1,256]{2,1,0:T(1,128)S(1)}, u32[]{:S(2)}, u32[]{:S(2)}) collective-permute-start(f32[8,1,256]{2,1,0:T(1,128)} %get-tuple-element.25), channel_id=1, source_target_pairs={{0,128},{128,256},{256,384},{1,129},{129,257},{257,385},{2,130},{1... | collective-permute-start | bytes 24584 | tf_op jit(solution)/shard_map/ppermute | solution.py:21
  22.6 0.0 copy-start
  22.6 2.1 %collective-permute-start.1 = (f32[8,1,256]{2,1,0:T(1,128)}, f32[8,1,256]{2,1,0:T(1,128)S(1)}, u32[]{:S(2)}, u32[]{:S(2)}) collective-permute-start(f32[8,1,256]{2,1,0:T(1,128)} %get-tuple-element.24), channel_id=1, source_target_pairs={{128,0},{256,128},{384,256},{129,1},{257,129},{385,257},{130,2},{2... | collective-permute-start | bytes 24584 | tf_op jit(solution)/shard_map/ppermute | solution.py:21
  24.7 1.2 copy.97
  25.9 0.8 concatenate.33
  26.7 1.5 %copy.98 = f32[128,1,1028]{2,1,0:T(1,128)} copy(f32[128,1,1028]{0,2,1:T(8,128)S(1)} %bitcast.37) | data formatting | bytes 1052672 | tf_op jit(solution)/shard_map/all_to_all | solution.py:149
  28.2 12.0 %all-to-all-start = ((f32[128,1,1028]{2,1,0:T(1,128)}), f32[128,1,1028]{2,1,0:T(1,128)S(1)}, u32[]{:S(2)}, u32[]{:S(2)}) async-start(f32[128,1,1028]{2,1,0:T(1,128)} %copy.98), calls=%async_computation | async-start | bytes 1179648 | tf_op jit(solution)/shard_map/all_to_all | solution.py:149
  40.3 0.0 copy-start.7
  40.3 0.9 fusion.17
  41.2 0.8 fusion.19
  42.0 0.5 reshape.48
  42.5 0.7 copy.96
  43.2 2.8 %reshape.47 = f32[32,32,2,128]{3,2,1,0:T(2,128)} reshape(f32[32,32,256]{2,1,0:T(8,128)} %param.14) | data formatting | bytes 2097152 | tf_op jit(solution)/shard_map/reshape | solution.py:39
  46.0 1.5 %copy.102 = f32[8,32,1]{2,1,0:T(8,128)} copy(f32[8,32,1]{1,0,2:T(8,128)} %bitcast.8) | data formatting | bytes 2048 | tf_op jit(solution)/shard_map/broadcast_in_dim | solution.py:31
  47.5 1.4 %copy.104 = f32[8,32,1]{2,1,0:T(8,128)} copy(f32[8,32,1]{1,0,2:T(8,128)} %bitcast.10) | data formatting | bytes 2048 | tf_op jit(solution)/shard_map/broadcast_in_dim | solution.py:32
  48.9 1.5 %fusion.8 = f32[8,32,256]{2,1,0:T(8,128)S(1)} fusion(f32[8,31,256]{2,1,0:T(8,128)} %get-tuple-element.23, f32[8,1,256]{2,1,0:T(1,128)S(1)} %collective-permute-done, f32[8,1,256]{2,1,0:T(1,128)S(1)} %collective-permute-done.1, f32[8,31,256]{2,1,0:T(8,128)} %get-tuple-element.22, f32[8,32,255]{2,1,0:T(8,128)} %get-tuple-element.19, f32[8,32,1]{2,1,0:T(8,128)} %copy.102, ...), kind=kLoop, calls=%fused_computation.14 | loop fusion | flops 720896 | bytes 1605632 | tf_op jit(solution)/shard_map/add | solution.py:160
  50.4 0.1 pad_maximum_fusion
  50.5 1.5 %reshape.49 = f32[32,32,2,128]{3,2,1,0:T(2,128)} reshape(f32[32,32,256]{2,1,0:T(8,128)S(1)} %pad_maximum_fusion) | data formatting | bytes 2097152 | tf_op jit(solution)/shard_map/reshape | solution.py:39
  52.1 2.8 %convolution_bitcast_fusion = f32[4,32,2,128]{3,0,2,1:T(4,128)S(1)} fusion(f32[32,32,2,128]{3,2,1,0:T(2,128)} %reshape.49, f32[32,2,32,32]{3,2,1,0:T(8,128)S(1)} %reshape.48), kind=kOutput, calls=%fused_computation.2 | convolution fusion | flops 12582912 | bytes 1310720 | tf_op jit(solution)/shard_map/rbij,jrbc->irbc/dot_general | solution.py:41
  54.8 0.1 copy.106
  54.9 0.1 reshape.50
  55.0 0.1 copy.107
  55.2 0.8 copy.109.top_ref
  56.0 6.4 %all-to-all-done = f32[128,1,1028]{2,1,0:T(1,128)S(1)} async-done(((f32[128,1,1028]{2,1,0:T(1,128)}), f32[128,1,1028]{2,1,0:T(1,128)S(1)}, u32[]{:S(2)}, u32[]{:S(2)}) %all-to-all-start) | async-done | bytes 526368 | tf_op jit(solution)/shard_map/all_to_all | solution.py:149
  62.3 0.9 copy.99
  63.3 0.2 copy.108
  63.5 0.1 reshape.57
  63.6 2.2 %fusion.24 = f32[256,16,32]{0,2,1:T(8,128)S(1)} fusion(f32[256,512,1]{1,0,2:T(8,128)S(1)} %reshape.57, f32[16,32,512]{2,1,0:T(8,128)} %constant.16), kind=kOutput, calls=%fused_computation.38 | convolution fusion | flops 805306368 | bytes 2097152 | tf_op jit(solution)/shard_map/dot_general | solution.py:151
  65.8 2.5 %copy.110.gain_ref = f32[256,16,32]{2,1,0:T(8,128)} copy(f32[256,16,32]{0,2,1:T(8,128)S(1)} %fusion.24) | data formatting | bytes 1048576 | tf_op jit(solution)/shard_map/dot_general | solution.py:151
  68.3 6.1 %shard_map.113 = f32[256,1,128]{2,1,0:T(1,128)} custom-call(s32[128,2]{1,0:T(8,128)} %bitcast.40, f32[256,128]{1,0:T(8,128)} %copy.109.top_ref, f32[256,16,32]{2,1,0:T(8,128)} %copy.110.gain_ref), custom_call_target="tpu_custom_call" | custom-call | tf_op jit(solution)/shard_map/pallas_call | solution.py:99
  74.4 1.9 %reduce_sum.9 = f32[256]{0:T(256)S(1)} reduce(f32[256,1,128]{2,1,0:T(1,128)} %shard_map.113, f32[]{:T(128)} %constant.3.clone.1), dimensions={1,2}, to_apply=%region_0.0 | reduce | flops 32512 | bytes 132100 | tf_op jit(solution)/shard_map/reduce_sum | solution.py:167
  76.4 0.1 reshape.53
  76.6 0.7 fusion.16
  77.3 9.2 %all-to-all-start.1 = ((f32[128,1,2]{2,1,0:T(1,128)}), f32[128,1,2]{2,1,0:T(1,128)S(1)}, u32[]{:S(2)}, u32[]{:S(2)}) async-start(f32[128,1,2]{2,1,0:T(1,128)} %bitcast.15), calls=%async_computation.1 | async-start | bytes 131072 | tf_op jit(solution)/shard_map/all_to_all | solution.py:170
  86.5 2.3 %fusion.2 = f32[32,2,128,32]{2,3,1,0:T(8,128)S(1)} fusion(f32[32,2,32,32]{3,2,1,0:T(8,128)S(1)} %reshape.48, f32[32,32,2,128]{3,2,1,0:T(2,128)S(1)} %copy-done.1), kind=kOutput, calls=%fused_computation.6 | convolution fusion | flops 100663296 | bytes 2359296 | tf_op jit(solution)/shard_map/rbji,jrbc->irbc/dot_general | solution.py:41
  88.8 1.5 %reshape.54.res_ref = f32[256]{0:T(256)} reshape(f32[128,2]{1,0:T(8,128)} %fusion.16) | data formatting | bytes 2048 | tf_op jit(solution)/shard_map/reshape | solution.py:171
  90.3 6.3 %shard_map.114 = f32[256,128]{1,0:T(8,128)} custom-call(s32[128,2]{1,0:T(8,128)} %bitcast.41, f32[256]{0:T(256)} %reshape.54.res_ref, f32[256,16,32]{2,1,0:T(8,128)} %copy.110.gain_ref), custom_call_target="tpu_custom_call" | custom-call | tf_op jit(solution)/shard_map/pallas_call | solution.py:110
  96.6 2.0 %all-to-all-done.1 = f32[128,1,2]{2,1,0:T(1,128)S(1)} async-done(((f32[128,1,2]{2,1,0:T(1,128)}), f32[128,1,2]{2,1,0:T(1,128)S(1)}, u32[]{:S(2)}, u32[]{:S(2)}) %all-to-all-start.1) | async-done | bytes 1056 | tf_op jit(solution)/shard_map/all_to_all | solution.py:170
  98.7 1.0 copy.114
  99.8 0.1 reshape.56
  99.8 1.8 %fusion = f32[32,32,2,128]{3,0,2,1:T(8,128)S(1)} fusion(f32[32,2,128,32]{2,3,1,0:T(8,128)S(1)} %fusion.2, f32[4,32,2,128]{3,2,1,0:T(2,128)S(1)} %reshape.56, f32[32,2,32,32]{3,2,1,0:T(8,128)S(1)} %reshape.48), kind=kOutput, calls=%fused_computation.1 | convolution fusion | flops 12845056 | bytes 2359296 | tf_op jit(solution)/shard_map/rbji,jrbc->irbc/dot_general | solution.py:41
  101.7 0.1 copy.118
  101.9 0.2 slice.104
  102.1 0.1 fusion.21
  102.3 0.2 slice_reduce_fusion
  102.5 2.6 %collective-permute-start.6 = (f32[8,32]{1,0:T(8,128)S(1)}, f32[8,32]{1,0:T(8,128)S(1)}, u32[]{:S(2)}, u32[]{:S(2)}) collective-permute-start(f32[8,32]{1,0:T(8,128)S(1)} %get-tuple-element.17), channel_id=1, source_target_pairs={{0,1},{1,2},{2,3},{3,4},{4,5},{5,6},{6,7},{7,8},{8,9},{9,10},{10,1... | collective-permute-start | bytes 3080 | tf_op jit(solution)/shard_map/ppermute | solution.py:21
  105.1 7.2 %collective-permute-start.7 = (f32[8,32]{1,0:T(8,128)S(1)}, f32[8,32]{1,0:T(8,128)S(1)}, u32[]{:S(2)}, u32[]{:S(2)}) collective-permute-start(f32[8,32]{1,0:T(8,128)S(1)} %get-tuple-element.16), channel_id=1, source_target_pairs={{1,0},{2,1},{3,2},{4,3},{5,4},{6,5},{7,6},{8,7},{9,8},{10,9},{11,1... | collective-permute-start | bytes 3080 | tf_op jit(solution)/shard_map/ppermute | solution.py:21
  112.3 6.1 %collective-permute-start.4 = (f32[8,1,256]{2,1,0:T(1,128)S(1)}, f32[8,1,256]{2,1,0:T(1,128)S(1)}, u32[]{:S(2)}, u32[]{:S(2)}) collective-permute-start(f32[8,1,256]{2,1,0:T(1,128)S(1)} %get-tuple-element.31), channel_id=1, source_target_pairs={{0,128},{128,256},{256,384},{1,129},{129,257},{257,385},{2,130},{1... | collective-permute-start | bytes 24584 | tf_op jit(solution)/shard_map/ppermute | solution.py:21
  118.5 1.9 %collective-permute-start.5 = (f32[8,1,256]{2,1,0:T(1,128)S(1)}, f32[8,1,256]{2,1,0:T(1,128)S(1)}, u32[]{:S(2)}, u32[]{:S(2)}) collective-permute-start(f32[8,1,256]{2,1,0:T(1,128)S(1)} %get-tuple-element.30), channel_id=1, source_target_pairs={{128,0},{256,128},{384,256},{129,1},{257,129},{385,257},{130,2},{2... | collective-permute-start | bytes 24584 | tf_op jit(solution)/shard_map/ppermute | solution.py:21
  120.4 0.1 slice.117
  120.5 0.4 copy.117
  120.9 0.6 slice.102
  121.6 0.6 copy.121
  122.2 0.1 copy.119
  122.4 0.1 copy.120
  122.5 1.0 collective-permute-done.5
  123.4 0.2 fusion.12
  123.7 1.0 pad_maximum_fusion.1
  (38 shorter events, 0.4 us)
Async XLA Ops:
  2.4 43.6 %collective-permute-start.2 = (f32[8,32]{1,0:T(8,128)}, f32[8,32]{1,0:T(8,128)}, u32[]{:S(2)}, u32[]{:S(2)}) collective-permute-start(f32[8,32]{1,0:T(8,128)} %bitcast.7), channel_id=1, source_target_pairs={{0,1},{1,2},{2,3},{3,4},{4,5},{5,6},{6,7},{7,8},{8,9},{9,10},{10,1... | collective-permute-start | bytes 3080 | tf_op jit(solution)/shard_map/ppermute | solution.py:21
  7.8 39.7 %collective-permute-start.3 = (f32[8,32]{1,0:T(8,128)}, f32[8,32]{1,0:T(8,128)}, u32[]{:S(2)}, u32[]{:S(2)}) collective-permute-start(f32[8,32]{1,0:T(8,128)} %bitcast.9), channel_id=1, source_target_pairs={{1,0},{2,1},{3,2},{4,3},{5,4},{6,5},{7,6},{8,7},{9,8},{10,9},{11,1... | collective-permute-start | bytes 3080 | tf_op jit(solution)/shard_map/ppermute | solution.py:21
  19.5 29.4 %collective-permute-start = (f32[8,1,256]{2,1,0:T(1,128)}, f32[8,1,256]{2,1,0:T(1,128)S(1)}, u32[]{:S(2)}, u32[]{:S(2)}) collective-permute-start(f32[8,1,256]{2,1,0:T(1,128)} %get-tuple-element.25), channel_id=1, source_target_pairs={{0,128},{128,256},{256,384},{1,129},{129,257},{257,385},{2,130},{1... | collective-permute-start | bytes 24584 | tf_op jit(solution)/shard_map/ppermute | solution.py:21
  22.6 17.7 %copy-start = (f32[32,32,256]{2,1,0:T(8,128)S(1)}, f32[32,32,256]{2,1,0:T(8,128)}, u32[]{:S(2)}) copy-start(f32[32,32,256]{2,1,0:T(8,128)} %param.10) | copy-start | bytes 3145732
  22.6 26.3 %collective-permute-start.1 = (f32[8,1,256]{2,1,0:T(1,128)}, f32[8,1,256]{2,1,0:T(1,128)S(1)}, u32[]{:S(2)}, u32[]{:S(2)}) collective-permute-start(f32[8,1,256]{2,1,0:T(1,128)} %get-tuple-element.24), channel_id=1, source_target_pairs={{128,0},{256,128},{384,256},{129,1},{257,129},{385,257},{130,2},{2... | collective-permute-start | bytes 24584 | tf_op jit(solution)/shard_map/ppermute | solution.py:21
  28.2 34.1 %all-to-all-start = ((f32[128,1,1028]{2,1,0:T(1,128)}), f32[128,1,1028]{2,1,0:T(1,128)S(1)}, u32[]{:S(2)}, u32[]{:S(2)}) async-start(f32[128,1,1028]{2,1,0:T(1,128)} %copy.98), calls=%async_computation | async-start | bytes 1179648 | tf_op jit(solution)/shard_map/all_to_all | solution.py:149
  40.3 1.7 %copy-start.7 = (f32[32,2,1024]{2,1,0:T(2,128)S(1)}, f32[32,2,1024]{2,1,0:T(2,128)}, u32[]{:S(2)}) copy-start(f32[32,2,1024]{2,1,0:T(2,128)} %param.12) | copy-start | bytes 786436
  41.1 1.3 %copy-start.8 = (s32[32,256]{1,0:T(8,128)S(1)}, s32[32,256]{1,0:T(8,128)}, u32[]{:S(2)}) copy-start(s32[32,256]{1,0:T(8,128)} %param.13) | copy-start | bytes 98308
  41.1 1.3 %copy-start.9 = (s32[1,1,128,2]{2,3,1,0:T(2,128)S(1)}, s32[1,1,128,2]{2,3,1,0:T(2,128)}, u32[]{:S(2)}) copy-start(s32[1,1,128,2]{2,3,1,0:T(2,128)} %param.15) | copy-start | bytes 3076
  42.0 7.0 %copy-start.3 = (f32[32,256]{1,0:T(8,128)S(1)}, f32[32,256]{1,0:T(8,128)}, u32[]{:S(2)}) copy-start(f32[32,256]{1,0:T(8,128)} %param.11) | copy-start | bytes 98308
  42.5 12.5 %copy-start.5 = (f32[32,256]{1,0:T(8,128)}, f32[32,256]{1,0:T(8,128)S(1)}, u32[]{:S(2)}) copy-start(f32[32,256]{1,0:T(8,128)S(1)} %convert_element_type.4) | copy-start | bytes 98308
  43.2 7.2 %slice-start = ((f32[32,32,256]{2,1,0:T(8,128)}), f32[24,32,256]{2,1,0:T(8,128)S(1)}, s32[]{:S(2)}) async-start(f32[32,32,256]{2,1,0:T(8,128)} %param.10), calls=%async_computation.2 | async-start | bytes 1572864 | tf_op jit(solution)/shard_map/slice | solution.py:160
  68.3 8.3 %copy-start.2 = (s32[1,1,128,2]{3,2,1,0:T(8,128)S(1)}, s32[1,1,128,2]{3,2,1,0:T(8,128)}, u32[]{:S(2)}) copy-start(s32[1,1,128,2]{3,2,1,0:T(8,128)} %copy.96) | copy-start | bytes 3076
  68.3 18.2 %copy-start.1 = (f32[32,32,2,128]{3,2,1,0:T(2,128)S(1)}, f32[32,32,2,128]{3,2,1,0:T(2,128)}, u32[]{:S(2)}) copy-start(f32[32,32,2,128]{3,2,1,0:T(2,128)} %reshape.47) | copy-start | bytes 3145732
  77.3 21.4 %all-to-all-start.1 = ((f32[128,1,2]{2,1,0:T(1,128)}), f32[128,1,2]{2,1,0:T(1,128)S(1)}, u32[]{:S(2)}, u32[]{:S(2)}) async-start(f32[128,1,2]{2,1,0:T(1,128)} %bitcast.15), calls=%async_computation.1 | async-start | bytes 131072 | tf_op jit(solution)/shard_map/all_to_all | solution.py:170
  88.8 10.9 %copy-start.6 = (f32[32,256]{1,0:T(8,128)S(1)}, f32[32,256]{1,0:T(8,128)}, u32[]{:S(2)}) copy-start(f32[32,256]{1,0:T(8,128)} %copy-done.5) | copy-start | bytes 98308
  99.8 2.3 %copy-start.4 = (f32[32,256]{1,0:T(8,128)S(1)}, f32[32,256]{1,0:T(8,128)}, u32[]{:S(2)}) copy-start(f32[32,256]{1,0:T(8,128)} %param.11) | copy-start | bytes 98308
  102.5 19.7 %collective-permute-start.6 = (f32[8,32]{1,0:T(8,128)S(1)}, f32[8,32]{1,0:T(8,128)S(1)}, u32[]{:S(2)}, u32[]{:S(2)}) collective-permute-start(f32[8,32]{1,0:T(8,128)S(1)} %get-tuple-element.17), channel_id=1, source_target_pairs={{0,1},{1,2},{2,3},{3,4},{4,5},{5,6},{6,7},{7,8},{8,9},{9,10},{10,1... | collective-permute-start | bytes 3080 | tf_op jit(solution)/shard_map/ppermute | solution.py:21
  105.1 17.3 %collective-permute-start.7 = (f32[8,32]{1,0:T(8,128)S(1)}, f32[8,32]{1,0:T(8,128)S(1)}, u32[]{:S(2)}, u32[]{:S(2)}) collective-permute-start(f32[8,32]{1,0:T(8,128)S(1)} %get-tuple-element.16), channel_id=1, source_target_pairs={{1,0},{2,1},{3,2},{4,3},{5,4},{6,5},{7,6},{8,7},{9,8},{10,9},{11,1... | collective-permute-start | bytes 3080 | tf_op jit(solution)/shard_map/ppermute | solution.py:21
  112.3 10.2 %collective-permute-start.4 = (f32[8,1,256]{2,1,0:T(1,128)S(1)}, f32[8,1,256]{2,1,0:T(1,128)S(1)}, u32[]{:S(2)}, u32[]{:S(2)}) collective-permute-start(f32[8,1,256]{2,1,0:T(1,128)S(1)} %get-tuple-element.31), channel_id=1, source_target_pairs={{0,128},{128,256},{256,384},{1,129},{129,257},{257,385},{2,130},{1... | collective-permute-start | bytes 24584 | tf_op jit(solution)/shard_map/ppermute | solution.py:21
  118.5 5.0 %collective-permute-start.5 = (f32[8,1,256]{2,1,0:T(1,128)S(1)}, f32[8,1,256]{2,1,0:T(1,128)S(1)}, u32[]{:S(2)}, u32[]{:S(2)}) collective-permute-start(f32[8,1,256]{2,1,0:T(1,128)S(1)} %get-tuple-element.30), channel_id=1, source_target_pairs={{128,0},{256,128},{384,256},{129,1},{257,129},{385,257},{130,2},{2... | collective-permute-start | bytes 24584 | tf_op jit(solution)/shard_map/ppermute | solution.py:21

commit v14 on v13

--- a/solution.py
+++ b/solution.py
@@ -172,8 +172,13 @@
     bar, residual_out = lax.optimization_barrier((bar, residual_out))
 
     base = columns(matrices, adjoint_in, True)
-    topbar = bar.reshape(tile_cols, tile_rows, LTOP).transpose(2, 1, 0) * mask_float
-    mixedbar = base + columns(matrices[:, :, :LTOP, :], topbar, True)
+    topbar = bar.reshape(blocks, tile_cols // blocks, tile_rows, LTOP) * mask_float.T.reshape(
+        blocks, tile_cols // blocks, tile_rows, 1
+    )
+    correction = jnp.einsum(
+        "rbji,bcrj->irbc", matrices[:, :, :LTOP, :], topbar, precision=lax.Precision.HIGHEST
+    ).reshape(levels, tile_rows, tile_cols)
+    mixedbar = base + correction
     deepbar = mixedbar[levels - LG :]
     gradient = jnp.concatenate(
         [mixedbar[: levels - LG], deepbar + stencil(conductance * deepbar)], 0

time: 126 us -> 126 us (level)
    dot_general x3 -> x2, matrix products: 6.92 us -> 5.07 us  [columns(): out = jnp.einsum(form, matrices, grouped, precision=lax.Precision.HIGHEST)]
    dot_general x0 -> x1, matrix products: none -> 1.84 us  [per_device(): jnp.einsum('rbji,bcrj->irbc', matrices[:, :, :LTOP, :], topbar, precision...]
    reshape x3 -> x2, local copies, waits for them, and re-layouts: 4.37 us -> 4.3 us  [columns(): grouped = field.reshape(levels, height, blocks, breadth // blocks)]
    unnamed x25 -> x23, local copies, waits for them, and re-layouts: 4.07 us -> 4.06 us
where the time goes in v14:
time: 126 us; the launch traced here: 125 us
  starting transfers between devices  59.7 us (47%)
  local copies, waits for them, and re-layouts  28 us (22%)
  Pallas kernels  12.4 us (10%)
  matrix products  9.16 us (7%)
  waiting for transfers between devices  8.81 us (7%)
  other arithmetic  6.18 us (5%)
    ppermute x4, starting transfers between devices, neighbours(): lax.ppermute(edge_low, axis, backward)  21.5 us
    ppermute x4, starting transfers between devices, neighbours(): lax.ppermute(edge_high, axis, forward)  16.4 us
    all_to_all x1, starting transfers between devices, per_device(): lax.all_to_all(packed, 'lon', split_axis=0, concat_axis=0, tiled=True)  12 us
    all_to_all x1, starting transfers between devices, per_device(): lax.all_to_all(residual, 'lon', split_axis=0, concat_axis=0, tiled=True)  9.79 us
    pallas_call x1, Pallas kernels, scatter(): pl.pallas_call(scatter_kernel, out_shape=jax.ShapeDtypeStruct(top_shape,...  6.23 us
    pallas_call x1, Pallas kernels, predict(): pl.pallas_call(predict_kernel, out_shape=jax.ShapeDtypeStruct((slots, 1,...  6.14 us
    all_to_all x1, waiting for transfers between devices, per_device(): lax.all_to_all(packed, 'lon', split_axis=0, concat_axis=0, tiled=True)  5.79 us
    dot_general x2, matrix products, columns(): out = jnp.einsum(form, matrices, grouped, precision=lax.Precision.HIGHEST)  5.07 us
  transfers between devices with their start and end apart: 10, of which 3 were waited for; matrix products, arithmetic and copies ran while one was open for 22% of the time, Pallas kernels for 5%

profile of v14, /device:TPU:9, one launch (start us, length us, event | category | flops | bytes accessed | tf_op | source)
XLA Modules:
  0.0 125.2 jit_solution(3455396148023760029)
XLA Ops:
  0.6 1.1 fusion.18
  1.7 0.7 copy.122
  2.4 4.6 %collective-permute-start.2 = (f32[8,32]{1,0:T(8,128)}, f32[8,32]{1,0:T(8,128)}, u32[]{:S(2)}, u32[]{:S(2)}) collective-permute-start(f32[8,32]{1,0:T(8,128)} %bitcast.7), channel_id=1, source_target_pairs={{0,1},{1,2},{2,3},{3,4},{4,5},{5,6},{6,7},{7,8},{8,9},{9,10},{10,1... | collective-permute-start | bytes 3080 | tf_op jit(solution)/shard_map/ppermute | solution.py:21
  7.1 0.7 copy.123
  7.8 10.3 %collective-permute-start.3 = (f32[8,32]{1,0:T(8,128)}, f32[8,32]{1,0:T(8,128)}, u32[]{:S(2)}, u32[]{:S(2)}) collective-permute-start(f32[8,32]{1,0:T(8,128)} %bitcast.9), channel_id=1, source_target_pairs={{1,0},{2,1},{3,2},{4,3},{5,4},{6,5},{7,6},{8,7},{9,8},{10,9},{11,1... | collective-permute-start | bytes 3080 | tf_op jit(solution)/shard_map/ppermute | solution.py:21
  18.0 1.5 %fusion.20 = (f32[8,1,256]{2,1,0:T(1,128)}, f32[8,1,256]{2,1,0:T(1,128)}) fusion(f32[32,32,256]{2,1,0:T(8,128)} %param.10), kind=kLoop, calls=%fused_computation.35 | loop fusion | bytes 32768 | tf_op jit(solution)/shard_map/slice | solution.py:27
  19.5 3.0 %collective-permute-start = (f32[8,1,256]{2,1,0:T(1,128)}, f32[8,1,256]{2,1,0:T(1,128)S(1)}, u32[]{:S(2)}, u32[]{:S(2)}) collective-permute-start(f32[8,1,256]{2,1,0:T(1,128)} %get-tuple-element.25), channel_id=1, source_target_pairs={{0,128},{128,256},{256,384},{1,129},{129,257},{257,385},{2,130},{1... | collective-permute-start | bytes 24584 | tf_op jit(solution)/shard_map/ppermute | solution.py:21
  22.6 2.1 %collective-permute-start.1 = (f32[8,1,256]{2,1,0:T(1,128)}, f32[8,1,256]{2,1,0:T(1,128)S(1)}, u32[]{:S(2)}, u32[]{:S(2)}) collective-permute-start(f32[8,1,256]{2,1,0:T(1,128)} %get-tuple-element.24), channel_id=1, source_target_pairs={{128,0},{256,128},{384,256},{129,1},{257,129},{385,257},{130,2},{2... | collective-permute-start | bytes 24584 | tf_op jit(solution)/shard_map/ppermute | solution.py:21
  24.7 1.2 copy.95
  25.9 0.8 concatenate.33
  26.7 1.5 %copy.96 = f32[128,1,1028]{2,1,0:T(1,128)} copy(f32[128,1,1028]{0,2,1:T(8,128)S(1)} %bitcast.39) | data formatting | bytes 1052672 | tf_op jit(solution)/shard_map/all_to_all | solution.py:149
  28.2 12.0 %all-to-all-start = ((f32[128,1,1028]{2,1,0:T(1,128)}), f32[128,1,1028]{2,1,0:T(1,128)S(1)}, u32[]{:S(2)}, u32[]{:S(2)}) async-start(f32[128,1,1028]{2,1,0:T(1,128)} %copy.96), calls=%async_computation | async-start | bytes 1179648 | tf_op jit(solution)/shard_map/all_to_all | solution.py:149
  40.3 0.9 fusion.17
  41.2 0.8 fusion.19
  42.0 0.6 convert_bitcast_fusion
  42.6 0.5 reshape.47
  43.1 0.7 copy.94
  43.8 2.8 %reshape.46 = f32[32,32,2,128]{3,2,1,0:T(2,128)} reshape(f32[32,32,256]{2,1,0:T(8,128)} %param.14) | data formatting | bytes 2097152 | tf_op jit(solution)/shard_map/reshape | solution.py:39
  46.6 1.5 %copy.100 = f32[8,32,1]{2,1,0:T(8,128)} copy(f32[8,32,1]{1,0,2:T(8,128)} %bitcast.8) | data formatting | bytes 2048 | tf_op jit(solution)/shard_map/broadcast_in_dim | solution.py:31
  48.1 1.4 %copy.102 = f32[8,32,1]{2,1,0:T(8,128)} copy(f32[8,32,1]{1,0,2:T(8,128)} %bitcast.10) | data formatting | bytes 2048 | tf_op jit(solution)/shard_map/broadcast_in_dim | solution.py:32
  49.5 1.5 %fusion.8 = f32[8,32,256]{2,1,0:T(8,128)S(1)} fusion(f32[8,31,256]{2,1,0:T(8,128)} %get-tuple-element.23, f32[8,1,256]{2,1,0:T(1,128)S(1)} %collective-permute-done, f32[8,1,256]{2,1,0:T(1,128)S(1)} %collective-permute-done.1, f32[8,31,256]{2,1,0:T(8,128)} %get-tuple-element.22, f32[8,32,255]{2,1,0:T(8,128)} %get-tuple-element.19, f32[8,32,1]{2,1,0:T(8,128)} %copy.100, ...), kind=kLoop, calls=%fused_computation.14 | loop fusion | flops 720896 | bytes 1605632 | tf_op jit(solution)/shard_map/add | solution.py:160
  51.0 0.1 pad_maximum_fusion
  51.1 1.5 %reshape.48 = f32[32,32,2,128]{3,2,1,0:T(2,128)} reshape(f32[32,32,256]{2,1,0:T(8,128)S(1)} %pad_maximum_fusion) | data formatting | bytes 2097152 | tf_op jit(solution)/shard_map/reshape | solution.py:39
  52.6 2.8 %convolution_bitcast_fusion = f32[4,32,2,128]{3,0,2,1:T(4,128)S(1)} fusion(f32[32,32,2,128]{3,2,1,0:T(2,128)} %reshape.48, f32[32,2,32,32]{3,2,1,0:T(8,128)S(1)} %reshape.47), kind=kOutput, calls=%fused_computation.2 | convolution fusion | flops 12582912 | bytes 1310720 | tf_op jit(solution)/shard_map/rbij,jrbc->irbc/dot_general | solution.py:41
  55.4 0.1 copy.104
  55.5 0.1 reshape.49
  55.6 0.1 copy.105
  55.8 0.8 copy.107.top_ref
  56.5 5.8 %all-to-all-done = f32[128,1,1028]{2,1,0:T(1,128)S(1)} async-done(((f32[128,1,1028]{2,1,0:T(1,128)}), f32[128,1,1028]{2,1,0:T(1,128)S(1)}, u32[]{:S(2)}, u32[]{:S(2)}) %all-to-all-start) | async-done | bytes 526368 | tf_op jit(solution)/shard_map/all_to_all | solution.py:149
  62.3 0.9 copy.97
  63.3 0.2 copy.106
  63.5 0.1 reshape.55
  63.6 2.2 %fusion.24 = f32[256,16,32]{0,2,1:T(8,128)S(1)} fusion(f32[256,512,1]{1,0,2:T(8,128)S(1)} %reshape.55, f32[16,32,512]{2,1,0:T(8,128)} %constant.16), kind=kOutput, calls=%fused_computation.39 | convolution fusion | flops 805306368 | bytes 2097152 | tf_op jit(solution)/shard_map/dot_general | solution.py:151
  65.8 2.5 %copy.108.gain_ref = f32[256,16,32]{2,1,0:T(8,128)} copy(f32[256,16,32]{0,2,1:T(8,128)S(1)} %fusion.24) | data formatting | bytes 1048576 | tf_op jit(solution)/shard_map/dot_general | solution.py:151
  68.3 6.1 %shard_map.113 = f32[256,1,128]{2,1,0:T(1,128)} custom-call(s32[128,2]{1,0:T(8,128)} %bitcast.42, f32[256,128]{1,0:T(8,128)} %copy.107.top_ref, f32[256,16,32]{2,1,0:T(8,128)} %copy.108.gain_ref), custom_call_target="tpu_custom_call" | custom-call | tf_op jit(solution)/shard_map/pallas_call | solution.py:99
  74.4 1.9 %reduce_sum.9 = f32[256]{0:T(256)S(1)} reduce(f32[256,1,128]{2,1,0:T(1,128)} %shard_map.113, f32[]{:T(128)} %constant.3.clone.1), dimensions={1,2}, to_apply=%region_0.0 | reduce | flops 32512 | bytes 132100 | tf_op jit(solution)/shard_map/reduce_sum | solution.py:167
  76.4 0.1 reshape.52
  76.6 0.7 fusion.16
  77.3 9.8 %all-to-all-start.1 = ((f32[128,1,2]{2,1,0:T(1,128)}), f32[128,1,2]{2,1,0:T(1,128)S(1)}, u32[]{:S(2)}, u32[]{:S(2)}) async-start(f32[128,1,2]{2,1,0:T(1,128)} %bitcast.15), calls=%async_computation.1 | async-start | bytes 131072 | tf_op jit(solution)/shard_map/all_to_all | solution.py:170
  87.1 2.3 %fusion.2 = f32[32,2,128,32]{2,3,1,0:T(8,128)S(1)} fusion(f32[32,2,32,32]{3,2,1,0:T(8,128)S(1)} %reshape.47, f32[32,32,2,128]{3,2,1,0:T(2,128)S(1)} %copy-done.1), kind=kOutput, calls=%fused_computation.6 | convolution fusion | flops 100663296 | bytes 2359296 | tf_op jit(solution)/shard_map/rbji,jrbc->irbc/dot_general | solution.py:41
  89.4 1.5 %reshape.53.res_ref = f32[256]{0:T(256)} reshape(f32[128,2]{1,0:T(8,128)} %fusion.16) | data formatting | bytes 2048 | tf_op jit(solution)/shard_map/reshape | solution.py:171
  91.0 6.2 %shard_map.114 = f32[256,128]{1,0:T(8,128)} custom-call(s32[128,2]{1,0:T(8,128)} %bitcast.43, f32[256]{0:T(256)} %reshape.53.res_ref, f32[256,16,32]{2,1,0:T(8,128)} %copy.108.gain_ref), custom_call_target="tpu_custom_call" | custom-call | tf_op jit(solution)/shard_map/pallas_call | solution.py:110
  97.2 2.1 %all-to-all-done.1 = f32[128,1,2]{2,1,0:T(1,128)S(1)} async-done(((f32[128,1,2]{2,1,0:T(1,128)}), f32[128,1,2]{2,1,0:T(1,128)S(1)}, u32[]{:S(2)}, u32[]{:S(2)}) %all-to-all-start.1) | async-done | bytes 1056 | tf_op jit(solution)/shard_map/all_to_all | solution.py:170
  99.2 1.0 copy.112
  100.2 0.1 reshape.54
  100.3 0.1 broadcast_multiply_fusion.1
  100.4 1.8 %fusion = f32[32,32,2,128]{3,0,2,1:T(8,128)S(1)} fusion(f32[32,2,128,32]{2,3,1,0:T(8,128)S(1)} %fusion.2, f32[2,128,32,4]{1,0,3,2:T(2,128)S(1)} %broadcast_multiply_fusion.1, f32[32,2,32,32]{3,2,1,0:T(8,128)S(1)} %reshape.47), kind=kOutput, calls=%fused_computation.1 | convolution fusion | flops 12845056 | bytes 2359296 | tf_op jit(solution)/shard_map/rbji,bcrj->irbc/dot_general | solution.py:178
  102.3 0.1 copy.115
  102.4 0.2 slice.104
  102.7 0.1 fusion.21
  102.8 0.2 slice_reduce_fusion
  103.1 2.5 %collective-permute-start.6 = (f32[8,32]{1,0:T(8,128)S(1)}, f32[8,32]{1,0:T(8,128)S(1)}, u32[]{:S(2)}, u32[]{:S(2)}) collective-permute-start(f32[8,32]{1,0:T(8,128)S(1)} %get-tuple-element.17), channel_id=1, source_target_pairs={{0,1},{1,2},{2,3},{3,4},{4,5},{5,6},{6,7},{7,8},{8,9},{9,10},{10,1... | collective-permute-start | bytes 3080 | tf_op jit(solution)/shard_map/ppermute | solution.py:21
  105.6 7.2 %collective-permute-start.7 = (f32[8,32]{1,0:T(8,128)S(1)}, f32[8,32]{1,0:T(8,128)S(1)}, u32[]{:S(2)}, u32[]{:S(2)}) collective-permute-start(f32[8,32]{1,0:T(8,128)S(1)} %get-tuple-element.16), channel_id=1, source_target_pairs={{1,0},{2,1},{3,2},{4,3},{5,4},{6,5},{7,6},{8,7},{9,8},{10,9},{11,1... | collective-permute-start | bytes 3080 | tf_op jit(solution)/shard_map/ppermute | solution.py:21
  112.9 6.1 %collective-permute-start.4 = (f32[8,1,256]{2,1,0:T(1,128)S(1)}, f32[8,1,256]{2,1,0:T(1,128)S(1)}, u32[]{:S(2)}, u32[]{:S(2)}) collective-permute-start(f32[8,1,256]{2,1,0:T(1,128)S(1)} %get-tuple-element.31), channel_id=1, source_target_pairs={{0,128},{128,256},{256,384},{1,129},{129,257},{257,385},{2,130},{1... | collective-permute-start | bytes 24584 | tf_op jit(solution)/shard_map/ppermute | solution.py:21
  119.0 1.9 %collective-permute-start.5 = (f32[8,1,256]{2,1,0:T(1,128)S(1)}, f32[8,1,256]{2,1,0:T(1,128)S(1)}, u32[]{:S(2)}, u32[]{:S(2)}) collective-permute-start(f32[8,1,256]{2,1,0:T(1,128)S(1)} %get-tuple-element.30), channel_id=1, source_target_pairs={{128,0},{256,128},{384,256},{129,1},{257,129},{385,257},{130,2},{2... | collective-permute-start | bytes 24584 | tf_op jit(solution)/shard_map/ppermute | solution.py:21
  121.0 0.1 slice.117
  121.1 0.4 copy.114
  121.5 0.6 slice.102
  122.1 0.6 copy.118
  122.8 0.1 copy.116
  122.9 0.1 copy.117
  123.0 1.0 collective-permute-done.5
  124.0 0.2 fusion.12
  124.2 1.0 pad_maximum_fusion.1
  (36 shorter events, 0.3 us)
Async XLA Ops:
  2.4 44.2 %collective-permute-start.2 = (f32[8,32]{1,0:T(8,128)}, f32[8,32]{1,0:T(8,128)}, u32[]{:S(2)}, u32[]{:S(2)}) collective-permute-start(f32[8,32]{1,0:T(8,128)} %bitcast.7), channel_id=1, source_target_pairs={{0,1},{1,2},{2,3},{3,4},{4,5},{5,6},{6,7},{7,8},{8,9},{9,10},{10,1... | collective-permute-start | bytes 3080 | tf_op jit(solution)/shard_map/ppermute | solution.py:21
  7.8 40.3 %collective-permute-start.3 = (f32[8,32]{1,0:T(8,128)}, f32[8,32]{1,0:T(8,128)}, u32[]{:S(2)}, u32[]{:S(2)}) collective-permute-start(f32[8,32]{1,0:T(8,128)} %bitcast.9), channel_id=1, source_target_pairs={{1,0},{2,1},{3,2},{4,3},{5,4},{6,5},{7,6},{8,7},{9,8},{10,9},{11,1... | collective-permute-start | bytes 3080 | tf_op jit(solution)/shard_map/ppermute | solution.py:21
  19.5 30.0 %collective-permute-start = (f32[8,1,256]{2,1,0:T(1,128)}, f32[8,1,256]{2,1,0:T(1,128)S(1)}, u32[]{:S(2)}, u32[]{:S(2)}) collective-permute-start(f32[8,1,256]{2,1,0:T(1,128)} %get-tuple-element.25), channel_id=1, source_target_pairs={{0,128},{128,256},{256,384},{1,129},{129,257},{257,385},{2,130},{1... | collective-permute-start | bytes 24584 | tf_op jit(solution)/shard_map/ppermute | solution.py:21
  22.6 17.7 %copy-start = (f32[32,32,256]{2,1,0:T(8,128)S(1)}, f32[32,32,256]{2,1,0:T(8,128)}, u32[]{:S(2)}) copy-start(f32[32,32,256]{2,1,0:T(8,128)} %param.10) | copy-start | bytes 3145732
  22.6 26.9 %collective-permute-start.1 = (f32[8,1,256]{2,1,0:T(1,128)}, f32[8,1,256]{2,1,0:T(1,128)S(1)}, u32[]{:S(2)}, u32[]{:S(2)}) collective-permute-start(f32[8,1,256]{2,1,0:T(1,128)} %get-tuple-element.24), channel_id=1, source_target_pairs={{128,0},{256,128},{384,256},{129,1},{257,129},{385,257},{130,2},{2... | collective-permute-start | bytes 24584 | tf_op jit(solution)/shard_map/ppermute | solution.py:21
  26.7 15.2 %copy-start.7 = (s32[32,256]{1,0:T(8,128)S(1)}, s32[32,256]{1,0:T(8,128)}, u32[]{:S(2)}) copy-start(s32[32,256]{1,0:T(8,128)} %param.13) | copy-start | bytes 98308
  28.2 34.1 %all-to-all-start = ((f32[128,1,1028]{2,1,0:T(1,128)}), f32[128,1,1028]{2,1,0:T(1,128)S(1)}, u32[]{:S(2)}, u32[]{:S(2)}) async-start(f32[128,1,1028]{2,1,0:T(1,128)} %copy.96), calls=%async_computation | async-start | bytes 1179648 | tf_op jit(solution)/shard_map/all_to_all | solution.py:149
  40.3 2.3 %copy-start.5 = (f32[32,2,1024]{2,1,0:T(2,128)S(1)}, f32[32,2,1024]{2,1,0:T(2,128)}, u32[]{:S(2)}) copy-start(f32[32,2,1024]{2,1,0:T(2,128)} %param.12) | copy-start | bytes 786436
  41.1 1.9 %copy-start.8 = (s32[1,1,128,2]{2,3,1,0:T(2,128)S(1)}, s32[1,1,128,2]{2,3,1,0:T(2,128)}, u32[]{:S(2)}) copy-start(s32[1,1,128,2]{2,3,1,0:T(2,128)} %param.15) | copy-start | bytes 3076
  42.6 6.9 %copy-start.3 = (f32[32,256]{1,0:T(8,128)S(1)}, f32[32,256]{1,0:T(8,128)}, u32[]{:S(2)}) copy-start(f32[32,256]{1,0:T(8,128)} %param.11) | copy-start | bytes 98308
  43.8 7.2 %slice-start = ((f32[32,32,256]{2,1,0:T(8,128)}), f32[24,32,256]{2,1,0:T(8,128)S(1)}, s32[]{:S(2)}) async-start(f32[32,32,256]{2,1,0:T(8,128)} %param.10), calls=%async_computation.2 | async-start | bytes 1572864 | tf_op jit(solution)/shard_map/slice | solution.py:160
  68.3 8.3 %copy-start.2 = (s32[1,1,128,2]{3,2,1,0:T(8,128)S(1)}, s32[1,1,128,2]{3,2,1,0:T(8,128)}, u32[]{:S(2)}) copy-start(s32[1,1,128,2]{3,2,1,0:T(8,128)} %copy.94) | copy-start | bytes 3076
  68.3 18.8 %copy-start.1 = (f32[32,32,2,128]{3,2,1,0:T(2,128)S(1)}, f32[32,32,2,128]{3,2,1,0:T(2,128)}, u32[]{:S(2)}) copy-start(f32[32,32,2,128]{3,2,1,0:T(2,128)} %reshape.46) | copy-start | bytes 3145732
  76.5 12.8 %copy-start.6 = (f32[256,32]{0,1:T(8,128)S(1)}, f32[256,32]{0,1:T(8,128)}, u32[]{:S(2)}) copy-start(f32[256,32]{0,1:T(8,128)} %get-tuple-element.32) | copy-start | bytes 98308
  77.3 22.0 %all-to-all-start.1 = ((f32[128,1,2]{2,1,0:T(1,128)}), f32[128,1,2]{2,1,0:T(1,128)S(1)}, u32[]{:S(2)}, u32[]{:S(2)}) async-start(f32[128,1,2]{2,1,0:T(1,128)} %bitcast.15), calls=%async_computation.1 | async-start | bytes 131072 | tf_op jit(solution)/shard_map/all_to_all | solution.py:170
  100.4 2.3 %copy-start.4 = (f32[32,256]{1,0:T(8,128)S(1)}, f32[32,256]{1,0:T(8,128)}, u32[]{:S(2)}) copy-start(f32[32,256]{1,0:T(8,128)} %param.11) | copy-start | bytes 98308
  103.1 19.7 %collective-permute-start.6 = (f32[8,32]{1,0:T(8,128)S(1)}, f32[8,32]{1,0:T(8,128)S(1)}, u32[]{:S(2)}, u32[]{:S(2)}) collective-permute-start(f32[8,32]{1,0:T(8,128)S(1)} %get-tuple-element.17), channel_id=1, source_target_pairs={{0,1},{1,2},{2,3},{3,4},{4,5},{5,6},{6,7},{7,8},{8,9},{9,10},{10,1... | collective-permute-start | bytes 3080 | tf_op jit(solution)/shard_map/ppermute | solution.py:21
  105.6 17.3 %collective-permute-start.7 = (f32[8,32]{1,0:T(8,128)S(1)}, f32[8,32]{1,0:T(8,128)S(1)}, u32[]{:S(2)}, u32[]{:S(2)}) collective-permute-start(f32[8,32]{1,0:T(8,128)S(1)} %get-tuple-element.16), channel_id=1, source_target_pairs={{1,0},{2,1},{3,2},{4,3},{5,4},{6,5},{7,6},{8,7},{9,8},{10,9},{11,1... | collective-permute-start | bytes 3080 | tf_op jit(solution)/shard_map/ppermute | solution.py:21
  112.9 10.2 %collective-permute-start.4 = (f32[8,1,256]{2,1,0:T(1,128)S(1)}, f32[8,1,256]{2,1,0:T(1,128)S(1)}, u32[]{:S(2)}, u32[]{:S(2)}) collective-permute-start(f32[8,1,256]{2,1,0:T(1,128)S(1)} %get-tuple-element.31), channel_id=1, source_target_pairs={{0,128},{128,256},{256,384},{1,129},{129,257},{257,385},{2,130},{1... | collective-permute-start | bytes 24584 | tf_op jit(solution)/shard_map/ppermute | solution.py:21
  119.0 5.0 %collective-permute-start.5 = (f32[8,1,256]{2,1,0:T(1,128)S(1)}, f32[8,1,256]{2,1,0:T(1,128)S(1)}, u32[]{:S(2)}, u32[]{:S(2)}) collective-permute-start(f32[8,1,256]{2,1,0:T(1,128)S(1)} %get-tuple-element.30), channel_id=1, source_target_pairs={{128,0},{256,128},{384,256},{129,1},{257,129},{385,257},{130,2},{2... | collective-permute-start | bytes 24584 | tf_op jit(solution)/shard_map/ppermute | solution.py:21
